TPU v7x, 32 devices: a whole 2x2x4 slice. The times are simulated.
32 devices in a mesh: gz: 4 (over x, core), gy: 4 (over z), gx: 2 (over y).
Axes of the slice: x: 2, y: 2, z: 4, core: 2. Of those that a mesh axis runs over, the one named last changes fastest.
Arguments:
- volume: bfloat16 [32, 4, 32, 384], P('gz', 'gy', 'gx'), may hold values from -80 to 80
- cotangent: bfloat16 [32, 4, 32, 384], P('gz', 'gy', 'gx'), may hold values from -6 to 6
- w_project: bfloat16 [3, 384, 1152], P(None, 'gy', ('gz', 'gx')), may hold values from -0.3125 to 0.3125
- w_output: bfloat16 [3, 384, 384], P(None, 'gy', ('gz', 'gx')), may hold values from -0.3125 to 0.3125
Outputs:
- grad_volume: bfloat16 [32, 4, 32, 384], P('gz', 'gy', 'gx')
All inputs are finite; a program needn't handle non-finite values.
Results may differ from a plain program's by a relative error of at most 0.015.
Values may be sent and summed in bfloat16 or wider, within the bound.
No kernel may reach another device: no remote copies, remote signals or barrier semaphores. Data moves between devices by JAX's collectives and lax.ppermute only.
A program may use at most 64 MiB of HBM per device.

v0:
```python
import jax
import jax.numpy as jnp
from jax import lax
from jax.sharding import PartitionSpec as P

HEADS = 6


def head_norm(vector):
    return (vector * lax.rsqrt(jnp.mean(vector * vector, axis=-1, keepdims=True) + 1e-06)).astype(
        jnp.bfloat16
    )


def sublayer(line_rows, w_inner, w_outer):
    feat_len = line_rows.shape[-1]
    head_size = feat_len // HEADS
    stream = line_rows.astype(jnp.float32)
    normed = (stream * lax.rsqrt(jnp.mean(stream * stream, axis=-1, keepdims=True) + 1e-06)).astype(
        jnp.bfloat16
    )
    packed = jnp.dot(normed, w_inner, preferred_element_type=jnp.float32)
    head_shape = line_rows.shape[:3] + (HEADS, head_size)
    queries = head_norm(packed[..., :feat_len].reshape(head_shape))
    key_part = head_norm(packed[..., feat_len : 2 * feat_len].reshape(head_shape))
    value_part = packed[..., 2 * feat_len :].reshape(head_shape).astype(jnp.bfloat16)
    scores = jnp.einsum(
        "plqhe,pkqhe->pqhlk", queries, key_part, preferred_element_type=jnp.float32
    ) * head_size ** (-0.5)
    powers = jnp.exp(scores)
    attn_weights = (powers / jnp.sum(powers, axis=-1, keepdims=True)).astype(jnp.bfloat16)
    mixed_out = jnp.einsum(
        "pqhlk,pkqhe->plqhe", attn_weights, value_part, preferred_element_type=jnp.float32
    )
    mixed_out = mixed_out.astype(jnp.bfloat16).reshape(line_rows.shape)
    update = jnp.dot(mixed_out, w_outer, preferred_element_type=jnp.float32)
    return (stream + update).astype(jnp.bfloat16)


def along_depth(member, w_inner, w_outer):
    depth_len, row_len, rest_len, feat_len = member.shape
    flat_lines = member.reshape(1, depth_len, row_len * rest_len, feat_len)
    return sublayer(flat_lines, w_inner, w_outer).reshape(member.shape)


def along_rows(member, w_inner, w_outer):
    return sublayer(member, w_inner, w_outer)


def along_columns(member, w_inner, w_outer):
    depth_len, row_len, col_len, feat_len = member.shape
    flat_lines = member.reshape(depth_len * row_len, col_len, 1, feat_len)
    return sublayer(flat_lines, w_inner, w_outer).reshape(member.shape)


def backward_pass(local_fn, activ_lines, grad_lines):
    _, pullback = jax.vjp(local_fn, activ_lines)
    return pullback(grad_lines)[0]


def depth_out(stacked):
    return lax.all_to_all(stacked, "gz", split_axis=3, concat_axis=1, tiled=True)


def depth_in(stacked):
    return lax.all_to_all(stacked, "gz", split_axis=1, concat_axis=3, tiled=True)


def rows_out(stacked):
    return lax.all_to_all(stacked, "gy", split_axis=3, concat_axis=2, tiled=True)


def rows_in(stacked):
    return lax.all_to_all(stacked, "gy", split_axis=2, concat_axis=3, tiled=True)


def columns_out(stacked):
    return lax.all_to_all(stacked, "gx", split_axis=1, concat_axis=3, tiled=True)


def columns_in(stacked):
    return lax.all_to_all(stacked, "gx", split_axis=3, concat_axis=1, tiled=True)


def local(volume, cotangent, w_project, w_output):
    part_proj, part_outp = (
        lax.all_gather(w_project, "gy", axis=1, tiled=True),
        lax.all_gather(w_output, "gy", axis=1, tiled=True),
    )
    proj_full, outp_full = (
        lax.all_gather(part_proj, ("gz", "gx"), axis=2, tiled=True),
        lax.all_gather(part_outp, ("gz", "gx"), axis=2, tiled=True),
    )

    def depth_fn(member):
        return along_depth(member, proj_full[0], outp_full[0])

    def row_fn(member):
        return along_rows(member, proj_full[1], outp_full[1])

    def column_fn(member):
        return along_columns(member, proj_full[2], outp_full[2])

    depth_act = depth_out(volume[None])[0]
    field_one = depth_in(depth_fn(depth_act)[None])[0]
    row_act = rows_out(field_one[None])[0]
    field_two = rows_in(row_fn(row_act)[None])[0]
    paired = columns_out(jnp.stack([cotangent, field_two]))
    grad_two = columns_in(backward_pass(column_fn, paired[1], paired[0])[None])[0]
    row_grad = rows_out(grad_two[None])[0]
    grad_one = rows_in(backward_pass(row_fn, row_act, row_grad)[None])[0]
    depth_grad = depth_out(grad_one[None])[0]
    grad_zero = depth_in(backward_pass(depth_fn, depth_act, depth_grad)[None])[0]
    return grad_zero


def solution(mesh):
    return jax.shard_map(
        local,
        mesh=mesh,
        in_specs=(
            P("gz", "gy", "gx", None),
            P("gz", "gy", "gx", None),
            P(None, "gy", ("gz", "gx")),
            P(None, "gy", ("gz", "gx")),
        ),
        out_specs=P("gz", "gy", "gx", None),
        check_vma=False,
    )
```

profile of v0, /device:TPU:0, one launch (start us, length us, event | category | flops | bytes accessed | tf_op | source)
XLA Modules:
  0.0 244.8 jit_solution(7430313849005049411)
XLA Ops:
  6.5 1.1 copy.364
  7.6 21.3 %all_gather.12 = bf16[3,384,144]{2,0,1:T(4,128)(2,1)S(1)} all-gather(bf16[3,96,144]{2,0,1:T(4,128)(2,1)S(1)} %copy.364), channel_id=1, replica_groups=mesh['gz'=4,'gy'=4,'gx'=2] {'gy'}, dimensions={1}, use_global_device_ids=true | all-gather | bytes 414720 | tf_op jit(solution)/shard_map/all_gather | solution.py:87
  28.9 1.3 copy.365
  31.0 3.3 %all-to-all-start = ((bf16[1,8,1,16,384]{4,1,2,0,3:T(8,128)(2,1)}), bf16[1,8,1,16,384]{4,1,2,0,3:T(8,128)(2,1)S(1)}, u32[]{:S(2)}, u32[]{:S(2)}) async-start(bf16[1,8,1,16,384]{4,1,2,0,3:T(8,128)(2,1)} %bitcast.315), calls=%async_computation | async-start | bytes 196608 | tf_op jit(solution)/shard_map/all_to_all | solution.py:62
  34.4 15.0 %all_gather.14 = bf16[3,384,48]{2,0,1:T(4,128)(2,1)S(1)} all-gather(bf16[3,96,48]{2,0,1:T(4,128)(2,1)S(1)} %copy.376), channel_id=1, replica_groups=mesh['gz'=4,'gy'=4,'gx'=2] {'gy'}, dimensions={1}, use_global_device_ids=true | all-gather | bytes 138240 | tf_op jit(solution)/shard_map/all_gather | solution.py:88
  49.7 20.0 %all_gather.15 = bf16[3,384,384]{1,2,0:T(8,128)(2,1)S(1)} all-gather(bf16[3,384,48]{1,2,0:T(8,128)(2,1)S(1)} %copy.377), channel_id=1, replica_groups=mesh['gz'=4,'gy'=4,'gx'=2] {'gz','gx'}, dimensions={2}, use_global_device_ids=true | all-gather | bytes 995328 | tf_op jit(solution)/shard_map/all_gather | solution.py:92
  70.4 1.6 convolution_bitcast_fusion.1
  76.5 7.0 %all_to_all.132 = bf16[1,32,1,4,384]{4,3,2,0,1:T(4,128)(2,1)S(1)} all-to-all(bf16[1,32,1,4,384]{4,3,2,0,1:T(4,128)(2,1)S(1)} %copy.379), channel_id=1, replica_groups=mesh['gz'=4,'gy'=4,'gx'=2] {'gz'}, dimensions={1} | all-to-all | bytes 196608 | tf_op jit(solution)/shard_map/all_to_all | solution.py:66
  83.6 8.7 %all_to_all.133 = bf16[1,8,1,16,384]{4,1,2,0,3:T(8,128)(2,1)S(1)} all-to-all(bf16[1,8,1,16,384]{4,1,2,0,3:T(8,128)(2,1)S(1)} %bitcast.338), channel_id=1, replica_groups=mesh['gz'=4,'gy'=4,'gx'=2] {'gy'}, dimensions={3} | all-to-all | bytes 196608 | tf_op jit(solution)/shard_map/all_to_all | solution.py:70
  93.1 1.6 fusion.30
  96.1 0.9 multiply_convert_fusion.4
  98.3 1.6 fusion.120
  102.1 8.2 %all_to_all.134 = bf16[1,8,4,4,384]{4,1,3,0,2:T(8,128)(2,1)S(1)} all-to-all(bf16[1,8,4,4,384]{4,1,3,0,2:T(8,128)(2,1)S(1)} %fusion.28), channel_id=1, replica_groups=mesh['gz'=4,'gy'=4,'gx'=2] {'gy'}, dimensions={2} | all-to-all | bytes 196608 | tf_op jit(solution)/shard_map/all_to_all | solution.py:74
  110.3 0.9 pad_maximum_fusion
  111.2 7.2 %all_to_all.135 = bf16[2,8,1,16,384]{4,3,2,0,1:T(8,128)(2,1)S(1)} all-to-all(bf16[2,8,1,16,384]{4,3,2,0,1:T(8,128)(2,1)S(1)} %pad_maximum_fusion), channel_id=1, replica_groups=mesh['gz'=4,'gy'=4,'gx'=2] {'gx'}, dimensions={1} | all-to-all | bytes 393216 | tf_op jit(solution)/shard_map/all_to_all | solution.py:78
  119.4 1.6 convolution_bitcast_fusion
  122.5 1.0 reshape.732
  123.5 0.8 multiply_reduce_fusion.1
  124.3 0.9 copy.399
  126.6 1.9 reshape.731
  128.5 1.8 reshape.734
  130.3 1.9 multiply_reduce_fusion
  132.2 1.5 copy.401
  135.8 1.8 reshape.733
  137.6 1.7 convolution_convert_fusion.17
  139.4 1.8 reshape.729
  141.1 1.8 convert_element_type.402
  142.9 1.3 multiply_convert_fusion.1
  144.2 1.2 multiply_convert_fusion
  145.8 1.9 fusion.21
  147.9 1.7 multiply_reduce_fusion.10
  149.6 1.6 multiply_reduce_fusion.11
  151.3 1.7 copy.406
  153.0 1.8 reshape.735
  156.3 1.4 add_add_fusion.5
  157.7 1.0 copy.415
  158.7 1.8 reshape.736
  160.6 1.3 add_add_fusion.4
  162.1 0.8 reshape.737
  162.9 1.9 multiply_reduce_fusion.14
  164.8 1.1 fusion.89
  166.0 6.7 %all_to_all.136 = bf16[1,4,1,32,384]{4,1,2,0,3:T(4,128)(2,1)S(1)} all-to-all(bf16[1,4,1,32,384]{4,1,2,0,3:T(4,128)(2,1)S(1)} %copy.424), channel_id=1, replica_groups=mesh['gz'=4,'gy'=4,'gx'=2] {'gx'}, dimensions={3} | all-to-all | bytes 196608 | tf_op jit(solution)/shard_map/all_to_all | solution.py:82
  173.3 1.6 all_to_all.112
  174.9 3.9 %all-to-all-start.6 = ((bf16[1,8,1,16,384]{4,1,2,0,3:T(8,128)(2,1)}), bf16[1,8,1,16,384]{4,1,2,0,3:T(8,128)(2,1)}, u32[]{:S(2)}, u32[]{:S(2)}) async-start(bf16[1,8,1,16,384]{4,1,2,0,3:T(8,128)(2,1)} %all_to_all.112), calls=%async_computation.6 | async-start | bytes 196608 | tf_op jit(solution)/shard_map/all_to_all | solution.py:70
  179.5 5.2 %all-to-all-done.6 = bf16[1,8,1,16,384]{4,1,2,0,3:T(8,128)(2,1)} async-done(((bf16[1,8,1,16,384]{4,1,2,0,3:T(8,128)(2,1)}), bf16[1,8,1,16,384]{4,1,2,0,3:T(8,128)(2,1)}, u32[]{:S(2)}, u32[]{:S(2)}) %all-to-all-start.6) | async-done | bytes 98336 | tf_op jit(solution)/shard_map/all_to_all | solution.py:70
  184.7 1.7 convolution_convert_fusion.15
  186.4 1.8 reshape.740
  188.2 2.1 fusion.14
  190.3 1.6 multiply_reduce_fusion.9
  192.2 1.1 fusion.61
  194.7 0.9 multiply_multiply_fusion.4
  196.4 1.3 add_add_fusion.3
  197.7 1.1 fusion.48
  199.2 2.0 add_add_fusion.2
  201.2 1.0 copy.427
  202.4 1.1 copy.446
  204.6 1.7 multiply_reduce_fusion.13
  206.4 1.7 fusion.88
  208.0 3.9 %all-to-all-start.7 = ((bf16[1,8,4,4,384]{4,1,3,0,2:T(8,128)(2,1)}), bf16[1,8,4,4,384]{4,1,3,0,2:T(8,128)(2,1)}, u32[]{:S(2)}, u32[]{:S(2)}) async-start(bf16[1,8,4,4,384]{4,1,3,0,2:T(8,128)(2,1)} %fusion.88), calls=%async_computation.7 | async-start | bytes 196608 | tf_op jit(solution)/shard_map/all_to_all | solution.py:74
  212.1 5.8 %all-to-all-done.7 = bf16[1,8,4,4,384]{4,1,3,0,2:T(8,128)(2,1)} async-done(((bf16[1,8,4,4,384]{4,1,3,0,2:T(8,128)(2,1)}), bf16[1,8,4,4,384]{4,1,3,0,2:T(8,128)(2,1)}, u32[]{:S(2)}, u32[]{:S(2)}) %all-to-all-start.7) | async-done | bytes 98336 | tf_op jit(solution)/shard_map/all_to_all | solution.py:74
  217.9 3.5 %all-to-all-start.8 = ((bf16[1,8,1,16,384]{4,1,2,0,3:T(8,128)(2,1)}), bf16[1,8,1,16,384]{4,1,2,0,3:T(8,128)(2,1)S(1)}, u32[]{:S(2)}, u32[]{:S(2)}) async-start(bf16[1,8,1,16,384]{4,1,2,0,3:T(8,128)(2,1)} %bitcast.68), calls=%async_computation.8 | async-start | bytes 196608 | tf_op jit(solution)/shard_map/all_to_all | solution.py:62
  221.5 4.0 %all-to-all-done.8 = bf16[1,8,1,16,384]{4,1,2,0,3:T(8,128)(2,1)S(1)} async-done(((bf16[1,8,1,16,384]{4,1,2,0,3:T(8,128)(2,1)}), bf16[1,8,1,16,384]{4,1,2,0,3:T(8,128)(2,1)S(1)}, u32[]{:S(2)}, u32[]{:S(2)}) %all-to-all-start.8) | async-done | bytes 98336 | tf_op jit(solution)/shard_map/all_to_all | solution.py:62
  228.8 1.6 fusion.56
  230.6 6.7 %all_to_all.137 = bf16[1,32,1,4,384]{4,3,2,0,1:T(4,128)(2,1)S(1)} all-to-all(bf16[1,32,1,4,384]{4,3,2,0,1:T(4,128)(2,1)S(1)} %copy.469), channel_id=1, replica_groups=mesh['gz'=4,'gy'=4,'gx'=2] {'gz'}, dimensions={1} | all-to-all | bytes 196608 | tf_op jit(solution)/shard_map/all_to_all | solution.py:66
  (213 shorter events, 29.3 us)
Async XLA Ops:
  6.5 23.8 %copy-start.38 = (bf16[8,1,16,384]{3,2,1,0:T(8,128)(2,1)S(1)}, bf16[8,1,16,384]{3,2,1,0:T(8,128)(2,1)}, u32[]{:S(2)}) copy-start(bf16[8,1,16,384]{3,2,1,0:T(8,128)(2,1)} %param.4) | copy-start | bytes 294916
  6.5 27.8 %copy-start.42 = (bf16[3,96,48]{1,2,0:T(8,128)(2,1)S(1)}, bf16[3,96,48]{1,2,0:T(8,128)(2,1)}, u32[]{:S(2)}) copy-start(bf16[3,96,48]{1,2,0:T(8,128)(2,1)} %param.7) | copy-start | bytes 82948
  6.5 63.9 %all-gather.2.cloned.1.call-start = ((), (), s32[]{:S(2)}) async-start(), calls=%async_computation.10 | async-start | bytes 2985984 | tf_op jit(solution)/shard_map/all_gather | solution.py:91
  31.0 38.7 %all-to-all-start = ((bf16[1,8,1,16,384]{4,1,2,0,3:T(8,128)(2,1)}), bf16[1,8,1,16,384]{4,1,2,0,3:T(8,128)(2,1)S(1)}, u32[]{:S(2)}, u32[]{:S(2)}) async-start(bf16[1,8,1,16,384]{4,1,2,0,3:T(8,128)(2,1)} %bitcast.315), calls=%async_computation | async-start | bytes 196608 | tf_op jit(solution)/shard_map/all_to_all | solution.py:62
  69.7 6.5 %copy-start.1 = (bf16[1,8,1,16,384]{4,1,2,0,3:T(8,128)(2,1)}, bf16[1,8,1,16,384]{4,1,2,0,3:T(8,128)(2,1)S(1)}, u32[]{:S(2)}) copy-start(bf16[1,8,1,16,384]{4,1,2,0,3:T(8,128)(2,1)S(1)} %all-to-all-done) | copy-start | bytes 294916
  72.8 3.1 %copy-start.11 = (bf16[32,4,6,64]{3,2,0,1:T(8,128)(2,1)}, bf16[32,4,6,64]{3,2,0,1:T(8,128)(2,1)S(1)}, u32[]{:S(2)}) copy-start(bf16[32,4,6,64]{3,2,0,1:T(8,128)(2,1)S(1)} %convert_element_type.371) | copy-start | bytes 294916
  73.1 0.6 copy-start.33
  74.1 2.4 copy-start.35
  74.1 2.3 copy-start.31
  74.6 1.3 copy-start.15
  74.6 1.3 copy-start.17
  74.9 0.8 copy-start.7
  74.9 19.8 %copy-start.40 = (f32[4,6,32]{2,1,0:T(8,128)}, f32[4,6,32]{2,1,0:T(8,128)S(1)}, u32[]{:S(2)}) copy-start(f32[4,6,32]{2,1,0:T(8,128)S(1)} %get-tuple-element.25) | copy-start | bytes 9220
  92.3 9.5 %copy-start.3 = (bf16[1,8,1,16,384]{4,1,2,0,3:T(8,128)(2,1)}, bf16[1,8,1,16,384]{4,1,2,0,3:T(8,128)(2,1)S(1)}, u32[]{:S(2)}) copy-start(bf16[1,8,1,16,384]{4,1,2,0,3:T(8,128)(2,1)S(1)} %all_to_all.133) | copy-start | bytes 294916
  95.0 5.9 %copy-start.26 = (bf16[8,4,4,6,64]{4,3,0,2,1:T(8,128)(2,1)}, bf16[8,4,4,6,64]{4,3,0,2,1:T(8,128)(2,1)S(1)}, u32[]{:S(2)}) copy-start(bf16[8,4,4,6,64]{4,3,0,2,1:T(8,128)(2,1)S(1)} %convert_element_type.384) | copy-start | bytes 294916
  95.3 0.6 copy-start.25
  96.1 0.9 copy-start.24
  97.3 0.6 copy-start.22
  98.1 2.7 %copy-start.20 = (f32[8,4,4,6]{0,3,2,1:T(8,128)}, f32[8,4,4,6]{0,3,2,1:T(8,128)S(1)}, u32[]{:S(2)}) copy-start(f32[8,4,4,6]{0,3,2,1:T(8,128)S(1)} %copy.384) | copy-start | bytes 9220
  98.3 3.0 %copy-start.28 = (bf16[8,4,4,6,64]{4,0,3,2,1:T(8,128)(2,1)}, bf16[8,4,4,6,64]{4,0,3,2,1:T(8,128)(2,1)S(1)}, u32[]{:S(2)}) copy-start(bf16[8,4,4,6,64]{4,0,3,2,1:T(8,128)(2,1)S(1)} %multiply_convert_fusion.5) | copy-start | bytes 294916
  100.0 0.8 copy-start.5
  100.0 0.9 copy-start.9
  100.9 0.7 copy-start.30
  142.9 4.7 %copy-start.13 = (bf16[4,32,1,6,64]{4,3,1,0,2:T(8,128)(2,1)S(1)}, bf16[4,32,1,6,64]{4,3,1,0,2:T(8,128)(2,1)}, u32[]{:S(2)}) copy-start(bf16[4,32,1,6,64]{4,3,1,0,2:T(8,128)(2,1)} %reshape.729) | copy-start | bytes 294916
  142.9 4.7 %copy-start.14 = (bf16[4,32,6,64]{3,2,1,0:T(8,128)(2,1)S(1)}, bf16[4,32,6,64]{3,2,1,0:T(8,128)(2,1)}, u32[]{:S(2)}) copy-start(bf16[4,32,6,64]{3,2,1,0:T(8,128)(2,1)} %convert_element_type.402) | copy-start | bytes 294916
  145.8 3.8 %copy-start = (f32[4,32,1,6,64]{4,3,1,0,2:T(8,128)S(1)}, f32[4,32,1,6,64]{4,3,1,0,2:T(8,128)}, u32[]{:S(2)}) copy-start(f32[4,32,1,6,64]{4,3,1,0,2:T(8,128)} %reshape.734) | copy-start | bytes 589828
  147.9 6.9 %copy-start.37 = (f32[4,32,6]{1,0,2:T(4,128)S(1)}, f32[4,32,6]{1,0,2:T(4,128)}, u32[]{:S(2)}) copy-start(f32[4,32,6]{1,0,2:T(4,128)} %copy.401) | copy-start | bytes 9220
  156.2 4.3 %copy-start.39 = (f32[4,32,6]{1,2,0:T(8,128)S(1)}, f32[4,32,6]{1,2,0:T(8,128)}, u32[]{:S(2)}) copy-start(f32[4,32,6]{1,2,0:T(8,128)} %copy.418) | copy-start | bytes 9220
  162.9 15.9 %copy-start.10 = (f32[8,4,6,4]{3,2,1,0:T(8,128)S(1)}, f32[8,4,6,4]{3,2,1,0:T(8,128)}, u32[]{:S(2)}) copy-start(f32[8,4,6,4]{3,2,1,0:T(8,128)} %copy-done.9) | copy-start | bytes 9220
  162.9 27.4 %copy-start.6 = (f32[8,4,6,4,4]{3,4,2,1,0:T(4,128)S(1)}, f32[8,4,6,4,4]{3,4,2,1,0:T(4,128)}, u32[]{:S(2)}) copy-start(f32[8,4,6,4,4]{3,4,2,1,0:T(4,128)} %copy-done.5) | copy-start | bytes 36868
  174.9 9.8 %all-to-all-start.6 = ((bf16[1,8,1,16,384]{4,1,2,0,3:T(8,128)(2,1)}), bf16[1,8,1,16,384]{4,1,2,0,3:T(8,128)(2,1)}, u32[]{:S(2)}, u32[]{:S(2)}) async-start(bf16[1,8,1,16,384]{4,1,2,0,3:T(8,128)(2,1)} %all_to_all.112), calls=%async_computation.6 | async-start | bytes 196608 | tf_op jit(solution)/shard_map/all_to_all | solution.py:70
  188.2 3.9 %copy-start.27 = (bf16[8,4,4,6,64]{4,0,3,2,1:T(8,128)(2,1)S(1)}, bf16[8,4,4,6,64]{4,0,3,2,1:T(8,128)(2,1)}, u32[]{:S(2)}) copy-start(bf16[8,4,4,6,64]{4,0,3,2,1:T(8,128)(2,1)} %multiply_convert_fusion.4) | copy-start | bytes 294916
  188.2 5.1 %copy-start.29 = (bf16[8,4,4,6,64]{4,0,3,2,1:T(8,128)(2,1)S(1)}, bf16[8,4,4,6,64]{4,0,3,2,1:T(8,128)(2,1)}, u32[]{:S(2)}) copy-start(bf16[8,4,4,6,64]{4,0,3,2,1:T(8,128)(2,1)} %copy-done.28) | copy-start | bytes 294916
  192.2 6.8 %copy-start.23 = (f32[8,4,4,6]{3,0,2,1:T(8,128)S(1)}, f32[8,4,4,6]{3,0,2,1:T(8,128)}, u32[]{:S(2)}) copy-start(f32[8,4,4,6]{3,0,2,1:T(8,128)} %copy-done.22) | copy-start | bytes 9220
  192.2 7.0 %copy-start.21 = (f32[8,4,4,6]{0,3,2,1:T(8,128)S(1)}, f32[8,4,4,6]{0,3,2,1:T(8,128)}, u32[]{:S(2)}) copy-start(f32[8,4,4,6]{0,3,2,1:T(8,128)} %copy-done.20) | copy-start | bytes 9220
  193.7 0.7 copy-start.19
  199.2 5.4 %copy-start.4 = (bf16[1,8,1,16,384]{4,1,2,0,3:T(8,128)(2,1)S(1)}, bf16[1,8,1,16,384]{4,1,2,0,3:T(8,128)(2,1)}, u32[]{:S(2)}) copy-start(bf16[1,8,1,16,384]{4,1,2,0,3:T(8,128)(2,1)} %copy-done.3) | copy-start | bytes 294916
  202.4 3.9 %copy-start.44 = (f32[8,16]{0,1:T(8,128)S(1)}, f32[8,16]{0,1:T(8,128)}, u32[]{:S(2)}) copy-start(f32[8,16]{0,1:T(8,128)} %get-tuple-element.17) | copy-start | bytes 1540
  203.5 8.5 %copy-start.43 = (f32[4,8,4]{1,0,2:T(4,128)S(1)}, f32[4,8,4]{1,0,2:T(4,128)}, u32[]{:S(2)}) copy-start(f32[4,8,4]{1,0,2:T(4,128)} %get-tuple-element.13) | copy-start | bytes 1540
  203.5 17.9 %copy-start.41 = (f32[4,6,32]{2,1,0:T(8,128)S(1)}, f32[4,6,32]{2,1,0:T(8,128)}, u32[]{:S(2)}) copy-start(f32[4,6,32]{2,1,0:T(8,128)} %copy-done.40) | copy-start | bytes 9220
  203.5 17.9 %copy-start.32 = (f32[32,4,6]{0,1,2:T(4,128)S(1)}, f32[32,4,6]{0,1,2:T(4,128)}, u32[]{:S(2)}) copy-start(f32[32,4,6]{0,1,2:T(4,128)} %copy-done.31) | copy-start | bytes 9220
  204.4 21.5 %copy-start.8 = (f32[4,6,32,32]{2,3,1,0:T(8,128)S(1)}, f32[4,6,32,32]{2,3,1,0:T(8,128)}, u32[]{:S(2)}) copy-start(f32[4,6,32,32]{2,3,1,0:T(8,128)} %copy-done.7) | copy-start | bytes 294916
  204.6 21.5 %copy-start.12 = (bf16[32,4,6,64]{3,2,0,1:T(8,128)(2,1)S(1)}, bf16[32,4,6,64]{3,2,0,1:T(8,128)(2,1)}, u32[]{:S(2)}) copy-start(bf16[32,4,6,64]{3,2,0,1:T(8,128)(2,1)} %copy-done.11) | copy-start | bytes 294916
  206.3 20.0 %copy-start.18 = (bf16[32,4,6,64]{3,2,0,1:T(8,128)(2,1)S(1)}, bf16[32,4,6,64]{3,2,0,1:T(8,128)(2,1)}, u32[]{:S(2)}) copy-start(bf16[32,4,6,64]{3,2,0,1:T(8,128)(2,1)} %copy-done.17) | copy-start | bytes 294916
  208.0 9.8 %all-to-all-start.7 = ((bf16[1,8,4,4,384]{4,1,3,0,2:T(8,128)(2,1)}), bf16[1,8,4,4,384]{4,1,3,0,2:T(8,128)(2,1)}, u32[]{:S(2)}, u32[]{:S(2)}) async-start(bf16[1,8,4,4,384]{4,1,3,0,2:T(8,128)(2,1)} %fusion.88), calls=%async_computation.7 | async-start | bytes 196608 | tf_op jit(solution)/shard_map/all_to_all | solution.py:74
  217.9 7.6 %all-to-all-start.8 = ((bf16[1,8,1,16,384]{4,1,2,0,3:T(8,128)(2,1)}), bf16[1,8,1,16,384]{4,1,2,0,3:T(8,128)(2,1)S(1)}, u32[]{:S(2)}, u32[]{:S(2)}) async-start(bf16[1,8,1,16,384]{4,1,2,0,3:T(8,128)(2,1)} %bitcast.68), calls=%async_computation.8 | async-start | bytes 196608 | tf_op jit(solution)/shard_map/all_to_all | solution.py:62
  225.7 1.1 copy-start.16
  226.3 1.1 copy-start.36
  226.3 1.1 copy-start.34
  227.5 1.3 copy-start.2
Sparse Core Ops, SparseCore 0:
  30.4 30.7 all-gather.1
where the time goes:
time: 247 us; the launch traced here: 245 us
  blocking collectives  101 us (41%)
  local copies, waits for them, and re-layouts  45.4 us (18%)
  matrix products  28.5 us (12%)
  other arithmetic  25.9 us (10%)
  waiting for transfers between devices  15 us (6%)
  starting transfers between devices  14.7 us (6%)
  between operations  14.6 us (6%)
    all_gather x1, blocking collectives, local(): lax.all_gather(w_project, 'gy', axis=1, tiled=True)  21.3 us
    all_gather x1, blocking collectives, local(): lax.all_gather(part_outp, ('gz', 'gx'), axis=2, tiled=True)  20 us
    all_gather x1, blocking collectives, local(): lax.all_gather(w_output, 'gy', axis=1, tiled=True)  15 us
    all_to_all x2, blocking collectives, depth_in(): lax.all_to_all(stacked, 'gz', split_axis=1, concat_axis=3, tiled=True)  13.7 us
    dot_general x6, matrix products, sublayer(): packed = jnp.dot(normed, w_inner, preferred_element_type=jnp.float32)  9.92 us
    all_to_all x1, blocking collectives, rows_out(): lax.all_to_all(stacked, 'gy', split_axis=3, concat_axis=2, tiled=True)  8.69 us
    all_to_all x1, blocking collectives, rows_in(): lax.all_to_all(stacked, 'gy', split_axis=2, concat_axis=3, tiled=True)  8.21 us
    dot_general x9, matrix products, sublayer(): jnp.einsum('plqhe,pkqhe->pqhlk', queries, key_part, preferred_element_typ...  7.53 us
  transfers between devices with their start and end apart: 5, of which 3 were waited for; matrix products, arithmetic and copies ran while one was open for 1% of the time, Pallas kernels for 0%

commit v1 on v0

v1 whole, which is shorter than its diff:
```python
import jax
import jax.numpy as jnp
from jax import lax
from jax.sharding import PartitionSpec as P

HEADS = 6
ALL = ("gz", "gy", "gx")


def head_norm(vector):
    return (vector * lax.rsqrt(jnp.mean(vector * vector, axis=-1, keepdims=True) + 1e-06)).astype(
        jnp.bfloat16
    )


def sublayer(line_rows, w_inner, w_outer):
    feat_len = line_rows.shape[-1]
    head_size = feat_len // HEADS
    stream = line_rows.astype(jnp.float32)
    normed = (stream * lax.rsqrt(jnp.mean(stream * stream, axis=-1, keepdims=True) + 1e-06)).astype(
        jnp.bfloat16
    )
    packed = jnp.dot(normed, w_inner, preferred_element_type=jnp.float32)
    head_shape = line_rows.shape[:3] + (HEADS, head_size)
    queries = head_norm(packed[..., :feat_len].reshape(head_shape))
    key_part = head_norm(packed[..., feat_len : 2 * feat_len].reshape(head_shape))
    value_part = packed[..., 2 * feat_len :].reshape(head_shape).astype(jnp.bfloat16)
    scores = jnp.einsum(
        "plqhe,pkqhe->pqhlk", queries, key_part, preferred_element_type=jnp.float32
    ) * head_size ** (-0.5)
    powers = jnp.exp(scores)
    attn_weights = (powers / jnp.sum(powers, axis=-1, keepdims=True)).astype(jnp.bfloat16)
    mixed_out = jnp.einsum(
        "pqhlk,pkqhe->plqhe", attn_weights, value_part, preferred_element_type=jnp.float32
    )
    mixed_out = mixed_out.astype(jnp.bfloat16).reshape(line_rows.shape)
    update = jnp.dot(mixed_out, w_outer, preferred_element_type=jnp.float32)
    return (stream + update).astype(jnp.bfloat16)


def full_weights(w_project, w_output, index, sizes):
    nz, ny, nx = sizes
    proj, outp = w_project[index], w_output[index]
    din, dproj = proj.shape
    cat = jnp.concatenate([proj, outp], axis=1)
    got = lax.all_gather(cat, ALL, axis=0, tiled=False)
    got = got.reshape(nz, ny, nx, din, cat.shape[1])
    got = jnp.transpose(got, (1, 3, 0, 2, 4)).reshape(ny * din, nz * nx, cat.shape[1])
    w_inner = got[:, :, :dproj].reshape(ny * din, nz * nx * dproj)
    w_outer = got[:, :, dproj:].reshape(ny * din, -1)
    return w_inner, w_outer


def depth_fn(member, w_inner, w_outer):
    depth_len, row_len, rest_len, feat_len = member.shape
    flat_lines = member.reshape(1, depth_len, row_len * rest_len, feat_len)
    return sublayer(flat_lines, w_inner, w_outer).reshape(member.shape)


def plane_fn(plane, w_row, w_col):
    after_rows = sublayer(plane[None], *w_row)[0]
    return sublayer(after_rows[:, :, None, :], *w_col)[:, :, 0, :]


def to_planes(depth_lines, sizes):
    nz, ny, nx = sizes
    z_len, yl, kx, feat = depth_lines.shape
    got = lax.all_to_all(depth_lines, ALL, 0, 0, tiled=True)
    got = got.reshape(nz, ny, nx, yl, kx, feat)
    return jnp.transpose(got, (1, 3, 2, 0, 4, 5)).reshape(ny * yl, nx * nz * kx, feat)


def from_planes(plane, sizes):
    nz, ny, nx = sizes
    rows, cols, feat = plane.shape
    yl, kx = rows // ny, cols // (nx * nz)
    parts = plane.reshape(ny, yl, nx, nz, kx, feat)
    parts = jnp.transpose(parts, (3, 0, 2, 1, 4, 5)).reshape(nz * ny * nx, yl, kx, feat)
    return lax.all_to_all(parts, ALL, 0, 0, tiled=True)


def block_to_plane(block, sizes):
    nz, ny, nx = sizes
    zl, yl, xl, feat = block.shape
    got = lax.all_to_all(block, ("gy", "gx"), 0, 0, tiled=True)
    got = got.reshape(ny, nx, yl, xl, feat)
    return jnp.transpose(got, (0, 2, 1, 3, 4)).reshape(ny * yl, nx * xl, feat)


def local(volume, cotangent, w_project, w_output, sizes):
    w_depth = full_weights(w_project, w_output, 0, sizes)
    w_row = full_weights(w_project, w_output, 1, sizes)
    w_col = full_weights(w_project, w_output, 2, sizes)

    depth_act = lax.all_to_all(volume, "gz", 2, 0, tiled=True)
    cot_plane = block_to_plane(cotangent, sizes)

    field_one, depth_pullback = jax.vjp(lambda m: depth_fn(m, *w_depth), depth_act)
    plane_one = to_planes(field_one, sizes)
    _, plane_pullback = jax.vjp(lambda p: plane_fn(p, w_row, w_col), plane_one)
    grad_plane = plane_pullback(cot_plane)[0]
    grad_one = from_planes(grad_plane, sizes)
    grad_zero = depth_pullback(grad_one)[0]
    return lax.all_to_all(grad_zero, "gz", 0, 2, tiled=True)


def along_rows(member, w_inner, w_outer):
    return sublayer(member, w_inner, w_outer)


def along_columns(member, w_inner, w_outer):
    depth_len, row_len, col_len, feat_len = member.shape
    flat_lines = member.reshape(depth_len * row_len, col_len, 1, feat_len)
    return sublayer(flat_lines, w_inner, w_outer).reshape(member.shape)


def line_swap(stacked, axis, split_axis, concat_axis):
    return lax.all_to_all(stacked, axis, split_axis=split_axis, concat_axis=concat_axis, tiled=True)


def local_general(volume, cotangent, w_project, w_output, sizes):
    w_depth = full_weights(w_project, w_output, 0, sizes)
    w_row = full_weights(w_project, w_output, 1, sizes)
    w_col = full_weights(w_project, w_output, 2, sizes)

    def row_fn(member):
        return along_rows(member, *w_row)

    def column_fn(member):
        return along_columns(member, *w_col)

    depth_act = line_swap(volume, "gz", 2, 0)
    field_one, depth_pullback = jax.vjp(lambda m: depth_fn(m, *w_depth), depth_act)
    field_one = line_swap(field_one, "gz", 0, 2)
    row_act = line_swap(field_one, "gy", 2, 1)
    field_two, row_pullback = jax.vjp(row_fn, row_act)
    field_two = line_swap(field_two, "gy", 1, 2)
    paired = line_swap(jnp.stack([cotangent, field_two]), "gx", 1, 3)
    _, column_pullback = jax.vjp(column_fn, paired[1])
    grad_two = line_swap(column_pullback(paired[0])[0], "gx", 2, 0)
    grad_one = line_swap(row_pullback(line_swap(grad_two, "gy", 2, 1))[0], "gy", 1, 2)
    grad_zero = depth_pullback(line_swap(grad_one, "gz", 2, 0))[0]
    return line_swap(grad_zero, "gz", 0, 2)


def solution(mesh):
    sizes = (mesh.shape["gz"], mesh.shape["gy"], mesh.shape["gx"])

    def body(volume, *rest):
        one_depth = volume.shape[0] * sizes[0] == mesh.size
        return (local if one_depth else local_general)(volume, *rest, sizes)

    return jax.shard_map(
        body,
        mesh=mesh,
        in_specs=(
            P("gz", "gy", "gx", None),
            P("gz", "gy", "gx", None),
            P(None, "gy", ("gz", "gx")),
            P(None, "gy", ("gz", "gx")),
        ),
        out_specs=P("gz", "gy", "gx", None),
        check_vma=False,
    )
```

time: 247 us -> 312 us (1.26)
  waiting for transfers between devices: 15 us -> 146 us
  blocking collectives: 101 us -> 15 us
  local copies, waits for them, and re-layouts: 45.4 us -> 76.9 us
  matrix products: 28.5 us -> 17.5 us
    all_gather x1 -> x3, waiting for transfers between devices: 0.01 us -> 133 us  [full_weights(): got = lax.all_gather(cat, ALL, axis=0, tiled=False)]
    all_gather x3 -> x0, blocking collectives: 56.3 us -> none  [the longest x1 21.3 us: local(): lax.all_gather(w_project, 'gy', axis=1, tiled=True)]
    all_to_all x6 -> x2, blocking collectives: 44.5 us -> 15 us  [the longest x1 8.33 us: local(): depth_act = lax.all_to_all(volume, 'gz', 2, 0, tiled=True)]
    reshape x2 -> x9, local copies, waits for them, and re-layouts: 0.11 us -> 13.2 us  [the longest x3 8.39 us: full_weights(): got = got.reshape(nz, ny, nx, din, cat.shape[1])]
    dot_general x6, matrix products: 9.92 us -> 3.68 us  [sublayer(): packed = jnp.dot(normed, w_inner, preferred_element_type=jnp.float32)]
    slice x0 -> x8, local copies, waits for them, and re-layouts: none -> 5.58 us  [the longest x3 2.57 us: full_weights(): w_outer = got[:, :, dproj:].reshape(ny * din, -1)]
    rsqrt x10 -> x12, local copies, waits for them, and re-layouts: 3.21 us -> 8.07 us  [head_norm(): lax.rsqrt(jnp.mean(vector * vector, axis=-1, keepdims=True) + 1e-06)]
    reduce_sum x4 -> x6, local copies, waits for them, and re-layouts: 2.64 us -> 6.05 us  [head_norm(): jnp.mean(vector * vector, axis=-1, keepdims=True) + 1e-06]
  transfers between devices with their start and end apart: 5 -> 6, of which waited for: 3 -> 5; matrix products, arithmetic and copies ran while one was open for 1% -> 12% of each run, Pallas kernels for 0% -> 0%
where the time goes in v1:
time: 312 us; the launch traced here: 310 us
  waiting for transfers between devices  146 us (47%)
  local copies, waits for them, and re-layouts  76.9 us (25%)
  other arithmetic  27.8 us (9%)
  matrix products  17.5 us (6%)
  blocking collectives  15 us (5%)
  between operations  14.4 us (5%)
  starting transfers between devices  12.2 us (4%)
    all_gather x3, waiting for transfers between devices, full_weights(): got = lax.all_gather(cat, ALL, axis=0, tiled=False)  133 us
    reshape x3, local copies, waits for them, and re-layouts, full_weights(): got = got.reshape(nz, ny, nx, din, cat.shape[1])  8.39 us
    all_to_all x1, blocking collectives, local(): depth_act = lax.all_to_all(volume, 'gz', 2, 0, tiled=True)  8.33 us
    reshape x9, local copies, waits for them, and re-layouts, sublayer(): key_part = head_norm(packed[..., feat_len:2 * feat_len].reshape(head_shape))  8.21 us
    rsqrt x12, local copies, waits for them, and re-layouts, head_norm(): lax.rsqrt(jnp.mean(vector * vector, axis=-1, keepdims=True) + 1e-06)  8.07 us
    all_to_all x1, waiting for transfers between devices, from_planes(): return lax.all_to_all(parts, ALL, 0, 0, tiled=True)  7.56 us
    reshape x9, local copies, waits for them, and re-layouts, sublayer(): queries = head_norm(packed[..., :feat_len].reshape(head_shape))  7.11 us
    all_to_all x1, blocking collectives, local(): return lax.all_to_all(grad_zero, 'gz', 0, 2, tiled=True)  6.67 us
  transfers between devices with their start and end apart: 6, of which 5 were waited for; matrix products, arithmetic and copies ran while one was open for 12% of the time, Pallas kernels for 0%

profile of v1, /device:TPU:0, one launch (start us, length us, event | category | flops | bytes accessed | tf_op | source)
XLA Modules:
  0.0 310.3 jit_solution(6159842277848257346)
XLA Ops:
  7.4 0.8 fusion.120
  11.0 0.9 copy.516
  11.9 8.3 %all_to_all.42 = bf16[8,1,16,384]{3,0,1,2:T(8,128)(2,1)S(1)} all-to-all(bf16[8,1,16,384]{3,0,1,2:T(8,128)(2,1)S(1)} %copy.516), channel_id=1, replica_groups=mesh['gz'=4,'gy'=4,'gx'=2] {'gz'}, dimensions={2} | all-to-all | bytes 196608 | tf_op jit(solution)/shard_map/all_to_all | solution.py:95
  20.3 5.8 %all-to-all-start = ((bf16[8,1,16,384]{3,2,1,0:T(8,128)(2,1)}), bf16[8,1,16,384]{3,2,1,0:T(8,128)(2,1)S(1)}, u32[]{:S(2)}, u32[]{:S(2)}) async-start(bf16[8,1,16,384]{3,2,1,0:T(8,128)(2,1)} %param.5), calls=%async_computation | async-start | bytes 196608 | tf_op jit(solution)/shard_map/all_to_all | solution.py:85
  26.9 41.2 %all-gather.9.cloned.1.call-done = bf16[3072,192]{1,0:T(8,128)(2,1)} async-done(((bf16[96,192]{1,0:T(8,128)(2,1)}), bf16[3072,192]{1,0:T(8,128)(2,1)}) %all-gather.9.cloned.1.call-update) | async-done | bytes 1179664 | tf_op jit(solution)/shard_map/all_gather | solution.py:46
  68.1 2.8 copy.522
  70.9 1.1 reshape.953
  74.0 1.2 reshape.957
  75.3 1.8 convert_element_type.403
  80.3 1.3 fusion.103
  81.6 0.8 copy.527
  82.4 1.2 multiply_convert_fusion.4
  84.0 1.0 fusion.6
  85.7 39.3 %all-gather.11.cloned.1.call-done = bf16[3072,192]{1,0:T(8,128)(2,1)} async-done(((bf16[96,192]{1,0:T(8,128)(2,1)}), bf16[3072,192]{1,0:T(8,128)(2,1)}) %all-gather.11.cloned.1.call-update) | async-done | bytes 1179664 | tf_op jit(solution)/shard_map/all_gather | solution.py:46
  125.0 2.8 copy.538
  127.8 1.1 reshape.963
  129.7 52.1 %all-gather.7.cloned.1.call-done = bf16[3072,192]{1,0:T(8,128)(2,1)} async-done(((bf16[96,192]{1,0:T(8,128)(2,1)}), bf16[3072,192]{1,0:T(8,128)(2,1)}) %all-gather.7.cloned.1.call-update) | async-done | bytes 1179664 | tf_op jit(solution)/shard_map/all_gather | solution.py:46
  181.9 2.8 copy.514
  184.7 1.9 reshape.948
  186.6 1.0 slice.100
  187.6 1.3 slice.97
  191.3 3.7 %all-to-all-start.2 = ((bf16[32,1,4,384]{3,2,1,0:T(4,128)(2,1)}), bf16[32,1,4,384]{3,2,1,0:T(4,128)(2,1)S(1)}, u32[]{:S(2)}, u32[]{:S(2)}) async-start(bf16[32,1,4,384]{3,2,1,0:T(4,128)(2,1)} %copy.534), calls=%async_computation.2 | async-start | bytes 196608 | tf_op jit(solution)/shard_map/all_to_all | solution.py:68
  195.3 0.9 reshape.950
  196.2 6.3 %all-to-all-done.2 = bf16[32,1,4,384]{3,2,1,0:T(4,128)(2,1)S(1)} async-done(((bf16[32,1,4,384]{3,2,1,0:T(4,128)(2,1)}), bf16[32,1,4,384]{3,2,1,0:T(4,128)(2,1)S(1)}, u32[]{:S(2)}, u32[]{:S(2)}) %all-to-all-start.2) | async-done | bytes 98336 | tf_op jit(solution)/shard_map/all_to_all | solution.py:68
  206.9 0.9 reshape.967
  208.0 0.8 multiply_reduce_fusion.3
  208.8 1.5 copy.540
  212.4 0.9 reshape.965
  213.3 1.0 reshape.997
  214.3 1.8 convert_element_type.418
  216.1 1.2 multiply_convert_fusion.2
  217.4 1.3 multiply_convert_fusion.3
  221.7 1.8 reshape.969
  223.5 1.3 multiply_reduce_fusion.15
  226.6 0.8 fusion.117
  227.4 1.9 reshape.973
  229.3 1.9 multiply_reduce_fusion.1
  231.1 1.5 copy.551
  234.7 1.8 reshape.972
  236.6 1.9 reshape.975
  238.4 1.9 multiply_reduce_fusion
  240.3 1.5 copy.553
  243.9 1.8 reshape.974
  245.7 1.8 convert_element_type.434
  247.5 1.3 multiply_convert_fusion.1
  248.8 1.3 multiply_convert_fusion
  251.4 1.7 multiply_reduce_fusion.10
  253.1 1.6 multiply_reduce_fusion.11
  255.5 1.8 reshape.976
  259.4 1.4 add_add_fusion.5
  260.8 1.0 copy.567
  261.9 1.9 reshape.977
  263.7 1.4 add_add_fusion.4
  265.2 1.0 copy.575
  266.2 1.9 reshape.978
  268.1 1.6 multiply_reduce_fusion.14
  270.2 0.9 reshape.980
  271.1 2.0 fusion.14
  273.1 1.6 multiply_reduce_fusion.9
  276.8 0.9 reshape.982
  278.4 1.2 add_add_fusion.3
  281.2 2.6 all-to-all-start.3
  283.8 7.6 %all-to-all-done.3 = bf16[32,1,4,384]{3,2,1,0:T(4,128)(2,1)S(1)} async-done(((bf16[32,1,4,384]{3,2,1,0:T(4,128)(2,1)}), bf16[32,1,4,384]{3,2,1,0:T(4,128)(2,1)S(1)}, u32[]{:S(2)}, u32[]{:S(2)}) %all-to-all-start.3) | async-done | bytes 98336 | tf_op jit(solution)/shard_map/all_to_all | solution.py:79
  296.4 6.7 %all_to_all.43 = bf16[32,1,4,384]{3,2,1,0:T(4,128)(2,1)S(1)} all-to-all(bf16[32,1,4,384]{3,2,1,0:T(4,128)(2,1)S(1)} %copy.626), channel_id=1, replica_groups=mesh['gz'=4,'gy'=4,'gx'=2] {'gz'}, dimensions={0} | all-to-all | bytes 196608 | tf_op jit(solution)/shard_map/all_to_all | solution.py:104
  (260 shorter events, 43.5 us)
Async XLA Ops:
  6.5 61.5 %all-gather.9.cloned.1.call-start = ((), (), s32[]{:S(2)}) async-start(), calls=%async_computation.6 | async-start | bytes 1622016 | tf_op jit(solution)/shard_map/all_gather | solution.py:46
  9.0 115.9 %all-gather.11.cloned.1.call-start = ((), (), s32[]{:S(2)}) async-start(), calls=%async_computation.7 | async-start | bytes 1622016 | tf_op jit(solution)/shard_map/all_gather | solution.py:46
  10.0 171.8 %all-gather.7.cloned.1.call-start = ((), (), s32[]{:S(2)}) async-start(), calls=%async_computation.5 | async-start | bytes 1622016 | tf_op jit(solution)/shard_map/all_gather | solution.py:46
  20.3 170.1 %copy-start.11 = (bf16[8,1,16,384]{3,0,1,2:T(8,128)(2,1)}, bf16[8,1,16,384]{3,0,1,2:T(8,128)(2,1)S(1)}, u32[]{:S(2)}) copy-start(bf16[8,1,16,384]{3,0,1,2:T(8,128)(2,1)S(1)} %all_to_all.42) | copy-start | bytes 294916
  20.3 171.1 %all-to-all-start = ((bf16[8,1,16,384]{3,2,1,0:T(8,128)(2,1)}), bf16[8,1,16,384]{3,2,1,0:T(8,128)(2,1)S(1)}, u32[]{:S(2)}, u32[]{:S(2)}) async-start(bf16[8,1,16,384]{3,2,1,0:T(8,128)(2,1)} %param.5), calls=%async_computation | async-start | bytes 196608 | tf_op jit(solution)/shard_map/all_to_all | solution.py:85
  72.1 1.1 copy-start.4
  73.2 0.7 copy-start.13
  74.0 9.7 %copy-start = (f32[1,32,4,6,64]{4,3,1,2,0:T(8,128)}, f32[1,32,4,6,64]{4,3,1,2,0:T(8,128)S(1)}, u32[]{:S(2)}) copy-start(f32[1,32,4,6,64]{4,3,1,2,0:T(8,128)S(1)} %reshape.958) | copy-start | bytes 589828
  82.4 1.5 copy-start.20
  83.7 1.3 copy-start.24
  83.7 1.2 copy-start.26
  83.9 41.0 %copy-start.16 = (f32[4,6,32,32]{2,3,1,0:T(8,128)}, f32[4,6,32,32]{2,3,1,0:T(8,128)S(1)}, u32[]{:S(2)}) copy-start(f32[4,6,32,32]{2,3,1,0:T(8,128)S(1)} %get-tuple-element.26) | copy-start | bytes 294916
  84.0 43.8 %copy-start.53 = (f32[4,6,32]{2,1,0:T(8,128)}, f32[4,6,32]{2,1,0:T(8,128)S(1)}, u32[]{:S(2)}) copy-start(f32[4,6,32]{2,1,0:T(8,128)S(1)} %get-tuple-element.25) | copy-start | bytes 9220
  186.6 2.9 copy-start.41
  186.6 3.5 %copy-start.38 = (bf16[1,32,4,6,64]{4,1,3,2,0:T(8,128)(2,1)S(1)}, bf16[1,32,4,6,64]{4,1,3,2,0:T(8,128)(2,1)}, u32[]{:S(2)}) copy-start(bf16[1,32,4,6,64]{4,1,3,2,0:T(8,128)(2,1)} %fusion.6) | copy-start | bytes 294916
  186.6 3.8 %copy-start.9 = (bf16[384,8,48]{0,2,1:T(8,128)(2,1)S(1)}, bf16[384,8,48]{0,2,1:T(8,128)(2,1)}, u32[]{:S(2)}) copy-start(bf16[384,8,48]{0,2,1:T(8,128)(2,1)} %slice.91) | copy-start | bytes 884740
  191.3 13.1 %copy-start.29 = (bf16[8,1,16,384]{3,2,1,0:T(8,128)(2,1)}, bf16[8,1,16,384]{3,2,1,0:T(8,128)(2,1)S(1)}, u32[]{:S(2)}) copy-start(bf16[8,1,16,384]{3,2,1,0:T(8,128)(2,1)S(1)} %all-to-all-done) | copy-start | bytes 294916
  191.3 11.1 %all-to-all-start.2 = ((bf16[32,1,4,384]{3,2,1,0:T(4,128)(2,1)}), bf16[32,1,4,384]{3,2,1,0:T(4,128)(2,1)S(1)}, u32[]{:S(2)}, u32[]{:S(2)}) async-start(bf16[32,1,4,384]{3,2,1,0:T(4,128)(2,1)} %copy.534), calls=%async_computation.2 | async-start | bytes 196608 | tf_op jit(solution)/shard_map/all_to_all | solution.py:68
  205.6 2.3 copy-start.44
  217.4 2.8 copy-start.32
  217.4 2.8 copy-start.36
  218.8 1.9 copy-start.34
  219.3 0.8 copy-start.14
  219.3 0.9 copy-start.18
  224.9 2.5 copy-start.56
  247.5 2.9 copy-start.22
  248.8 1.8 copy-start.23
  250.4 1.0 copy-start.2
  250.6 2.5 copy-start.3
  253.1 4.9 %copy-start.47 = (f32[4,32,6]{1,0,2:T(4,128)S(1)}, f32[4,32,6]{1,0,2:T(4,128)}, u32[]{:S(2)}) copy-start(f32[4,32,6]{1,0,2:T(4,128)} %copy.551) | copy-start | bytes 9220
  258.8 5.0 %copy-start.52 = (f32[4,32,6]{1,2,0:T(8,128)S(1)}, f32[4,32,6]{1,2,0:T(8,128)}, u32[]{:S(2)}) copy-start(f32[4,32,6]{1,2,0:T(8,128)} %copy.570) | copy-start | bytes 9220
  265.1 4.6 %copy-start.59 = (f32[4,32]{1,0:T(4,128)S(1)}, f32[4,32]{1,0:T(4,128)}, u32[]{:S(2)}) copy-start(f32[4,32]{1,0:T(4,128)} %copy-done.58) | copy-start | bytes 1540
  265.2 4.6 %copy-start.57 = (f32[4,32]{1,0:T(4,128)S(1)}, f32[4,32]{1,0:T(4,128)}, u32[]{:S(2)}) copy-start(f32[4,32]{1,0:T(4,128)} %copy-done.56) | copy-start | bytes 1540
  268.1 1.7 copy-start.7
  268.1 1.7 copy-start.30
  268.1 1.8 copy-start.8
  269.7 3.4 %copy-start.15 = (f32[32,6,4,4]{2,3,1,0:T(4,128)S(1)}, f32[32,6,4,4]{2,3,1,0:T(4,128)}, u32[]{:S(2)}) copy-start(f32[32,6,4,4]{2,3,1,0:T(4,128)} %copy-done.14) | copy-start | bytes 36868
  269.7 3.4 %copy-start.40 = (f32[32,6,4]{2,1,0:T(8,128)S(1)}, f32[32,6,4]{2,1,0:T(8,128)}, u32[]{:S(2)}) copy-start(f32[32,6,4]{2,1,0:T(8,128)} %multiply_divide_fusion) | copy-start | bytes 9220
  269.9 4.9 %copy-start.19 = (f32[32,6,4]{2,1,0:T(8,128)S(1)}, f32[32,6,4]{2,1,0:T(8,128)}, u32[]{:S(2)}) copy-start(f32[32,6,4]{2,1,0:T(8,128)} %copy-done.18) | copy-start | bytes 9220
  273.1 1.9 copy-start.33
  273.1 2.4 copy-start.35
  274.8 1.1 copy-start.55
  274.8 1.4 copy-start.45
  275.0 1.4 copy-start.46
  275.0 1.5 copy-start.37
  275.5 2.2 copy-start.51
  275.9 0.7 copy-start.28
  276.8 1.5 copy-start.50
  278.2 1.7 copy-start.31
  279.9 3.9 %copy-start.54 = (f32[4,6,32]{2,1,0:T(8,128)S(1)}, f32[4,6,32]{2,1,0:T(8,128)}, u32[]{:S(2)}) copy-start(f32[4,6,32]{2,1,0:T(8,128)} %copy-done.53) | copy-start | bytes 9220
  279.9 11.5 %copy-start.10 = (bf16[384,8,48]{0,2,1:T(8,128)(2,1)S(1)}, bf16[384,8,48]{0,2,1:T(8,128)(2,1)}, u32[]{:S(2)}) copy-start(bf16[384,8,48]{0,2,1:T(8,128)(2,1)} %slice.91) | copy-start | bytes 884740
  280.0 11.9 %copy-start.17 = (f32[4,6,32,32]{2,3,1,0:T(8,128)S(1)}, f32[4,6,32,32]{2,3,1,0:T(8,128)}, u32[]{:S(2)}) copy-start(f32[4,6,32,32]{2,3,1,0:T(8,128)} %copy-done.16) | copy-start | bytes 294916
  280.5 11.5 %copy-start.21 = (bf16[32,4,6,64]{3,2,0,1:T(8,128)(2,1)S(1)}, bf16[32,4,6,64]{3,2,0,1:T(8,128)(2,1)}, u32[]{:S(2)}) copy-start(bf16[32,4,6,64]{3,2,0,1:T(8,128)(2,1)} %convert_element_type.403) | copy-start | bytes 294916
  281.2 10.2 %all-to-all-start.3 = ((bf16[32,1,4,384]{3,2,1,0:T(4,128)(2,1)}), bf16[32,1,4,384]{3,2,1,0:T(4,128)(2,1)S(1)}, u32[]{:S(2)}, u32[]{:S(2)}) async-start(bf16[32,1,4,384]{3,2,1,0:T(4,128)(2,1)} %bitcast.70), calls=%async_computation.3 | async-start | bytes 196608 | tf_op jit(solution)/shard_map/all_to_all | solution.py:79
  291.6 1.0 copy-start.27
  292.0 1.1 copy-start.1
  292.0 1.1 copy-start.25
  293.2 0.7 copy-start.43
  293.2 0.7 copy-start.42
  293.2 0.8 copy-start.49
  293.8 0.8 copy-start.48
  294.6 1.2 copy-start.5
  294.6 1.2 copy-start.12
  294.9 1.3 copy-start.60
  (3 other events, 1.9 us)
Sparse Core Ops, SparseCore 0:
  10.2 57.8 all-gather.8
  71.0 53.9 all-gather.10
  127.9 53.9 all-gather.6

commit v2 on v1

--- a/solution.py
+++ b/solution.py
@@ -4,51 +4,53 @@
 from jax.sharding import PartitionSpec as P
 
 HEADS = 6
+HIGHEST = lax.Precision.HIGHEST
 ALL = ("gz", "gy", "gx")
 
 
-def head_norm(vector):
-    return (vector * lax.rsqrt(jnp.mean(vector * vector, axis=-1, keepdims=True) + 1e-06)).astype(
-        jnp.bfloat16
-    )
+def head_map(feat_len):
+    head_size = feat_len // HEADS
+    return (jnp.arange(feat_len)[:, None] // head_size == jnp.arange(HEADS)[None, :]).astype(jnp.float32)
+
+
+def head_norm(vector, ones):
+    head_size = vector.shape[-1] // HEADS
+    sums = jnp.dot(vector * vector, ones, precision=HIGHEST)
+    scale = lax.rsqrt(sums / head_size + 1e-06)
+    return (vector * jnp.dot(scale, ones.T, precision=HIGHEST)).astype(jnp.bfloat16)
 
 
 def sublayer(line_rows, w_inner, w_outer):
     feat_len = line_rows.shape[-1]
     head_size = feat_len // HEADS
+    ones = head_map(feat_len)
+    mask = ones.T.astype(jnp.bfloat16)
     stream = line_rows.astype(jnp.float32)
-    normed = (stream * lax.rsqrt(jnp.mean(stream * stream, axis=-1, keepdims=True) + 1e-06)).astype(
-        jnp.bfloat16
-    )
+    normed = (stream * lax.rsqrt(jnp.mean(stream * stream, axis=-1, keepdims=True) + 1e-06)).astype(jnp.bfloat16)
     packed = jnp.dot(normed, w_inner, preferred_element_type=jnp.float32)
-    head_shape = line_rows.shape[:3] + (HEADS, head_size)
-    queries = head_norm(packed[..., :feat_len].reshape(head_shape))
-    key_part = head_norm(packed[..., feat_len : 2 * feat_len].reshape(head_shape))
-    value_part = packed[..., 2 * feat_len :].reshape(head_shape).astype(jnp.bfloat16)
-    scores = jnp.einsum(
-        "plqhe,pkqhe->pqhlk", queries, key_part, preferred_element_type=jnp.float32
-    ) * head_size ** (-0.5)
+    queries = head_norm(packed[..., :feat_len], ones)
+    key_part = head_norm(packed[..., feat_len : 2 * feat_len], ones)
+    value_part = packed[..., 2 * feat_len :].astype(jnp.bfloat16)
+    key_heads = key_part[..., None, :] * mask
+    scores = jnp.einsum("plqd,pkqhd->pqhlk", queries, key_heads, preferred_element_type=jnp.float32) * head_size ** (-0.5)
     powers = jnp.exp(scores)
     attn_weights = (powers / jnp.sum(powers, axis=-1, keepdims=True)).astype(jnp.bfloat16)
-    mixed_out = jnp.einsum(
-        "pqhlk,pkqhe->plqhe", attn_weights, value_part, preferred_element_type=jnp.float32
-    )
-    mixed_out = mixed_out.astype(jnp.bfloat16).reshape(line_rows.shape)
+    mixed_heads = jnp.einsum("pqhlk,pkqd->plqhd", attn_weights, value_part, preferred_element_type=jnp.float32)
+    mixed_out = jnp.sum(mixed_heads * mask.astype(jnp.float32), axis=-2).astype(jnp.bfloat16)
     update = jnp.dot(mixed_out, w_outer, preferred_element_type=jnp.float32)
     return (stream + update).astype(jnp.bfloat16)
 
 
-def full_weights(w_project, w_output, index, sizes):
+def full_weights(w_project, w_output, sizes):
     nz, ny, nx = sizes
-    proj, outp = w_project[index], w_output[index]
-    din, dproj = proj.shape
-    cat = jnp.concatenate([proj, outp], axis=1)
+    subs, din, dproj = w_project.shape
+    cat = jnp.concatenate([w_project, w_output], axis=2)
     got = lax.all_gather(cat, ALL, axis=0, tiled=False)
-    got = got.reshape(nz, ny, nx, din, cat.shape[1])
-    got = jnp.transpose(got, (1, 3, 0, 2, 4)).reshape(ny * din, nz * nx, cat.shape[1])
-    w_inner = got[:, :, :dproj].reshape(ny * din, nz * nx * dproj)
-    w_outer = got[:, :, dproj:].reshape(ny * din, -1)
-    return w_inner, w_outer
+    got = got.reshape(nz, ny, nx, subs, din, cat.shape[2])
+    got = jnp.transpose(got, (3, 1, 4, 0, 2, 5)).reshape(subs, ny * din, nz * nx, cat.shape[2])
+    w_inner = got[:, :, :, :dproj].reshape(subs, ny * din, nz * nx * dproj)
+    w_outer = got[:, :, :, dproj:].reshape(subs, ny * din, -1)
+    return [(w_inner[i], w_outer[i]) for i in range(subs)]
 
 
 def depth_fn(member, w_inner, w_outer):
@@ -88,9 +90,7 @@
 
 
 def local(volume, cotangent, w_project, w_output, sizes):
-    w_depth = full_weights(w_project, w_output, 0, sizes)
-    w_row = full_weights(w_project, w_output, 1, sizes)
-    w_col = full_weights(w_project, w_output, 2, sizes)
+    w_depth, w_row, w_col = full_weights(w_project, w_output, sizes)
 
     depth_act = lax.all_to_all(volume, "gz", 2, 0, tiled=True)
     cot_plane = block_to_plane(cotangent, sizes)
@@ -119,9 +119,7 @@
 
 
 def local_general(volume, cotangent, w_project, w_output, sizes):
-    w_depth = full_weights(w_project, w_output, 0, sizes)
-    w_row = full_weights(w_project, w_output, 1, sizes)
-    w_col = full_weights(w_project, w_output, 2, sizes)
+    w_depth, w_row, w_col = full_weights(w_project, w_output, sizes)
 
     def row_fn(member):
         return along_rows(member, *w_row)

time: 312 us -> 165 us (0.53)
  waiting for transfers between devices: 146 us -> 67.5 us
  local copies, waits for them, and re-layouts: 76.9 us -> 28 us
  other arithmetic: 27.8 us -> 5.29 us
  blocking collectives: 15 us -> 6.67 us
  matrix products: 17.5 us -> 25.8 us
  starting transfers between devices: 12.2 us -> 16.5 us
    all_gather x3 -> x1, waiting for transfers between devices: 133 us -> 50.2 us  [full_weights(): got = lax.all_gather(cat, ALL, axis=0, tiled=False)]
    reshape x30 -> x2, local copies, waits for them, and re-layouts: 32.6 us -> 16.5 us  [the longest x1 9.65 us: full_weights(): got = got.reshape(nz, ny, nx, subs, din, cat.shape[2])]
    dot_general x17 -> x41, matrix products: 11.6 us -> 21.2 us  [the longest x9 6.72 us: sublayer(): jnp.einsum('plqd,pkqhd->pqhlk', queries, key_heads, preferred_element_typ...]
    all_to_all x1 -> x0, blocking collectives: 8.33 us -> none  [local(): depth_act = lax.all_to_all(volume, 'gz', 2, 0, tiled=True)]
    rsqrt x12 -> x0, local copies, waits for them, and re-layouts: 8.07 us -> none  [head_norm(): lax.rsqrt(jnp.mean(vector * vector, axis=-1, keepdims=True) + 1e-06)]
    convert_element_type x8 -> x1, local copies, waits for them, and re-layouts: 7.4 us -> 0.13 us  [sublayer(): jnp.sum(mixed_heads * mask.astype(jnp.float32), axis=-2)]
    reduce_sum x6 -> x0, local copies, waits for them, and re-layouts: 6.05 us -> none  [head_norm(): jnp.mean(vector * vector, axis=-1, keepdims=True) + 1e-06]
    slice x14 -> x2, local copies, waits for them, and re-layouts: 8.4 us -> 2.42 us  [full_weights(): return [(w_inner[i], w_outer[i]) for i in range(subs)]]
  transfers between devices with their start and end apart: 6 -> 5, of which waited for: 5 -> 4; matrix products, arithmetic and copies ran while one was open for 12% -> 17% of each run, Pallas kernels for 0% -> 0%
where the time goes in v2:
time: 165 us; the launch traced here: 164 us
  waiting for transfers between devices  67.5 us (41%)
  local copies, waits for them, and re-layouts  28 us (17%)
  matrix products  25.8 us (16%)
  starting transfers between devices  16.5 us (10%)
  between operations  14.2 us (9%)
  blocking collectives  6.67 us (4%)
  other arithmetic  5.29 us (3%)
    all_gather x1, waiting for transfers between devices, full_weights(): got = lax.all_gather(cat, ALL, axis=0, tiled=False)  50.2 us
    reshape x1, local copies, waits for them, and re-layouts, full_weights(): got = got.reshape(nz, ny, nx, subs, din, cat.shape[2])  9.65 us
    all_to_all x1, waiting for transfers between devices, from_planes(): return lax.all_to_all(parts, ALL, 0, 0, tiled=True)  7.33 us
    reshape x1, local copies, waits for them, and re-layouts, full_weights(): jnp.transpose(got, (3, 1, 4, 0, 2, 5))  6.88 us
    dot_general x9, matrix products, sublayer(): jnp.einsum('plqd,pkqhd->pqhlk', queries, key_heads, preferred_element_typ...  6.72 us
    all_to_all x1, blocking collectives, local(): return lax.all_to_all(grad_zero, 'gz', 0, 2, tiled=True)  6.67 us
    all_to_all x1, starting transfers between devices, block_to_plane(): got = lax.all_to_all(block, ('gy', 'gx'), 0, 0, tiled=True)  6.35 us
    all_to_all x1, waiting for transfers between devices, to_planes(): got = lax.all_to_all(depth_lines, ALL, 0, 0, tiled=True)  6.29 us
  transfers between devices with their start and end apart: 5, of which 4 were waited for; matrix products, arithmetic and copies ran while one was open for 17% of the time, Pallas kernels for 0%

profile of v2, /device:TPU:0, one launch (start us, length us, event | category | flops | bytes accessed | tf_op | source)
XLA Modules:
  0.0 163.9 jit_solution(4668314066329188043)
XLA Ops:
  6.5 1.0 copy.178
  7.6 0.9 copy.179
  8.4 0.8 pad_maximum_fusion
  9.2 1.6 copy.182
  10.8 4.2 %all-to-all-start.1 = ((bf16[8,1,16,384]{3,0,1,2:T(8,128)(2,1)}), bf16[8,1,16,384]{3,0,1,2:T(8,128)(2,1)S(1)}, u32[]{:S(2)}, u32[]{:S(2)}) async-start(bf16[8,1,16,384]{3,0,1,2:T(8,128)(2,1)} %copy.182), calls=%async_computation.1 | async-start | bytes 196608 | tf_op jit(solution)/shard_map/all_to_all | solution.py:95
  15.0 0.6 fusion.322
  15.6 3.7 %all-to-all-done.1 = bf16[8,1,16,384]{3,0,1,2:T(8,128)(2,1)S(1)} async-done(((bf16[8,1,16,384]{3,0,1,2:T(8,128)(2,1)}), bf16[8,1,16,384]{3,0,1,2:T(8,128)(2,1)S(1)}, u32[]{:S(2)}, u32[]{:S(2)}) %all-to-all-start.1) | async-done | bytes 98336 | tf_op jit(solution)/shard_map/all_to_all | solution.py:95
  19.3 6.4 %all-to-all-start = ((bf16[8,1,16,384]{3,2,1,0:T(8,128)(2,1)}), bf16[8,1,16,384]{3,2,1,0:T(8,128)(2,1)}, u32[]{:S(2)}, u32[]{:S(2)}) async-start(bf16[8,1,16,384]{3,2,1,0:T(8,128)(2,1)} %param.5), calls=%async_computation | async-start | bytes 196608 | tf_op jit(solution)/shard_map/all_to_all | solution.py:87
  25.8 0.6 multiply_add_fusion.1
  26.4 0.7 add.121
  27.0 50.2 %all-gather.3.cloned.1.call-done = bf16[96,96,192]{2,1,0:T(8,128)(2,1)} async-done(((bf16[3,96,192]{2,1,0:T(8,128)(2,1)}), bf16[96,96,192]{2,1,0:T(8,128)(2,1)}) %all-gather.3.cloned.1.call-update) | async-done | bytes 3538960 | tf_op jit(solution)/shard_map/all_gather | solution.py:48
  77.2 9.7 %copy.180 = bf16[4,4,2,3,96,192]{4,1,5,2,0,3:T(4,128)(2,1)} copy(bf16[4,4,2,3,96,192]{5,4,3,2,1,0:T(8,128)(2,1)} %bitcast.603) | data formatting | bytes 7077888 | tf_op jit(solution)/shard_map/reshape | solution.py:49
  86.9 6.9 %reshape.794 = bf16[3,384,8,192]{1,3,2,0:T(8,128)(2,1)S(1)} reshape(bf16[3,4,96,4,2,192]{2,1,5,4,3,0:T(4,128)(2,1)} %bitcast.598) | data formatting | bytes 7077888 | tf_op jit(solution)/shard_map/reshape | solution.py:50
  93.8 1.5 fusion.338
  95.3 0.4 convolution_bitcast_fusion.2
  95.7 0.4 fusion.102
  96.1 0.4 fusion.101
  96.5 0.9 fusion.337
  98.8 0.4 fusion.9
  99.5 0.7 copy.189
  100.2 3.1 %all-to-all-start.2 = ((bf16[32,1,4,384]{3,2,1,0:T(4,128)(2,1)}), bf16[32,1,4,384]{3,2,1,0:T(4,128)(2,1)S(1)}, u32[]{:S(2)}, u32[]{:S(2)}) async-start(bf16[32,1,4,384]{3,2,1,0:T(4,128)(2,1)} %copy.189), calls=%async_computation.2 | async-start | bytes 196608 | tf_op jit(solution)/shard_map/all_to_all | solution.py:70
  103.3 1.1 fusion.71
  104.4 6.3 %all-to-all-done.2 = bf16[32,1,4,384]{3,2,1,0:T(4,128)(2,1)S(1)} async-done(((bf16[32,1,4,384]{3,2,1,0:T(4,128)(2,1)}), bf16[32,1,4,384]{3,2,1,0:T(4,128)(2,1)S(1)}, u32[]{:S(2)}, u32[]{:S(2)}) %all-to-all-start.2) | async-done | bytes 98336 | tf_op jit(solution)/shard_map/all_to_all | solution.py:70
  110.9 0.6 multiply_add_fusion
  111.6 0.4 convolution_bitcast_fusion.1
  112.0 0.4 fusion.100
  112.4 0.4 fusion.99
  112.8 0.7 fusion.234
  114.2 0.7 fusion.226
  115.0 3.5 %fusion.342 = (f32[32,6,4]{1,2,0:T(4,128)S(1)}, f32[1,32,6,4,4]{2,3,4,1,0:T(4,128)S(1)}) fusion(bf16[4,32,384,1]{2,1,0,3:T(8,128)(2,1)} %get-tuple-element.13, bf16[4,32,6,384]{3,1,2,0:T(8,128)(2,1)S(1)} %broadcast_multiply_fusion), kind=kOutput, calls=%fused_computation.398 | convolution fusion | flops 2364672 | bytes 703488 | tf_op jit(solution)/shard_map/jvp(plqd,pkqhd->pqhlk)/dot_general | solution.py:35
  118.6 0.8 fusion
  119.8 0.4 convolution_bitcast_fusion
  120.2 0.4 fusion.98
  120.6 0.4 fusion.97
  121.0 0.3 fusion.255
  122.4 0.7 fusion.146
  123.7 0.4 fusion.96
  124.1 0.3 add_add_fusion.8
  124.5 0.4 fusion.95
  124.8 0.3 add_add_fusion.7
  125.2 0.4 multiply_reduce_fusion.1
  125.6 1.0 fusion.180
  127.0 0.4 fusion.53
  127.4 2.4 %fusion.1 = bf16[32,6,4,4]{1,3,2,0:T(4,128)(2,1)S(1)} fusion(f32[4,32,384]{2,0,1:T(4,128)S(1)} %copy.202, f32[6,384]{1,0:T(8,128)S(1)} %get-tuple-element.25, bf16[4,32,384,1]{2,1,0,3:T(8,128)(2,1)S(1)} %copy-done.21), kind=kOutput, calls=%fused_computation.5 | convolution fusion | flops 2654208 | bytes 310272 | tf_op jit(solution)/shard_map/transpose(jvp(pqhlk,pkqd->plqhd))/dot_general | solution.py:38
  130.0 0.8 fusion.13
  131.0 0.6 convolution_bitcast_fusion.8
  131.7 0.4 fusion.94
  132.1 0.3 add_add_fusion.5
  132.4 0.4 fusion.93
  132.8 0.3 add_add_fusion.4
  133.3 0.4 multiply_reduce_fusion
  133.8 0.7 copy.212
  134.5 2.8 %all-to-all-start.3 = ((bf16[32,1,4,384]{3,2,1,0:T(4,128)(2,1)}), bf16[32,1,4,384]{3,2,1,0:T(4,128)(2,1)S(1)}, u32[]{:S(2)}, u32[]{:S(2)}) async-start(bf16[32,1,4,384]{3,2,1,0:T(4,128)(2,1)} %bitcast.132), calls=%async_computation.3 | async-start | bytes 196608 | tf_op jit(solution)/shard_map/all_to_all | solution.py:81
  137.4 7.3 %all-to-all-done.3 = bf16[32,1,4,384]{3,2,1,0:T(4,128)(2,1)S(1)} async-done(((bf16[32,1,4,384]{3,2,1,0:T(4,128)(2,1)}), bf16[32,1,4,384]{3,2,1,0:T(4,128)(2,1)S(1)}, u32[]{:S(2)}, u32[]{:S(2)}) %all-to-all-start.3) | async-done | bytes 98336 | tf_op jit(solution)/shard_map/all_to_all | solution.py:81
  145.2 0.7 fusion.142
  146.3 0.5 copy-done.23
  147.1 0.4 copy-done.18
  147.6 0.4 fusion.92
  147.9 0.3 add_add_fusion.2
  148.3 0.4 fusion.91
  148.7 0.3 add_add_fusion.1
  149.1 0.4 fusion.202
  149.7 6.7 %all_to_all.42 = bf16[32,1,4,384]{3,2,1,0:T(4,128)(2,1)S(1)} all-to-all(bf16[32,1,4,384]{3,2,1,0:T(4,128)(2,1)S(1)} %copy.218), channel_id=1, replica_groups=mesh['gz'=4,'gy'=4,'gx'=2] {'gz'}, dimensions={0} | all-to-all | bytes 196608 | tf_op jit(solution)/shard_map/all_to_all | solution.py:104
  156.4 0.7 all_to_all.36
  (121 shorter events, 7.4 us)
Async XLA Ops:
  6.5 70.7 %all-gather.3.cloned.1.call-start = ((), (), s32[]{:S(2)}) async-start(), calls=%async_computation.5 | async-start | bytes 4866048 | tf_op jit(solution)/shard_map/all_gather | solution.py:48
  10.8 8.5 %all-to-all-start.1 = ((bf16[8,1,16,384]{3,0,1,2:T(8,128)(2,1)}), bf16[8,1,16,384]{3,0,1,2:T(8,128)(2,1)S(1)}, u32[]{:S(2)}, u32[]{:S(2)}) async-start(bf16[8,1,16,384]{3,0,1,2:T(8,128)(2,1)} %copy.182), calls=%async_computation.1 | async-start | bytes 196608 | tf_op jit(solution)/shard_map/all_to_all | solution.py:95
  19.3 67.6 %copy-start.9 = (bf16[8,1,16,384]{3,0,1,2:T(8,128)(2,1)}, bf16[8,1,16,384]{3,0,1,2:T(8,128)(2,1)S(1)}, u32[]{:S(2)}) copy-start(bf16[8,1,16,384]{3,0,1,2:T(8,128)(2,1)S(1)} %all-to-all-done.1) | copy-start | bytes 294916
  19.3 80.9 %all-to-all-start = ((bf16[8,1,16,384]{3,2,1,0:T(8,128)(2,1)}), bf16[8,1,16,384]{3,2,1,0:T(8,128)(2,1)}, u32[]{:S(2)}, u32[]{:S(2)}) async-start(bf16[8,1,16,384]{3,2,1,0:T(8,128)(2,1)} %param.5), calls=%async_computation | async-start | bytes 196608 | tf_op jit(solution)/shard_map/all_to_all | solution.py:87
  93.8 1.5 copy-start.10
  93.8 1.5 copy-start.28
  95.3 2.2 %copy-start.4 = (bf16[1,384,8,144]{1,3,2,0:T(8,128)(2,1)}, bf16[1,384,8,144]{1,3,2,0:T(8,128)(2,1)S(1)}, u32[]{:S(2)}) copy-start(bf16[1,384,8,144]{1,3,2,0:T(8,128)(2,1)S(1)} %get-tuple-element.10) | copy-start | bytes 2654212
  95.7 3.1 %copy-start = (f32[1,32,4,1152]{3,1,2,0:T(8,128)}, f32[1,32,4,1152]{3,1,2,0:T(8,128)S(1)}, u32[]{:S(2)}) copy-start(f32[1,32,4,1152]{3,1,2,0:T(8,128)S(1)} %convolution_bitcast_fusion.2) | copy-start | bytes 1769476
  96.1 2.0 %copy-start.17 = (f32[32,4,6]{0,2,1:T(8,128)}, f32[32,4,6]{0,2,1:T(8,128)S(1)}, u32[]{:S(2)}) copy-start(f32[32,4,6]{0,2,1:T(8,128)S(1)} %fusion.102) | copy-start | bytes 9220
  96.5 1.7 %copy-start.19 = (f32[32,4,6]{0,2,1:T(8,128)}, f32[32,4,6]{0,2,1:T(8,128)S(1)}, u32[]{:S(2)}) copy-start(f32[32,4,6]{0,2,1:T(8,128)S(1)} %fusion.101) | copy-start | bytes 9220
  96.5 1.7 %copy-start.29 = (bf16[6,384]{1,0:T(8,128)(2,1)S(1)}, bf16[6,384]{1,0:T(8,128)(2,1)}, u32[]{:S(2)}) copy-start(bf16[6,384]{1,0:T(8,128)(2,1)} %get-tuple-element.26) | copy-start | bytes 13828
  97.4 1.9 %copy-start.7 = (bf16[1,384,8,48]{1,3,2,0:T(8,128)(2,1)}, bf16[1,384,8,48]{1,3,2,0:T(8,128)(2,1)S(1)}, u32[]{:S(2)}) copy-start(bf16[1,384,8,48]{1,3,2,0:T(8,128)(2,1)S(1)} %get-tuple-element.7) | copy-start | bytes 884740
  98.2 0.6 copy-start.22
  98.2 1.0 copy-start.24
  98.5 0.8 copy-start.15
  98.5 1.0 copy-start.33
  98.8 4.5 %copy-start.12 = (bf16[1,384,8,48]{1,3,2,0:T(8,128)(2,1)S(1)}, bf16[1,384,8,48]{1,3,2,0:T(8,128)(2,1)}, u32[]{:S(2)}) copy-start(bf16[1,384,8,48]{1,3,2,0:T(8,128)(2,1)} %get-tuple-element.5) | copy-start | bytes 884740
  99.2 12.4 %copy-start.2 = (bf16[1,384,8,144]{1,3,2,0:T(8,128)(2,1)S(1)}, bf16[1,384,8,144]{1,3,2,0:T(8,128)(2,1)}, u32[]{:S(2)}) copy-start(bf16[1,384,8,144]{1,3,2,0:T(8,128)(2,1)} %get-tuple-element.9) | copy-start | bytes 2654212
  100.2 10.5 %all-to-all-start.2 = ((bf16[32,1,4,384]{3,2,1,0:T(4,128)(2,1)}), bf16[32,1,4,384]{3,2,1,0:T(4,128)(2,1)S(1)}, u32[]{:S(2)}, u32[]{:S(2)}) async-start(bf16[32,1,4,384]{3,2,1,0:T(4,128)(2,1)} %copy.189), calls=%async_computation.2 | async-start | bytes 196608 | tf_op jit(solution)/shard_map/all_to_all | solution.py:70
  112.0 2.8 %copy-start.30 = (bf16[6,384]{1,0:T(8,128)(2,1)S(1)}, bf16[6,384]{1,0:T(8,128)(2,1)}, u32[]{:S(2)}) copy-start(bf16[6,384]{1,0:T(8,128)(2,1)} %get-tuple-element.26) | copy-start | bytes 13828
  114.9 3.7 %copy-start.13 = (bf16[4,32,6,384]{3,1,2,0:T(8,128)(2,1)}, bf16[4,32,6,384]{3,1,2,0:T(8,128)(2,1)S(1)}, u32[]{:S(2)}) copy-start(bf16[4,32,6,384]{3,1,2,0:T(8,128)(2,1)S(1)} %broadcast_multiply_fusion) | copy-start | bytes 1769476
  115.0 3.6 %copy-start.21 = (bf16[4,32,384,1]{2,1,0,3:T(8,128)(2,1)S(1)}, bf16[4,32,384,1]{2,1,0,3:T(8,128)(2,1)}, u32[]{:S(2)}) copy-start(bf16[4,32,384,1]{2,1,0,3:T(8,128)(2,1)} %fusion.234) | copy-start | bytes 294916
  118.5 1.0 copy-start.6
  118.5 1.3 copy-start.3
  120.2 1.5 copy-start.31
  127.4 2.6 %copy-start.26 = (bf16[4,32,384,1]{2,1,0,3:T(8,128)(2,1)S(1)}, bf16[4,32,384,1]{2,1,0,3:T(8,128)(2,1)}, u32[]{:S(2)}) copy-start(bf16[4,32,384,1]{2,1,0,3:T(8,128)(2,1)} %get-tuple-element.13) | copy-start | bytes 294916
  130.0 1.1 copy-start.14
  131.7 1.5 copy-start.27
  133.2 4.1 %copy-start.34 = (f32[4,6,32]{2,1,0:T(8,128)S(1)}, f32[4,6,32]{2,1,0:T(8,128)}, u32[]{:S(2)}) copy-start(f32[4,6,32]{2,1,0:T(8,128)} %copy-done.33) | copy-start | bytes 9220
  133.2 11.4 %copy-start.8 = (bf16[1,384,8,48]{1,3,2,0:T(8,128)(2,1)S(1)}, bf16[1,384,8,48]{1,3,2,0:T(8,128)(2,1)}, u32[]{:S(2)}) copy-start(bf16[1,384,8,48]{1,3,2,0:T(8,128)(2,1)} %copy-done.7) | copy-start | bytes 884740
  133.7 11.2 %copy-start.16 = (f32[1,4,6,32,32]{3,4,2,1,0:T(8,128)S(1)}, f32[1,4,6,32,32]{3,4,2,1,0:T(8,128)}, u32[]{:S(2)}) copy-start(f32[1,4,6,32,32]{3,4,2,1,0:T(8,128)} %copy-done.15) | copy-start | bytes 294916
  134.5 10.2 %all-to-all-start.3 = ((bf16[32,1,4,384]{3,2,1,0:T(4,128)(2,1)}), bf16[32,1,4,384]{3,2,1,0:T(4,128)(2,1)S(1)}, u32[]{:S(2)}, u32[]{:S(2)}) async-start(bf16[32,1,4,384]{3,2,1,0:T(4,128)(2,1)} %bitcast.132), calls=%async_computation.3 | async-start | bytes 196608 | tf_op jit(solution)/shard_map/all_to_all | solution.py:81
  137.3 7.9 %copy-start.1 = (f32[1,32,4,1152]{3,1,2,0:T(8,128)S(1)}, f32[1,32,4,1152]{3,1,2,0:T(8,128)}, u32[]{:S(2)}) copy-start(f32[1,32,4,1152]{3,1,2,0:T(8,128)} %copy-done) | copy-start | bytes 1769476
  144.9 1.1 copy-start.25
  144.9 1.1 copy-start.32
  146.0 0.9 copy-start.23
  146.9 0.7 copy-start.18
  146.9 1.4 copy-start.20
  147.6 1.5 copy-start.5
  147.6 1.5 copy-start.11
  148.7 0.8 copy-start.35
Sparse Core Ops, SparseCore 0:
  10.2 66.9 all-gather.2

commit v3 on v2

--- a/solution.py
+++ b/solution.py
@@ -41,16 +41,24 @@
     return (stream + update).astype(jnp.bfloat16)
 
 
-def full_weights(w_project, w_output, sizes):
+def arrange(got, sizes, dproj):
     nz, ny, nx = sizes
-    subs, din, dproj = w_project.shape
-    cat = jnp.concatenate([w_project, w_output], axis=2)
-    got = lax.all_gather(cat, ALL, axis=0, tiled=False)
-    got = got.reshape(nz, ny, nx, subs, din, cat.shape[2])
-    got = jnp.transpose(got, (3, 1, 4, 0, 2, 5)).reshape(subs, ny * din, nz * nx, cat.shape[2])
+    subs, din, width = got.shape[1:]
+    got = got.reshape(nz, ny, nx, subs, din, width)
+    got = jnp.transpose(got, (3, 1, 4, 0, 2, 5)).reshape(subs, ny * din, nz * nx, width)
     w_inner = got[:, :, :, :dproj].reshape(subs, ny * din, nz * nx * dproj)
     w_outer = got[:, :, :, dproj:].reshape(subs, ny * din, -1)
     return [(w_inner[i], w_outer[i]) for i in range(subs)]
+
+
+def full_weights(w_project, w_output, sizes):
+    subs, din, dproj = w_project.shape
+    cat = jnp.concatenate([w_project, w_output], axis=2)
+    devices = sizes[0] * sizes[1] * sizes[2]
+    first = jnp.broadcast_to(cat[:1][None], (devices,) + cat[:1].shape)
+    first = lax.all_to_all(first, ALL, 0, 0, tiled=True)
+    rest = lax.all_gather(cat[1:], ALL, axis=0, tiled=False)
+    return arrange(first, sizes, dproj) + arrange(rest, sizes, dproj)
 
 
 def depth_fn(member, w_inner, w_outer):

time: 165 us -> 163 us (0.988)
  waiting for transfers between devices: 67.5 us -> 61.8 us
  starting transfers between devices: 16.5 us -> 19.8 us
  other arithmetic: 5.29 us -> 3.36 us
    all_gather x1, waiting for transfers between devices: 50.2 us -> 2.14 us  [full_weights(): rest = lax.all_gather(cat[1:], ALL, axis=0, tiled=False)]
    all_to_all x0 -> x1, waiting for transfers between devices: none -> 42.2 us  [full_weights(): first = lax.all_to_all(first, ALL, 0, 0, tiled=True)]
    reshape x2 -> x3, local copies, waits for them, and re-layouts: 16.5 us -> 9.71 us  [the longest x1 5.39 us: arrange(): got = got.reshape(nz, ny, nx, subs, din, width)]
    all_to_all x0 -> x1, starting transfers between devices: none -> 5.44 us  [full_weights(): first = lax.all_to_all(first, ALL, 0, 0, tiled=True)]
    unnamed x75 -> x147, local copies, waits for them, and re-layouts: 5.27 us -> 8.92 us
    all_to_all x1, starting transfers between devices: 6.35 us -> 4 us  [block_to_plane(): got = lax.all_to_all(block, ('gy', 'gx'), 0, 0, tiled=True)]
    slice x2 -> x4, local copies, waits for them, and re-layouts: 2.42 us -> 3.67 us  [the longest x2 3.55 us: arrange(): return [(w_inner[i], w_outer[i]) for i in range(subs)]]
  transfers between devices with their start and end apart: 5 -> 6, of which waited for: 4 -> 5; matrix products, arithmetic and copies ran while one was open for 17% -> 20% of each run, Pallas kernels for 0% -> 0%
where the time goes in v3:
time: 163 us; the launch traced here: 162 us
  waiting for transfers between devices  61.8 us (38%)
  local copies, waits for them, and re-layouts  29.4 us (18%)
  matrix products  26.6 us (16%)
  starting transfers between devices  19.8 us (12%)
  between operations  14.6 us (9%)
  blocking collectives  6.67 us (4%)
  other arithmetic  3.36 us (2%)
    all_to_all x1, waiting for transfers between devices, full_weights(): first = lax.all_to_all(first, ALL, 0, 0, tiled=True)  42.2 us
    unnamed x147, local copies, waits for them, and re-layouts  8.92 us
    all_to_all x1, waiting for transfers between devices, from_planes(): return lax.all_to_all(parts, ALL, 0, 0, tiled=True)  7.55 us
    all_to_all x1, waiting for transfers between devices, to_planes(): got = lax.all_to_all(depth_lines, ALL, 0, 0, tiled=True)  7.52 us
    dot_general x8, matrix products, sublayer(): jnp.einsum('pqhlk,pkqd->plqhd', attn_weights, value_part, preferred_eleme...  7 us
    all_to_all x1, blocking collectives, local(): return lax.all_to_all(grad_zero, 'gz', 0, 2, tiled=True)  6.67 us
    dot_general x9, matrix products, sublayer(): jnp.einsum('plqd,pkqhd->pqhlk', queries, key_heads, preferred_element_typ...  6.45 us
    all_to_all x1, starting transfers between devices, full_weights(): first = lax.all_to_all(first, ALL, 0, 0, tiled=True)  5.44 us
  transfers between devices with their start and end apart: 6, of which 5 were waited for; matrix products, arithmetic and copies ran while one was open for 20% of the time, Pallas kernels for 0%

profile of v3, /device:TPU:0, one launch (start us, length us, event | category | flops | bytes accessed | tf_op | source)
XLA Modules:
  0.0 162.2 jit_solution(3424042149618016184)
XLA Ops:
  6.5 1.6 copy.188
  8.1 4.2 %all-to-all-start.1 = ((bf16[8,1,16,384]{3,0,1,2:T(8,128)(2,1)}), bf16[8,1,16,384]{3,0,1,2:T(8,128)(2,1)S(1)}, u32[]{:S(2)}, u32[]{:S(2)}) async-start(bf16[8,1,16,384]{3,0,1,2:T(8,128)(2,1)} %copy.188), calls=%async_computation.1 | async-start | bytes 196608 | tf_op jit(solution)/shard_map/all_to_all | solution.py:103
  12.3 0.9 copy.185
  13.2 1.0 copy.184
  14.3 2.3 %all-to-all-done.1 = bf16[8,1,16,384]{3,0,1,2:T(8,128)(2,1)S(1)} async-done(((bf16[8,1,16,384]{3,0,1,2:T(8,128)(2,1)}), bf16[8,1,16,384]{3,0,1,2:T(8,128)(2,1)S(1)}, u32[]{:S(2)}, u32[]{:S(2)}) %all-to-all-start.1) | async-done | bytes 98336 | tf_op jit(solution)/shard_map/all_to_all | solution.py:103
  16.6 1.3 broadcast_in_dim.28
  18.0 5.4 %all-to-all-start.2 = ((bf16[32,1,96,192]{3,2,1,0:T(8,128)(2,1)}), bf16[32,1,96,192]{3,2,1,0:T(8,128)(2,1)S(1)}, u32[]{:S(2)}, u32[]{:S(2)}) async-start(bf16[32,1,96,192]{3,2,1,0:T(8,128)(2,1)} %broadcast_in_dim.28), calls=%async_computation.2 | async-start | bytes 3145728 | tf_op jit(solution)/shard_map/all_to_all | solution.py:59
  23.5 0.7 fusion.225
  24.4 42.2 %all-to-all-done.2 = bf16[32,1,96,192]{3,2,1,0:T(8,128)(2,1)S(1)} async-done(((bf16[32,1,96,192]{3,2,1,0:T(8,128)(2,1)}), bf16[32,1,96,192]{3,2,1,0:T(8,128)(2,1)S(1)}, u32[]{:S(2)}, u32[]{:S(2)}) %all-to-all-start.2) | async-done | bytes 1179680 | tf_op jit(solution)/shard_map/all_to_all | solution.py:59
  66.6 1.2 copy.192
  67.8 1.1 reshape.802
  69.0 0.4 convolution_bitcast_fusion.2
  69.5 0.4 fusion.101
  70.4 0.4 fusion.102
  71.9 0.4 fusion.9
  72.5 0.7 copy.196
  73.2 2.7 %all-to-all-start.3 = ((bf16[32,1,4,384]{3,2,1,0:T(4,128)(2,1)}), bf16[32,1,4,384]{3,2,1,0:T(4,128)(2,1)S(1)}, u32[]{:S(2)}, u32[]{:S(2)}) async-start(bf16[32,1,4,384]{3,2,1,0:T(4,128)(2,1)} %copy.196), calls=%async_computation.3 | async-start | bytes 196608 | tf_op jit(solution)/shard_map/all_to_all | solution.py:78
  75.9 0.7 add.121
  76.6 7.5 %all-to-all-done.3 = bf16[32,1,4,384]{3,2,1,0:T(4,128)(2,1)S(1)} async-done(((bf16[32,1,4,384]{3,2,1,0:T(4,128)(2,1)}), bf16[32,1,4,384]{3,2,1,0:T(4,128)(2,1)S(1)}, u32[]{:S(2)}, u32[]{:S(2)}) %all-to-all-start.3) | async-done | bytes 98336 | tf_op jit(solution)/shard_map/all_to_all | solution.py:78
  84.1 4.0 %all-to-all-start = ((bf16[8,1,16,384]{3,2,1,0:T(8,128)(2,1)}), bf16[8,1,16,384]{3,2,1,0:T(8,128)(2,1)S(1)}, u32[]{:S(2)}, u32[]{:S(2)}) async-start(bf16[8,1,16,384]{3,2,1,0:T(8,128)(2,1)} %param.5), calls=%async_computation | async-start | bytes 196608 | tf_op jit(solution)/shard_map/all_to_all | solution.py:95
  88.3 0.7 add.120
  89.0 0.7 convert_element_type.493
  89.8 2.1 %all-gather.3.cloned.1.call-done = bf16[64,96,192]{2,1,0:T(8,128)(2,1)} async-done(((bf16[2,96,192]{2,1,0:T(8,128)(2,1)}), bf16[64,96,192]{2,1,0:T(8,128)(2,1)}) %all-gather.3.cloned.1.call-update) | async-done | bytes 2359312 | tf_op jit(solution)/shard_map/all_gather | solution.py:60
  91.9 5.4 %copy.186 = bf16[4,4,2,2,96,192]{4,1,5,2,0,3:T(4,128)(2,1)S(1)} copy(bf16[4,4,2,2,96,192]{5,4,3,2,1,0:T(8,128)(2,1)} %bitcast.613) | data formatting | bytes 4718592 | tf_op jit(solution)/shard_map/reshape | solution.py:47
  97.3 3.2 %reshape.799 = bf16[2,384,8,192]{1,3,2,0:T(8,128)(2,1)} reshape(bf16[2,4,96,4,2,192]{2,1,5,4,3,0:T(4,128)(2,1)S(1)} %bitcast.605) | data formatting | bytes 4718592 | tf_op jit(solution)/shard_map/reshape | solution.py:48
  100.6 1.8 %fusion.339 = (bf16[1,384,8,48]{1,3,2,0:T(8,128)(2,1)}, bf16[1,384,8,48]{1,3,2,0:T(8,128)(2,1)S(1)}) fusion(bf16[2,384,8,192]{1,3,2,0:T(8,128)(2,1)} %reshape.799), kind=kLoop, calls=%fused_computation.397 | loop fusion | bytes 1179648 | tf_op jit(solution)/shard_map/slice | solution.py:51
  102.4 1.7 %fusion.340 = (bf16[1,384,8,144]{1,3,2,0:T(8,128)(2,1)S(1)}, bf16[1,384,8,144]{1,3,2,0:T(8,128)(2,1)S(1)}) fusion(bf16[2,384,8,192]{1,3,2,0:T(8,128)(2,1)} %reshape.799), kind=kLoop, calls=%fused_computation.398 | loop fusion | bytes 3538944 | tf_op jit(solution)/shard_map/slice | solution.py:51
  104.1 0.4 convolution_bitcast_fusion.1
  105.0 0.4 fusion.100
  106.4 2.5 %fusion.344 = (f32[32,6,4]{1,2,0:T(4,128)S(1)}, f32[1,32,6,4,4]{2,3,4,1,0:T(4,128)S(1)}) fusion(bf16[4,32,384,1]{2,1,0,3:T(8,128)(2,1)S(1)} %get-tuple-element.11, bf16[4,32,6,384]{3,1,2,0:T(8,128)(2,1)S(1)} %broadcast_multiply_fusion), kind=kOutput, calls=%fused_computation.402 | convolution fusion | flops 2364672 | bytes 703488 | tf_op jit(solution)/shard_map/jvp(plqd,pkqhd->pqhlk)/dot_general | solution.py:35
  109.0 0.7 multiply_divide_fusion
  109.8 0.8 fusion
  111.0 0.5 copy-done.64
  111.5 0.4 convolution_bitcast_fusion
  112.3 0.4 fusion.98
  112.7 0.6 copy-done.37
  114.1 1.1 fusion.345
  115.2 0.6 copy-done.68
  115.8 0.6 multiply_divide_fusion.2
  116.4 1.2 fusion.71
  117.7 1.3 fusion.84
  119.0 0.7 fusion.146
  120.1 0.5 copy-done.54
  120.9 0.4 copy-done.42
  121.4 0.4 fusion.95
  122.8 0.4 multiply_reduce_fusion.1
  123.4 0.4 copy-done.7
  124.2 0.4 fusion.53
  124.7 2.4 %fusion.1 = bf16[32,6,4,4]{1,3,2,0:T(4,128)(2,1)S(1)} fusion(f32[4,32,384]{2,0,1:T(4,128)S(1)} %copy.209, f32[6,384]{1,0:T(8,128)S(1)} %get-tuple-element.23, bf16[4,32,384,1]{2,1,0,3:T(8,128)(2,1)S(1)} %copy-done.46), kind=kOutput, calls=%fused_computation.5 | convolution fusion | flops 2654208 | bytes 310272 | tf_op jit(solution)/shard_map/transpose(jvp(pqhlk,pkqd->plqhd))/dot_general | solution.py:38
  127.3 0.7 convolution_bitcast_fusion.8
  128.2 0.8 fusion.13
  129.0 0.4 fusion.94
  129.7 0.4 fusion.93
  130.5 0.4 multiply_reduce_fusion
  131.1 0.9 copy.219
  132.0 3.4 %all-to-all-start.4 = ((bf16[32,1,4,384]{3,2,1,0:T(4,128)(2,1)}), bf16[32,1,4,384]{3,2,1,0:T(4,128)(2,1)S(1)}, u32[]{:S(2)}, u32[]{:S(2)}) async-start(bf16[32,1,4,384]{3,2,1,0:T(4,128)(2,1)} %bitcast.135), calls=%async_computation.4 | async-start | bytes 196608 | tf_op jit(solution)/shard_map/all_to_all | solution.py:89
  135.5 7.6 %all-to-all-done.4 = bf16[32,1,4,384]{3,2,1,0:T(4,128)(2,1)S(1)} async-done(((bf16[32,1,4,384]{3,2,1,0:T(4,128)(2,1)}), bf16[32,1,4,384]{3,2,1,0:T(4,128)(2,1)S(1)}, u32[]{:S(2)}, u32[]{:S(2)}) %all-to-all-start.4) | async-done | bytes 98336 | tf_op jit(solution)/shard_map/all_to_all | solution.py:89
  143.6 0.7 fusion.142
  144.6 0.5 copy-done.48
  145.5 0.4 copy-done.40
  145.9 0.4 fusion.91
  147.4 0.4 fusion.202
  148.0 6.7 %all_to_all.47 = bf16[32,1,4,384]{3,2,1,0:T(4,128)(2,1)S(1)} all-to-all(bf16[32,1,4,384]{3,2,1,0:T(4,128)(2,1)S(1)} %copy.225), channel_id=1, replica_groups=mesh['gz'=4,'gy'=4,'gx'=2] {'gz'}, dimensions={0} | all-to-all | bytes 196608 | tf_op jit(solution)/shard_map/all_to_all | solution.py:112
  154.7 0.7 all_to_all.40
  (201 shorter events, 11.5 us)
Async XLA Ops:
  8.1 8.5 %all-to-all-start.1 = ((bf16[8,1,16,384]{3,0,1,2:T(8,128)(2,1)}), bf16[8,1,16,384]{3,0,1,2:T(8,128)(2,1)S(1)}, u32[]{:S(2)}, u32[]{:S(2)}) async-start(bf16[8,1,16,384]{3,0,1,2:T(8,128)(2,1)} %copy.188), calls=%async_computation.1 | async-start | bytes 196608 | tf_op jit(solution)/shard_map/all_to_all | solution.py:103
  18.0 48.6 %all-to-all-start.2 = ((bf16[32,1,96,192]{3,2,1,0:T(8,128)(2,1)}), bf16[32,1,96,192]{3,2,1,0:T(8,128)(2,1)S(1)}, u32[]{:S(2)}, u32[]{:S(2)}) async-start(bf16[32,1,96,192]{3,2,1,0:T(8,128)(2,1)} %broadcast_in_dim.28), calls=%async_computation.2 | async-start | bytes 3145728 | tf_op jit(solution)/shard_map/all_to_all | solution.py:59
  23.4 68.5 %all-gather.3.cloned.1.call-start = ((), (), s32[]{:S(2)}) async-start(), calls=%async_computation.6 | async-start | bytes 3244032 | tf_op jit(solution)/shard_map/all_gather | solution.py:60
  24.2 47.2 %copy-start.58 = (bf16[6,384]{1,0:T(8,128)(2,1)}, bf16[6,384]{1,0:T(8,128)(2,1)S(1)}, u32[]{:S(2)}) copy-start(bf16[6,384]{1,0:T(8,128)(2,1)S(1)} %get-tuple-element.24) | copy-start | bytes 13828
  68.9 3.4 %copy-start.4 = (bf16[1,384,8,48]{1,3,2,0:T(8,128)(2,1)}, bf16[1,384,8,48]{1,3,2,0:T(8,128)(2,1)S(1)}, u32[]{:S(2)}) copy-start(bf16[1,384,8,48]{1,3,2,0:T(8,128)(2,1)S(1)} %slice.88) | copy-start | bytes 884740
  69.0 2.2 %copy-start.2 = (bf16[1,384,8,144]{1,3,2,0:T(8,128)(2,1)}, bf16[1,384,8,144]{1,3,2,0:T(8,128)(2,1)S(1)}, u32[]{:S(2)}) copy-start(bf16[1,384,8,144]{1,3,2,0:T(8,128)(2,1)S(1)} %slice.84) | copy-start | bytes 2654212
  69.4 2.4 %copy-start = (f32[1,32,4,1152]{3,1,2,0:T(8,128)}, f32[1,32,4,1152]{3,1,2,0:T(8,128)S(1)}, u32[]{:S(2)}) copy-start(f32[1,32,4,1152]{3,1,2,0:T(8,128)S(1)} %convolution_bitcast_fusion.2) | copy-start | bytes 1769476
  70.4 1.3 copy-start.10
  71.2 1.1 copy-start.8
  71.2 1.0 copy-start.47
  71.7 0.8 copy-start.25
  73.2 10.9 %all-to-all-start.3 = ((bf16[32,1,4,384]{3,2,1,0:T(4,128)(2,1)}), bf16[32,1,4,384]{3,2,1,0:T(4,128)(2,1)S(1)}, u32[]{:S(2)}, u32[]{:S(2)}) async-start(bf16[32,1,4,384]{3,2,1,0:T(4,128)(2,1)} %copy.196), calls=%async_computation.3 | async-start | bytes 196608 | tf_op jit(solution)/shard_map/all_to_all | solution.py:78
  84.1 32.3 %all-to-all-start = ((bf16[8,1,16,384]{3,2,1,0:T(8,128)(2,1)}), bf16[8,1,16,384]{3,2,1,0:T(8,128)(2,1)S(1)}, u32[]{:S(2)}, u32[]{:S(2)}) async-start(bf16[8,1,16,384]{3,2,1,0:T(8,128)(2,1)} %param.5), calls=%async_computation | async-start | bytes 196608 | tf_op jit(solution)/shard_map/all_to_all | solution.py:95
  102.4 8.2 %copy-start.6 = (bf16[1,384,8,48]{1,3,2,0:T(8,128)(2,1)}, bf16[1,384,8,48]{1,3,2,0:T(8,128)(2,1)S(1)}, u32[]{:S(2)}) copy-start(bf16[1,384,8,48]{1,3,2,0:T(8,128)(2,1)S(1)} %get-tuple-element.6) | copy-start | bytes 884740
  102.4 1.7 %copy-start.24 = (bf16[4,32,384]{2,1,0:T(8,128)(2,1)S(1)}, bf16[4,32,384]{2,1,0:T(8,128)(2,1)}, u32[]{:S(2)}) copy-start(bf16[4,32,384]{2,1,0:T(8,128)(2,1)} %convert_element_type.493) | copy-start | bytes 294916
  104.6 1.8 %copy-start.59 = (bf16[6,384]{1,0:T(8,128)(2,1)S(1)}, bf16[6,384]{1,0:T(8,128)(2,1)}, u32[]{:S(2)}) copy-start(bf16[6,384]{1,0:T(8,128)(2,1)} %copy-done.58) | copy-start | bytes 13828
  105.4 4.4 %copy-start.45 = (bf16[4,32,384,1]{2,1,0,3:T(8,128)(2,1)}, bf16[4,32,384,1]{2,1,0,3:T(8,128)(2,1)S(1)}, u32[]{:S(2)}) copy-start(bf16[4,32,384,1]{2,1,0,3:T(8,128)(2,1)S(1)} %fusion.235) | copy-start | bytes 294916
  105.9 3.0 %copy-start.14 = (f32[4,32,384]{2,1,0:T(8,128)}, f32[4,32,384]{2,1,0:T(8,128)S(1)}, u32[]{:S(2)}) copy-start(f32[4,32,384]{2,1,0:T(8,128)S(1)} %fusion.260) | copy-start | bytes 589828
  106.3 2.6 %copy-start.12 = (f32[1,4,32,384]{3,2,1,0:T(8,128)}, f32[1,4,32,384]{3,2,1,0:T(8,128)S(1)}, u32[]{:S(2)}) copy-start(f32[1,4,32,384]{3,2,1,0:T(8,128)S(1)} %convolution_bitcast_fusion.13) | copy-start | bytes 589828
  106.3 2.6 %copy-start.51 = (bf16[4,32,384,1]{2,1,0,3:T(8,128)(2,1)}, bf16[4,32,384,1]{2,1,0,3:T(8,128)(2,1)S(1)}, u32[]{:S(2)}) copy-start(bf16[4,32,384,1]{2,1,0,3:T(8,128)(2,1)S(1)} %get-tuple-element.11) | copy-start | bytes 294916
  106.4 3.3 %copy-start.22 = (bf16[4,32,6,384]{3,1,2,0:T(8,128)(2,1)}, bf16[4,32,6,384]{3,1,2,0:T(8,128)(2,1)S(1)}, u32[]{:S(2)}) copy-start(bf16[4,32,6,384]{3,1,2,0:T(8,128)(2,1)S(1)} %broadcast_multiply_fusion) | copy-start | bytes 1769476
  109.8 2.2 %copy-start.43 = (bf16[32,6,4,4]{1,2,3,0:T(4,128)(2,1)}, bf16[32,6,4,4]{1,2,3,0:T(4,128)(2,1)S(1)}, u32[]{:S(2)}) copy-start(bf16[32,6,4,4]{1,2,3,0:T(4,128)(2,1)S(1)} %fusion.222) | copy-start | bytes 18436
  111.0 3.1 %copy-start.62 = (f32[4,32]{1,0:T(4,128)}, f32[4,32]{1,0:T(4,128)S(1)}, u32[]{:S(2)}) copy-start(f32[4,32]{1,0:T(4,128)S(1)} %fusion.323) | copy-start | bytes 1540
  112.3 1.3 copy-start.41
  113.7 1.5 copy-start.16
  114.0 1.2 copy-start.18
  114.1 1.1 copy-start.53
  114.1 1.1 copy-start.55
  116.4 2.6 %copy-start.27 = (f32[4,1,6,32,32]{3,4,2,0,1:T(8,128)S(1)}, f32[4,1,6,32,32]{3,4,2,0,1:T(8,128)}, u32[]{:S(2)}) copy-start(f32[4,1,6,32,32]{3,4,2,0,1:T(8,128)} %get-tuple-element.32) | copy-start | bytes 294916
  116.4 2.6 %copy-start.57 = (f32[4,6,32]{2,1,0:T(8,128)S(1)}, f32[4,6,32]{2,1,0:T(8,128)}, u32[]{:S(2)}) copy-start(f32[4,6,32]{2,1,0:T(8,128)} %multiply_divide_fusion.2) | copy-start | bytes 9220
  117.6 2.1 %copy-start.56 = (bf16[4,32,384,1]{2,1,3,0:T(8,128)(2,1)S(1)}, bf16[4,32,384,1]{2,1,3,0:T(8,128)(2,1)}, u32[]{:S(2)}) copy-start(bf16[4,32,384,1]{2,1,3,0:T(8,128)(2,1)} %copy-done.55) | copy-start | bytes 294916
  117.6 2.1 %copy-start.60 = (bf16[6,384]{1,0:T(8,128)(2,1)S(1)}, bf16[6,384]{1,0:T(8,128)(2,1)}, u32[]{:S(2)}) copy-start(bf16[6,384]{1,0:T(8,128)(2,1)} %copy-done.58) | copy-start | bytes 13828
  117.7 2.1 %copy-start.69 = (f32[4,6,32]{2,1,0:T(8,128)S(1)}, f32[4,6,32]{2,1,0:T(8,128)}, u32[]{:S(2)}) copy-start(f32[4,6,32]{2,1,0:T(8,128)} %copy-done.68) | copy-start | bytes 9220
  119.7 0.9 copy-start.54
  120.6 1.1 copy-start.19
  120.6 1.4 copy-start.38
  121.4 1.1 copy-start.17
  122.5 0.8 copy-start.65
  122.5 0.8 copy-start.63
  122.8 1.0 copy-start.7
  123.3 0.9 copy-start.44
  123.8 0.9 copy-start.46
  124.2 2.9 %copy-start.21 = (f32[1,32,6,4,4]{2,3,4,1,0:T(4,128)S(1)}, f32[1,32,6,4,4]{2,3,4,1,0:T(4,128)}, u32[]{:S(2)}) copy-start(f32[1,32,6,4,4]{2,3,4,1,0:T(4,128)} %copy-done.20) | copy-start | bytes 36868
  124.2 2.9 %copy-start.30 = (f32[32,6,4]{1,2,0:T(4,128)S(1)}, f32[32,6,4]{1,2,0:T(4,128)}, u32[]{:S(2)}) copy-start(f32[32,6,4]{1,2,0:T(4,128)} %multiply_divide_fusion) | copy-start | bytes 9220
  124.7 2.6 %copy-start.23 = (bf16[4,32,6,384]{3,1,2,0:T(8,128)(2,1)S(1)}, bf16[4,32,6,384]{3,1,2,0:T(8,128)(2,1)}, u32[]{:S(2)}) copy-start(bf16[4,32,6,384]{3,1,2,0:T(8,128)(2,1)} %copy-done.22) | copy-start | bytes 1769476
  124.7 2.6 %copy-start.29 = (f32[32,6,4]{1,2,0:T(4,128)S(1)}, f32[32,6,4]{1,2,0:T(4,128)}, u32[]{:S(2)}) copy-start(f32[32,6,4]{1,2,0:T(4,128)} %copy-done.28) | copy-start | bytes 9220
  127.3 0.9 copy-start.52
  128.2 1.2 copy-start.15
  128.2 1.5 copy-start.34
  129.0 1.1 copy-start.13
  130.1 0.8 copy-start.71
  130.5 4.9 %copy-start.67 = (f32[4,6,32]{2,1,0:T(8,128)S(1)}, f32[4,6,32]{2,1,0:T(8,128)}, u32[]{:S(2)}) copy-start(f32[4,6,32]{2,1,0:T(8,128)} %copy-done.66) | copy-start | bytes 9220
  130.5 12.5 %copy-start.5 = (bf16[1,384,8,48]{1,3,2,0:T(8,128)(2,1)S(1)}, bf16[1,384,8,48]{1,3,2,0:T(8,128)(2,1)}, u32[]{:S(2)}) copy-start(bf16[1,384,8,48]{1,3,2,0:T(8,128)(2,1)} %copy-done.4) | copy-start | bytes 884740
  130.9 12.3 %copy-start.26 = (f32[1,4,6,32,32]{3,4,2,1,0:T(8,128)S(1)}, f32[1,4,6,32,32]{3,4,2,1,0:T(8,128)}, u32[]{:S(2)}) copy-start(f32[1,4,6,32,32]{3,4,2,1,0:T(8,128)} %copy-done.25) | copy-start | bytes 294916
  132.0 11.0 %all-to-all-start.4 = ((bf16[32,1,4,384]{3,2,1,0:T(4,128)(2,1)}), bf16[32,1,4,384]{3,2,1,0:T(4,128)(2,1)S(1)}, u32[]{:S(2)}, u32[]{:S(2)}) async-start(bf16[32,1,4,384]{3,2,1,0:T(4,128)(2,1)} %bitcast.135), calls=%async_computation.4 | async-start | bytes 196608 | tf_op jit(solution)/shard_map/all_to_all | solution.py:89
  135.4 8.1 %copy-start.1 = (f32[1,32,4,1152]{3,1,2,0:T(8,128)S(1)}, f32[1,32,4,1152]{3,1,2,0:T(8,128)}, u32[]{:S(2)}) copy-start(f32[1,32,4,1152]{3,1,2,0:T(8,128)} %copy-done) | copy-start | bytes 1769476
  143.2 1.1 copy-start.50
  143.2 1.1 copy-start.61
  144.3 0.9 copy-start.48
  145.2 1.1 copy-start.11
  145.2 1.4 copy-start.32
  145.9 1.1 copy-start.9
  145.9 1.5 copy-start.3
  147.0 0.8 copy-start.70
  (14 other events, 9.5 us)
Sparse Core Ops, SparseCore 0:
  27.1 64.7 all-gather.2

commit v4 on v3

--- a/solution.py
+++ b/solution.py
@@ -51,14 +51,51 @@
     return [(w_inner[i], w_outer[i]) for i in range(subs)]
 
 
-def full_weights(w_project, w_output, sizes):
+def core_pairs(mesh):
+    nz = mesh.shape["gz"]
+    devices = list(mesh.devices.flat)
+    count = len(devices)
+    cores = [getattr(d, "core_on_chip", None) for d in devices]
+    coords = [tuple(getattr(d, "coords", ())) for d in devices]
+    if None not in cores and set(cores) == {0, 1}:
+        place = {(coords[i], cores[i]): i for i in range(count)}
+        partner = [place.get((coords[i], 1 - cores[i])) for i in range(count)]
+        if None not in partner:
+            return cores, partner
+    if nz % 2:
+        return None, None
+    rest = count // nz
+    cores = [(i // rest) % 2 for i in range(count)]
+    partner = [i ^ rest if (i // rest) % 2 == 0 else i - rest for i in range(count)]
+    return cores, partner
+
+
+def gather_blocks(block, cores, partner, sizes):
+    count = sizes[0] * sizes[1] * sizes[2]
+    if cores is None:
+        return lax.all_gather(block, ALL, axis=0, tiled=False)
+    groups = [[i for i in range(count) if cores[i] == c] for c in (0, 1)]
+    mine = lax.all_gather(block, ALL, axis=0, tiled=False, axis_index_groups=groups)
+    other = lax.ppermute(mine, ALL, [(i, partner[i]) for i in range(count)])
+    core = jnp.asarray(cores, jnp.int32)[lax.axis_index(ALL)]
+    both = jnp.concatenate(
+        [jnp.where(core == 0, mine, other), jnp.where(core == 0, other, mine)]
+    )
+    order = groups[0] + groups[1]
+    nz = sizes[0]
+    rest = count // nz
+    swapped = [(2 * x + c) * rest + r for c in range(2) for x in range(nz // 2) for r in range(rest)]
+    if order == swapped:
+        both = both.reshape((2, nz // 2, count // nz) + block.shape)
+        return jnp.swapaxes(both, 0, 1).reshape((count,) + block.shape)
+    inverse = sorted(range(count), key=lambda i: order[i])
+    return jnp.take(both, jnp.asarray(inverse, jnp.int32), axis=0)
+
+
+def full_weights(w_project, w_output, sizes, pairs):
     subs, din, dproj = w_project.shape
     cat = jnp.concatenate([w_project, w_output], axis=2)
-    devices = sizes[0] * sizes[1] * sizes[2]
-    first = jnp.broadcast_to(cat[:1][None], (devices,) + cat[:1].shape)
-    first = lax.all_to_all(first, ALL, 0, 0, tiled=True)
-    rest = lax.all_gather(cat[1:], ALL, axis=0, tiled=False)
-    return arrange(first, sizes, dproj) + arrange(rest, sizes, dproj)
+    return arrange(gather_blocks(cat, *pairs, sizes), sizes, dproj)
 
 
 def depth_fn(member, w_inner, w_outer):
@@ -97,8 +134,8 @@
     return jnp.transpose(got, (0, 2, 1, 3, 4)).reshape(ny * yl, nx * xl, feat)
 
 
-def local(volume, cotangent, w_project, w_output, sizes):
-    w_depth, w_row, w_col = full_weights(w_project, w_output, sizes)
+def local(volume, cotangent, w_project, w_output, sizes, pairs):
+    w_depth, w_row, w_col = full_weights(w_project, w_output, sizes, pairs)
 
     depth_act = lax.all_to_all(volume, "gz", 2, 0, tiled=True)
     cot_plane = block_to_plane(cotangent, sizes)
@@ -126,8 +163,8 @@
     return lax.all_to_all(stacked, axis, split_axis=split_axis, concat_axis=concat_axis, tiled=True)
 
 
-def local_general(volume, cotangent, w_project, w_output, sizes):
-    w_depth, w_row, w_col = full_weights(w_project, w_output, sizes)
+def local_general(volume, cotangent, w_project, w_output, sizes, pairs):
+    w_depth, w_row, w_col = full_weights(w_project, w_output, sizes, pairs)
 
     def row_fn(member):
         return along_rows(member, *w_row)
@@ -151,10 +188,11 @@
 
 def solution(mesh):
     sizes = (mesh.shape["gz"], mesh.shape["gy"], mesh.shape["gx"])
+    pairs = core_pairs(mesh)
 
     def body(volume, *rest):
         one_depth = volume.shape[0] * sizes[0] == mesh.size
-        return (local if one_depth else local_general)(volume, *rest, sizes)
+        return (local if one_depth else local_general)(volume, *rest, sizes, pairs)
 
     return jax.shard_map(
         body,

time: 163 us -> 185 us (1.13)
  waiting for transfers between devices: 61.8 us -> 81.1 us
  other arithmetic: 3.36 us -> 8.27 us
  starting transfers between devices: 19.8 us -> 15.3 us
    all_gather x1, waiting for transfers between devices: 2.14 us -> 65.8 us  [gather_blocks(): lax.all_gather(block, ALL, axis=0, tiled=False, axis_index_groups=groups)]
    all_to_all x1 -> x0, waiting for transfers between devices: 42.2 us -> none  [full_weights(): first = lax.all_to_all(first, ALL, 0, 0, tiled=True)]
    transpose x1, local copies, waits for them, and re-layouts: 1.17 us -> 9.66 us  [arrange(): jnp.transpose(got, (3, 1, 4, 0, 2, 5))]
    all_to_all x1 -> x0, starting transfers between devices: 5.44 us -> none  [full_weights(): first = lax.all_to_all(first, ALL, 0, 0, tiled=True)]
    reshape x1 -> x0, local copies, waits for them, and re-layouts: 5.39 us -> none  [arrange(): got = got.reshape(nz, ny, nx, subs, din, width)]
    unnamed x147 -> x79, local copies, waits for them, and re-layouts: 8.92 us -> 4.01 us
    reshape x2 -> x1, local copies, waits for them, and re-layouts: 4.32 us -> 6.88 us  [arrange(): jnp.transpose(got, (3, 1, 4, 0, 2, 5))]
    transpose x0 -> x1, local copies, waits for them, and re-layouts: none -> 2.54 us  [gather_blocks(): return jnp.swapaxes(both, 0, 1).reshape((count,) + block.shape)]
  transfers between devices with their start and end apart: 6 -> 6, of which waited for: 5 -> 4; matrix products, arithmetic and copies ran while one was open for 20% -> 18% of each run, Pallas kernels for 0% -> 0%
where the time goes in v4:
time: 185 us; the launch traced here: 184 us
  waiting for transfers between devices  81.1 us (44%)
  local copies, waits for them, and re-layouts  30.6 us (17%)
  matrix products  26.8 us (14%)
  starting transfers between devices  15.3 us (8%)
  between operations  15.1 us (8%)
  other arithmetic  8.27 us (4%)
  blocking collectives  6.67 us (4%)
    all_gather x1, waiting for transfers between devices, gather_blocks(): lax.all_gather(block, ALL, axis=0, tiled=False, axis_index_groups=groups)  65.8 us
    transpose x1, local copies, waits for them, and re-layouts, arrange(): jnp.transpose(got, (3, 1, 4, 0, 2, 5))  9.66 us
    all_to_all x1, waiting for transfers between devices, from_planes(): return lax.all_to_all(parts, ALL, 0, 0, tiled=True)  7.34 us
    reshape x1, local copies, waits for them, and re-layouts, arrange(): jnp.transpose(got, (3, 1, 4, 0, 2, 5))  6.88 us
    dot_general x9, matrix products, sublayer(): jnp.einsum('plqd,pkqhd->pqhlk', queries, key_heads, preferred_element_typ...  6.76 us
    all_to_all x1, blocking collectives, local(): return lax.all_to_all(grad_zero, 'gz', 0, 2, tiled=True)  6.67 us
    all_to_all x1, waiting for transfers between devices, to_planes(): got = lax.all_to_all(depth_lines, ALL, 0, 0, tiled=True)  6.28 us
    dot_general x8, matrix products, sublayer(): jnp.einsum('pqhlk,pkqd->plqhd', attn_weights, value_part, preferred_eleme...  5.94 us
  transfers between devices with their start and end apart: 6, of which 4 were waited for; matrix products, arithmetic and copies ran while one was open for 18% of the time, Pallas kernels for 0%

profile of v4, /device:TPU:0, one launch (start us, length us, event | category | flops | bytes accessed | tf_op | source)
XLA Modules:
  0.0 183.8 jit_solution(14618442254983251265)
XLA Ops:
  6.5 1.0 copy.214
  7.6 0.9 copy.215
  8.4 0.8 pad_maximum_fusion.1
  9.2 65.8 %all-gather.3.cloned.1.call-done = bf16[48,96,192]{2,1,0:T(8,128)(2,1)} async-done(((bf16[3,96,192]{2,1,0:T(8,128)(2,1)}), bf16[48,96,192]{2,1,0:T(8,128)(2,1)}) %all-gather.3.cloned.1.call-update) | async-done | bytes 1769488 | tf_op jit(solution)/shard_map/all_gather | solution.py:78
  75.1 1.6 copy.219
  76.6 3.3 %all-to-all-start.1 = ((bf16[8,1,16,384]{3,0,1,2:T(8,128)(2,1)}), bf16[8,1,16,384]{3,0,1,2:T(8,128)(2,1)S(1)}, u32[]{:S(2)}, u32[]{:S(2)}) async-start(bf16[8,1,16,384]{3,0,1,2:T(8,128)(2,1)} %copy.219), calls=%async_computation.1 | async-start | bytes 196608 | tf_op jit(solution)/shard_map/all_to_all | solution.py:140
  79.9 0.6 fusion.322
  80.5 1.3 dynamic_slice.3
  82.6 1.6 all-to-all-done.1
  84.2 4.0 %all-to-all-start = ((bf16[8,1,16,384]{3,2,1,0:T(8,128)(2,1)}), bf16[8,1,16,384]{3,2,1,0:T(8,128)(2,1)}, u32[]{:S(2)}, u32[]{:S(2)}) async-start(bf16[8,1,16,384]{3,2,1,0:T(8,128)(2,1)} %param.6), calls=%async_computation | async-start | bytes 196608 | tf_op jit(solution)/shard_map/all_to_all | solution.py:132
  88.3 0.6 multiply_add_fusion.1
  88.9 0.7 add.133
  89.6 2.0 %broadcast_select_fusion.1 = (bf16[16,3,96,192]{3,2,1,0:T(8,128)(2,1)S(1)}, bf16[16,3,96,192]{3,2,1,0:T(8,128)(2,1)S(1)}) fusion(bf16[16,3,96,192]{3,2,1,0:T(8,128)(2,1)} %bitcast.622, bf16[16,3,96,192]{3,2,1,0:T(8,128)(2,1)S(1)} %collective-permute-done, pred[]{:T(512)} %bitcast.1), kind=kLoop, calls=%fused_computation.5 | loop fusion | flops 1769472 | bytes 7077889 | tf_op jit(solution)/shard_map/jit(_where)/select_n | solution.py:82
  91.6 0.8 pad_maximum_fusion
  92.3 2.5 %copy.216 = bf16[2,2,8,3,96,192]{5,4,3,2,1,0:T(8,128)(2,1)} copy(bf16[2,2,8,3,96,192]{5,4,3,2,0,1:T(8,128)(2,1)S(1)} %bitcast.604) | data formatting | bytes 7077888 | tf_op jit(solution)/shard_map/transpose | solution.py:90
  94.9 9.7 %copy.217 = bf16[3,4,96,4,2,192]{2,1,5,4,3,0:T(4,128)(2,1)} copy(bf16[3,4,96,4,2,192]{5,2,0,4,1,3:T(8,128)(2,1)} %bitcast.605) | data formatting | bytes 7077888 | tf_op jit(solution)/shard_map/transpose | solution.py:48
  104.5 6.9 %reshape.796 = bf16[3,384,8,192]{1,3,2,0:T(8,128)(2,1)S(1)} reshape(bf16[3,4,96,4,2,192]{2,1,5,4,3,0:T(4,128)(2,1)} %copy.217) | data formatting | bytes 7077888 | tf_op jit(solution)/shard_map/reshape | solution.py:48
  111.5 1.5 fusion.338
  113.0 0.4 convolution_bitcast_fusion.2
  113.4 0.4 fusion.102
  113.8 0.4 fusion.101
  114.2 0.9 fusion.337
  116.3 0.4 fusion.9
  116.9 0.7 copy.226
  117.6 5.2 %all-to-all-start.2 = ((bf16[32,1,4,384]{3,2,1,0:T(4,128)(2,1)}), bf16[32,1,4,384]{3,2,1,0:T(4,128)(2,1)S(1)}, u32[]{:S(2)}, u32[]{:S(2)}) async-start(bf16[32,1,4,384]{3,2,1,0:T(4,128)(2,1)} %copy.226), calls=%async_computation.2 | async-start | bytes 196608 | tf_op jit(solution)/shard_map/all_to_all | solution.py:115
  122.8 1.1 fusion.71
  123.9 6.3 %all-to-all-done.2 = bf16[32,1,4,384]{3,2,1,0:T(4,128)(2,1)S(1)} async-done(((bf16[32,1,4,384]{3,2,1,0:T(4,128)(2,1)}), bf16[32,1,4,384]{3,2,1,0:T(4,128)(2,1)S(1)}, u32[]{:S(2)}, u32[]{:S(2)}) %all-to-all-start.2) | async-done | bytes 98336 | tf_op jit(solution)/shard_map/all_to_all | solution.py:115
  130.3 0.6 multiply_add_fusion
  131.1 0.4 convolution_bitcast_fusion.1
  131.5 0.4 fusion.100
  131.9 0.4 fusion.99
  133.1 0.9 broadcast_multiply_fusion
  134.1 3.6 %fusion.342 = (f32[32,6,4]{1,2,0:T(4,128)S(1)}, f32[1,32,6,4,4]{2,3,4,1,0:T(4,128)S(1)}) fusion(bf16[4,32,384,1]{2,1,0,3:T(8,128)(2,1)S(1)} %get-tuple-element.15, bf16[4,32,6,384]{3,1,2,0:T(8,128)(2,1)} %broadcast_multiply_fusion), kind=kOutput, calls=%fused_computation.401 | convolution fusion | flops 2364672 | bytes 703488 | tf_op jit(solution)/shard_map/jvp(plqd,pkqhd->pqhlk)/dot_general | solution.py:35
  137.7 0.8 fusion
  138.9 0.4 convolution_bitcast_fusion
  139.3 0.4 fusion.98
  139.7 0.4 fusion.97
  140.1 0.3 fusion.255
  141.4 0.7 fusion.146
  142.8 0.4 fusion.96
  143.1 0.3 add_add_fusion.8
  143.5 0.4 fusion.95
  143.9 0.3 add_add_fusion.7
  144.2 0.4 multiply_reduce_fusion.1
  144.7 1.0 fusion.180
  146.1 0.4 fusion.53
  146.5 2.4 %fusion.1 = bf16[32,6,4,4]{1,3,2,0:T(4,128)(2,1)S(1)} fusion(f32[4,32,384]{2,0,1:T(4,128)S(1)} %copy.239, f32[6,384]{1,0:T(8,128)S(1)} %get-tuple-element.27, bf16[4,32,384,1]{2,1,0,3:T(8,128)(2,1)S(1)} %copy-done.21), kind=kOutput, calls=%fused_computation.8 | convolution fusion | flops 2654208 | bytes 310272 | tf_op jit(solution)/shard_map/transpose(jvp(pqhlk,pkqd->plqhd))/dot_general | solution.py:38
  149.1 0.8 fusion.13
  150.1 0.6 convolution_bitcast_fusion.8
  150.8 0.6 copy.370
  151.4 0.4 fusion.94
  152.1 0.4 fusion.93
  153.0 1.4 multiply_reduce_fusion
  154.5 0.7 copy.249
  155.2 2.8 %all-to-all-start.3 = ((bf16[32,1,4,384]{3,2,1,0:T(4,128)(2,1)}), bf16[32,1,4,384]{3,2,1,0:T(4,128)(2,1)S(1)}, u32[]{:S(2)}, u32[]{:S(2)}) async-start(bf16[32,1,4,384]{3,2,1,0:T(4,128)(2,1)} %bitcast.136), calls=%async_computation.3 | async-start | bytes 196608 | tf_op jit(solution)/shard_map/all_to_all | solution.py:126
  158.0 7.3 %all-to-all-done.3 = bf16[32,1,4,384]{3,2,1,0:T(4,128)(2,1)S(1)} async-done(((bf16[32,1,4,384]{3,2,1,0:T(4,128)(2,1)}), bf16[32,1,4,384]{3,2,1,0:T(4,128)(2,1)S(1)}, u32[]{:S(2)}, u32[]{:S(2)}) %all-to-all-start.3) | async-done | bytes 98336 | tf_op jit(solution)/shard_map/all_to_all | solution.py:126
  165.9 0.7 fusion.142
  167.4 0.4 fusion.92
  167.8 0.3 add_add_fusion.2
  168.2 0.4 fusion.91
  168.5 0.3 add_add_fusion.1
  168.9 0.4 fusion.202
  169.5 6.7 %all_to_all.42 = bf16[32,1,4,384]{3,2,1,0:T(4,128)(2,1)S(1)} all-to-all(bf16[32,1,4,384]{3,2,1,0:T(4,128)(2,1)S(1)} %copy.255), channel_id=1, replica_groups=mesh['gz'=4,'gy'=4,'gx'=2] {'gz'}, dimensions={0} | all-to-all | bytes 196608 | tf_op jit(solution)/shard_map/all_to_all | solution.py:149
  176.3 0.7 all_to_all.36
  (131 shorter events, 7.8 us)
Async XLA Ops:
  6.5 68.5 %all-gather.3.cloned.1.call-start = ((), (), s32[]{:S(2)}) async-start(), calls=%async_computation.5 | async-start | bytes 2506752 | tf_op jit(solution)/shard_map/all_gather | solution.py:78
  75.1 14.5 %collective-permute-start = (bf16[16,3,96,192]{3,2,1,0:T(8,128)(2,1)}, bf16[16,3,96,192]{3,2,1,0:T(8,128)(2,1)S(1)}, u32[]{:S(2)}, u32[]{:S(2)}) collective-permute-start(bf16[16,3,96,192]{3,2,1,0:T(8,128)(2,1)} %bitcast.621), channel_id=1, source_target_pairs={{0,8},{1,9},{2,10},{3,11},{4,12},{5,13},{6,14},{7,15},{8,0},{9,1},... | collective-permute-start | bytes 5308424 | tf_op jit(solution)/shard_map/ppermute | solution.py:79
  76.6 7.6 %all-to-all-start.1 = ((bf16[8,1,16,384]{3,0,1,2:T(8,128)(2,1)}), bf16[8,1,16,384]{3,0,1,2:T(8,128)(2,1)S(1)}, u32[]{:S(2)}, u32[]{:S(2)}) async-start(bf16[8,1,16,384]{3,0,1,2:T(8,128)(2,1)} %copy.219), calls=%async_computation.1 | async-start | bytes 196608 | tf_op jit(solution)/shard_map/all_to_all | solution.py:140
  84.2 7.4 %copy-start.9 = (bf16[8,1,16,384]{3,0,1,2:T(8,128)(2,1)}, bf16[8,1,16,384]{3,0,1,2:T(8,128)(2,1)S(1)}, u32[]{:S(2)}) copy-start(bf16[8,1,16,384]{3,0,1,2:T(8,128)(2,1)S(1)} %all-to-all-done.1) | copy-start | bytes 294916
  84.2 33.4 %all-to-all-start = ((bf16[8,1,16,384]{3,2,1,0:T(8,128)(2,1)}), bf16[8,1,16,384]{3,2,1,0:T(8,128)(2,1)}, u32[]{:S(2)}, u32[]{:S(2)}) async-start(bf16[8,1,16,384]{3,2,1,0:T(8,128)(2,1)} %param.6), calls=%async_computation | async-start | bytes 196608 | tf_op jit(solution)/shard_map/all_to_all | solution.py:132
  111.4 1.5 copy-start.10
  111.4 1.5 copy-start.29
  113.0 2.2 %copy-start.4 = (bf16[1,384,8,144]{1,3,2,0:T(8,128)(2,1)}, bf16[1,384,8,144]{1,3,2,0:T(8,128)(2,1)S(1)}, u32[]{:S(2)}) copy-start(bf16[1,384,8,144]{1,3,2,0:T(8,128)(2,1)S(1)} %get-tuple-element.12) | copy-start | bytes 2654212
  113.4 2.8 %copy-start = (f32[1,32,4,1152]{3,1,2,0:T(8,128)}, f32[1,32,4,1152]{3,1,2,0:T(8,128)S(1)}, u32[]{:S(2)}) copy-start(f32[1,32,4,1152]{3,1,2,0:T(8,128)S(1)} %convolution_bitcast_fusion.2) | copy-start | bytes 1769476
  113.8 2.1 %copy-start.16 = (f32[32,4,6]{0,2,1:T(8,128)}, f32[32,4,6]{0,2,1:T(8,128)S(1)}, u32[]{:S(2)}) copy-start(f32[32,4,6]{0,2,1:T(8,128)S(1)} %fusion.102) | copy-start | bytes 9220
  114.2 1.7 copy-start.18
  114.2 1.7 copy-start.30
  115.1 1.5 copy-start.7
  115.9 0.8 copy-start.22
  115.9 0.8 copy-start.24
  116.2 0.7 copy-start.34
  116.2 7.7 %copy-start.14 = (f32[1,4,6,32,32]{3,4,2,1,0:T(8,128)}, f32[1,4,6,32,32]{3,4,2,1,0:T(8,128)S(1)}, u32[]{:S(2)}) copy-start(f32[1,4,6,32,32]{3,4,2,1,0:T(8,128)S(1)} %get-tuple-element.30) | copy-start | bytes 294916
  116.2 6.6 %copy-start.12 = (bf16[1,384,8,48]{1,3,2,0:T(8,128)(2,1)S(1)}, bf16[1,384,8,48]{1,3,2,0:T(8,128)(2,1)}, u32[]{:S(2)}) copy-start(bf16[1,384,8,48]{1,3,2,0:T(8,128)(2,1)} %get-tuple-element.7) | copy-start | bytes 884740
  116.2 14.8 %copy-start.2 = (bf16[1,384,8,144]{1,3,2,0:T(8,128)(2,1)S(1)}, bf16[1,384,8,144]{1,3,2,0:T(8,128)(2,1)}, u32[]{:S(2)}) copy-start(bf16[1,384,8,144]{1,3,2,0:T(8,128)(2,1)} %get-tuple-element.11) | copy-start | bytes 2654212
  117.6 12.6 %all-to-all-start.2 = ((bf16[32,1,4,384]{3,2,1,0:T(4,128)(2,1)}), bf16[32,1,4,384]{3,2,1,0:T(4,128)(2,1)S(1)}, u32[]{:S(2)}, u32[]{:S(2)}) async-start(bf16[32,1,4,384]{3,2,1,0:T(4,128)(2,1)} %copy.226), calls=%async_computation.2 | async-start | bytes 196608 | tf_op jit(solution)/shard_map/all_to_all | solution.py:115
  131.1 2.0 %copy-start.31 = (bf16[6,384]{1,0:T(8,128)(2,1)S(1)}, bf16[6,384]{1,0:T(8,128)(2,1)}, u32[]{:S(2)}) copy-start(bf16[6,384]{1,0:T(8,128)(2,1)} %get-tuple-element.28) | copy-start | bytes 13828
  132.3 5.4 %copy-start.20 = (bf16[4,32,384,1]{2,1,0,3:T(8,128)(2,1)}, bf16[4,32,384,1]{2,1,0,3:T(8,128)(2,1)S(1)}, u32[]{:S(2)}) copy-start(bf16[4,32,384,1]{2,1,0,3:T(8,128)(2,1)S(1)} %fusion.234) | copy-start | bytes 294916
  133.1 4.6 %copy-start.26 = (bf16[4,32,384,1]{2,1,0,3:T(8,128)(2,1)}, bf16[4,32,384,1]{2,1,0,3:T(8,128)(2,1)S(1)}, u32[]{:S(2)}) copy-start(bf16[4,32,384,1]{2,1,0,3:T(8,128)(2,1)S(1)} %get-tuple-element.15) | copy-start | bytes 294916
  134.0 4.5 %copy-start.6 = (bf16[1,384,8,48]{1,3,2,0:T(8,128)(2,1)S(1)}, bf16[1,384,8,48]{1,3,2,0:T(8,128)(2,1)}, u32[]{:S(2)}) copy-start(bf16[1,384,8,48]{1,3,2,0:T(8,128)(2,1)} %get-tuple-element.8) | copy-start | bytes 884740
  137.6 1.3 copy-start.3
  144.6 1.8 copy-start.21
  146.1 3.0 %copy-start.27 = (bf16[4,32,384,1]{2,1,0,3:T(8,128)(2,1)S(1)}, bf16[4,32,384,1]{2,1,0,3:T(8,128)(2,1)}, u32[]{:S(2)}) copy-start(bf16[4,32,384,1]{2,1,0,3:T(8,128)(2,1)} %copy-done.26) | copy-start | bytes 294916
  146.1 3.0 %copy-start.32 = (bf16[6,384]{1,0:T(8,128)(2,1)S(1)}, bf16[6,384]{1,0:T(8,128)(2,1)}, u32[]{:S(2)}) copy-start(bf16[6,384]{1,0:T(8,128)(2,1)} %get-tuple-element.28) | copy-start | bytes 13828
  149.1 1.1 copy-start.13
  150.8 2.1 %copy-start.28 = (f32[4,2,4,4]{3,2,1,0:T(4,128)S(1)}, f32[4,2,4,4]{3,2,1,0:T(4,128)}, u32[]{:S(2)}) copy-start(f32[4,2,4,4]{3,2,1,0:T(4,128)} %get-tuple-element.19) | copy-start | bytes 1540
  152.9 5.1 %copy-start.35 = (f32[4,6,32]{2,1,0:T(8,128)S(1)}, f32[4,6,32]{2,1,0:T(8,128)}, u32[]{:S(2)}) copy-start(f32[4,6,32]{2,1,0:T(8,128)} %copy-done.34) | copy-start | bytes 9220
  152.9 12.5 %copy-start.8 = (bf16[1,384,8,48]{1,3,2,0:T(8,128)(2,1)S(1)}, bf16[1,384,8,48]{1,3,2,0:T(8,128)(2,1)}, u32[]{:S(2)}) copy-start(bf16[1,384,8,48]{1,3,2,0:T(8,128)(2,1)} %copy-done.7) | copy-start | bytes 884740
  153.0 12.6 %copy-start.15 = (f32[1,4,6,32,32]{3,4,2,1,0:T(8,128)S(1)}, f32[1,4,6,32,32]{3,4,2,1,0:T(8,128)}, u32[]{:S(2)}) copy-start(f32[1,4,6,32,32]{3,4,2,1,0:T(8,128)} %copy-done.14) | copy-start | bytes 294916
  154.5 11.4 %copy-start.1 = (f32[1,32,4,1152]{3,1,2,0:T(8,128)S(1)}, f32[1,32,4,1152]{3,1,2,0:T(8,128)}, u32[]{:S(2)}) copy-start(f32[1,32,4,1152]{3,1,2,0:T(8,128)} %copy-done) | copy-start | bytes 1769476
  155.2 10.2 %all-to-all-start.3 = ((bf16[32,1,4,384]{3,2,1,0:T(4,128)(2,1)}), bf16[32,1,4,384]{3,2,1,0:T(4,128)(2,1)S(1)}, u32[]{:S(2)}, u32[]{:S(2)}) async-start(bf16[32,1,4,384]{3,2,1,0:T(4,128)(2,1)} %bitcast.136), calls=%async_computation.3 | async-start | bytes 196608 | tf_op jit(solution)/shard_map/all_to_all | solution.py:126
  165.6 1.1 copy-start.25
  165.6 1.1 copy-start.33
  165.6 1.1 copy-start.36
  165.9 1.1 copy-start.23
  166.7 0.7 copy-start.17
  167.0 1.1 copy-start.19
  167.4 1.5 copy-start.5
  167.4 1.5 copy-start.11
  168.2 1.2 copy-start.37
Sparse Core Ops, SparseCore 0:
  10.0 65.0 all-gather.2

commit v5 on v2

--- a/solution.py
+++ b/solution.py
@@ -20,14 +20,20 @@
     return (vector * jnp.dot(scale, ones.T, precision=HIGHEST)).astype(jnp.bfloat16)
 
 
-def sublayer(line_rows, w_inner, w_outer):
+def project(rows, weights, lo, hi):
+    full = jnp.einsum("...d,acdn->...acn", rows, weights, preferred_element_type=jnp.float32)
+    part = full[..., lo:hi]
+    return part.reshape(part.shape[:-3] + (-1,))
+
+
+def sublayer(line_rows, weights, dproj):
     feat_len = line_rows.shape[-1]
     head_size = feat_len // HEADS
     ones = head_map(feat_len)
     mask = ones.T.astype(jnp.bfloat16)
     stream = line_rows.astype(jnp.float32)
     normed = (stream * lax.rsqrt(jnp.mean(stream * stream, axis=-1, keepdims=True) + 1e-06)).astype(jnp.bfloat16)
-    packed = jnp.dot(normed, w_inner, preferred_element_type=jnp.float32)
+    packed = project(normed, weights, 0, dproj)
     queries = head_norm(packed[..., :feat_len], ones)
     key_part = head_norm(packed[..., feat_len : 2 * feat_len], ones)
     value_part = packed[..., 2 * feat_len :].astype(jnp.bfloat16)
@@ -37,7 +43,7 @@
     attn_weights = (powers / jnp.sum(powers, axis=-1, keepdims=True)).astype(jnp.bfloat16)
     mixed_heads = jnp.einsum("pqhlk,pkqd->plqhd", attn_weights, value_part, preferred_element_type=jnp.float32)
     mixed_out = jnp.sum(mixed_heads * mask.astype(jnp.float32), axis=-2).astype(jnp.bfloat16)
-    update = jnp.dot(mixed_out, w_outer, preferred_element_type=jnp.float32)
+    update = project(mixed_out, weights, dproj, weights.shape[-1])
     return (stream + update).astype(jnp.bfloat16)
 
 
@@ -45,18 +51,15 @@
     nz, ny, nx = sizes
     subs, din, dproj = w_project.shape
     cat = jnp.concatenate([w_project, w_output], axis=2)
-    got = lax.all_gather(cat, ALL, axis=0, tiled=False)
-    got = got.reshape(nz, ny, nx, subs, din, cat.shape[2])
-    got = jnp.transpose(got, (3, 1, 4, 0, 2, 5)).reshape(subs, ny * din, nz * nx, cat.shape[2])
-    w_inner = got[:, :, :, :dproj].reshape(subs, ny * din, nz * nx * dproj)
-    w_outer = got[:, :, :, dproj:].reshape(subs, ny * din, -1)
-    return [(w_inner[i], w_outer[i]) for i in range(subs)]
+    got = lax.all_gather(cat, ("gz", "gx", "gy"), axis=1, tiled=False)
+    got = got.reshape(subs, nz, nx, ny * din, cat.shape[2])
+    return [(got[i], dproj) for i in range(subs)]
 
 
-def depth_fn(member, w_inner, w_outer):
+def depth_fn(member, weights, dproj):
     depth_len, row_len, rest_len, feat_len = member.shape
     flat_lines = member.reshape(1, depth_len, row_len * rest_len, feat_len)
-    return sublayer(flat_lines, w_inner, w_outer).reshape(member.shape)
+    return sublayer(flat_lines, weights, dproj).reshape(member.shape)
 
 
 def plane_fn(plane, w_row, w_col):
@@ -104,14 +107,14 @@
     return lax.all_to_all(grad_zero, "gz", 0, 2, tiled=True)
 
 
-def along_rows(member, w_inner, w_outer):
-    return sublayer(member, w_inner, w_outer)
+def along_rows(member, weights, dproj):
+    return sublayer(member, weights, dproj)
 
 
-def along_columns(member, w_inner, w_outer):
+def along_columns(member, weights, dproj):
     depth_len, row_len, col_len, feat_len = member.shape
     flat_lines = member.reshape(depth_len * row_len, col_len, 1, feat_len)
-    return sublayer(flat_lines, w_inner, w_outer).reshape(member.shape)
+    return sublayer(flat_lines, weights, dproj).reshape(member.shape)
 
 
 def line_swap(stacked, axis, split_axis, concat_axis):

time: 165 us -> 257 us (1.56); the launches traced: 164 us -> 253 us
  local copies, waits for them, and re-layouts: 28 us -> 89.9 us
  starting transfers between devices: 16.5 us -> 30.2 us
  matrix products: 25.8 us -> 36.4 us
    slice x2 -> x11, local copies, waits for them, and re-layouts: 2.42 us -> 44.6 us  [the longest x4 35.9 us: full_weights(): return [(got[i], dproj) for i in range(subs)]]
    squeeze x0 -> x3, local copies, waits for them, and re-layouts: none -> 11.3 us  [full_weights(): return [(got[i], dproj) for i in range(subs)]]
    all_to_all x1, starting transfers between devices: 3.08 us -> 13.7 us  [to_planes(): got = lax.all_to_all(depth_lines, ALL, 0, 0, tiled=True)]
    all_to_all x1, waiting for transfers between devices: 0.01 us -> 6.9 us  [block_to_plane(): got = lax.all_to_all(block, ('gy', 'gx'), 0, 0, tiled=True)]
    all_to_all x1, waiting for transfers between devices: 6.29 us -> 0.01 us  [to_planes(): got = lax.all_to_all(depth_lines, ALL, 0, 0, tiled=True)]
    unnamed x75 -> x143, local copies, waits for them, and re-layouts: 5.27 us -> 10.6 us
    dot_general x11, matrix products: 4.55 us -> 9.38 us  [project(): jnp.einsum('...d,acdn->...acn', rows, weights, preferred_element_type=jnp...]
    all_to_all x1, starting transfers between devices: 2.79 us -> 5.97 us  [from_planes(): return lax.all_to_all(parts, ALL, 0, 0, tiled=True)]
  transfers between devices with their start and end apart: 5 -> 5, of which waited for: 4 -> 4; matrix products, arithmetic and copies ran while one was open for 17% -> 10% of each run, Pallas kernels for 0% -> 0%
where the time goes in v5:
time: 257 us; the launch traced here: 253 us
  local copies, waits for them, and re-layouts  89.9 us (35%)
  waiting for transfers between devices  68.1 us (26%)
  matrix products  36.4 us (14%)
  starting transfers between devices  30.2 us (12%)
  between operations  15 us (6%)
  blocking collectives  6.67 us (3%)
  other arithmetic  6.6 us (3%)
    all_gather x1, waiting for transfers between devices, full_weights(): got = lax.all_gather(cat, ('gz', 'gx', 'gy'), axis=1, tiled=False)  49.3 us
    slice x4, local copies, waits for them, and re-layouts, full_weights(): return [(got[i], dproj) for i in range(subs)]  35.9 us
    reshape x11, local copies, waits for them, and re-layouts, project(): return part.reshape(part.shape[:-3] + (-1,))  15.7 us
    all_to_all x1, starting transfers between devices, to_planes(): got = lax.all_to_all(depth_lines, ALL, 0, 0, tiled=True)  13.7 us
    squeeze x3, local copies, waits for them, and re-layouts, full_weights(): return [(got[i], dproj) for i in range(subs)]  11.3 us
    unnamed x143, local copies, waits for them, and re-layouts  10.6 us
    dot_general x11, matrix products, project(): jnp.einsum('...d,acdn->...acn', rows, weights, preferred_element_type=jnp...  9.38 us
    slice x6, local copies, waits for them, and re-layouts, project(): part = full[..., lo:hi]  8 us
  transfers between devices with their start and end apart: 5, of which 4 were waited for; matrix products, arithmetic and copies ran while one was open for 10% of the time, Pallas kernels for 0%

profile of v5, /device:TPU:0, one launch (start us, length us, event | category | flops | bytes accessed | tf_op | source)
XLA Modules:
  0.0 252.9 jit_solution(16222625559598440439)
XLA Ops:
  6.5 0.9 copy.301
  7.5 1.1 copy.300
  8.5 0.9 pad_maximum_fusion
  10.1 4.2 %all-to-all-start.1 = ((bf16[8,1,16,384]{3,0,1,2:T(8,128)(2,1)}), bf16[8,1,16,384]{3,0,1,2:T(8,128)(2,1)S(1)}, u32[]{:S(2)}, u32[]{:S(2)}) async-start(bf16[8,1,16,384]{3,0,1,2:T(8,128)(2,1)} %copy.304), calls=%async_computation.1 | async-start | bytes 196608 | tf_op jit(solution)/shard_map/all_to_all | solution.py:98
  14.4 4.3 %all-to-all-done.1 = bf16[8,1,16,384]{3,0,1,2:T(8,128)(2,1)S(1)} async-done(((bf16[8,1,16,384]{3,0,1,2:T(8,128)(2,1)}), bf16[8,1,16,384]{3,0,1,2:T(8,128)(2,1)S(1)}, u32[]{:S(2)}, u32[]{:S(2)}) %all-to-all-start.1) | async-done | bytes 98336 | tf_op jit(solution)/shard_map/all_to_all | solution.py:98
  18.6 6.4 %all-to-all-start = ((bf16[8,1,16,384]{3,2,1,0:T(8,128)(2,1)}), bf16[8,1,16,384]{3,2,1,0:T(8,128)(2,1)S(1)}, u32[]{:S(2)}, u32[]{:S(2)}) async-start(bf16[8,1,16,384]{3,2,1,0:T(8,128)(2,1)} %param.5), calls=%async_computation | async-start | bytes 196608 | tf_op jit(solution)/shard_map/all_to_all | solution.py:90
  25.1 0.7 add.151
  25.8 6.9 %all-to-all-done = bf16[8,1,16,384]{3,2,1,0:T(8,128)(2,1)S(1)} async-done(((bf16[8,1,16,384]{3,2,1,0:T(8,128)(2,1)}), bf16[8,1,16,384]{3,2,1,0:T(8,128)(2,1)S(1)}, u32[]{:S(2)}, u32[]{:S(2)}) %all-to-all-start) | async-done | bytes 98336 | tf_op jit(solution)/shard_map/all_to_all | solution.py:90
  32.9 0.8 copy.299
  33.7 49.3 %all-gather.3.cloned.1.call-done = bf16[3,3072,192]{2,0,1:T(4,128)(2,1)} async-done(((bf16[3,96,192]{2,0,1:T(4,128)(2,1)}), bf16[3,3072,192]{2,0,1:T(4,128)(2,1)}) %all-gather.3.cloned.1.call-update) | async-done | bytes 3538960 | tf_op jit(solution)/shard_map/all_gather | solution.py:54
  83.0 15.2 %fusion.348 = (bf16[1,3072,192]{2,0,1:T(2,128)(2,1)S(1)}, bf16[1,3072,192]{2,0,1:T(2,128)(2,1)}, bf16[1,3072,192]{2,0,1:T(2,128)(2,1)}) fusion(bf16[3,3072,192]{2,0,1:T(4,128)(2,1)} %all-gather.3.cloned.1.call-done), kind=kLoop, calls=%fused_computation.414 | loop fusion | bytes 7077888 | tf_op jit(solution)/shard_map/slice | solution.py:56
  98.2 7.3 %copy.308 = bf16[1,3072,192]{1,2,0:T(8,128)(2,1)} copy(bf16[1,3072,192]{2,0,1:T(2,128)(2,1)} %get-tuple-element.10) | data formatting | bytes 2359296 | tf_op jit(solution)/shard_map/slice | solution.py:56
  105.5 4.0 %squeeze.11 = bf16[4,2,384,192]{2,1,0,3:T(2,128)(2,1)} reshape(bf16[1,3072,192]{1,2,0:T(8,128)(2,1)} %copy.308) | data formatting | bytes 2359296 | tf_op jit(solution)/shard_map/squeeze | solution.py:56
  109.5 2.0 convolution_bitcast_fusion.5
  111.4 1.8 copy.310
  113.2 3.3 %reshape.897 = f32[1,32,4,1152]{3,1,2,0:T(8,128)} reshape(f32[1,32,4,4,2,144]{5,4,3,1,2,0:T(2,128)} %copy.310) | data formatting | bytes 1179648 | tf_op jit(solution)/shard_map/jvp()/reshape | solution.py:26
  116.6 1.3 fusion.108
  117.8 1.3 fusion.109
  119.9 1.1 fusion.238
  122.2 1.3 fusion.9
  124.4 1.2 copy.313
  125.6 1.7 reshape.903
  127.3 0.7 copy.314
  128.0 13.7 %all-to-all-start.2 = ((bf16[32,1,4,384]{3,2,1,0:T(4,128)(2,1)}), bf16[32,1,4,384]{3,2,1,0:T(4,128)(2,1)S(1)}, u32[]{:S(2)}, u32[]{:S(2)}) async-start(bf16[32,1,4,384]{3,2,1,0:T(4,128)(2,1)} %copy.314), calls=%async_computation.2 | async-start | bytes 196608 | tf_op jit(solution)/shard_map/all_to_all | solution.py:73
  141.7 7.3 %copy.317 = bf16[1,3072,192]{1,2,0:T(8,128)(2,1)} copy(bf16[1,3072,192]{2,0,1:T(2,128)(2,1)} %get-tuple-element.11) | data formatting | bytes 2359296 | tf_op jit(solution)/shard_map/slice | solution.py:56
  149.0 4.0 %squeeze.12 = bf16[4,2,384,192]{2,1,0,3:T(2,128)(2,1)} reshape(bf16[1,3072,192]{1,2,0:T(8,128)(2,1)} %copy.317) | data formatting | bytes 2359296 | tf_op jit(solution)/shard_map/squeeze | solution.py:56
  152.9 6.1 %copy.302 = bf16[1,3072,192]{1,2,0:T(8,128)(2,1)} copy(bf16[1,3072,192]{2,0,1:T(2,128)(2,1)S(1)} %get-tuple-element.9) | data formatting | bytes 2359296 | tf_op jit(solution)/shard_map/slice | solution.py:56
  159.1 3.4 %squeeze.10 = bf16[4,2,384,192]{2,1,0,3:T(2,128)(2,1)S(1)} reshape(bf16[1,3072,192]{1,2,0:T(8,128)(2,1)} %copy.302) | data formatting | bytes 2359296 | tf_op jit(solution)/shard_map/squeeze | solution.py:56
  162.5 1.2 fusion.69
  165.3 1.8 copy.320
  167.1 2.5 reshape.904
  170.3 0.7 slice.177
  171.0 0.7 copy-done.7
  171.7 0.7 reshape.943
  172.5 1.8 reshape.941
  175.0 0.7 copy-done.12
  175.8 0.8 copy-done.24
  176.7 2.5 fusion.352
  179.2 0.7 multiply_divide_fusion
  180.0 0.8 fusion
  181.5 1.0 fusion.144
  184.3 1.8 copy.330
  186.1 2.5 reshape.910
  191.6 0.7 fusion.160
  192.4 1.0 fusion.81
  193.4 1.1 fusion.20
  194.5 0.9 fusion.92
  195.5 1.2 copy.335
  196.7 2.4 reshape.921
  199.1 1.4 fusion.102
  200.5 1.4 add_add_fusion.7
  202.6 0.8 pad_add_fusion.2
  203.4 1.7 reshape.919
  205.2 1.6 fusion.181
  208.1 2.4 fusion.1
  211.6 0.8 fusion.13
  214.7 0.7 reshape.927
  216.6 0.7 copy.349
  217.3 6.0 %all-to-all-start.3 = ((bf16[32,1,4,384]{3,2,1,0:T(4,128)(2,1)}), bf16[32,1,4,384]{3,2,1,0:T(4,128)(2,1)S(1)}, u32[]{:S(2)}, u32[]{:S(2)}) async-start(bf16[32,1,4,384]{3,2,1,0:T(4,128)(2,1)} %bitcast.144), calls=%async_computation.3 | async-start | bytes 196608 | tf_op jit(solution)/shard_map/all_to_all | solution.py:84
  223.3 7.5 %all-to-all-done.3 = bf16[32,1,4,384]{3,2,1,0:T(4,128)(2,1)S(1)} async-done(((bf16[32,1,4,384]{3,2,1,0:T(4,128)(2,1)}), bf16[32,1,4,384]{3,2,1,0:T(4,128)(2,1)S(1)}, u32[]{:S(2)}, u32[]{:S(2)}) %all-to-all-start.3) | async-done | bytes 98336 | tf_op jit(solution)/shard_map/all_to_all | solution.py:84
  232.4 0.7 fusion.156
  236.5 0.7 reshape.936
  238.3 6.7 %all_to_all.42 = bf16[32,1,4,384]{3,2,1,0:T(4,128)(2,1)S(1)} all-to-all(bf16[32,1,4,384]{3,2,1,0:T(4,128)(2,1)S(1)} %copy.359), channel_id=1, replica_groups=mesh['gz'=4,'gy'=4,'gx'=2] {'gz'}, dimensions={0} | all-to-all | bytes 196608 | tf_op jit(solution)/shard_map/all_to_all | solution.py:107
  245.0 0.7 all_to_all.36
  (226 shorter events, 25.0 us)
Async XLA Ops:
  6.5 2.9 %copy-start.48 = (bf16[8,1,16,384]{3,2,1,0:T(8,128)(2,1)S(1)}, bf16[8,1,16,384]{3,2,1,0:T(8,128)(2,1)}, u32[]{:S(2)}) copy-start(bf16[8,1,16,384]{3,2,1,0:T(8,128)(2,1)} %param.4) | copy-start | bytes 294916
  6.5 76.5 %all-gather.3.cloned.1.call-start = ((), (), s32[]{:S(2)}) async-start(), calls=%async_computation.5 | async-start | bytes 6488064 | tf_op jit(solution)/shard_map/all_gather | solution.py:54
  10.1 8.5 %all-to-all-start.1 = ((bf16[8,1,16,384]{3,0,1,2:T(8,128)(2,1)}), bf16[8,1,16,384]{3,0,1,2:T(8,128)(2,1)S(1)}, u32[]{:S(2)}, u32[]{:S(2)}) async-start(bf16[8,1,16,384]{3,0,1,2:T(8,128)(2,1)} %copy.304), calls=%async_computation.1 | async-start | bytes 196608 | tf_op jit(solution)/shard_map/all_to_all | solution.py:98
  14.3 106.7 %copy-start.58 = (bf16[6,384]{1,0:T(8,128)(2,1)}, bf16[6,384]{1,0:T(8,128)(2,1)S(1)}, u32[]{:S(2)}) copy-start(bf16[6,384]{1,0:T(8,128)(2,1)S(1)} %get-tuple-element.28) | copy-start | bytes 13828
  18.6 108.7 %copy-start.4 = (bf16[8,1,16,384]{3,0,1,2:T(8,128)(2,1)}, bf16[8,1,16,384]{3,0,1,2:T(8,128)(2,1)S(1)}, u32[]{:S(2)}) copy-start(bf16[8,1,16,384]{3,0,1,2:T(8,128)(2,1)S(1)} %all-to-all-done.1) | copy-start | bytes 294916
  18.6 14.1 %all-to-all-start = ((bf16[8,1,16,384]{3,2,1,0:T(8,128)(2,1)}), bf16[8,1,16,384]{3,2,1,0:T(8,128)(2,1)S(1)}, u32[]{:S(2)}, u32[]{:S(2)}) async-start(bf16[8,1,16,384]{3,2,1,0:T(8,128)(2,1)} %param.5), calls=%async_computation | async-start | bytes 196608 | tf_op jit(solution)/shard_map/all_to_all | solution.py:90
  32.7 1.0 copy-start.22
  117.8 3.5 %copy-start.42 = (f32[32,4,6]{0,2,1:T(8,128)}, f32[32,4,6]{0,2,1:T(8,128)S(1)}, u32[]{:S(2)}) copy-start(f32[32,4,6]{0,2,1:T(8,128)S(1)} %fusion.108) | copy-start | bytes 9220
  119.2 2.2 copy-start.34
  119.5 1.9 copy-start.10
  119.9 1.8 copy-start.8
  121.0 2.5 copy-start.53
  121.4 0.8 copy-start.26
  121.4 2.8 %copy-start.67 = (f32[4,6,32]{2,1,0:T(8,128)}, f32[4,6,32]{2,1,0:T(8,128)S(1)}, u32[]{:S(2)}) copy-start(f32[4,6,32]{2,1,0:T(8,128)S(1)} %get-tuple-element.29) | copy-start | bytes 9220
  121.4 2.1 copy-start
  128.0 35.7 %all-to-all-start.2 = ((bf16[32,1,4,384]{3,2,1,0:T(4,128)(2,1)}), bf16[32,1,4,384]{3,2,1,0:T(4,128)(2,1)S(1)}, u32[]{:S(2)}, u32[]{:S(2)}) async-start(bf16[32,1,4,384]{3,2,1,0:T(4,128)(2,1)} %copy.314), calls=%async_computation.2 | async-start | bytes 196608 | tf_op jit(solution)/shard_map/all_to_all | solution.py:73
  159.1 3.4 %copy-start.31 = (bf16[4,32,1,4,2,48]{5,1,4,0,3,2:T(8,128)(2,1)S(1)}, bf16[4,32,1,4,2,48]{5,1,4,0,3,2:T(8,128)(2,1)}, u32[]{:S(2)}) copy-start(bf16[4,32,1,4,2,48]{5,1,4,0,3,2:T(8,128)(2,1)} %copy.299) | copy-start | bytes 294916
  162.5 2.2 copy-start.2
  170.0 5.8 %copy-start.38 = (f32[4,32,6]{1,2,0:T(8,128)}, f32[4,32,6]{1,2,0:T(8,128)S(1)}, u32[]{:S(2)}) copy-start(f32[4,32,6]{1,2,0:T(8,128)S(1)} %fusion.106) | copy-start | bytes 9220
  170.3 5.4 %copy-start.36 = (f32[4,32,6]{1,2,0:T(8,128)}, f32[4,32,6]{1,2,0:T(8,128)S(1)}, u32[]{:S(2)}) copy-start(f32[4,32,6]{1,2,0:T(8,128)S(1)} %fusion.107) | copy-start | bytes 9220
  171.7 4.0 %copy-start.59 = (bf16[6,384]{1,0:T(8,128)(2,1)S(1)}, bf16[6,384]{1,0:T(8,128)(2,1)}, u32[]{:S(2)}) copy-start(bf16[6,384]{1,0:T(8,128)(2,1)} %copy-done.58) | copy-start | bytes 13828
  174.6 1.1 copy-start.14
  175.7 3.4 %copy-start.55 = (bf16[4,32,384,1]{2,1,0,3:T(8,128)(2,1)}, bf16[4,32,384,1]{2,1,0,3:T(8,128)(2,1)S(1)}, u32[]{:S(2)}) copy-start(bf16[4,32,384,1]{2,1,0,3:T(8,128)(2,1)S(1)} %get-tuple-element.15) | copy-start | bytes 294916
  175.8 0.8 copy-start.24
  176.7 3.3 %copy-start.49 = (bf16[1,4,32,384]{3,2,1,0:T(8,128)(2,1)S(1)}, bf16[1,4,32,384]{3,2,1,0:T(8,128)(2,1)}, u32[]{:S(2)}) copy-start(bf16[1,4,32,384]{3,2,1,0:T(8,128)(2,1)} %slice.177) | copy-start | bytes 294916
  179.1 0.8 copy-start.20
  179.1 2.3 copy-start.29
  180.0 0.8 copy-start.45
  182.5 0.7 copy-start.65
  188.6 2.7 %copy-start.60 = (bf16[6,384]{1,0:T(8,128)(2,1)S(1)}, bf16[6,384]{1,0:T(8,128)(2,1)}, u32[]{:S(2)}) copy-start(bf16[6,384]{1,0:T(8,128)(2,1)} %copy-done.58) | copy-start | bytes 13828
  190.2 1.4 copy-start.18
  190.2 1.4 copy-start.33
  194.5 1.0 copy-start.6
  199.1 2.7 %copy-start.28 = (bf16[4,32,384]{2,1,0:T(8,128)(2,1)S(1)}, bf16[4,32,384]{2,1,0:T(8,128)(2,1)}, u32[]{:S(2)}) copy-start(bf16[4,32,384]{2,1,0:T(8,128)(2,1)} %fusion.20) | copy-start | bytes 294916
  199.1 2.7 %copy-start.41 = (f32[4,32,6]{1,2,0:T(8,128)S(1)}, f32[4,32,6]{1,2,0:T(8,128)}, u32[]{:S(2)}) copy-start(f32[4,32,6]{1,2,0:T(8,128)} %copy-done.40) | copy-start | bytes 9220
  199.1 3.1 %copy-start.17 = (f32[4,32,384]{2,1,0:T(8,128)S(1)}, f32[4,32,384]{2,1,0:T(8,128)}, u32[]{:S(2)}) copy-start(f32[4,32,384]{2,1,0:T(8,128)} %copy-done.16) | copy-start | bytes 589828
  199.1 3.5 %copy-start.47 = (bf16[4,32,1,384]{3,1,0,2:T(8,128)(2,1)S(1)}, bf16[4,32,1,384]{3,1,0,2:T(8,128)(2,1)}, u32[]{:S(2)}) copy-start(bf16[4,32,1,384]{3,1,0,2:T(8,128)(2,1)} %fusion.92) | copy-start | bytes 294916
  205.1 1.6 copy-start.66
  205.2 1.6 copy-start.23
  205.2 1.6 copy-start.64
  207.2 0.9 copy-start.50
  207.7 2.8 %copy-start.21 = (f32[1,32,6,4,4]{2,3,4,1,0:T(4,128)S(1)}, f32[1,32,6,4,4]{2,3,4,1,0:T(4,128)}, u32[]{:S(2)}) copy-start(f32[1,32,6,4,4]{2,3,4,1,0:T(4,128)} %copy-done.20) | copy-start | bytes 36868
  207.7 2.8 %copy-start.32 = (f32[32,6,4]{1,2,0:T(4,128)S(1)}, f32[32,6,4]{1,2,0:T(4,128)}, u32[]{:S(2)}) copy-start(f32[32,6,4]{1,2,0:T(4,128)} %multiply_divide_fusion) | copy-start | bytes 9220
  207.7 2.9 %copy-start.25 = (bf16[4,32,6,384]{3,1,2,0:T(8,128)(2,1)S(1)}, bf16[4,32,6,384]{3,1,2,0:T(8,128)(2,1)}, u32[]{:S(2)}) copy-start(bf16[4,32,6,384]{3,1,2,0:T(8,128)(2,1)} %copy-done.24) | copy-start | bytes 1769476
  207.8 2.9 %copy-start.30 = (f32[32,6,4]{1,2,0:T(4,128)S(1)}, f32[32,6,4]{1,2,0:T(4,128)}, u32[]{:S(2)}) copy-start(f32[32,6,4]{1,2,0:T(4,128)} %copy-done.29) | copy-start | bytes 9220
  210.7 0.9 copy-start.56
  210.7 0.9 copy-start.61
  211.6 0.9 copy-start.46
  212.5 1.1 copy-start.15
  212.5 1.4 copy-start.37
  212.5 1.8 copy-start.13
  214.7 0.9 copy-start.19
  216.1 7.1 %copy-start.68 = (f32[4,6,32]{2,1,0:T(8,128)S(1)}, f32[4,6,32]{2,1,0:T(8,128)}, u32[]{:S(2)}) copy-start(f32[4,6,32]{2,1,0:T(8,128)} %copy-done.67) | copy-start | bytes 9220
  216.1 15.1 %copy-start.1 = (bf16[4,2,384,192]{2,1,0,3:T(2,128)(2,1)S(1)}, bf16[4,2,384,192]{2,1,0,3:T(2,128)(2,1)}, u32[]{:S(2)}) copy-start(bf16[4,2,384,192]{2,1,0,3:T(2,128)(2,1)} %squeeze.11) | copy-start | bytes 3538948
  217.3 13.5 %all-to-all-start.3 = ((bf16[32,1,4,384]{3,2,1,0:T(4,128)(2,1)}), bf16[32,1,4,384]{3,2,1,0:T(4,128)(2,1)S(1)}, u32[]{:S(2)}, u32[]{:S(2)}) async-start(bf16[32,1,4,384]{3,2,1,0:T(4,128)(2,1)} %bitcast.144), calls=%async_computation.3 | async-start | bytes 196608 | tf_op jit(solution)/shard_map/all_to_all | solution.py:84
  231.2 1.1 copy-start.3
  231.2 1.2 copy-start.27
  231.2 1.9 copy-start.54
  231.2 1.9 copy-start.62
  233.1 0.9 copy-start.52
  234.3 1.1 copy-start.11
  234.3 1.4 copy-start.35
  235.0 1.1 copy-start.9
  236.5 0.9 copy-start.5
  (11 other events, 7.3 us)
Sparse Core Ops, SparseCore 0:
  10.2 72.7 all-gather.2

commit v6 on v2

--- a/solution.py
+++ b/solution.py
@@ -42,15 +42,12 @@
 
 
 def full_weights(w_project, w_output, sizes):
-    nz, ny, nx = sizes
     subs, din, dproj = w_project.shape
     cat = jnp.concatenate([w_project, w_output], axis=2)
-    got = lax.all_gather(cat, ALL, axis=0, tiled=False)
-    got = got.reshape(nz, ny, nx, subs, din, cat.shape[2])
-    got = jnp.transpose(got, (3, 1, 4, 0, 2, 5)).reshape(subs, ny * din, nz * nx, cat.shape[2])
-    w_inner = got[:, :, :, :dproj].reshape(subs, ny * din, nz * nx * dproj)
-    w_outer = got[:, :, :, dproj:].reshape(subs, ny * din, -1)
-    return [(w_inner[i], w_outer[i]) for i in range(subs)]
+    rows = lax.all_gather(cat, "gy", axis=1, tiled=True)
+    proj = lax.all_gather(rows[:, :, :dproj], ("gz", "gx"), axis=2, tiled=True)
+    outp = lax.all_gather(rows[:, :, dproj:], ("gz", "gx"), axis=2, tiled=True)
+    return [(proj[i], outp[i]) for i in range(subs)]
 
 
 def depth_fn(member, w_inner, w_outer):

time: 165 us -> 142 us (0.86)
  waiting for transfers between devices: 67.5 us -> 16.6 us
  blocking collectives: 6.67 us -> 50.3 us
  local copies, waits for them, and re-layouts: 28 us -> 11.8 us
  matrix products: 25.8 us -> 29.9 us
  starting transfers between devices: 16.5 us -> 13.9 us
    all_gather x1, waiting for transfers between devices: 50.2 us -> 2.01 us  [full_weights(): proj = lax.all_gather(rows[:, :, :dproj], ('gz', 'gx'), axis=2, tiled=True)]
    all_gather x0 -> x2, blocking collectives: none -> 43.7 us  [the longest x1 22.4 us: full_weights(): outp = lax.all_gather(rows[:, :, dproj:], ('gz', 'gx'), axis=2, tiled=True)]
    reshape x2 -> x0, local copies, waits for them, and re-layouts: 16.5 us -> none  [the longest x1 9.65 us: full_weights(): got = got.reshape(nz, ny, nx, subs, din, cat.shape[2])]
    dot_general x6, matrix products: 2.49 us -> 7.26 us  [sublayer(): packed = jnp.dot(normed, w_inner, preferred_element_type=jnp.float32)]
    all_to_all x1, waiting for transfers between devices: 3.7 us -> 0.01 us  [local(): depth_act = lax.all_to_all(volume, 'gz', 2, 0, tiled=True)]
    all_to_all x1, starting transfers between devices: 6.35 us -> 3.37 us  [block_to_plane(): got = lax.all_to_all(block, ('gy', 'gx'), 0, 0, tiled=True)]
    unnamed x75 -> x47, local copies, waits for them, and re-layouts: 5.27 us -> 3.9 us
  transfers between devices with their start and end apart: 5 -> 5, of which waited for: 4 -> 3; matrix products, arithmetic and copies ran while one was open for 17% -> 5% of each run, Pallas kernels for 0% -> 0%
where the time goes in v6:
time: 142 us; the launch traced here: 141 us
  blocking collectives  50.3 us (35%)
  matrix products  29.9 us (21%)
  waiting for transfers between devices  16.6 us (12%)
  between operations  14.1 us (10%)
  starting transfers between devices  13.9 us (10%)
  local copies, waits for them, and re-layouts  11.8 us (8%)
  other arithmetic  4.15 us (3%)
    all_gather x1, blocking collectives, full_weights(): outp = lax.all_gather(rows[:, :, dproj:], ('gz', 'gx'), axis=2, tiled=True)  22.4 us
    all_gather x1, blocking collectives, full_weights(): rows = lax.all_gather(cat, 'gy', axis=1, tiled=True)  21.3 us
    all_to_all x1, waiting for transfers between devices, from_planes(): return lax.all_to_all(parts, ALL, 0, 0, tiled=True)  7.34 us
    dot_general x6, matrix products, sublayer(): packed = jnp.dot(normed, w_inner, preferred_element_type=jnp.float32)  7.26 us
    all_to_all x1, waiting for transfers between devices, to_planes(): got = lax.all_to_all(depth_lines, ALL, 0, 0, tiled=True)  7.18 us
    dot_general x9, matrix products, sublayer(): jnp.einsum('plqd,pkqhd->pqhlk', queries, key_heads, preferred_element_typ...  6.92 us
    all_to_all x1, blocking collectives, local(): return lax.all_to_all(grad_zero, 'gz', 0, 2, tiled=True)  6.67 us
    dot_general x8, matrix products, sublayer(): jnp.einsum('pqhlk,pkqd->plqhd', attn_weights, value_part, preferred_eleme...  5.96 us
  transfers between devices with their start and end apart: 5, of which 3 were waited for; matrix products, arithmetic and copies ran while one was open for 5% of the time, Pallas kernels for 0%

profile of v6, /device:TPU:0, one launch (start us, length us, event | category | flops | bytes accessed | tf_op | source)
XLA Modules:
  0.0 140.8 jit_solution(10131053995212700068)
XLA Ops:
  6.5 1.1 copy.124
  7.6 0.9 copy.125
  8.7 21.3 %all_gather.9 = bf16[3,384,192]{2,0,1:T(4,128)(2,1)S(1)} all-gather(bf16[3,96,192]{2,0,1:T(4,128)(2,1)S(1)} %pad_maximum_fusion), channel_id=1, replica_groups=mesh['gz'=4,'gy'=4,'gx'=2] {'gy'}, dimensions={1}, use_global_device_ids=true | all-gather | bytes 552960 | tf_op jit(solution)/shard_map/all_gather | solution.py:47
  30.0 1.3 copy.132
  31.4 0.7 copy.128
  32.1 3.3 %all-to-all-start.1 = ((bf16[8,1,16,384]{3,0,1,2:T(8,128)(2,1)}), bf16[8,1,16,384]{3,0,1,2:T(8,128)(2,1)S(1)}, u32[]{:S(2)}, u32[]{:S(2)}) async-start(bf16[8,1,16,384]{3,0,1,2:T(8,128)(2,1)} %copy.128), calls=%async_computation.1 | async-start | bytes 196608 | tf_op jit(solution)/shard_map/all_to_all | solution.py:92
  35.9 22.4 %all_gather.10 = bf16[3,384,384]{1,2,0:T(8,128)(2,1)S(1)} all-gather(bf16[3,384,48]{1,2,0:T(8,128)(2,1)S(1)} %copy.126), channel_id=1, replica_groups=mesh['gz'=4,'gy'=4,'gx'=2] {'gz','gx'}, dimensions={2}, use_global_device_ids=true | all-gather | bytes 995328 | tf_op jit(solution)/shard_map/all_gather | solution.py:49
  58.3 3.4 %all-to-all-start = ((bf16[8,1,16,384]{3,2,1,0:T(8,128)(2,1)}), bf16[8,1,16,384]{3,2,1,0:T(8,128)(2,1)S(1)}, u32[]{:S(2)}, u32[]{:S(2)}) async-start(bf16[8,1,16,384]{3,2,1,0:T(8,128)(2,1)} %param.5), calls=%async_computation | async-start | bytes 196608 | tf_op jit(solution)/shard_map/all_to_all | solution.py:84
  61.8 0.7 add.121
  62.5 2.0 %all-gather.2.cloned.1.call-done = bf16[3,384,1152]{1,2,0:T(8,128)(2,1)} async-done(((bf16[3,384,144]{1,2,0:T(8,128)(2,1)}), bf16[3,384,1152]{1,2,0:T(8,128)(2,1)}) %all-gather.2.cloned.1.call-update) | async-done | bytes 2654224 | tf_op jit(solution)/shard_map/all_gather | solution.py:48
  64.5 1.6 %convolution_bitcast_fusion.2 = f32[1,32,4,1152]{3,1,2,0:T(8,128)S(1)} fusion(bf16[3,384,1152]{1,2,0:T(8,128)(2,1)} %all-gather.2.cloned.1.call-done, bf16[8,1,4,4,384]{4,0,3,2,1:T(8,128)(2,1)S(1)} %bitcast.611, f32[4,8,4]{1,2,0:T(4,128)S(1)} %get-tuple-element.14), kind=kOutput, calls=%fused_computation.2 | convolution fusion | flops 113393664 | bytes 1573376 | tf_op jit(solution)/shard_map/jvp()/dot_general | solution.py:30
  66.1 0.4 fusion.102
  66.4 0.4 fusion.101
  67.1 0.3 fusion.261
  67.7 0.3 convolution_bitcast_fusion.14
  68.7 0.4 fusion.9
  69.3 0.7 copy.136
  70.0 4.4 %all-to-all-start.2 = ((bf16[32,1,4,384]{3,2,1,0:T(4,128)(2,1)}), bf16[32,1,4,384]{3,2,1,0:T(4,128)(2,1)S(1)}, u32[]{:S(2)}, u32[]{:S(2)}) async-start(bf16[32,1,4,384]{3,2,1,0:T(4,128)(2,1)} %copy.136), calls=%async_computation.2 | async-start | bytes 196608 | tf_op jit(solution)/shard_map/all_to_all | solution.py:67
  74.7 7.2 %all-to-all-done.2 = bf16[32,1,4,384]{3,2,1,0:T(4,128)(2,1)S(1)} async-done(((bf16[32,1,4,384]{3,2,1,0:T(4,128)(2,1)}), bf16[32,1,4,384]{3,2,1,0:T(4,128)(2,1)S(1)}, u32[]{:S(2)}, u32[]{:S(2)}) %all-to-all-start.2) | async-done | bytes 98336 | tf_op jit(solution)/shard_map/all_to_all | solution.py:67
  82.0 0.6 multiply_add_fusion
  82.8 1.6 %convolution_bitcast_fusion.1 = f32[1,4,32,1152]{3,2,1,0:T(8,128)S(1)} fusion(bf16[4,32,384]{2,1,0:T(8,128)(2,1)S(1)} %convert_element_type.493, bf16[3,384,1152]{1,2,0:T(8,128)(2,1)} %all-gather.2.cloned.1.call-done), kind=kOutput, calls=%fused_computation.1 | convolution fusion | flops 113246208 | bytes 1572864 | tf_op jit(solution)/shard_map/jvp()/dot_general | solution.py:30
  84.3 0.4 fusion.100
  84.7 0.4 fusion.99
  85.1 0.7 fusion.234
  85.8 0.7 copy_bitcast_fusion
  86.8 0.3 convolution_bitcast_fusion.13
  87.1 0.7 fusion.226
  87.8 0.9 broadcast_multiply_fusion
  88.7 1.0 reshape.809
  89.7 3.7 %fusion.340 = (f32[32,6,4]{1,2,0:T(4,128)S(1)}, f32[1,32,6,4,4]{2,3,4,1,0:T(4,128)S(1)}) fusion(bf16[4,32,384,1]{2,1,0,3:T(8,128)(2,1)} %get-tuple-element.7, bf16[4,32,6,384]{3,1,2,0:T(8,128)(2,1)} %broadcast_multiply_fusion), kind=kOutput, calls=%fused_computation.402 | convolution fusion | flops 2364672 | bytes 703488 | tf_op jit(solution)/shard_map/jvp(plqd,pkqhd->pqhlk)/dot_general | solution.py:35
  93.4 0.8 fusion
  94.6 0.4 convolution_bitcast_fusion
  95.0 0.4 fusion.98
  95.4 0.4 fusion.97
  95.8 0.3 fusion.255
  96.1 0.3 fusion.253
  97.1 0.7 fusion.146
  98.5 0.4 fusion.96
  98.9 0.4 add_add_fusion.8
  99.2 0.4 fusion.95
  99.6 0.3 add_add_fusion.7
  99.9 0.4 multiply_reduce_fusion.1
  100.9 0.4 fusion.53
  101.2 2.4 %fusion.1 = bf16[32,6,4,4]{1,3,2,0:T(4,128)(2,1)S(1)} fusion(f32[4,32,384]{2,0,1:T(4,128)S(1)} %copy.147, f32[6,384]{1,0:T(8,128)S(1)} %get-tuple-element.19, bf16[4,32,384,1]{2,1,0,3:T(8,128)(2,1)S(1)} %copy-done.11), kind=kOutput, calls=%fused_computation.5 | convolution fusion | flops 2654208 | bytes 310272 | tf_op jit(solution)/shard_map/transpose(jvp(pqhlk,pkqd->plqhd))/dot_general | solution.py:38
  103.9 0.8 fusion.13
  104.9 0.7 convolution_bitcast_fusion.8
  105.6 0.6 copy.259
  106.3 0.4 fusion.94
  106.7 0.3 add_add_fusion.5
  107.0 0.4 fusion.93
  107.4 0.3 add_add_fusion.4
  107.7 0.8 add.120
  108.6 1.7 %multiply_reduce_fusion = (f32[4,32]{1,0:T(4,128)S(1)}, f32[4,32,384]{2,1,0:T(8,128)S(1)}) fusion(f32[4,32,384]{2,1,0:T(8,128)S(1)} %reshape.809, bf16[3,384,1152]{1,2,0:T(8,128)(2,1)} %all-gather.2.cloned.1.call-done, f32[1,4,32,384]{3,2,1,0:T(8,128)S(1)} %add_add_fusion.4, f32[1,4,32,384]{3,2,1,0:T(8,128)S(1)} %add_add_fusion.5, ...), kind=kOutput, calls=%fused_computation.268 | convolution fusion | flops 113885056 | bytes 1769984 | tf_op jit(solution)/shard_map/transpose(jvp())/dot_general | solution.py:30
  110.4 0.7 copy.156
  111.1 2.8 %all-to-all-start.3 = ((bf16[32,1,4,384]{3,2,1,0:T(4,128)(2,1)}), bf16[32,1,4,384]{3,2,1,0:T(4,128)(2,1)S(1)}, u32[]{:S(2)}, u32[]{:S(2)}) async-start(bf16[32,1,4,384]{3,2,1,0:T(4,128)(2,1)} %bitcast.127), calls=%async_computation.3 | async-start | bytes 196608 | tf_op jit(solution)/shard_map/all_to_all | solution.py:78
  113.9 7.3 %all-to-all-done.3 = bf16[32,1,4,384]{3,2,1,0:T(4,128)(2,1)S(1)} async-done(((bf16[32,1,4,384]{3,2,1,0:T(4,128)(2,1)}), bf16[32,1,4,384]{3,2,1,0:T(4,128)(2,1)S(1)}, u32[]{:S(2)}, u32[]{:S(2)}) %all-to-all-start.3) | async-done | bytes 98336 | tf_op jit(solution)/shard_map/all_to_all | solution.py:78
  121.8 0.7 fusion.142
  123.3 0.4 fusion.92
  123.6 0.4 add_add_fusion.2
  124.0 0.4 fusion.91
  124.4 0.3 add_add_fusion.1
  124.7 1.6 %fusion.202 = (f32[32,4]{0,1:T(4,128)S(1)}, f32[32,4,384]{2,0,1:T(8,128)S(1)}) fusion(bf16[3,384,1152]{1,2,0:T(8,128)(2,1)} %all-gather.2.cloned.1.call-done, f32[1,32,4,384]{3,1,2,0:T(8,128)S(1)} %add_add_fusion.1, f32[1,32,4,384]{3,1,2,0:T(8,128)S(1)} %add_add_fusion.2, bf16[1,32,4,384]{3,1,2,0:T(8,128)(2,1)S(1)} %fusion.87, ...), kind=kOutput, calls=%fused_computation.263 | convolution fusion | flops 113934208 | bytes 1671680 | tf_op jit(solution)/shard_map/transpose(jvp())/dot_general | solution.py:30
  126.5 6.7 %all_to_all.42 = bf16[32,1,4,384]{3,2,1,0:T(4,128)(2,1)S(1)} all-to-all(bf16[32,1,4,384]{3,2,1,0:T(4,128)(2,1)S(1)} %copy.160), channel_id=1, replica_groups=mesh['gz'=4,'gy'=4,'gx'=2] {'gz'}, dimensions={0} | all-to-all | bytes 196608 | tf_op jit(solution)/shard_map/all_to_all | solution.py:101
  133.3 0.7 all_to_all.36
  (94 shorter events, 7.2 us)
Async XLA Ops:
  6.5 57.9 %all-gather.2.cloned.1.call-start = ((), (), s32[]{:S(2)}) async-start(), calls=%async_computation.5 | async-start | bytes 2985984 | tf_op jit(solution)/shard_map/all_gather | solution.py:48
  7.6 23.8 %copy-start.10 = (bf16[8,1,16,384]{3,2,1,0:T(8,128)(2,1)S(1)}, bf16[8,1,16,384]{3,2,1,0:T(8,128)(2,1)}, u32[]{:S(2)}) copy-start(bf16[8,1,16,384]{3,2,1,0:T(8,128)(2,1)} %param.4) | copy-start | bytes 294916
  32.1 26.2 %all-to-all-start.1 = ((bf16[8,1,16,384]{3,0,1,2:T(8,128)(2,1)}), bf16[8,1,16,384]{3,0,1,2:T(8,128)(2,1)S(1)}, u32[]{:S(2)}, u32[]{:S(2)}) async-start(bf16[8,1,16,384]{3,0,1,2:T(8,128)(2,1)} %copy.128), calls=%async_computation.1 | async-start | bytes 196608 | tf_op jit(solution)/shard_map/all_to_all | solution.py:92
  35.9 67.9 %copy-start.17 = (bf16[6,384]{1,0:T(8,128)(2,1)}, bf16[6,384]{1,0:T(8,128)(2,1)S(1)}, u32[]{:S(2)}) copy-start(bf16[6,384]{1,0:T(8,128)(2,1)S(1)} %get-tuple-element.20) | copy-start | bytes 13828
  58.3 11.7 %all-to-all-start = ((bf16[8,1,16,384]{3,2,1,0:T(8,128)(2,1)}), bf16[8,1,16,384]{3,2,1,0:T(8,128)(2,1)S(1)}, u32[]{:S(2)}, u32[]{:S(2)}) async-start(bf16[8,1,16,384]{3,2,1,0:T(8,128)(2,1)} %param.5), calls=%async_computation | async-start | bytes 196608 | tf_op jit(solution)/shard_map/all_to_all | solution.py:84
  66.4 0.6 copy-start.4
  67.1 0.6 copy-start.8
  68.0 0.6 copy-start.12
  68.1 1.0 copy-start.14
  68.4 0.9 copy-start.2
  68.4 6.3 %copy-start.19 = (f32[4,6,32]{2,1,0:T(8,128)}, f32[4,6,32]{2,1,0:T(8,128)S(1)}, u32[]{:S(2)}) copy-start(f32[4,6,32]{2,1,0:T(8,128)S(1)} %get-tuple-element.21) | copy-start | bytes 9220
  70.0 11.9 %all-to-all-start.2 = ((bf16[32,1,4,384]{3,2,1,0:T(4,128)(2,1)}), bf16[32,1,4,384]{3,2,1,0:T(4,128)(2,1)S(1)}, u32[]{:S(2)}, u32[]{:S(2)}) async-start(bf16[32,1,4,384]{3,2,1,0:T(4,128)(2,1)} %copy.136), calls=%async_computation.2 | async-start | bytes 196608 | tf_op jit(solution)/shard_map/all_to_all | solution.py:67
  85.1 2.7 %copy-start.6 = (f32[4,32,6]{1,2,0:T(8,128)}, f32[4,32,6]{1,2,0:T(8,128)S(1)}, u32[]{:S(2)}) copy-start(f32[4,32,6]{1,2,0:T(8,128)S(1)} %fusion.99) | copy-start | bytes 9220
  89.7 3.8 %copy-start.11 = (bf16[4,32,384,1]{2,1,0,3:T(8,128)(2,1)S(1)}, bf16[4,32,384,1]{2,1,0,3:T(8,128)(2,1)}, u32[]{:S(2)}) copy-start(bf16[4,32,384,1]{2,1,0,3:T(8,128)(2,1)} %fusion.234) | copy-start | bytes 294916
  89.7 4.9 %copy-start = (bf16[3,384,1152]{1,2,0:T(8,128)(2,1)S(1)}, bf16[3,384,1152]{1,2,0:T(8,128)(2,1)}, u32[]{:S(2)}) copy-start(bf16[3,384,1152]{1,2,0:T(8,128)(2,1)} %all-gather.2.cloned.1.call-done) | copy-start | bytes 7962628
  100.8 3.0 %copy-start.16 = (bf16[4,32,384,1]{2,1,0,3:T(8,128)(2,1)S(1)}, bf16[4,32,384,1]{2,1,0,3:T(8,128)(2,1)}, u32[]{:S(2)}) copy-start(bf16[4,32,384,1]{2,1,0,3:T(8,128)(2,1)} %get-tuple-element.7) | copy-start | bytes 294916
  103.9 1.1 copy-start.1
  104.9 2.1 %copy-start.7 = (f32[4,32,6]{1,2,0:T(8,128)S(1)}, f32[4,32,6]{1,2,0:T(8,128)}, u32[]{:S(2)}) copy-start(f32[4,32,6]{1,2,0:T(8,128)} %copy-done.6) | copy-start | bytes 9220
  108.5 5.3 %copy-start.20 = (f32[4,6,32]{2,1,0:T(8,128)S(1)}, f32[4,6,32]{2,1,0:T(8,128)}, u32[]{:S(2)}) copy-start(f32[4,6,32]{2,1,0:T(8,128)} %copy-done.19) | copy-start | bytes 9220
  108.5 12.9 %copy-start.3 = (f32[1,4,6,32,32]{3,4,2,1,0:T(8,128)S(1)}, f32[1,4,6,32,32]{3,4,2,1,0:T(8,128)}, u32[]{:S(2)}) copy-start(f32[1,4,6,32,32]{3,4,2,1,0:T(8,128)} %copy-done.2) | copy-start | bytes 294916
  111.1 10.2 %all-to-all-start.3 = ((bf16[32,1,4,384]{3,2,1,0:T(4,128)(2,1)}), bf16[32,1,4,384]{3,2,1,0:T(4,128)(2,1)S(1)}, u32[]{:S(2)}, u32[]{:S(2)}) async-start(bf16[32,1,4,384]{3,2,1,0:T(4,128)(2,1)} %bitcast.127), calls=%async_computation.3 | async-start | bytes 196608 | tf_op jit(solution)/shard_map/all_to_all | solution.py:78
  121.5 1.1 copy-start.15
  121.5 1.1 copy-start.18
  121.8 1.1 copy-start.13
  122.5 0.7 copy-start.5
  122.9 1.1 copy-start.9
  124.0 2.3 %copy-start.21 = (f32[32,4]{0,1:T(4,128)S(1)}, f32[32,4]{0,1:T(4,128)}, u32[]{:S(2)}) copy-start(f32[32,4]{0,1:T(4,128)} %add.121) | copy-start | bytes 1540
Sparse Core Ops, SparseCore 0:
  31.5 32.9 all-gather.1

commit v7 on v6

--- a/solution.py
+++ b/solution.py
@@ -44,7 +44,9 @@
 def full_weights(w_project, w_output, sizes):
     subs, din, dproj = w_project.shape
     cat = jnp.concatenate([w_project, w_output], axis=2)
-    rows = lax.all_gather(cat, "gy", axis=1, tiled=True)
+    ny = sizes[1]
+    rows = lax.all_to_all(jnp.broadcast_to(cat[None], (ny,) + cat.shape), "gy", 0, 0, tiled=True)
+    rows = jnp.swapaxes(rows, 0, 1).reshape(subs, ny * din, cat.shape[2])
     proj = lax.all_gather(rows[:, :, :dproj], ("gz", "gx"), axis=2, tiled=True)
     outp = lax.all_gather(rows[:, :, dproj:], ("gz", "gx"), axis=2, tiled=True)
     return [(proj[i], outp[i]) for i in range(subs)]

time: 142 us -> 143 us (level)
  waiting for transfers between devices: 16.6 us -> 18.8 us
  local copies, waits for them, and re-layouts: 11.8 us -> 9.7 us
    all_to_all x0 -> x1, blocking collectives: none -> 22 us  [full_weights(): lax.all_to_all(jnp.broadcast_to(cat[None], (ny,) + cat.shape), 'gy', 0, 0...]
    all_gather x1 -> x0, blocking collectives: 21.3 us -> none  [full_weights(): rows = lax.all_gather(cat, 'gy', axis=1, tiled=True)]
    all_to_all x1, waiting for transfers between devices: 0.01 us -> 4.23 us  [local(): depth_act = lax.all_to_all(volume, 'gz', 2, 0, tiled=True)]
    all_gather x1, waiting for transfers between devices: 2.01 us -> 0.01 us  [full_weights(): proj = lax.all_gather(rows[:, :, :dproj], ('gz', 'gx'), axis=2, tiled=True)]
    unnamed x47 -> x45, local copies, waits for them, and re-layouts: 3.9 us -> 1.92 us
  transfers between devices with their start and end apart: 5 -> 5, of which waited for: 3 -> 3; matrix products, arithmetic and copies ran while one was open for 5% -> 4% of each run, Pallas kernels for 0% -> 0%
where the time goes in v7:
time: 143 us; the launch traced here: 142 us
  blocking collectives  50.5 us (35%)
  matrix products  29.8 us (21%)
  waiting for transfers between devices  18.8 us (13%)
  between operations  14.1 us (10%)
  starting transfers between devices  13.9 us (10%)
  local copies, waits for them, and re-layouts  9.7 us (7%)
  other arithmetic  4.92 us (3%)
    all_to_all x1, blocking collectives, full_weights(): lax.all_to_all(jnp.broadcast_to(cat[None], (ny,) + cat.shape), 'gy', 0, 0...  22 us
    all_gather x1, blocking collectives, full_weights(): outp = lax.all_gather(rows[:, :, dproj:], ('gz', 'gx'), axis=2, tiled=True)  21.7 us
    all_to_all x1, waiting for transfers between devices, from_planes(): return lax.all_to_all(parts, ALL, 0, 0, tiled=True)  7.34 us
    dot_general x6, matrix products, sublayer(): packed = jnp.dot(normed, w_inner, preferred_element_type=jnp.float32)  7.22 us
    all_to_all x1, waiting for transfers between devices, to_planes(): got = lax.all_to_all(depth_lines, ALL, 0, 0, tiled=True)  7.18 us
    dot_general x9, matrix products, sublayer(): jnp.einsum('plqd,pkqhd->pqhlk', queries, key_heads, preferred_element_typ...  6.93 us
    all_to_all x1, blocking collectives, local(): return lax.all_to_all(grad_zero, 'gz', 0, 2, tiled=True)  6.67 us
    dot_general x8, matrix products, sublayer(): jnp.einsum('pqhlk,pkqd->plqhd', attn_weights, value_part, preferred_eleme...  5.95 us
  transfers between devices with their start and end apart: 5, of which 3 were waited for; matrix products, arithmetic and copies ran while one was open for 4% of the time, Pallas kernels for 0%

profile of v7, /device:TPU:0, one launch (start us, length us, event | category | flops | bytes accessed | tf_op | source)
XLA Modules:
  0.0 141.7 jit_solution(1157745169390944367)
XLA Ops:
  6.5 0.9 pad_maximum_fusion
  7.7 22.0 %all_to_all.47 = bf16[4,3,96,192]{3,2,1,0:T(8,128)(2,1)S(1)} all-to-all(bf16[4,3,96,192]{3,2,1,0:T(8,128)(2,1)S(1)} %broadcast_in_dim.24), channel_id=1, replica_groups=mesh['gz'=4,'gy'=4,'gx'=2] {'gy'}, dimensions={0} | all-to-all | bytes 884736 | tf_op jit(solution)/shard_map/all_to_all | solution.py:48
  29.7 1.0 copy.129
  30.7 0.4 reshape.777
  31.1 0.8 slice.73
  31.9 0.7 copy.131
  32.6 3.3 %all-to-all-start.2 = ((bf16[8,1,16,384]{3,0,1,2:T(8,128)(2,1)}), bf16[8,1,16,384]{3,0,1,2:T(8,128)(2,1)S(1)}, u32[]{:S(2)}, u32[]{:S(2)}) async-start(bf16[8,1,16,384]{3,0,1,2:T(8,128)(2,1)} %copy.131), calls=%async_computation.2 | async-start | bytes 196608 | tf_op jit(solution)/shard_map/all_to_all | solution.py:94
  35.9 4.2 %all-to-all-done.2 = bf16[8,1,16,384]{3,0,1,2:T(8,128)(2,1)S(1)} async-done(((bf16[8,1,16,384]{3,0,1,2:T(8,128)(2,1)}), bf16[8,1,16,384]{3,0,1,2:T(8,128)(2,1)S(1)}, u32[]{:S(2)}, u32[]{:S(2)}) %all-to-all-start.2) | async-done | bytes 98336 | tf_op jit(solution)/shard_map/all_to_all | solution.py:94
  40.2 3.7 %all-to-all-start = ((bf16[8,1,16,384]{3,2,1,0:T(8,128)(2,1)}), bf16[8,1,16,384]{3,2,1,0:T(8,128)(2,1)S(1)}, u32[]{:S(2)}, u32[]{:S(2)}) async-start(bf16[8,1,16,384]{3,2,1,0:T(8,128)(2,1)} %param.5), calls=%async_computation | async-start | bytes 196608 | tf_op jit(solution)/shard_map/all_to_all | solution.py:86
  44.0 0.7 add.121
  44.7 21.7 %all_gather.6 = bf16[3,384,384]{1,2,0:T(8,128)(2,1)S(1)} all-gather(bf16[3,384,48]{1,2,0:T(8,128)(2,1)S(1)} %slice.71), channel_id=1, replica_groups=mesh['gz'=4,'gy'=4,'gx'=2] {'gz','gx'}, dimensions={2}, use_global_device_ids=true | all-gather | bytes 995328 | tf_op jit(solution)/shard_map/all_gather | solution.py:51
  66.4 1.6 %convolution_bitcast_fusion.2 = f32[1,32,4,1152]{3,1,2,0:T(8,128)S(1)} fusion(bf16[3,384,1152]{1,2,0:T(8,128)(2,1)} %all-gather.2.cloned.1.call-done, bf16[8,1,4,4,384]{4,0,3,2,1:T(8,128)(2,1)S(1)} %bitcast.612, f32[4,8,4]{1,2,0:T(4,128)S(1)} %get-tuple-element.14), kind=kOutput, calls=%fused_computation.2 | convolution fusion | flops 113393664 | bytes 1573376 | tf_op jit(solution)/shard_map/jvp()/dot_general | solution.py:30
  68.0 0.4 fusion.102
  68.4 0.4 fusion.101
  69.0 0.3 fusion.261
  69.6 0.3 convolution_bitcast_fusion.14
  70.6 0.4 fusion.9
  71.3 0.7 copy.138
  72.0 4.1 %all-to-all-start.3 = ((bf16[32,1,4,384]{3,2,1,0:T(4,128)(2,1)}), bf16[32,1,4,384]{3,2,1,0:T(4,128)(2,1)S(1)}, u32[]{:S(2)}, u32[]{:S(2)}) async-start(bf16[32,1,4,384]{3,2,1,0:T(4,128)(2,1)} %copy.138), calls=%async_computation.3 | async-start | bytes 196608 | tf_op jit(solution)/shard_map/all_to_all | solution.py:69
  76.3 7.2 %all-to-all-done.3 = bf16[32,1,4,384]{3,2,1,0:T(4,128)(2,1)S(1)} async-done(((bf16[32,1,4,384]{3,2,1,0:T(4,128)(2,1)}), bf16[32,1,4,384]{3,2,1,0:T(4,128)(2,1)S(1)}, u32[]{:S(2)}, u32[]{:S(2)}) %all-to-all-start.3) | async-done | bytes 98336 | tf_op jit(solution)/shard_map/all_to_all | solution.py:69
  83.6 0.6 multiply_add_fusion
  84.4 1.6 %convolution_bitcast_fusion.1 = f32[1,4,32,1152]{3,2,1,0:T(8,128)S(1)} fusion(bf16[4,32,384]{2,1,0:T(8,128)(2,1)S(1)} %convert_element_type.493, bf16[3,384,1152]{1,2,0:T(8,128)(2,1)} %all-gather.2.cloned.1.call-done), kind=kOutput, calls=%fused_computation.1 | convolution fusion | flops 113246208 | bytes 1572864 | tf_op jit(solution)/shard_map/jvp()/dot_general | solution.py:30
  85.9 0.4 fusion.100
  86.3 0.4 fusion.99
  86.7 0.7 fusion.234
  87.3 0.7 copy_bitcast_fusion
  88.4 0.3 convolution_bitcast_fusion.13
  88.7 0.7 fusion.226
  89.4 0.9 broadcast_multiply_fusion
  90.3 1.0 reshape.814
  91.3 3.7 %fusion.340 = (f32[32,6,4]{1,2,0:T(4,128)S(1)}, f32[1,32,6,4,4]{2,3,4,1,0:T(4,128)S(1)}) fusion(bf16[4,32,384,1]{2,1,0,3:T(8,128)(2,1)} %get-tuple-element.7, bf16[4,32,6,384]{3,1,2,0:T(8,128)(2,1)} %broadcast_multiply_fusion), kind=kOutput, calls=%fused_computation.402 | convolution fusion | flops 2364672 | bytes 703488 | tf_op jit(solution)/shard_map/jvp(plqd,pkqhd->pqhlk)/dot_general | solution.py:35
  95.0 0.8 fusion
  96.2 0.4 convolution_bitcast_fusion
  96.6 0.4 fusion.98
  97.0 0.4 fusion.97
  97.4 0.3 fusion.255
  97.7 0.3 fusion.253
  98.7 0.7 fusion.146
  100.1 0.4 fusion.96
  100.5 0.4 add_add_fusion.8
  100.8 0.4 fusion.95
  101.2 0.3 add_add_fusion.7
  101.5 0.4 multiply_reduce_fusion.1
  102.5 0.4 fusion.53
  102.8 2.4 %fusion.1 = bf16[32,6,4,4]{1,3,2,0:T(4,128)(2,1)S(1)} fusion(f32[4,32,384]{2,0,1:T(4,128)S(1)} %copy.149, f32[6,384]{1,0:T(8,128)S(1)} %get-tuple-element.19, bf16[4,32,384,1]{2,1,0,3:T(8,128)(2,1)S(1)} %copy-done.11), kind=kOutput, calls=%fused_computation.5 | convolution fusion | flops 2654208 | bytes 310272 | tf_op jit(solution)/shard_map/transpose(jvp(pqhlk,pkqd->plqhd))/dot_general | solution.py:38
  105.5 0.8 fusion.13
  106.5 0.7 convolution_bitcast_fusion.8
  107.3 0.4 fusion.94
  107.6 0.3 add_add_fusion.5
  108.0 0.4 fusion.93
  108.4 0.3 add_add_fusion.4
  108.7 0.8 add.120
  109.5 1.6 %multiply_reduce_fusion = (f32[4,32]{1,0:T(4,128)S(1)}, f32[4,32,384]{2,1,0:T(8,128)S(1)}) fusion(f32[4,32,384]{2,1,0:T(8,128)S(1)} %reshape.814, bf16[3,384,1152]{1,2,0:T(8,128)(2,1)} %all-gather.2.cloned.1.call-done, f32[1,4,32,384]{3,2,1,0:T(8,128)S(1)} %add_add_fusion.4, f32[1,4,32,384]{3,2,1,0:T(8,128)S(1)} %add_add_fusion.5, ...), kind=kOutput, calls=%fused_computation.267 | convolution fusion | flops 113885056 | bytes 1769984 | tf_op jit(solution)/shard_map/transpose(jvp())/dot_general | solution.py:30
  111.3 0.7 copy.158
  112.0 2.8 %all-to-all-start.4 = ((bf16[32,1,4,384]{3,2,1,0:T(4,128)(2,1)}), bf16[32,1,4,384]{3,2,1,0:T(4,128)(2,1)S(1)}, u32[]{:S(2)}, u32[]{:S(2)}) async-start(bf16[32,1,4,384]{3,2,1,0:T(4,128)(2,1)} %bitcast.128), calls=%async_computation.4 | async-start | bytes 196608 | tf_op jit(solution)/shard_map/all_to_all | solution.py:80
  114.8 7.3 %all-to-all-done.4 = bf16[32,1,4,384]{3,2,1,0:T(4,128)(2,1)S(1)} async-done(((bf16[32,1,4,384]{3,2,1,0:T(4,128)(2,1)}), bf16[32,1,4,384]{3,2,1,0:T(4,128)(2,1)S(1)}, u32[]{:S(2)}, u32[]{:S(2)}) %all-to-all-start.4) | async-done | bytes 98336 | tf_op jit(solution)/shard_map/all_to_all | solution.py:80
  122.7 0.7 fusion.142
  124.2 0.4 fusion.92
  124.6 0.4 add_add_fusion.2
  124.9 0.4 fusion.91
  125.3 0.3 add_add_fusion.1
  125.7 1.6 %fusion.202 = (f32[32,4]{0,1:T(4,128)S(1)}, f32[32,4,384]{2,0,1:T(8,128)S(1)}) fusion(bf16[3,384,1152]{1,2,0:T(8,128)(2,1)} %all-gather.2.cloned.1.call-done, f32[1,32,4,384]{3,1,2,0:T(8,128)S(1)} %add_add_fusion.1, f32[1,32,4,384]{3,1,2,0:T(8,128)S(1)} %add_add_fusion.2, bf16[1,32,4,384]{3,1,2,0:T(8,128)(2,1)S(1)} %fusion.87, ...), kind=kOutput, calls=%fused_computation.262 | convolution fusion | flops 113934208 | bytes 1671680 | tf_op jit(solution)/shard_map/transpose(jvp())/dot_general | solution.py:30
  127.5 6.7 %all_to_all.48 = bf16[32,1,4,384]{3,2,1,0:T(4,128)(2,1)S(1)} all-to-all(bf16[32,1,4,384]{3,2,1,0:T(4,128)(2,1)S(1)} %copy.162), channel_id=1, replica_groups=mesh['gz'=4,'gy'=4,'gx'=2] {'gz'}, dimensions={0} | all-to-all | bytes 196608 | tf_op jit(solution)/shard_map/all_to_all | solution.py:103
  134.2 0.7 all_to_all.40
  (95 shorter events, 6.8 us)
Async XLA Ops:
  6.5 59.9 %all-gather.2.cloned.1.call-start = ((), (), s32[]{:S(2)}) async-start(), calls=%async_computation.6 | async-start | bytes 2985984 | tf_op jit(solution)/shard_map/all_gather | solution.py:50
  29.7 2.2 %copy-start.10 = (bf16[8,1,16,384]{3,2,1,0:T(8,128)(2,1)S(1)}, bf16[8,1,16,384]{3,2,1,0:T(8,128)(2,1)}, u32[]{:S(2)}) copy-start(bf16[8,1,16,384]{3,2,1,0:T(8,128)(2,1)} %param.4) | copy-start | bytes 294916
  32.6 7.6 %all-to-all-start.2 = ((bf16[8,1,16,384]{3,0,1,2:T(8,128)(2,1)}), bf16[8,1,16,384]{3,0,1,2:T(8,128)(2,1)S(1)}, u32[]{:S(2)}, u32[]{:S(2)}) async-start(bf16[8,1,16,384]{3,0,1,2:T(8,128)(2,1)} %copy.131), calls=%async_computation.2 | async-start | bytes 196608 | tf_op jit(solution)/shard_map/all_to_all | solution.py:94
  35.9 69.5 %copy-start.17 = (bf16[6,384]{1,0:T(8,128)(2,1)}, bf16[6,384]{1,0:T(8,128)(2,1)S(1)}, u32[]{:S(2)}) copy-start(bf16[6,384]{1,0:T(8,128)(2,1)S(1)} %get-tuple-element.20) | copy-start | bytes 13828
  40.2 31.8 %all-to-all-start = ((bf16[8,1,16,384]{3,2,1,0:T(8,128)(2,1)}), bf16[8,1,16,384]{3,2,1,0:T(8,128)(2,1)S(1)}, u32[]{:S(2)}, u32[]{:S(2)}) async-start(bf16[8,1,16,384]{3,2,1,0:T(8,128)(2,1)} %param.5), calls=%async_computation | async-start | bytes 196608 | tf_op jit(solution)/shard_map/all_to_all | solution.py:86
  68.4 0.6 copy-start.4
  69.0 0.6 copy-start.8
  70.0 0.6 copy-start.12
  70.0 1.0 copy-start.14
  70.3 0.9 copy-start.2
  70.3 5.9 %copy-start.19 = (f32[4,6,32]{2,1,0:T(8,128)}, f32[4,6,32]{2,1,0:T(8,128)S(1)}, u32[]{:S(2)}) copy-start(f32[4,6,32]{2,1,0:T(8,128)S(1)} %get-tuple-element.21) | copy-start | bytes 9220
  72.0 11.5 %all-to-all-start.3 = ((bf16[32,1,4,384]{3,2,1,0:T(4,128)(2,1)}), bf16[32,1,4,384]{3,2,1,0:T(4,128)(2,1)S(1)}, u32[]{:S(2)}, u32[]{:S(2)}) async-start(bf16[32,1,4,384]{3,2,1,0:T(4,128)(2,1)} %copy.138), calls=%async_computation.3 | async-start | bytes 196608 | tf_op jit(solution)/shard_map/all_to_all | solution.py:69
  86.7 2.7 %copy-start.6 = (f32[4,32,6]{1,2,0:T(8,128)}, f32[4,32,6]{1,2,0:T(8,128)S(1)}, u32[]{:S(2)}) copy-start(f32[4,32,6]{1,2,0:T(8,128)S(1)} %fusion.99) | copy-start | bytes 9220
  91.3 3.8 %copy-start.11 = (bf16[4,32,384,1]{2,1,0,3:T(8,128)(2,1)S(1)}, bf16[4,32,384,1]{2,1,0,3:T(8,128)(2,1)}, u32[]{:S(2)}) copy-start(bf16[4,32,384,1]{2,1,0,3:T(8,128)(2,1)} %fusion.234) | copy-start | bytes 294916
  91.3 4.9 %copy-start = (bf16[3,384,1152]{1,2,0:T(8,128)(2,1)S(1)}, bf16[3,384,1152]{1,2,0:T(8,128)(2,1)}, u32[]{:S(2)}) copy-start(bf16[3,384,1152]{1,2,0:T(8,128)(2,1)} %all-gather.2.cloned.1.call-done) | copy-start | bytes 7962628
  102.4 3.0 %copy-start.16 = (bf16[4,32,384,1]{2,1,0,3:T(8,128)(2,1)S(1)}, bf16[4,32,384,1]{2,1,0,3:T(8,128)(2,1)}, u32[]{:S(2)}) copy-start(bf16[4,32,384,1]{2,1,0,3:T(8,128)(2,1)} %get-tuple-element.7) | copy-start | bytes 294916
  105.5 1.1 copy-start.1
  106.5 1.4 %copy-start.7 = (f32[4,32,6]{1,2,0:T(8,128)S(1)}, f32[4,32,6]{1,2,0:T(8,128)}, u32[]{:S(2)}) copy-start(f32[4,32,6]{1,2,0:T(8,128)} %copy-done.6) | copy-start | bytes 9220
  109.5 5.3 %copy-start.20 = (f32[4,6,32]{2,1,0:T(8,128)S(1)}, f32[4,6,32]{2,1,0:T(8,128)}, u32[]{:S(2)}) copy-start(f32[4,6,32]{2,1,0:T(8,128)} %copy-done.19) | copy-start | bytes 9220
  109.5 12.9 %copy-start.3 = (f32[1,4,6,32,32]{3,4,2,1,0:T(8,128)S(1)}, f32[1,4,6,32,32]{3,4,2,1,0:T(8,128)}, u32[]{:S(2)}) copy-start(f32[1,4,6,32,32]{3,4,2,1,0:T(8,128)} %copy-done.2) | copy-start | bytes 294916
  112.0 10.2 %all-to-all-start.4 = ((bf16[32,1,4,384]{3,2,1,0:T(4,128)(2,1)}), bf16[32,1,4,384]{3,2,1,0:T(4,128)(2,1)S(1)}, u32[]{:S(2)}, u32[]{:S(2)}) async-start(bf16[32,1,4,384]{3,2,1,0:T(4,128)(2,1)} %bitcast.128), calls=%async_computation.4 | async-start | bytes 196608 | tf_op jit(solution)/shard_map/all_to_all | solution.py:80
  122.4 1.1 copy-start.15
  122.4 1.1 copy-start.18
  122.7 1.1 copy-start.13
  123.5 0.7 copy-start.5
  123.8 1.1 copy-start.9
  124.9 2.3 %copy-start.21 = (f32[32,4]{0,1:T(4,128)S(1)}, f32[32,4]{0,1:T(4,128)}, u32[]{:S(2)}) copy-start(f32[32,4]{0,1:T(4,128)} %add.121) | copy-start | bytes 1540
Sparse Core Ops, SparseCore 0:
  32.0 32.1 all-gather.1

commit v8 on v6

--- a/solution.py
+++ b/solution.py
@@ -43,11 +43,20 @@
 
 def full_weights(w_project, w_output, sizes):
     subs, din, dproj = w_project.shape
+    dout = w_output.shape[2]
+    blocks = sizes[0] * sizes[2]
     cat = jnp.concatenate([w_project, w_output], axis=2)
     rows = lax.all_gather(cat, "gy", axis=1, tiled=True)
-    proj = lax.all_gather(rows[:, :, :dproj], ("gz", "gx"), axis=2, tiled=True)
-    outp = lax.all_gather(rows[:, :, dproj:], ("gz", "gx"), axis=2, tiled=True)
-    return [(proj[i], outp[i]) for i in range(subs)]
+    feat = rows.shape[1]
+    weights = []
+    for index in range(subs):
+        proj, outp = rows[index, :, :dproj], rows[index, :, dproj:]
+        stacked = jnp.concatenate([proj, outp.reshape(-1, dproj)], axis=0)
+        got = lax.all_gather(stacked, ("gz", "gx"), axis=1, tiled=True)
+        w_inner = got[:feat]
+        w_outer = got[feat:].reshape(-1, blocks, dproj).swapaxes(0, 1).reshape(blocks, feat, dout)
+        weights.append((w_inner, w_outer.swapaxes(0, 1).reshape(feat, blocks * dout)))
+    return weights
 
 
 def depth_fn(member, w_inner, w_outer):

time: 142 us -> 175 us (1.23)
  waiting for transfers between devices: 16.6 us -> 70.5 us
  blocking collectives: 50.3 us -> 28 us
  local copies, waits for them, and re-layouts: 11.8 us -> 17.5 us
  matrix products: 29.9 us -> 26.9 us
    all_gather x1 -> x3, waiting for transfers between devices: 2.01 us -> 52.7 us  [full_weights(): got = lax.all_gather(stacked, ('gz', 'gx'), axis=1, tiled=True)]
    all_gather x1 -> x0, blocking collectives: 22.4 us -> none  [full_weights(): outp = lax.all_gather(rows[:, :, dproj:], ('gz', 'gx'), axis=2, tiled=True)]
    all_to_all x1, waiting for transfers between devices: 0.01 us -> 3.21 us  [local(): depth_act = lax.all_to_all(volume, 'gz', 2, 0, tiled=True)]
    slice x3 -> x6, local copies, waits for them, and re-layouts: 1.84 us -> 4.84 us  [the longest x2 2.88 us: full_weights(): proj, outp = (rows[index, :, :dproj], rows[index, :, dproj:])]
    reshape x0 -> x3, local copies, waits for them, and re-layouts: none -> 2.64 us  [full_weights(): got[feat:].reshape(-1, blocks, dproj).swapaxes(0, 1)]
    dot_general x6, matrix products: 7.26 us -> 4.82 us  [sublayer(): packed = jnp.dot(normed, w_inner, preferred_element_type=jnp.float32)]
    concatenate x0 -> x3, other arithmetic: none -> 2 us  [full_weights(): stacked = jnp.concatenate([proj, outp.reshape(-1, dproj)], axis=0)]
    unnamed x47 -> x33, local copies, waits for them, and re-layouts: 3.9 us -> 5.2 us
  transfers between devices with their start and end apart: 5 -> 7, of which waited for: 3 -> 6; matrix products, arithmetic and copies ran while one was open for 5% -> 9% of each run, Pallas kernels for 0% -> 0%
where the time goes in v8:
time: 175 us; the launch traced here: 174 us
  waiting for transfers between devices  70.5 us (40%)
  blocking collectives  28 us (16%)
  matrix products  26.9 us (15%)
  local copies, waits for them, and re-layouts  17.5 us (10%)
  starting transfers between devices  14.3 us (8%)
  between operations  13.9 us (8%)
  other arithmetic  3.31 us (2%)
    all_gather x3, waiting for transfers between devices, full_weights(): got = lax.all_gather(stacked, ('gz', 'gx'), axis=1, tiled=True)  52.7 us
    all_gather x1, blocking collectives, full_weights(): rows = lax.all_gather(cat, 'gy', axis=1, tiled=True)  21.3 us
    all_to_all x1, waiting for transfers between devices, from_planes(): return lax.all_to_all(parts, ALL, 0, 0, tiled=True)  7.34 us
    all_to_all x1, waiting for transfers between devices, to_planes(): got = lax.all_to_all(depth_lines, ALL, 0, 0, tiled=True)  7.19 us
    all_to_all x1, blocking collectives, local(): return lax.all_to_all(grad_zero, 'gz', 0, 2, tiled=True)  6.67 us
    dot_general x8, matrix products, sublayer(): jnp.einsum('pqhlk,pkqd->plqhd', attn_weights, value_part, preferred_eleme...  6.58 us
    dot_general x9, matrix products, sublayer(): jnp.einsum('plqd,pkqhd->pqhlk', queries, key_heads, preferred_element_typ...  5.67 us
    unnamed x33, local copies, waits for them, and re-layouts  5.2 us
  transfers between devices with their start and end apart: 7, of which 6 were waited for; matrix products, arithmetic and copies ran while one was open for 9% of the time, Pallas kernels for 0%

profile of v8, /device:TPU:0, one launch (start us, length us, event | category | flops | bytes accessed | tf_op | source)
XLA Modules:
  0.0 174.3 jit_solution(14183859709879158051)
XLA Ops:
  6.5 0.9 copy.335
  7.4 1.1 copy.334
  8.7 21.3 %all_gather.12 = bf16[3,384,192]{2,0,1:T(4,128)(2,1)S(1)} all-gather(bf16[3,96,192]{2,0,1:T(4,128)(2,1)S(1)} %pad_maximum_fusion), channel_id=1, replica_groups=mesh['gz'=4,'gy'=4,'gx'=2] {'gy'}, dimensions={1}, use_global_device_ids=true | all-gather | bytes 552960 | tf_op jit(solution)/shard_map/all_gather | solution.py:49
  30.0 2.0 %slice_reduce_fusion.2 = (bf16[384,48]{1,0:T(8,128)(2,1)S(1)}, bf16[384,48]{1,0:T(8,128)(2,1)S(1)}, bf16[384,48]{1,0:T(8,128)(2,1)S(1)}) fusion(bf16[3,384,192]{2,0,1:T(4,128)(2,1)S(1)} %all_gather.12), kind=kLoop, calls=%fused_computation.234 | loop fusion | bytes 221184 | tf_op jit(solution)/shard_map/slice | solution.py:53
  32.0 0.8 fusion.337
  33.1 0.6 copy.425
  33.7 0.7 pad_maximum_fusion.2
  34.7 0.6 copy.427
  35.3 0.7 pad_maximum_fusion.3
  36.0 0.7 copy.341
  36.7 3.3 %all-to-all-start.1 = ((bf16[8,1,16,384]{3,0,1,2:T(8,128)(2,1)}), bf16[8,1,16,384]{3,0,1,2:T(8,128)(2,1)S(1)}, u32[]{:S(2)}, u32[]{:S(2)}) async-start(bf16[8,1,16,384]{3,0,1,2:T(8,128)(2,1)} %copy.341), calls=%async_computation.1 | async-start | bytes 196608 | tf_op jit(solution)/shard_map/all_to_all | solution.py:101
  40.3 0.6 copy.424
  40.9 0.7 pad_maximum_fusion.1
  41.6 3.2 %all-to-all-done.1 = bf16[8,1,16,384]{3,0,1,2:T(8,128)(2,1)S(1)} async-done(((bf16[8,1,16,384]{3,0,1,2:T(8,128)(2,1)}), bf16[8,1,16,384]{3,0,1,2:T(8,128)(2,1)S(1)}, u32[]{:S(2)}, u32[]{:S(2)}) %all-to-all-start.1) | async-done | bytes 98336 | tf_op jit(solution)/shard_map/all_to_all | solution.py:101
  44.9 3.4 %all-to-all-start = ((bf16[8,1,16,384]{3,2,1,0:T(8,128)(2,1)}), bf16[8,1,16,384]{3,2,1,0:T(8,128)(2,1)S(1)}, u32[]{:S(2)}, u32[]{:S(2)}) async-start(bf16[8,1,16,384]{3,2,1,0:T(8,128)(2,1)} %param.5), calls=%async_computation | async-start | bytes 196608 | tf_op jit(solution)/shard_map/all_to_all | solution.py:93
  48.6 9.7 %all-gather.6.cloned.1.call-done = bf16[512,1152]{0,1:T(8,128)(2,1)} async-done(((bf16[512,144]{0,1:T(8,128)(2,1)}), bf16[512,1152]{0,1:T(8,128)(2,1)}) %all-gather.6.cloned.1.call-update) | async-done | bytes 1179664 | tf_op jit(solution)/shard_map/all_gather | solution.py:55
  58.3 1.6 convolution_bitcast_fusion.2
  59.8 0.4 fusion.101
  60.2 0.3 convolution_bitcast_fusion.14
  60.6 0.4 fusion.102
  60.9 0.3 fusion.263
  61.7 1.0 fusion.9
  62.7 21.0 %all-gather.8.cloned.1.call-done = bf16[512,1152]{0,1:T(8,128)(2,1)} async-done(((bf16[512,144]{0,1:T(8,128)(2,1)}), bf16[512,1152]{0,1:T(8,128)(2,1)}) %all-gather.8.cloned.1.call-update) | async-done | bytes 1179664 | tf_op jit(solution)/shard_map/all_gather | solution.py:55
  83.7 1.0 slice.103
  84.9 0.9 reshape.811
  86.3 0.9 reshape.802
  87.5 22.0 %all-gather.4.cloned.1.call-done = bf16[512,1152]{0,1:T(8,128)(2,1)} async-done(((bf16[512,144]{0,1:T(8,128)(2,1)}), bf16[512,1152]{0,1:T(8,128)(2,1)}) %all-gather.4.cloned.1.call-update) | async-done | bytes 1179664 | tf_op jit(solution)/shard_map/all_gather | solution.py:55
  109.5 1.0 slice.89
  110.7 0.9 reshape.793
  112.2 0.7 copy.354
  112.8 4.8 %all-to-all-start.2 = ((bf16[32,1,4,384]{3,2,1,0:T(4,128)(2,1)}), bf16[32,1,4,384]{3,2,1,0:T(4,128)(2,1)S(1)}, u32[]{:S(2)}, u32[]{:S(2)}) async-start(bf16[32,1,4,384]{3,2,1,0:T(4,128)(2,1)} %copy.354), calls=%async_computation.2 | async-start | bytes 196608 | tf_op jit(solution)/shard_map/all_to_all | solution.py:76
  117.9 7.2 %all-to-all-done.2 = bf16[32,1,4,384]{3,2,1,0:T(4,128)(2,1)S(1)} async-done(((bf16[32,1,4,384]{3,2,1,0:T(4,128)(2,1)}), bf16[32,1,4,384]{3,2,1,0:T(4,128)(2,1)S(1)}, u32[]{:S(2)}, u32[]{:S(2)}) %all-to-all-start.2) | async-done | bytes 98336 | tf_op jit(solution)/shard_map/all_to_all | solution.py:76
  125.4 1.6 convolution_bitcast_fusion.1
  127.0 0.4 fusion.99
  127.4 0.4 fusion.100
  128.6 2.5 %fusion.339 = (f32[32,6,4]{1,2,0:T(4,128)S(1)}, f32[1,32,6,4,4]{2,3,4,1,0:T(4,128)S(1)}) fusion(bf16[4,32,384,1]{2,1,0,3:T(8,128)(2,1)S(1)} %get-tuple-element.13, bf16[4,32,6,384]{3,1,2,0:T(8,128)(2,1)S(1)} %broadcast_multiply_fusion), kind=kOutput, calls=%fused_computation.403 | convolution fusion | flops 2364672 | bytes 703488 | tf_op jit(solution)/shard_map/jvp(plqd,pkqhd->pqhlk)/dot_general | solution.py:35
  131.1 0.8 fusion
  132.3 0.4 convolution_bitcast_fusion
  132.8 0.4 fusion.97
  133.1 0.4 fusion.98
  133.5 0.3 fusion.257
  134.9 0.7 fusion.146
  136.2 0.4 fusion.95
  137.0 0.4 fusion.96
  137.4 0.4 add_add_fusion.8
  137.7 0.4 multiply_reduce_fusion.1
  138.6 0.4 fusion.53
  139.0 2.4 %fusion.1 = bf16[32,6,4,4]{1,3,2,0:T(4,128)(2,1)S(1)} fusion(f32[4,32,384]{2,0,1:T(4,128)S(1)} %copy.373, f32[6,384]{1,0:T(8,128)S(1)} %get-tuple-element.17, bf16[4,32,384,1]{2,1,0,3:T(8,128)(2,1)S(1)} %fusion.236), kind=kOutput, calls=%fused_computation.5 | convolution fusion | flops 2654208 | bytes 310272 | tf_op jit(solution)/shard_map/transpose(jvp(pqhlk,pkqd->plqhd))/dot_general | solution.py:38
  141.6 0.6 convolution_bitcast_fusion.8
  142.2 0.8 fusion.13
  143.0 0.4 fusion.94
  143.7 0.4 fusion.93
  144.5 0.4 multiply_reduce_fusion
  145.1 0.7 copy.382
  145.7 2.8 %all-to-all-start.3 = ((bf16[32,1,4,384]{3,2,1,0:T(4,128)(2,1)}), bf16[32,1,4,384]{3,2,1,0:T(4,128)(2,1)S(1)}, u32[]{:S(2)}, u32[]{:S(2)}) async-start(bf16[32,1,4,384]{3,2,1,0:T(4,128)(2,1)} %bitcast.139), calls=%async_computation.3 | async-start | bytes 196608 | tf_op jit(solution)/shard_map/all_to_all | solution.py:87
  148.5 7.3 %all-to-all-done.3 = bf16[32,1,4,384]{3,2,1,0:T(4,128)(2,1)S(1)} async-done(((bf16[32,1,4,384]{3,2,1,0:T(4,128)(2,1)}), bf16[32,1,4,384]{3,2,1,0:T(4,128)(2,1)S(1)}, u32[]{:S(2)}, u32[]{:S(2)}) %all-to-all-start.3) | async-done | bytes 98336 | tf_op jit(solution)/shard_map/all_to_all | solution.py:87
  156.4 0.7 fusion.142
  157.5 0.6 copy-done.8
  158.3 0.4 fusion.91
  159.1 0.4 fusion.92
  159.4 0.3 add_add_fusion.2
  159.8 0.4 fusion.203
  160.4 6.7 %all_to_all.42 = bf16[32,1,4,384]{3,2,1,0:T(4,128)(2,1)S(1)} all-to-all(bf16[32,1,4,384]{3,2,1,0:T(4,128)(2,1)S(1)} %copy.386), channel_id=1, replica_groups=mesh['gz'=4,'gy'=4,'gx'=2] {'gz'}, dimensions={0} | all-to-all | bytes 196608 | tf_op jit(solution)/shard_map/all_to_all | solution.py:110
  167.1 0.7 all_to_all.36
  (109 shorter events, 10.3 us)
Async XLA Ops:
  6.5 51.7 %all-gather.6.cloned.1.call-start = ((), (), s32[]{:S(2)}) async-start(), calls=%async_computation.6 | async-start | bytes 1327104 | tf_op jit(solution)/shard_map/all_gather | solution.py:55
  33.0 3.0 %copy-start.5 = (bf16[8,1,16,384]{3,2,1,0:T(8,128)(2,1)S(1)}, bf16[8,1,16,384]{3,2,1,0:T(8,128)(2,1)}, u32[]{:S(2)}) copy-start(bf16[8,1,16,384]{3,2,1,0:T(8,128)(2,1)} %param.4) | copy-start | bytes 294916
  34.4 49.3 %all-gather.8.cloned.1.call-start = ((), (), s32[]{:S(2)}) async-start(), calls=%async_computation.7 | async-start | bytes 1327104 | tf_op jit(solution)/shard_map/all_gather | solution.py:55
  36.7 8.2 %all-to-all-start.1 = ((bf16[8,1,16,384]{3,0,1,2:T(8,128)(2,1)}), bf16[8,1,16,384]{3,0,1,2:T(8,128)(2,1)S(1)}, u32[]{:S(2)}, u32[]{:S(2)}) async-start(bf16[8,1,16,384]{3,0,1,2:T(8,128)(2,1)} %copy.341), calls=%async_computation.1 | async-start | bytes 196608 | tf_op jit(solution)/shard_map/all_to_all | solution.py:101
  40.0 69.5 %all-gather.4.cloned.1.call-start = ((), (), s32[]{:S(2)}) async-start(), calls=%async_computation.5 | async-start | bytes 1327104 | tf_op jit(solution)/shard_map/all_gather | solution.py:55
  44.9 68.0 %all-to-all-start = ((bf16[8,1,16,384]{3,2,1,0:T(8,128)(2,1)}), bf16[8,1,16,384]{3,2,1,0:T(8,128)(2,1)S(1)}, u32[]{:S(2)}, u32[]{:S(2)}) async-start(bf16[8,1,16,384]{3,2,1,0:T(8,128)(2,1)} %param.5), calls=%async_computation | async-start | bytes 196608 | tf_op jit(solution)/shard_map/all_to_all | solution.py:93
  61.3 1.4 copy-start.7
  61.4 1.3 copy-start.9
  61.7 23.0 %copy-start.3 = (f32[1,4,6,32,32]{3,4,2,1,0:T(8,128)}, f32[1,4,6,32,32]{3,4,2,1,0:T(8,128)S(1)}, u32[]{:S(2)}) copy-start(f32[1,4,6,32,32]{3,4,2,1,0:T(8,128)S(1)} %get-tuple-element.20) | copy-start | bytes 294916
  61.7 23.0 %copy-start.11 = (f32[4,6,32]{2,1,0:T(8,128)}, f32[4,6,32]{2,1,0:T(8,128)S(1)}, u32[]{:S(2)}) copy-start(f32[4,6,32]{2,1,0:T(8,128)S(1)} %get-tuple-element.19) | copy-start | bytes 9220
  84.9 1.2 slice-start
  110.7 1.2 copy-start.6
  112.8 12.2 %all-to-all-start.2 = ((bf16[32,1,4,384]{3,2,1,0:T(4,128)(2,1)}), bf16[32,1,4,384]{3,2,1,0:T(4,128)(2,1)S(1)}, u32[]{:S(2)}, u32[]{:S(2)}) async-start(bf16[32,1,4,384]{3,2,1,0:T(4,128)(2,1)} %copy.354), calls=%async_computation.2 | async-start | bytes 196608 | tf_op jit(solution)/shard_map/all_to_all | solution.py:76
  131.1 1.3 copy-start.2
  143.0 1.5 copy-start.1
  144.5 4.0 %copy-start.12 = (f32[4,6,32]{2,1,0:T(8,128)S(1)}, f32[4,6,32]{2,1,0:T(8,128)}, u32[]{:S(2)}) copy-start(f32[4,6,32]{2,1,0:T(8,128)} %copy-done.11) | copy-start | bytes 9220
  144.9 11.2 %copy-start.4 = (f32[1,4,6,32,32]{3,4,2,1,0:T(8,128)S(1)}, f32[1,4,6,32,32]{3,4,2,1,0:T(8,128)}, u32[]{:S(2)}) copy-start(f32[1,4,6,32,32]{3,4,2,1,0:T(8,128)} %copy-done.3) | copy-start | bytes 294916
  145.7 10.2 %all-to-all-start.3 = ((bf16[32,1,4,384]{3,2,1,0:T(4,128)(2,1)}), bf16[32,1,4,384]{3,2,1,0:T(4,128)(2,1)S(1)}, u32[]{:S(2)}, u32[]{:S(2)}) async-start(bf16[32,1,4,384]{3,2,1,0:T(4,128)(2,1)} %bitcast.139), calls=%async_computation.3 | async-start | bytes 196608 | tf_op jit(solution)/shard_map/all_to_all | solution.py:87
  156.1 1.1 copy-start.10
  157.1 0.9 copy-start.8
  158.3 1.5 copy-start
Sparse Core Ops, SparseCore 0:
  34.6 23.6 all-gather.5
  60.1 23.5 all-gather.7
  85.6 23.9 all-gather.3

commit v9 on v7

--- a/solution.py
+++ b/solution.py
@@ -45,7 +45,11 @@
     subs, din, dproj = w_project.shape
     cat = jnp.concatenate([w_project, w_output], axis=2)
     ny = sizes[1]
-    rows = lax.all_to_all(jnp.broadcast_to(cat[None], (ny,) + cat.shape), "gy", 0, 0, tiled=True)
+    shifted = [cat] + [
+        lax.ppermute(cat, "gy", [(i, (i + s) % ny) for i in range(ny)]) for s in range(1, ny)
+    ]
+    source = (lax.axis_index("gy") - jnp.arange(ny)) % ny
+    rows = jnp.take(jnp.stack(shifted), source, axis=0)
     rows = jnp.swapaxes(rows, 0, 1).reshape(subs, ny * din, cat.shape[2])
     proj = lax.all_gather(rows[:, :, :dproj], ("gz", "gx"), axis=2, tiled=True)
     outp = lax.all_gather(rows[:, :, dproj:], ("gz", "gx"), axis=2, tiled=True)

time: 143 us -> 141 us (0.986)
  blocking collectives: 50.5 us -> 28.4 us
  starting transfers between devices: 13.9 us -> 24.1 us
  waiting for transfers between devices: 18.8 us -> 27.1 us
  local copies, waits for them, and re-layouts: 9.7 us -> 12 us
    all_to_all x1 -> x0, blocking collectives: 22 us -> none  [full_weights(): lax.all_to_all(jnp.broadcast_to(cat[None], (ny,) + cat.shape), 'gy', 0, 0...]
    ppermute x0 -> x3, waiting for transfers between devices: none -> 8.3 us  [full_weights(): lax.ppermute(cat, 'gy', [(i, (i + s) % ny) for i in range(ny)])]
    ppermute x0 -> x3, starting transfers between devices: none -> 6.99 us  [full_weights(): lax.ppermute(cat, 'gy', [(i, (i + s) % ny) for i in range(ny)])]
    all_to_all x1, starting transfers between devices: 3.69 us -> 6.93 us  [block_to_plane(): got = lax.all_to_all(block, ('gy', 'gx'), 0, 0, tiled=True)]
  transfers between devices with their start and end apart: 5 -> 8, of which waited for: 3 -> 5; matrix products, arithmetic and copies ran while one was open for 4% -> 5% of each run, Pallas kernels for 0% -> 0%
where the time goes in v9:
time: 141 us; the launch traced here: 140 us
  matrix products  29.8 us (21%)
  blocking collectives  28.4 us (20%)
  waiting for transfers between devices  27.1 us (19%)
  starting transfers between devices  24.1 us (17%)
  between operations  14.1 us (10%)
  local copies, waits for them, and re-layouts  12 us (9%)
  other arithmetic  4.33 us (3%)
    all_gather x1, blocking collectives, full_weights(): outp = lax.all_gather(rows[:, :, dproj:], ('gz', 'gx'), axis=2, tiled=True)  21.7 us
    ppermute x3, waiting for transfers between devices, full_weights(): lax.ppermute(cat, 'gy', [(i, (i + s) % ny) for i in range(ny)])  8.3 us
    all_to_all x1, waiting for transfers between devices, from_planes(): return lax.all_to_all(parts, ALL, 0, 0, tiled=True)  7.34 us
    dot_general x6, matrix products, sublayer(): packed = jnp.dot(normed, w_inner, preferred_element_type=jnp.float32)  7.26 us
    all_to_all x1, waiting for transfers between devices, to_planes(): got = lax.all_to_all(depth_lines, ALL, 0, 0, tiled=True)  7.18 us
    ppermute x3, starting transfers between devices, full_weights(): lax.ppermute(cat, 'gy', [(i, (i + s) % ny) for i in range(ny)])  6.99 us
    all_to_all x1, starting transfers between devices, block_to_plane(): got = lax.all_to_all(block, ('gy', 'gx'), 0, 0, tiled=True)  6.93 us
    dot_general x9, matrix products, sublayer(): jnp.einsum('plqd,pkqhd->pqhlk', queries, key_heads, preferred_element_typ...  6.87 us
  transfers between devices with their start and end apart: 8, of which 5 were waited for; matrix products, arithmetic and copies ran while one was open for 5% of the time, Pallas kernels for 0%

profile of v9, /device:TPU:0, one launch (start us, length us, event | category | flops | bytes accessed | tf_op | source)
XLA Modules:
  0.0 139.8 jit_solution(5186529604211732104)
XLA Ops:
  6.5 0.9 constant_dynamic-update-slice_fusion.1
  7.4 0.8 constant_dynamic-update-slice_fusion
  8.2 3.1 %collective-permute-start = (bf16[3,96,192]{1,2,0:T(8,128)(2,1)S(1)}, bf16[3,96,192]{1,2,0:T(8,128)(2,1)S(1)}, u32[]{:S(2)}, u32[]{:S(2)}) collective-permute-start(bf16[3,96,192]{1,2,0:T(8,128)(2,1)S(1)} %constant_dynamic-update-slice_fusion), channel_id=1, source_target_pairs={{0,2},{2,4},{4,6},{6,0},{1,3},{3,5},{5,7},{7,1},{8,10},{10,12},{12... | collective-permute-start | bytes 331784 | tf_op jit(solution)/shard_map/ppermute | solution.py:49
  11.3 2.6 %collective-permute-start.1 = (bf16[3,96,192]{1,2,0:T(8,128)(2,1)S(1)}, bf16[3,96,192]{1,2,0:T(8,128)(2,1)S(1)}, u32[]{:S(2)}, u32[]{:S(2)}) collective-permute-start(bf16[3,96,192]{1,2,0:T(8,128)(2,1)S(1)} %constant_dynamic-update-slice_fusion), channel_id=1, source_target_pairs={{0,4},{2,6},{4,0},{6,2},{1,5},{3,7},{5,1},{7,3},{8,12},{10,14},{12... | collective-permute-start | bytes 331784 | tf_op jit(solution)/shard_map/ppermute | solution.py:49
  13.9 1.3 collective-permute-start.2
  15.3 2.8 %collective-permute-done = bf16[3,96,192]{1,2,0:T(8,128)(2,1)S(1)} collective-permute-done((bf16[3,96,192]{1,2,0:T(8,128)(2,1)S(1)}, bf16[3,96,192]{1,2,0:T(8,128)(2,1)S(1)}, u32[]{:S(2)}, u32[]{:S(2)}) %collective-permute-start) | collective-permute-done | bytes 110624 | tf_op jit(solution)/shard_map/ppermute | solution.py:49
  18.1 5.5 %collective-permute-done.1 = bf16[3,96,192]{1,2,0:T(8,128)(2,1)S(1)} collective-permute-done((bf16[3,96,192]{1,2,0:T(8,128)(2,1)S(1)}, bf16[3,96,192]{1,2,0:T(8,128)(2,1)S(1)}, u32[]{:S(2)}, u32[]{:S(2)}) %collective-permute-start.1) | collective-permute-done | bytes 110624 | tf_op jit(solution)/shard_map/ppermute | solution.py:49
  23.7 0.7 gather_fusion
  24.5 0.5 copy.126
  25.0 0.4 reshape.830
  25.4 0.8 slice.75
  26.2 0.7 copy.128
  26.9 3.3 %all-to-all-start.1 = ((bf16[8,1,16,384]{3,0,1,2:T(8,128)(2,1)}), bf16[8,1,16,384]{3,0,1,2:T(8,128)(2,1)S(1)}, u32[]{:S(2)}, u32[]{:S(2)}) async-start(bf16[8,1,16,384]{3,0,1,2:T(8,128)(2,1)} %copy.128), calls=%async_computation.1 | async-start | bytes 196608 | tf_op jit(solution)/shard_map/all_to_all | solution.py:98
  30.2 4.2 %all-to-all-done.1 = bf16[8,1,16,384]{3,0,1,2:T(8,128)(2,1)S(1)} async-done(((bf16[8,1,16,384]{3,0,1,2:T(8,128)(2,1)}), bf16[8,1,16,384]{3,0,1,2:T(8,128)(2,1)S(1)}, u32[]{:S(2)}, u32[]{:S(2)}) %all-to-all-start.1) | async-done | bytes 98336 | tf_op jit(solution)/shard_map/all_to_all | solution.py:98
  34.4 6.9 %all-to-all-start = ((bf16[8,1,16,384]{3,2,1,0:T(8,128)(2,1)}), bf16[8,1,16,384]{3,2,1,0:T(8,128)(2,1)S(1)}, u32[]{:S(2)}, u32[]{:S(2)}) async-start(bf16[8,1,16,384]{3,2,1,0:T(8,128)(2,1)} %param.5), calls=%async_computation | async-start | bytes 196608 | tf_op jit(solution)/shard_map/all_to_all | solution.py:90
  41.5 0.7 add.157
  42.2 21.7 %all_gather.6 = bf16[3,384,384]{1,2,0:T(8,128)(2,1)S(1)} all-gather(bf16[3,384,48]{1,2,0:T(8,128)(2,1)S(1)} %slice.73), channel_id=1, replica_groups=mesh['gz'=4,'gy'=4,'gx'=2] {'gz','gx'}, dimensions={2}, use_global_device_ids=true | all-gather | bytes 995328 | tf_op jit(solution)/shard_map/all_gather | solution.py:55
  63.9 1.6 %convolution_bitcast_fusion.2 = f32[1,32,4,1152]{3,1,2,0:T(8,128)S(1)} fusion(bf16[3,384,1152]{1,2,0:T(8,128)(2,1)} %all-gather.2.cloned.1.call-done, bf16[8,1,4,4,384]{4,0,3,2,1:T(8,128)(2,1)S(1)} %bitcast.619, f32[4,8,4]{1,2,0:T(4,128)S(1)} %get-tuple-element.14), kind=kOutput, calls=%fused_computation.3 | convolution fusion | flops 113393664 | bytes 1573376 | tf_op jit(solution)/shard_map/jvp()/dot_general | solution.py:30
  65.5 0.4 fusion.102
  65.9 0.4 fusion.101
  68.1 0.4 fusion.9
  68.8 0.7 copy.135
  69.4 4.1 %all-to-all-start.2 = ((bf16[32,1,4,384]{3,2,1,0:T(4,128)(2,1)}), bf16[32,1,4,384]{3,2,1,0:T(4,128)(2,1)S(1)}, u32[]{:S(2)}, u32[]{:S(2)}) async-start(bf16[32,1,4,384]{3,2,1,0:T(4,128)(2,1)} %copy.135), calls=%async_computation.2 | async-start | bytes 196608 | tf_op jit(solution)/shard_map/all_to_all | solution.py:73
  73.8 7.2 %all-to-all-done.2 = bf16[32,1,4,384]{3,2,1,0:T(4,128)(2,1)S(1)} async-done(((bf16[32,1,4,384]{3,2,1,0:T(4,128)(2,1)}), bf16[32,1,4,384]{3,2,1,0:T(4,128)(2,1)S(1)}, u32[]{:S(2)}, u32[]{:S(2)}) %all-to-all-start.2) | async-done | bytes 98336 | tf_op jit(solution)/shard_map/all_to_all | solution.py:73
  81.1 0.6 multiply_add_fusion
  81.9 1.6 %convolution_bitcast_fusion.1 = f32[1,4,32,1152]{3,2,1,0:T(8,128)S(1)} fusion(bf16[4,32,384]{2,1,0:T(8,128)(2,1)S(1)} %convert_element_type.493, bf16[3,384,1152]{1,2,0:T(8,128)(2,1)} %all-gather.2.cloned.1.call-done), kind=kOutput, calls=%fused_computation.2 | convolution fusion | flops 113246208 | bytes 1572864 | tf_op jit(solution)/shard_map/jvp()/dot_general | solution.py:30
  83.4 0.4 fusion.100
  83.8 0.4 fusion.99
  84.2 0.7 fusion.234
  84.9 0.7 copy_bitcast_fusion
  86.2 0.7 fusion.226
  86.9 0.9 broadcast_multiply_fusion
  87.8 1.0 reshape.867
  88.8 3.7 %fusion.343 = (f32[32,6,4]{1,2,0:T(4,128)S(1)}, f32[1,32,6,4,4]{2,3,4,1,0:T(4,128)S(1)}) fusion(bf16[4,32,384,1]{2,1,0,3:T(8,128)(2,1)} %get-tuple-element.7, bf16[4,32,6,384]{3,1,2,0:T(8,128)(2,1)} %broadcast_multiply_fusion), kind=kOutput, calls=%fused_computation.419 | convolution fusion | flops 2364672 | bytes 703488 | tf_op jit(solution)/shard_map/jvp(plqd,pkqhd->pqhlk)/dot_general | solution.py:35
  92.6 0.8 fusion
  93.7 0.4 convolution_bitcast_fusion
  94.1 0.4 fusion.98
  94.5 0.4 fusion.97
  94.9 0.3 fusion.255
  96.2 0.7 fusion.146
  97.6 0.4 fusion.96
  98.0 0.3 add_add_fusion.8
  98.3 0.4 fusion.95
  99.1 0.4 multiply_reduce_fusion.1
  100.0 0.4 fusion.53
  100.4 2.4 %fusion.1 = bf16[32,6,4,4]{1,3,2,0:T(4,128)(2,1)S(1)} fusion(f32[4,32,384]{2,0,1:T(4,128)S(1)} %copy.146, f32[6,384]{1,0:T(8,128)S(1)} %get-tuple-element.19, bf16[4,32,384,1]{2,1,0,3:T(8,128)(2,1)S(1)} %copy-done.11), kind=kOutput, calls=%fused_computation.6 | convolution fusion | flops 2654208 | bytes 310272 | tf_op jit(solution)/shard_map/transpose(jvp(pqhlk,pkqd->plqhd))/dot_general | solution.py:38
  103.0 0.8 fusion.13
  104.0 0.6 convolution_bitcast_fusion.8
  104.7 0.6 copy.258
  105.3 0.4 fusion.94
  106.1 0.4 fusion.93
  106.8 0.8 add.156
  107.6 1.7 %multiply_reduce_fusion = (f32[4,32]{1,0:T(4,128)S(1)}, f32[4,32,384]{2,1,0:T(8,128)S(1)}) fusion(f32[4,32,384]{2,1,0:T(8,128)S(1)} %reshape.867, bf16[3,384,1152]{1,2,0:T(8,128)(2,1)} %all-gather.2.cloned.1.call-done, f32[1,4,32,384]{3,2,1,0:T(8,128)S(1)} %add_add_fusion.4, f32[1,4,32,384]{3,2,1,0:T(8,128)S(1)} %add_add_fusion.5, ...), kind=kOutput, calls=%fused_computation.270 | convolution fusion | flops 113885056 | bytes 1769984 | tf_op jit(solution)/shard_map/transpose(jvp())/dot_general | solution.py:30
  109.5 0.7 copy.155
  110.1 2.8 %all-to-all-start.3 = ((bf16[32,1,4,384]{3,2,1,0:T(4,128)(2,1)}), bf16[32,1,4,384]{3,2,1,0:T(4,128)(2,1)S(1)}, u32[]{:S(2)}, u32[]{:S(2)}) async-start(bf16[32,1,4,384]{3,2,1,0:T(4,128)(2,1)} %bitcast.133), calls=%async_computation.3 | async-start | bytes 196608 | tf_op jit(solution)/shard_map/all_to_all | solution.py:84
  112.9 7.3 %all-to-all-done.3 = bf16[32,1,4,384]{3,2,1,0:T(4,128)(2,1)S(1)} async-done(((bf16[32,1,4,384]{3,2,1,0:T(4,128)(2,1)}), bf16[32,1,4,384]{3,2,1,0:T(4,128)(2,1)S(1)}, u32[]{:S(2)}, u32[]{:S(2)}) %all-to-all-start.3) | async-done | bytes 98336 | tf_op jit(solution)/shard_map/all_to_all | solution.py:84
  120.8 0.7 fusion.142
  122.3 0.4 fusion.92
  122.7 0.4 add_add_fusion.2
  123.1 0.4 fusion.91
  123.4 0.3 add_add_fusion.1
  123.8 1.6 %fusion.202 = (f32[32,4]{0,1:T(4,128)S(1)}, f32[32,4,384]{2,0,1:T(8,128)S(1)}) fusion(bf16[3,384,1152]{1,2,0:T(8,128)(2,1)} %all-gather.2.cloned.1.call-done, f32[1,32,4,384]{3,1,2,0:T(8,128)S(1)} %add_add_fusion.1, f32[1,32,4,384]{3,1,2,0:T(8,128)S(1)} %add_add_fusion.2, bf16[1,32,4,384]{3,1,2,0:T(8,128)(2,1)S(1)} %fusion.87, ...), kind=kOutput, calls=%fused_computation.265 | convolution fusion | flops 113934208 | bytes 1671680 | tf_op jit(solution)/shard_map/transpose(jvp())/dot_general | solution.py:30
  125.6 6.7 %all_to_all.42 = bf16[32,1,4,384]{3,2,1,0:T(4,128)(2,1)S(1)} all-to-all(bf16[32,1,4,384]{3,2,1,0:T(4,128)(2,1)S(1)} %copy.159), channel_id=1, replica_groups=mesh['gz'=4,'gy'=4,'gx'=2] {'gz'}, dimensions={0} | all-to-all | bytes 196608 | tf_op jit(solution)/shard_map/all_to_all | solution.py:107
  132.3 0.7 all_to_all.36
  (105 shorter events, 9.2 us)
Async XLA Ops:
  6.5 57.4 %all-gather.2.cloned.1.call-start = ((), (), s32[]{:S(2)}) async-start(), calls=%async_computation.5 | async-start | bytes 2985984 | tf_op jit(solution)/shard_map/all_gather | solution.py:54
  8.2 9.9 %collective-permute-start = (bf16[3,96,192]{1,2,0:T(8,128)(2,1)S(1)}, bf16[3,96,192]{1,2,0:T(8,128)(2,1)S(1)}, u32[]{:S(2)}, u32[]{:S(2)}) collective-permute-start(bf16[3,96,192]{1,2,0:T(8,128)(2,1)S(1)} %constant_dynamic-update-slice_fusion), channel_id=1, source_target_pairs={{0,2},{2,4},{4,6},{6,0},{1,3},{3,5},{5,7},{7,1},{8,10},{10,12},{12... | collective-permute-start | bytes 331784 | tf_op jit(solution)/shard_map/ppermute | solution.py:49
  11.3 12.3 %collective-permute-start.1 = (bf16[3,96,192]{1,2,0:T(8,128)(2,1)S(1)}, bf16[3,96,192]{1,2,0:T(8,128)(2,1)S(1)}, u32[]{:S(2)}, u32[]{:S(2)}) collective-permute-start(bf16[3,96,192]{1,2,0:T(8,128)(2,1)S(1)} %constant_dynamic-update-slice_fusion), channel_id=1, source_target_pairs={{0,4},{2,6},{4,0},{6,2},{1,5},{3,7},{5,1},{7,3},{8,12},{10,14},{12... | collective-permute-start | bytes 331784 | tf_op jit(solution)/shard_map/ppermute | solution.py:49
  13.9 9.7 %collective-permute-start.2 = (bf16[3,96,192]{1,2,0:T(8,128)(2,1)S(1)}, bf16[3,96,192]{1,2,0:T(8,128)(2,1)S(1)}, u32[]{:S(2)}, u32[]{:S(2)}) collective-permute-start(bf16[3,96,192]{1,2,0:T(8,128)(2,1)S(1)} %constant_dynamic-update-slice_fusion), channel_id=1, source_target_pairs={{0,6},{2,0},{4,2},{6,4},{1,7},{3,1},{5,3},{7,5},{8,14},{10,8},{12,... | collective-permute-start | bytes 331784 | tf_op jit(solution)/shard_map/ppermute | solution.py:49
  24.5 1.7 %copy-start.10 = (bf16[8,1,16,384]{3,2,1,0:T(8,128)(2,1)S(1)}, bf16[8,1,16,384]{3,2,1,0:T(8,128)(2,1)}, u32[]{:S(2)}) copy-start(bf16[8,1,16,384]{3,2,1,0:T(8,128)(2,1)} %param.4) | copy-start | bytes 294916
  26.9 7.6 %all-to-all-start.1 = ((bf16[8,1,16,384]{3,0,1,2:T(8,128)(2,1)}), bf16[8,1,16,384]{3,0,1,2:T(8,128)(2,1)S(1)}, u32[]{:S(2)}, u32[]{:S(2)}) async-start(bf16[8,1,16,384]{3,0,1,2:T(8,128)(2,1)} %copy.128), calls=%async_computation.1 | async-start | bytes 196608 | tf_op jit(solution)/shard_map/all_to_all | solution.py:98
  30.2 72.8 %copy-start.17 = (bf16[6,384]{1,0:T(8,128)(2,1)}, bf16[6,384]{1,0:T(8,128)(2,1)S(1)}, u32[]{:S(2)}) copy-start(bf16[6,384]{1,0:T(8,128)(2,1)S(1)} %get-tuple-element.20) | copy-start | bytes 13828
  34.4 35.0 %all-to-all-start = ((bf16[8,1,16,384]{3,2,1,0:T(8,128)(2,1)}), bf16[8,1,16,384]{3,2,1,0:T(8,128)(2,1)S(1)}, u32[]{:S(2)}, u32[]{:S(2)}) async-start(bf16[8,1,16,384]{3,2,1,0:T(8,128)(2,1)} %param.5), calls=%async_computation | async-start | bytes 196608 | tf_op jit(solution)/shard_map/all_to_all | solution.py:90
  65.9 0.6 copy-start.4
  66.5 0.6 copy-start.8
  67.5 0.6 copy-start.12
  67.5 1.0 copy-start.14
  67.8 0.9 copy-start.2
  67.8 5.9 %copy-start.19 = (f32[4,6,32]{2,1,0:T(8,128)}, f32[4,6,32]{2,1,0:T(8,128)S(1)}, u32[]{:S(2)}) copy-start(f32[4,6,32]{2,1,0:T(8,128)S(1)} %get-tuple-element.21) | copy-start | bytes 9220
  69.4 11.5 %all-to-all-start.2 = ((bf16[32,1,4,384]{3,2,1,0:T(4,128)(2,1)}), bf16[32,1,4,384]{3,2,1,0:T(4,128)(2,1)S(1)}, u32[]{:S(2)}, u32[]{:S(2)}) async-start(bf16[32,1,4,384]{3,2,1,0:T(4,128)(2,1)} %copy.135), calls=%async_computation.2 | async-start | bytes 196608 | tf_op jit(solution)/shard_map/all_to_all | solution.py:73
  84.2 2.7 %copy-start.6 = (f32[4,32,6]{1,2,0:T(8,128)}, f32[4,32,6]{1,2,0:T(8,128)S(1)}, u32[]{:S(2)}) copy-start(f32[4,32,6]{1,2,0:T(8,128)S(1)} %fusion.99) | copy-start | bytes 9220
  88.8 3.8 %copy-start.11 = (bf16[4,32,384,1]{2,1,0,3:T(8,128)(2,1)S(1)}, bf16[4,32,384,1]{2,1,0,3:T(8,128)(2,1)}, u32[]{:S(2)}) copy-start(bf16[4,32,384,1]{2,1,0,3:T(8,128)(2,1)} %fusion.234) | copy-start | bytes 294916
  88.8 4.9 %copy-start = (bf16[3,384,1152]{1,2,0:T(8,128)(2,1)S(1)}, bf16[3,384,1152]{1,2,0:T(8,128)(2,1)}, u32[]{:S(2)}) copy-start(bf16[3,384,1152]{1,2,0:T(8,128)(2,1)} %all-gather.2.cloned.1.call-done) | copy-start | bytes 7962628
  100.0 3.0 %copy-start.16 = (bf16[4,32,384,1]{2,1,0,3:T(8,128)(2,1)S(1)}, bf16[4,32,384,1]{2,1,0,3:T(8,128)(2,1)}, u32[]{:S(2)}) copy-start(bf16[4,32,384,1]{2,1,0,3:T(8,128)(2,1)} %get-tuple-element.7) | copy-start | bytes 294916
  103.0 1.1 copy-start.1
  104.0 2.0 %copy-start.7 = (f32[4,32,6]{1,2,0:T(8,128)S(1)}, f32[4,32,6]{1,2,0:T(8,128)}, u32[]{:S(2)}) copy-start(f32[4,32,6]{1,2,0:T(8,128)} %copy-done.6) | copy-start | bytes 9220
  107.6 5.3 %copy-start.20 = (f32[4,6,32]{2,1,0:T(8,128)S(1)}, f32[4,6,32]{2,1,0:T(8,128)}, u32[]{:S(2)}) copy-start(f32[4,6,32]{2,1,0:T(8,128)} %copy-done.19) | copy-start | bytes 9220
  107.6 12.9 %copy-start.3 = (f32[1,4,6,32,32]{3,4,2,1,0:T(8,128)S(1)}, f32[1,4,6,32,32]{3,4,2,1,0:T(8,128)}, u32[]{:S(2)}) copy-start(f32[1,4,6,32,32]{3,4,2,1,0:T(8,128)} %copy-done.2) | copy-start | bytes 294916
  110.1 10.2 %all-to-all-start.3 = ((bf16[32,1,4,384]{3,2,1,0:T(4,128)(2,1)}), bf16[32,1,4,384]{3,2,1,0:T(4,128)(2,1)S(1)}, u32[]{:S(2)}, u32[]{:S(2)}) async-start(bf16[32,1,4,384]{3,2,1,0:T(4,128)(2,1)} %bitcast.133), calls=%async_computation.3 | async-start | bytes 196608 | tf_op jit(solution)/shard_map/all_to_all | solution.py:84
  120.5 1.1 copy-start.15
  120.5 1.1 copy-start.18
  120.8 1.1 copy-start.13
  121.6 0.7 copy-start.5
  121.9 1.1 copy-start.9
  123.1 2.3 %copy-start.21 = (f32[32,4]{0,1:T(4,128)S(1)}, f32[32,4]{0,1:T(4,128)}, u32[]{:S(2)}) copy-start(f32[32,4]{0,1:T(4,128)} %add.157) | copy-start | bytes 1540
Sparse Core Ops, SparseCore 0:
  26.3 35.3 all-gather.1

commit v10 on v9

--- a/solution.py
+++ b/solution.py
@@ -51,8 +51,16 @@
     source = (lax.axis_index("gy") - jnp.arange(ny)) % ny
     rows = jnp.take(jnp.stack(shifted), source, axis=0)
     rows = jnp.swapaxes(rows, 0, 1).reshape(subs, ny * din, cat.shape[2])
-    proj = lax.all_gather(rows[:, :, :dproj], ("gz", "gx"), axis=2, tiled=True)
-    outp = lax.all_gather(rows[:, :, dproj:], ("gz", "gx"), axis=2, tiled=True)
+    feat = rows.shape[1]
+    blocks = sizes[0] * sizes[2]
+    dout = w_output.shape[2]
+    outp = rows[:, :, dproj:].reshape(subs, -1, dproj)
+    got = lax.all_gather(
+        jnp.concatenate([rows[:, :, :dproj], outp], axis=1), ("gz", "gx"), axis=2, tiled=True
+    )
+    proj = got[:, :feat]
+    outp = got[:, feat:].reshape(subs, -1, blocks, dproj).swapaxes(1, 2)
+    outp = outp.reshape(subs, blocks, feat, dout).swapaxes(1, 2).reshape(subs, feat, blocks * dout)
     return [(proj[i], outp[i]) for i in range(subs)]
 
 

time: 141 us -> 145 us (1.028)
  waiting for transfers between devices: 27.1 us -> 50.4 us
  blocking collectives: 28.4 us -> 6.67 us
  local copies, waits for them, and re-layouts: 12 us -> 18.4 us
  starting transfers between devices: 24.1 us -> 22 us
    all_gather x1 -> x0, blocking collectives: 21.7 us -> none  [full_weights(): outp = lax.all_gather(rows[:, :, dproj:], ('gz', 'gx'), axis=2, tiled=True)]
    all_gather x1, waiting for transfers between devices: 0.01 us -> 21.4 us  [full_weights(): lax.all_gather(jnp.concatenate([rows[:, :, :dproj], outp], axis=1), ('gz'...]
    reshape x0 -> x3, local copies, waits for them, and re-layouts: none -> 4.48 us  [the longest x1 4.13 us: full_weights(): outp.reshape(subs, blocks, feat, dout).swapaxes(1, 2)]
    ppermute x3, waiting for transfers between devices: 8.3 us -> 11.4 us  [full_weights(): lax.ppermute(cat, 'gy', [(i, (i + s) % ny) for i in range(ny)])]
    slice x2 -> x9, local copies, waits for them, and re-layouts: 0.78 us -> 3.3 us  [the longest x4 3.02 us: full_weights(): return [(proj[i], outp[i]) for i in range(subs)]]
    all_to_all x1, starting transfers between devices: 6.93 us -> 5.03 us  [block_to_plane(): got = lax.all_to_all(block, ('gy', 'gx'), 0, 0, tiled=True)]
    transpose x0 -> x1, local copies, waits for them, and re-layouts: none -> 1.54 us  [full_weights(): outp = got[:, feat:].reshape(subs, -1, blocks, dproj).swapaxes(1, 2)]
    unnamed x46 -> x60, local copies, waits for them, and re-layouts: 2.84 us -> 3.59 us
  transfers between devices with their start and end apart: 8 -> 8, of which waited for: 5 -> 6; matrix products, arithmetic and copies ran while one was open for 5% -> 12% of each run, Pallas kernels for 0% -> 0%
where the time goes in v10:
time: 145 us; the launch traced here: 144 us
  waiting for transfers between devices  50.4 us (35%)
  matrix products  28.7 us (20%)
  starting transfers between devices  22 us (15%)
  local copies, waits for them, and re-layouts  18.4 us (13%)
  between operations  14.3 us (10%)
  blocking collectives  6.67 us (5%)
  other arithmetic  3.58 us (2%)
    all_gather x1, waiting for transfers between devices, full_weights(): lax.all_gather(jnp.concatenate([rows[:, :, :dproj], outp], axis=1), ('gz'...  21.4 us
    ppermute x3, waiting for transfers between devices, full_weights(): lax.ppermute(cat, 'gy', [(i, (i + s) % ny) for i in range(ny)])  11.4 us
    all_to_all x1, waiting for transfers between devices, from_planes(): return lax.all_to_all(parts, ALL, 0, 0, tiled=True)  7.34 us
    all_to_all x1, blocking collectives, local(): return lax.all_to_all(grad_zero, 'gz', 0, 2, tiled=True)  6.67 us
    dot_general x8, matrix products, sublayer(): jnp.einsum('pqhlk,pkqd->plqhd', attn_weights, value_part, preferred_eleme...  6.57 us
    all_to_all x1, waiting for transfers between devices, to_planes(): got = lax.all_to_all(depth_lines, ALL, 0, 0, tiled=True)  6.51 us
    ppermute x3, starting transfers between devices, full_weights(): lax.ppermute(cat, 'gy', [(i, (i + s) % ny) for i in range(ny)])  6.09 us
    dot_general x6, matrix products, sublayer(): packed = jnp.dot(normed, w_inner, preferred_element_type=jnp.float32)  6.03 us
  transfers between devices with their start and end apart: 8, of which 6 were waited for; matrix products, arithmetic and copies ran while one was open for 12% of the time, Pallas kernels for 0%

profile of v10, /device:TPU:0, one launch (start us, length us, event | category | flops | bytes accessed | tf_op | source)
XLA Modules:
  0.0 144.0 jit_solution(2389788200276750524)
XLA Ops:
  6.5 0.9 constant_dynamic-update-slice_fusion.1
  7.4 0.8 constant_dynamic-update-slice_fusion
  8.2 5.1 %collective-permute-start.2 = (bf16[3,96,192]{1,2,0:T(8,128)(2,1)S(1)}, bf16[3,96,192]{1,2,0:T(8,128)(2,1)S(1)}, u32[]{:S(2)}, u32[]{:S(2)}) collective-permute-start(bf16[3,96,192]{1,2,0:T(8,128)(2,1)S(1)} %constant_dynamic-update-slice_fusion), channel_id=1, source_target_pairs={{0,6},{2,0},{4,2},{6,4},{1,7},{3,1},{5,3},{7,5},{8,14},{10,8},{12,... | collective-permute-start | bytes 331784 | tf_op jit(solution)/shard_map/ppermute | solution.py:49
  13.3 1.0 collective-permute-start
  14.4 3.2 %collective-permute-done.2 = bf16[3,96,192]{1,2,0:T(8,128)(2,1)S(1)} collective-permute-done((bf16[3,96,192]{1,2,0:T(8,128)(2,1)S(1)}, bf16[3,96,192]{1,2,0:T(8,128)(2,1)S(1)}, u32[]{:S(2)}, u32[]{:S(2)}) %collective-permute-start.2) | collective-permute-done | bytes 110624 | tf_op jit(solution)/shard_map/ppermute | solution.py:49
  17.6 8.2 %collective-permute-done.1 = bf16[3,96,192]{1,2,0:T(8,128)(2,1)S(1)} collective-permute-done((bf16[3,96,192]{1,2,0:T(8,128)(2,1)S(1)}, bf16[3,96,192]{1,2,0:T(8,128)(2,1)S(1)}, u32[]{:S(2)}, u32[]{:S(2)}) %collective-permute-start.1) | collective-permute-done | bytes 110624 | tf_op jit(solution)/shard_map/ppermute | solution.py:49
  25.9 0.7 gather_fusion
  26.7 0.5 copy.180
  27.2 0.4 reshape.846
  28.3 0.8 pad_maximum_fusion.1
  29.1 0.7 copy.186
  29.8 3.3 %all-to-all-start.1 = ((bf16[8,1,16,384]{3,0,1,2:T(8,128)(2,1)}), bf16[8,1,16,384]{3,0,1,2:T(8,128)(2,1)S(1)}, u32[]{:S(2)}, u32[]{:S(2)}) async-start(bf16[8,1,16,384]{3,0,1,2:T(8,128)(2,1)} %copy.186), calls=%async_computation.1 | async-start | bytes 196608 | tf_op jit(solution)/shard_map/all_to_all | solution.py:106
  33.1 0.6 fusion.322
  33.7 3.7 %all-to-all-done.1 = bf16[8,1,16,384]{3,0,1,2:T(8,128)(2,1)S(1)} async-done(((bf16[8,1,16,384]{3,0,1,2:T(8,128)(2,1)}), bf16[8,1,16,384]{3,0,1,2:T(8,128)(2,1)S(1)}, u32[]{:S(2)}, u32[]{:S(2)}) %all-to-all-start.1) | async-done | bytes 98336 | tf_op jit(solution)/shard_map/all_to_all | solution.py:106
  37.4 5.0 %all-to-all-start = ((bf16[8,1,16,384]{3,2,1,0:T(8,128)(2,1)}), bf16[8,1,16,384]{3,2,1,0:T(8,128)(2,1)S(1)}, u32[]{:S(2)}, u32[]{:S(2)}) async-start(bf16[8,1,16,384]{3,2,1,0:T(8,128)(2,1)} %param.5), calls=%async_computation | async-start | bytes 196608 | tf_op jit(solution)/shard_map/all_to_all | solution.py:98
  42.5 0.7 add.157
  43.2 21.4 %all-gather.2.cloned.1.call-done = bf16[3,512,1152]{1,2,0:T(8,128)(2,1)} async-done(((bf16[3,512,144]{1,2,0:T(8,128)(2,1)}), bf16[3,512,1152]{1,2,0:T(8,128)(2,1)}) %all-gather.2.cloned.1.call-update) | async-done | bytes 3538960 | tf_op jit(solution)/shard_map/all_gather | solution.py:58
  64.6 1.6 %convolution_bitcast_fusion.2 = f32[1,32,4,1152]{3,1,2,0:T(8,128)S(1)} fusion(bf16[3,512,1152]{1,2,0:T(8,128)(2,1)} %all-gather.2.cloned.1.call-done, bf16[8,1,4,4,384]{4,0,3,2,1:T(8,128)(2,1)S(1)} %bitcast.626, f32[4,8,4]{1,2,0:T(4,128)S(1)} %get-tuple-element.17), kind=kOutput, calls=%fused_computation.3 | convolution fusion | flops 113393664 | bytes 1573376 | tf_op jit(solution)/shard_map/jvp()/dot_general | solution.py:30
  66.2 0.4 fusion.101
  66.6 0.4 fusion.102
  67.0 0.6 copy-done.9
  68.3 1.5 %copy.183 = bf16[3,8,128,144]{3,2,1,0:T(8,128)(2,1)} copy(bf16[3,8,128,144]{2,3,1,0:T(8,128)(2,1)S(1)} %bitcast.620) | data formatting | bytes 1769472 | tf_op jit(solution)/shard_map/transpose | solution.py:62
  69.8 4.1 %reshape.849 = bf16[3,8,384,48]{3,2,1,0:T(8,128)(2,1)S(1)} reshape(bf16[3,8,128,144]{3,2,1,0:T(8,128)(2,1)} %copy.183) | data formatting | bytes 1769472 | tf_op jit(solution)/shard_map/reshape | solution.py:63
  74.0 1.5 %fusion.340 = (bf16[1,384,8,48]{3,1,2,0:T(8,128)(2,1)}, bf16[1,384,8,48]{3,1,2,0:T(8,128)(2,1)}, bf16[1,384,8,48]{3,1,2,0:T(8,128)(2,1)}) fusion(bf16[3,384,8,48]{3,1,2,0:T(8,128)(2,1)S(1)} %bitcast.619), kind=kLoop, calls=%fused_computation.414 | loop fusion | bytes 1769472 | tf_op jit(solution)/shard_map/slice | solution.py:64
  75.9 0.7 copy-done.7
  76.6 1.0 fusion.9
  77.6 1.0 copy.184
  79.7 0.7 copy.194
  80.4 4.8 %all-to-all-start.2 = ((bf16[32,1,4,384]{3,2,1,0:T(4,128)(2,1)}), bf16[32,1,4,384]{3,2,1,0:T(4,128)(2,1)S(1)}, u32[]{:S(2)}, u32[]{:S(2)}) async-start(bf16[32,1,4,384]{3,2,1,0:T(4,128)(2,1)} %copy.194), calls=%async_computation.2 | async-start | bytes 196608 | tf_op jit(solution)/shard_map/all_to_all | solution.py:81
  85.2 0.9 fusion.71
  86.1 6.5 %all-to-all-done.2 = bf16[32,1,4,384]{3,2,1,0:T(4,128)(2,1)S(1)} async-done(((bf16[32,1,4,384]{3,2,1,0:T(4,128)(2,1)}), bf16[32,1,4,384]{3,2,1,0:T(4,128)(2,1)S(1)}, u32[]{:S(2)}, u32[]{:S(2)}) %all-to-all-start.2) | async-done | bytes 98336 | tf_op jit(solution)/shard_map/all_to_all | solution.py:81
  92.8 0.6 multiply_add_fusion
  93.6 1.6 %convolution_bitcast_fusion.1 = f32[1,4,32,1152]{3,2,1,0:T(8,128)S(1)} fusion(bf16[4,32,384]{2,1,0:T(8,128)(2,1)S(1)} %convert_element_type.493, bf16[3,512,1152]{1,2,0:T(8,128)(2,1)} %all-gather.2.cloned.1.call-done), kind=kOutput, calls=%fused_computation.2 | convolution fusion | flops 113246208 | bytes 1572864 | tf_op jit(solution)/shard_map/jvp()/dot_general | solution.py:30
  95.1 0.4 fusion.99
  95.5 0.4 fusion.100
  96.8 2.5 %fusion.344 = (f32[32,6,4]{1,2,0:T(4,128)S(1)}, f32[1,32,6,4,4]{2,3,4,1,0:T(4,128)S(1)}) fusion(bf16[4,32,384,1]{2,1,0,3:T(8,128)(2,1)S(1)} %get-tuple-element.10, bf16[4,32,6,384]{3,1,2,0:T(8,128)(2,1)S(1)} %broadcast_multiply_fusion), kind=kOutput, calls=%fused_computation.418 | convolution fusion | flops 2364672 | bytes 703488 | tf_op jit(solution)/shard_map/jvp(plqd,pkqhd->pqhlk)/dot_general | solution.py:35
  99.4 0.8 fusion
  100.6 0.4 convolution_bitcast_fusion
  101.0 0.4 fusion.97
  101.4 0.4 fusion.98
  101.8 0.3 fusion.255
  103.1 0.7 fusion.146
  104.5 0.4 fusion.95
  105.2 0.4 fusion.96
  105.6 0.3 add_add_fusion.8
  106.0 0.4 multiply_reduce_fusion.1
  106.9 0.4 fusion.53
  107.3 2.4 %fusion.1 = bf16[32,6,4,4]{1,3,2,0:T(4,128)(2,1)S(1)} fusion(f32[4,32,384]{2,0,1:T(4,128)S(1)} %copy.207, f32[6,384]{1,0:T(8,128)S(1)} %get-tuple-element.22, bf16[4,32,384,1]{2,1,0,3:T(8,128)(2,1)S(1)} %copy-done.16), kind=kOutput, calls=%fused_computation.6 | convolution fusion | flops 2654208 | bytes 310272 | tf_op jit(solution)/shard_map/transpose(jvp(pqhlk,pkqd->plqhd))/dot_general | solution.py:38
  109.8 0.6 convolution_bitcast_fusion.8
  110.5 0.8 fusion.13
  111.3 0.4 fusion.94
  112.1 0.4 fusion.93
  112.8 1.6 %multiply_reduce_fusion = (f32[4,32]{1,0:T(4,128)S(1)}, f32[4,32,384]{2,1,0:T(8,128)S(1)}) fusion(f32[4,32,384]{2,1,0:T(8,128)S(1)} %reshape.886, bf16[3,512,1152]{1,2,0:T(8,128)(2,1)} %all-gather.2.cloned.1.call-done, f32[1,4,32,384]{3,2,1,0:T(8,128)S(1)} %add_add_fusion.4, f32[1,4,32,384]{3,2,1,0:T(8,128)S(1)} %add_add_fusion.5, ...), kind=kOutput, calls=%fused_computation.268 | convolution fusion | flops 113885056 | bytes 1769984 | tf_op jit(solution)/shard_map/transpose(jvp())/dot_general | solution.py:30
  114.6 0.7 copy.216
  115.3 2.8 %all-to-all-start.3 = ((bf16[32,1,4,384]{3,2,1,0:T(4,128)(2,1)}), bf16[32,1,4,384]{3,2,1,0:T(4,128)(2,1)S(1)}, u32[]{:S(2)}, u32[]{:S(2)}) async-start(bf16[32,1,4,384]{3,2,1,0:T(4,128)(2,1)} %bitcast.137), calls=%async_computation.3 | async-start | bytes 196608 | tf_op jit(solution)/shard_map/all_to_all | solution.py:92
  118.1 7.3 %all-to-all-done.3 = bf16[32,1,4,384]{3,2,1,0:T(4,128)(2,1)S(1)} async-done(((bf16[32,1,4,384]{3,2,1,0:T(4,128)(2,1)}), bf16[32,1,4,384]{3,2,1,0:T(4,128)(2,1)S(1)}, u32[]{:S(2)}, u32[]{:S(2)}) %all-to-all-start.3) | async-done | bytes 98336 | tf_op jit(solution)/shard_map/all_to_all | solution.py:92
  126.0 0.7 fusion.142
  127.5 0.4 fusion.91
  127.9 0.3 add_add_fusion.1
  128.2 0.4 fusion.92
  128.6 0.3 add_add_fusion.2
  129.1 0.4 fusion.202
  129.7 6.7 %all_to_all.42 = bf16[32,1,4,384]{3,2,1,0:T(4,128)(2,1)S(1)} all-to-all(bf16[32,1,4,384]{3,2,1,0:T(4,128)(2,1)S(1)} %copy.221), channel_id=1, replica_groups=mesh['gz'=4,'gy'=4,'gx'=2] {'gz'}, dimensions={0} | all-to-all | bytes 196608 | tf_op jit(solution)/shard_map/all_to_all | solution.py:115
  136.4 0.7 all_to_all.36
  (130 shorter events, 9.9 us)
Async XLA Ops:
  6.5 58.1 %all-gather.2.cloned.1.call-start = ((), (), s32[]{:S(2)}) async-start(), calls=%async_computation.5 | async-start | bytes 3981312 | tf_op jit(solution)/shard_map/all_gather | solution.py:58
  8.2 9.4 %collective-permute-start.2 = (bf16[3,96,192]{1,2,0:T(8,128)(2,1)S(1)}, bf16[3,96,192]{1,2,0:T(8,128)(2,1)S(1)}, u32[]{:S(2)}, u32[]{:S(2)}) collective-permute-start(bf16[3,96,192]{1,2,0:T(8,128)(2,1)S(1)} %constant_dynamic-update-slice_fusion), channel_id=1, source_target_pairs={{0,6},{2,0},{4,2},{6,4},{1,7},{3,1},{5,3},{7,5},{8,14},{10,8},{12,... | collective-permute-start | bytes 331784 | tf_op jit(solution)/shard_map/ppermute | solution.py:49
  13.3 12.5 %collective-permute-start.1 = (bf16[3,96,192]{1,2,0:T(8,128)(2,1)S(1)}, bf16[3,96,192]{1,2,0:T(8,128)(2,1)S(1)}, u32[]{:S(2)}, u32[]{:S(2)}) collective-permute-start(bf16[3,96,192]{1,2,0:T(8,128)(2,1)S(1)} %constant_dynamic-update-slice_fusion), channel_id=1, source_target_pairs={{0,4},{2,6},{4,0},{6,2},{1,5},{3,7},{5,1},{7,3},{8,12},{10,14},{12... | collective-permute-start | bytes 331784 | tf_op jit(solution)/shard_map/ppermute | solution.py:49
  13.3 12.5 %collective-permute-start = (bf16[3,96,192]{1,2,0:T(8,128)(2,1)S(1)}, bf16[3,96,192]{1,2,0:T(8,128)(2,1)S(1)}, u32[]{:S(2)}, u32[]{:S(2)}) collective-permute-start(bf16[3,96,192]{1,2,0:T(8,128)(2,1)S(1)} %constant_dynamic-update-slice_fusion), channel_id=1, source_target_pairs={{0,2},{2,4},{4,6},{6,0},{1,3},{3,5},{5,7},{7,1},{8,10},{10,12},{12... | collective-permute-start | bytes 331784 | tf_op jit(solution)/shard_map/ppermute | solution.py:49
  27.6 1.5 %copy-start.14 = (bf16[8,1,16,384]{3,2,1,0:T(8,128)(2,1)S(1)}, bf16[8,1,16,384]{3,2,1,0:T(8,128)(2,1)}, u32[]{:S(2)}) copy-start(bf16[8,1,16,384]{3,2,1,0:T(8,128)(2,1)} %param.4) | copy-start | bytes 294916
  29.8 7.6 %all-to-all-start.1 = ((bf16[8,1,16,384]{3,0,1,2:T(8,128)(2,1)}), bf16[8,1,16,384]{3,0,1,2:T(8,128)(2,1)S(1)}, u32[]{:S(2)}, u32[]{:S(2)}) async-start(bf16[8,1,16,384]{3,0,1,2:T(8,128)(2,1)} %copy.186), calls=%async_computation.1 | async-start | bytes 196608 | tf_op jit(solution)/shard_map/all_to_all | solution.py:106
  37.4 43.1 %all-to-all-start = ((bf16[8,1,16,384]{3,2,1,0:T(8,128)(2,1)}), bf16[8,1,16,384]{3,2,1,0:T(8,128)(2,1)S(1)}, u32[]{:S(2)}, u32[]{:S(2)}) async-start(bf16[8,1,16,384]{3,2,1,0:T(8,128)(2,1)} %param.5), calls=%async_computation | async-start | bytes 196608 | tf_op jit(solution)/shard_map/all_to_all | solution.py:98
  66.2 2.1 %slice-start = ((bf16[3,512,1152]{1,2,0:T(8,128)(2,1)}), bf16[3,128,1152]{1,2,0:T(8,128)(2,1)S(1)}, s32[]{:S(2)}) async-start(bf16[3,512,1152]{1,2,0:T(8,128)(2,1)} %all-gather.2.cloned.1.call-done), calls=%async_computation.6 | async-start | bytes 1769472 | tf_op jit(solution)/shard_map/slice | solution.py:62
  66.6 1.7 %copy-start.11 = (f32[32,4,6]{0,2,1:T(8,128)}, f32[32,4,6]{0,2,1:T(8,128)S(1)}, u32[]{:S(2)}) copy-start(f32[32,4,6]{0,2,1:T(8,128)S(1)} %fusion.101) | copy-start | bytes 9220
  67.0 0.6 copy-start.9
  74.0 1.5 %copy-start.22 = (bf16[6,384]{1,0:T(8,128)(2,1)S(1)}, bf16[6,384]{1,0:T(8,128)(2,1)}, u32[]{:S(2)}) copy-start(bf16[6,384]{1,0:T(8,128)(2,1)} %get-tuple-element.23) | copy-start | bytes 13828
  75.5 2.1 %copy-start.17 = (bf16[32,4,384]{2,0,1:T(8,128)(2,1)}, bf16[32,4,384]{2,0,1:T(8,128)(2,1)S(1)}, u32[]{:S(2)}) copy-start(bf16[32,4,384]{2,0,1:T(8,128)(2,1)S(1)} %get-tuple-element.13) | copy-start | bytes 294916
  75.5 2.1 %copy-start.19 = (bf16[32,4,384,1]{2,0,3,1:T(8,128)(2,1)}, bf16[32,4,384,1]{2,0,3,1:T(8,128)(2,1)S(1)}, u32[]{:S(2)}) copy-start(bf16[32,4,384,1]{2,0,3,1:T(8,128)(2,1)S(1)} %get-tuple-element.12) | copy-start | bytes 294916
  75.5 2.1 %copy-start.4 = (bf16[1,384,8,48]{3,1,2,0:T(8,128)(2,1)S(1)}, bf16[1,384,8,48]{3,1,2,0:T(8,128)(2,1)}, u32[]{:S(2)}) copy-start(bf16[1,384,8,48]{3,1,2,0:T(8,128)(2,1)} %get-tuple-element.5) | copy-start | bytes 884740
  75.8 0.8 copy-start.7
  75.8 1.8 %copy-start.26 = (f32[4,6,32]{2,1,0:T(8,128)}, f32[4,6,32]{2,1,0:T(8,128)S(1)}, u32[]{:S(2)}) copy-start(f32[4,6,32]{2,1,0:T(8,128)S(1)} %get-tuple-element.24) | copy-start | bytes 9220
  75.9 2.7 %copy-start.3 = (bf16[1,384,8,48]{3,1,2,0:T(8,128)(2,1)S(1)}, bf16[1,384,8,48]{3,1,2,0:T(8,128)(2,1)}, u32[]{:S(2)}) copy-start(bf16[1,384,8,48]{3,1,2,0:T(8,128)(2,1)} %get-tuple-element.6) | copy-start | bytes 884740
  76.6 2.3 %copy-start.2 = (bf16[1,384,8,48]{3,1,2,0:T(8,128)(2,1)S(1)}, bf16[1,384,8,48]{3,1,2,0:T(8,128)(2,1)}, u32[]{:S(2)}) copy-start(bf16[1,384,8,48]{3,1,2,0:T(8,128)(2,1)} %get-tuple-element.7) | copy-start | bytes 884740
  78.6 0.9 copy-start.13
  78.6 6.6 %copy-start.5 = (bf16[1,384,8,48]{1,3,2,0:T(8,128)(2,1)S(1)}, bf16[1,384,8,48]{1,3,2,0:T(8,128)(2,1)}, u32[]{:S(2)}) copy-start(bf16[1,384,8,48]{1,3,2,0:T(8,128)(2,1)} %copy.184) | copy-start | bytes 884740
  80.4 12.2 %all-to-all-start.2 = ((bf16[32,1,4,384]{3,2,1,0:T(4,128)(2,1)}), bf16[32,1,4,384]{3,2,1,0:T(4,128)(2,1)S(1)}, u32[]{:S(2)}, u32[]{:S(2)}) async-start(bf16[32,1,4,384]{3,2,1,0:T(4,128)(2,1)} %copy.194), calls=%async_computation.2 | async-start | bytes 196608 | tf_op jit(solution)/shard_map/all_to_all | solution.py:81
  95.1 1.6 %copy-start.23 = (bf16[6,384]{1,0:T(8,128)(2,1)S(1)}, bf16[6,384]{1,0:T(8,128)(2,1)}, u32[]{:S(2)}) copy-start(bf16[6,384]{1,0:T(8,128)(2,1)} %get-tuple-element.23) | copy-start | bytes 13828
  95.9 3.5 %copy-start.15 = (bf16[4,32,384,1]{2,1,0,3:T(8,128)(2,1)}, bf16[4,32,384,1]{2,1,0,3:T(8,128)(2,1)S(1)}, u32[]{:S(2)}) copy-start(bf16[4,32,384,1]{2,1,0,3:T(8,128)(2,1)S(1)} %fusion.234) | copy-start | bytes 294916
  96.8 3.7 %copy-start = (bf16[3,512,1152]{1,2,0:T(8,128)(2,1)S(1)}, bf16[3,512,1152]{1,2,0:T(8,128)(2,1)}, u32[]{:S(2)}) copy-start(bf16[3,512,1152]{1,2,0:T(8,128)(2,1)} %all-gather.2.cloned.1.call-done) | copy-start | bytes 10616836
  100.6 1.9 %copy-start.24 = (bf16[6,384]{1,0:T(8,128)(2,1)S(1)}, bf16[6,384]{1,0:T(8,128)(2,1)}, u32[]{:S(2)}) copy-start(bf16[6,384]{1,0:T(8,128)(2,1)} %get-tuple-element.23) | copy-start | bytes 13828
  101.0 1.9 %copy-start.6 = (f32[4,32,384]{2,1,0:T(8,128)S(1)}, f32[4,32,384]{2,1,0:T(8,128)}, u32[]{:S(2)}) copy-start(f32[4,32,384]{2,1,0:T(8,128)} %fusion.71) | copy-start | bytes 589828
  106.4 0.9 copy-start.16
  110.5 0.8 copy-start.21
  112.8 5.3 %copy-start.27 = (f32[4,6,32]{2,1,0:T(8,128)S(1)}, f32[4,6,32]{2,1,0:T(8,128)}, u32[]{:S(2)}) copy-start(f32[4,6,32]{2,1,0:T(8,128)} %copy-done.26) | copy-start | bytes 9220
  112.8 12.9 %copy-start.8 = (f32[1,4,6,32,32]{3,4,2,1,0:T(8,128)S(1)}, f32[1,4,6,32,32]{3,4,2,1,0:T(8,128)}, u32[]{:S(2)}) copy-start(f32[1,4,6,32,32]{3,4,2,1,0:T(8,128)} %copy-done.7) | copy-start | bytes 294916
  115.3 10.2 %all-to-all-start.3 = ((bf16[32,1,4,384]{3,2,1,0:T(4,128)(2,1)}), bf16[32,1,4,384]{3,2,1,0:T(4,128)(2,1)S(1)}, u32[]{:S(2)}, u32[]{:S(2)}) async-start(bf16[32,1,4,384]{3,2,1,0:T(4,128)(2,1)} %bitcast.137), calls=%async_computation.3 | async-start | bytes 196608 | tf_op jit(solution)/shard_map/all_to_all | solution.py:92
  125.7 1.1 copy-start.20
  125.7 1.1 copy-start.25
  126.0 1.1 copy-start.18
  126.8 0.7 copy-start.12
  126.8 1.4 %copy-start.10 = (f32[32,4,6]{0,2,1:T(8,128)S(1)}, f32[32,4,6]{0,2,1:T(8,128)}, u32[]{:S(2)}) copy-start(f32[32,4,6]{0,2,1:T(8,128)} %copy-done.9) | copy-start | bytes 9220
  127.1 2.0 %copy-start.1 = (bf16[3,512,1152]{1,2,0:T(8,128)(2,1)S(1)}, bf16[3,512,1152]{1,2,0:T(8,128)(2,1)}, u32[]{:S(2)}) copy-start(bf16[3,512,1152]{1,2,0:T(8,128)(2,1)} %all-gather.2.cloned.1.call-done) | copy-start | bytes 10616836
  128.2 1.3 copy-start.28
Sparse Core Ops, SparseCore 0:
  29.3 35.3 all-gather.1

commit v11 on v9

--- a/solution.py
+++ b/solution.py
@@ -51,9 +51,18 @@
     source = (lax.axis_index("gy") - jnp.arange(ny)) % ny
     rows = jnp.take(jnp.stack(shifted), source, axis=0)
     rows = jnp.swapaxes(rows, 0, 1).reshape(subs, ny * din, cat.shape[2])
-    proj = lax.all_gather(rows[:, :, :dproj], ("gz", "gx"), axis=2, tiled=True)
-    outp = lax.all_gather(rows[:, :, dproj:], ("gz", "gx"), axis=2, tiled=True)
-    return [(proj[i], outp[i]) for i in range(subs)]
+    feat = rows.shape[1]
+    blocks = sizes[0] * sizes[2]
+    dout = w_output.shape[2]
+    weights = []
+    for part in (rows[:1], rows[1:]):
+        count = part.shape[0]
+        stacked = jnp.concatenate([part[:, :, :dproj], part[:, :, dproj:].reshape(count, -1, dproj)], axis=1)
+        got = lax.all_gather(stacked, ("gz", "gx"), axis=2, tiled=True)
+        outp = got[:, feat:].reshape(count, -1, blocks, dproj).swapaxes(1, 2)
+        outp = outp.reshape(count, blocks, feat, dout).swapaxes(1, 2).reshape(count, feat, blocks * dout)
+        weights += [(got[i, :feat], outp[i]) for i in range(count)]
+    return weights
 
 
 def depth_fn(member, w_inner, w_outer):

time: 141 us -> 173 us (1.23)
  local copies, waits for them, and re-layouts: 12 us -> 41 us
  waiting for transfers between devices: 27.1 us -> 51.7 us
  blocking collectives: 28.4 us -> 6.67 us
    all_gather x1 -> x0, blocking collectives: 21.7 us -> none  [full_weights(): outp = lax.all_gather(rows[:, :, dproj:], ('gz', 'gx'), axis=2, tiled=True)]
    all_gather x1 -> x2, waiting for transfers between devices: 0.01 us -> 20.9 us  [full_weights(): got = lax.all_gather(stacked, ('gz', 'gx'), axis=2, tiled=True)]
    unnamed x46 -> x155, local copies, waits for them, and re-layouts: 2.84 us -> 16 us
    slice x2 -> x19, local copies, waits for them, and re-layouts: 0.78 us -> 13.2 us  [the longest x4 10.3 us: full_weights(): weights += [(got[i, :feat], outp[i]) for i in range(count)]]
    dot_general x6, matrix products: 7.26 us -> 2.51 us  [sublayer(): packed = jnp.dot(normed, w_inner, preferred_element_type=jnp.float32)]
    reshape x1 -> x6, local copies, waits for them, and re-layouts: 0.39 us -> 4.06 us  [the longest x2 3.57 us: full_weights(): outp.reshape(count, blocks, feat, dout).swapaxes(1, 2)]
    ppermute x3, waiting for transfers between devices: 8.3 us -> 11.4 us  [full_weights(): lax.ppermute(cat, 'gy', [(i, (i + s) % ny) for i in range(ny)])]
    all_to_all x1, starting transfers between devices: 6.93 us -> 4 us  [block_to_plane(): got = lax.all_to_all(block, ('gy', 'gx'), 0, 0, tiled=True)]
  transfers between devices with their start and end apart: 8 -> 9, of which waited for: 5 -> 7; matrix products, arithmetic and copies ran while one was open for 5% -> 27% of each run, Pallas kernels for 0% -> 0%
where the time goes in v11:
time: 173 us; the launch traced here: 172 us
  waiting for transfers between devices  51.7 us (30%)
  local copies, waits for them, and re-layouts  41 us (24%)
  matrix products  29.2 us (17%)
  starting transfers between devices  22.9 us (13%)
  between operations  14.8 us (9%)
  blocking collectives  6.67 us (4%)
  other arithmetic  5.52 us (3%)
    all_gather x2, waiting for transfers between devices, full_weights(): got = lax.all_gather(stacked, ('gz', 'gx'), axis=2, tiled=True)  20.9 us
    unnamed x155, local copies, waits for them, and re-layouts  16 us
    ppermute x3, waiting for transfers between devices, full_weights(): lax.ppermute(cat, 'gy', [(i, (i + s) % ny) for i in range(ny)])  11.4 us
    slice x4, local copies, waits for them, and re-layouts, full_weights(): weights += [(got[i, :feat], outp[i]) for i in range(count)]  10.3 us
    all_to_all x1, waiting for transfers between devices, from_planes(): return lax.all_to_all(parts, ALL, 0, 0, tiled=True)  7.34 us
    dot_general x8, matrix products, sublayer(): jnp.einsum('pqhlk,pkqd->plqhd', attn_weights, value_part, preferred_eleme...  6.98 us
    all_to_all x1, waiting for transfers between devices, to_planes(): got = lax.all_to_all(depth_lines, ALL, 0, 0, tiled=True)  6.93 us
    all_to_all x1, blocking collectives, local(): return lax.all_to_all(grad_zero, 'gz', 0, 2, tiled=True)  6.67 us
  transfers between devices with their start and end apart: 9, of which 7 were waited for; matrix products, arithmetic and copies ran while one was open for 27% of the time, Pallas kernels for 0%

profile of v11, /device:TPU:0, one launch (start us, length us, event | category | flops | bytes accessed | tf_op | source)
XLA Modules:
  0.0 171.8 jit_solution(6642469449570951718)
XLA Ops:
  6.5 0.9 constant_dynamic-update-slice_fusion.1
  7.4 0.8 constant_dynamic-update-slice_fusion
  8.2 5.1 %collective-permute-start.2 = (bf16[3,96,192]{1,2,0:T(8,128)(2,1)S(1)}, bf16[3,96,192]{1,2,0:T(8,128)(2,1)S(1)}, u32[]{:S(2)}, u32[]{:S(2)}) collective-permute-start(bf16[3,96,192]{1,2,0:T(8,128)(2,1)S(1)} %constant_dynamic-update-slice_fusion), channel_id=1, source_target_pairs={{0,6},{2,0},{4,2},{6,4},{1,7},{3,1},{5,3},{7,5},{8,14},{10,8},{12,... | collective-permute-start | bytes 331784 | tf_op jit(solution)/shard_map/ppermute | solution.py:49
  13.3 1.0 collective-permute-start
  14.4 3.2 %collective-permute-done.2 = bf16[3,96,192]{1,2,0:T(8,128)(2,1)S(1)} collective-permute-done((bf16[3,96,192]{1,2,0:T(8,128)(2,1)S(1)}, bf16[3,96,192]{1,2,0:T(8,128)(2,1)S(1)}, u32[]{:S(2)}, u32[]{:S(2)}) %collective-permute-start.2) | collective-permute-done | bytes 110624 | tf_op jit(solution)/shard_map/ppermute | solution.py:49
  17.6 8.2 %collective-permute-done.1 = bf16[3,96,192]{1,2,0:T(8,128)(2,1)S(1)} collective-permute-done((bf16[3,96,192]{1,2,0:T(8,128)(2,1)S(1)}, bf16[3,96,192]{1,2,0:T(8,128)(2,1)S(1)}, u32[]{:S(2)}, u32[]{:S(2)}) %collective-permute-start.1) | collective-permute-done | bytes 110624 | tf_op jit(solution)/shard_map/ppermute | solution.py:49
  25.9 0.7 gather_fusion
  27.5 0.7 pad_maximum_fusion.2
  28.6 0.7 slice.78
  30.0 1.0 pad_maximum_fusion.1
  31.1 0.7 copy.206
  31.7 3.3 %all-to-all-start.1 = ((bf16[8,1,16,384]{3,0,1,2:T(8,128)(2,1)}), bf16[8,1,16,384]{3,0,1,2:T(8,128)(2,1)S(1)}, u32[]{:S(2)}, u32[]{:S(2)}) async-start(bf16[8,1,16,384]{3,0,1,2:T(8,128)(2,1)} %copy.206), calls=%async_computation.1 | async-start | bytes 196608 | tf_op jit(solution)/shard_map/all_to_all | solution.py:107
  35.1 5.1 %all-to-all-done.1 = bf16[8,1,16,384]{3,0,1,2:T(8,128)(2,1)S(1)} async-done(((bf16[8,1,16,384]{3,0,1,2:T(8,128)(2,1)}), bf16[8,1,16,384]{3,0,1,2:T(8,128)(2,1)S(1)}, u32[]{:S(2)}, u32[]{:S(2)}) %all-to-all-start.1) | async-done | bytes 98336 | tf_op jit(solution)/shard_map/all_to_all | solution.py:107
  40.3 12.4 %all-gather.5.cloned.1.call-done = bf16[1,512,1152]{1,2,0:T(8,128)(2,1)} async-done(((bf16[1,512,144]{1,2,0:T(8,128)(2,1)}), bf16[1,512,1152]{1,2,0:T(8,128)(2,1)}) %all-gather.5.cloned.1.call-update) | async-done | bytes 1179664 | tf_op jit(solution)/shard_map/all_gather | solution.py:61
  52.7 1.0 slice.115
  53.9 0.9 reshape.864
  56.7 0.6 copy-done.34
  59.1 0.7 copy.218
  59.8 4.6 %all-to-all-start.2 = ((bf16[32,1,4,384]{3,2,1,0:T(4,128)(2,1)}), bf16[32,1,4,384]{3,2,1,0:T(4,128)(2,1)S(1)}, u32[]{:S(2)}, u32[]{:S(2)}) async-start(bf16[32,1,4,384]{3,2,1,0:T(4,128)(2,1)} %copy.218), calls=%async_computation.2 | async-start | bytes 196608 | tf_op jit(solution)/shard_map/all_to_all | solution.py:82
  64.4 0.6 add.157
  65.1 6.9 %all-to-all-done.2 = bf16[32,1,4,384]{3,2,1,0:T(4,128)(2,1)S(1)} async-done(((bf16[32,1,4,384]{3,2,1,0:T(4,128)(2,1)}), bf16[32,1,4,384]{3,2,1,0:T(4,128)(2,1)S(1)}, u32[]{:S(2)}, u32[]{:S(2)}) %all-to-all-start.2) | async-done | bytes 98336 | tf_op jit(solution)/shard_map/all_to_all | solution.py:82
  72.0 4.0 %all-to-all-start = ((bf16[8,1,16,384]{3,2,1,0:T(8,128)(2,1)}), bf16[8,1,16,384]{3,2,1,0:T(8,128)(2,1)}, u32[]{:S(2)}, u32[]{:S(2)}) async-start(bf16[8,1,16,384]{3,2,1,0:T(8,128)(2,1)} %param.5), calls=%async_computation | async-start | bytes 196608 | tf_op jit(solution)/shard_map/all_to_all | solution.py:99
  76.2 0.7 add.156
  77.1 8.5 %all-gather.3.cloned.1.call-done = bf16[2,512,1152]{1,0,2:T(2,128)(2,1)} async-done(((bf16[2,512,144]{1,0,2:T(2,128)(2,1)}), bf16[2,512,1152]{1,0,2:T(2,128)(2,1)}) %all-gather.3.cloned.1.call-update) | async-done | bytes 2359312 | tf_op jit(solution)/shard_map/all_gather | solution.py:61
  85.6 5.5 %fusion.344 = (bf16[1,384,1152]{1,0,2:T(2,128)(2,1)}, bf16[1,384,1152]{1,0,2:T(2,128)(2,1)S(1)}) fusion(bf16[2,512,1152]{1,0,2:T(2,128)(2,1)} %all-gather.3.cloned.1.call-done), kind=kLoop, calls=%fused_computation.417 | loop fusion | bytes 3538944 | tf_op jit(solution)/shard_map/slice | solution.py:64
  91.1 2.8 %copy.284 = bf16[1,384,1152]{2,1,0:T(8,128)(2,1)S(1)} copy(bf16[1,384,1152]{1,0,2:T(2,128)(2,1)S(1)} %get-tuple-element.6) | data formatting | bytes 1769472
  95.1 0.7 fusion.238
  95.7 0.9 copy.282
  96.6 1.4 copy.203
  98.0 2.7 %reshape.855 = bf16[2,8,384,48]{3,2,1,0:T(8,128)(2,1)} reshape(bf16[2,8,128,144]{3,2,1,0:T(8,128)(2,1)S(1)} %copy.203) | data formatting | bytes 1179648 | tf_op jit(solution)/shard_map/reshape | solution.py:63
  100.7 2.4 %fusion.345 = (bf16[1,384,8,48]{3,1,2,0:T(8,128)(2,1)}, bf16[1,384,8,48]{3,1,2,0:T(8,128)(2,1)S(1)}) fusion(bf16[2,384,8,48]{3,1,2,0:T(8,128)(2,1)} %bitcast.625), kind=kLoop, calls=%fused_computation.418 | loop fusion | bytes 1179648 | tf_op jit(solution)/shard_map/slice | solution.py:64
  103.4 4.1 %copy.285 = bf16[1,384,1152]{2,1,0:T(8,128)(2,1)S(1)} copy(bf16[1,384,1152]{1,0,2:T(2,128)(2,1)} %get-tuple-element.5) | data formatting | bytes 1769472
  108.2 0.7 copy-done.14
  109.1 0.8 copy-done.26
  109.9 2.5 %fusion.349 = (f32[32,6,4]{1,2,0:T(4,128)S(1)}, f32[1,32,6,4,4]{2,3,4,1,0:T(4,128)S(1)}) fusion(bf16[4,32,384,1]{2,1,0,3:T(8,128)(2,1)S(1)} %get-tuple-element.11, bf16[4,32,6,384]{3,1,2,0:T(8,128)(2,1)S(1)} %broadcast_multiply_fusion), kind=kOutput, calls=%fused_computation.422 | convolution fusion | flops 2364672 | bytes 703488 | tf_op jit(solution)/shard_map/jvp(plqd,pkqhd->pqhlk)/dot_general | solution.py:35
  112.4 0.7 multiply_divide_fusion
  113.2 0.8 fusion
  114.4 0.5 copy-done.67
  115.4 1.0 fusion.97
  116.4 1.0 fusion.98
  117.4 2.1 %copy.204 = bf16[1,384,8,48]{1,3,2,0:T(8,128)(2,1)} copy(bf16[1,384,8,48]{3,1,2,0:T(8,128)(2,1)} %get-tuple-element.7) | data formatting | bytes 589824 | tf_op jit(solution)/shard_map/slice | solution.py:64
  119.5 1.1 fusion.259
  120.5 1.1 fusion.257
  121.7 1.1 fusion.350
  122.8 0.6 copy-done.71
  123.4 0.6 multiply_divide_fusion.2
  124.0 1.2 fusion.71
  125.3 1.3 fusion.84
  126.7 0.7 fusion.150
  127.7 0.5 copy-done.56
  128.6 0.4 copy-done.43
  130.5 0.5 multiply_reduce_fusion.1
  131.0 1.0 fusion.184
  133.0 2.4 %fusion.1 = bf16[32,6,4,4]{1,3,2,0:T(4,128)(2,1)S(1)} fusion(f32[4,32,384]{2,0,1:T(4,128)S(1)} %copy.231, f32[6,384]{1,0:T(8,128)S(1)} %get-tuple-element.23, bf16[4,32,384,1]{2,1,0,3:T(8,128)(2,1)S(1)} %copy-done.48), kind=kOutput, calls=%fused_computation.6 | convolution fusion | flops 2654208 | bytes 310272 | tf_op jit(solution)/shard_map/transpose(jvp(pqhlk,pkqd->plqhd))/dot_general | solution.py:38
  135.6 0.6 convolution_bitcast_fusion.8
  136.5 0.8 fusion.13
  138.8 0.5 multiply_reduce_fusion
  139.4 0.7 copy.240
  140.1 4.8 %all-to-all-start.3 = ((bf16[32,1,4,384]{3,2,1,0:T(4,128)(2,1)}), bf16[32,1,4,384]{3,2,1,0:T(4,128)(2,1)S(1)}, u32[]{:S(2)}, u32[]{:S(2)}) async-start(bf16[32,1,4,384]{3,2,1,0:T(4,128)(2,1)} %bitcast.140), calls=%async_computation.3 | async-start | bytes 196608 | tf_op jit(solution)/shard_map/all_to_all | solution.py:93
  145.0 7.3 %all-to-all-done.3 = bf16[32,1,4,384]{3,2,1,0:T(4,128)(2,1)S(1)} async-done(((bf16[32,1,4,384]{3,2,1,0:T(4,128)(2,1)}), bf16[32,1,4,384]{3,2,1,0:T(4,128)(2,1)S(1)}, u32[]{:S(2)}, u32[]{:S(2)}) %all-to-all-start.3) | async-done | bytes 98336 | tf_op jit(solution)/shard_map/all_to_all | solution.py:93
  152.9 0.7 fusion.146
  153.9 0.5 copy-done.50
  157.5 6.7 %all_to_all.42 = bf16[32,1,4,384]{3,2,1,0:T(4,128)(2,1)S(1)} all-to-all(bf16[32,1,4,384]{3,2,1,0:T(4,128)(2,1)S(1)} %copy.245), channel_id=1, replica_groups=mesh['gz'=4,'gy'=4,'gx'=2] {'gz'}, dimensions={0} | all-to-all | bytes 196608 | tf_op jit(solution)/shard_map/all_to_all | solution.py:116
  164.3 0.7 all_to_all.36
  (242 shorter events, 18.3 us)
Async XLA Ops:
  6.5 46.2 %all-gather.5.cloned.1.call-start = ((), (), s32[]{:S(2)}) async-start(), calls=%async_computation.6 | async-start | bytes 1327104 | tf_op jit(solution)/shard_map/all_gather | solution.py:61
  8.2 9.4 %collective-permute-start.2 = (bf16[3,96,192]{1,2,0:T(8,128)(2,1)S(1)}, bf16[3,96,192]{1,2,0:T(8,128)(2,1)S(1)}, u32[]{:S(2)}, u32[]{:S(2)}) collective-permute-start(bf16[3,96,192]{1,2,0:T(8,128)(2,1)S(1)} %constant_dynamic-update-slice_fusion), channel_id=1, source_target_pairs={{0,6},{2,0},{4,2},{6,4},{1,7},{3,1},{5,3},{7,5},{8,14},{10,8},{12,... | collective-permute-start | bytes 331784 | tf_op jit(solution)/shard_map/ppermute | solution.py:49
  13.3 12.5 %collective-permute-start.1 = (bf16[3,96,192]{1,2,0:T(8,128)(2,1)S(1)}, bf16[3,96,192]{1,2,0:T(8,128)(2,1)S(1)}, u32[]{:S(2)}, u32[]{:S(2)}) collective-permute-start(bf16[3,96,192]{1,2,0:T(8,128)(2,1)S(1)} %constant_dynamic-update-slice_fusion), channel_id=1, source_target_pairs={{0,4},{2,6},{4,0},{6,2},{1,5},{3,7},{5,1},{7,3},{8,12},{10,14},{12... | collective-permute-start | bytes 331784 | tf_op jit(solution)/shard_map/ppermute | solution.py:49
  13.3 12.5 %collective-permute-start = (bf16[3,96,192]{1,2,0:T(8,128)(2,1)S(1)}, bf16[3,96,192]{1,2,0:T(8,128)(2,1)S(1)}, u32[]{:S(2)}, u32[]{:S(2)}) collective-permute-start(bf16[3,96,192]{1,2,0:T(8,128)(2,1)S(1)} %constant_dynamic-update-slice_fusion), channel_id=1, source_target_pairs={{0,2},{2,4},{4,6},{6,0},{1,3},{3,5},{5,7},{7,1},{8,10},{10,12},{12... | collective-permute-start | bytes 331784 | tf_op jit(solution)/shard_map/ppermute | solution.py:49
  28.2 57.4 %all-gather.3.cloned.1.call-start = ((), (), s32[]{:S(2)}) async-start(), calls=%async_computation.5 | async-start | bytes 2654208 | tf_op jit(solution)/shard_map/all_gather | solution.py:61
  29.3 1.7 %copy-start.46 = (bf16[8,1,16,384]{3,2,1,0:T(8,128)(2,1)S(1)}, bf16[8,1,16,384]{3,2,1,0:T(8,128)(2,1)}, u32[]{:S(2)}) copy-start(bf16[8,1,16,384]{3,2,1,0:T(8,128)(2,1)} %param.4) | copy-start | bytes 294916
  31.7 8.5 %all-to-all-start.1 = ((bf16[8,1,16,384]{3,0,1,2:T(8,128)(2,1)}), bf16[8,1,16,384]{3,0,1,2:T(8,128)(2,1)S(1)}, u32[]{:S(2)}, u32[]{:S(2)}) async-start(bf16[8,1,16,384]{3,0,1,2:T(8,128)(2,1)} %copy.206), calls=%async_computation.1 | async-start | bytes 196608 | tf_op jit(solution)/shard_map/all_to_all | solution.py:107
  35.1 22.7 %copy-start.60 = (bf16[6,384]{1,0:T(8,128)(2,1)}, bf16[6,384]{1,0:T(8,128)(2,1)S(1)}, u32[]{:S(2)}) copy-start(bf16[6,384]{1,0:T(8,128)(2,1)S(1)} %get-tuple-element.24) | copy-start | bytes 13828
  40.2 18.7 %copy-start.8 = (bf16[8,1,16,384]{3,0,1,2:T(8,128)(2,1)}, bf16[8,1,16,384]{3,0,1,2:T(8,128)(2,1)S(1)}, u32[]{:S(2)}) copy-start(bf16[8,1,16,384]{3,0,1,2:T(8,128)(2,1)S(1)} %all-to-all-done.1) | copy-start | bytes 294916
  53.9 1.3 copy-start.22
  55.1 3.8 %copy-start.6 = (bf16[1,384,8,48]{1,3,2,0:T(8,128)(2,1)}, bf16[1,384,8,48]{1,3,2,0:T(8,128)(2,1)S(1)}, u32[]{:S(2)}) copy-start(bf16[1,384,8,48]{1,3,2,0:T(8,128)(2,1)S(1)} %copy.216) | copy-start | bytes 884740
  56.0 1.8 %copy-start.41 = (f32[32,4,6]{0,2,1:T(8,128)}, f32[32,4,6]{0,2,1:T(8,128)S(1)}, u32[]{:S(2)}) copy-start(f32[32,4,6]{0,2,1:T(8,128)S(1)} %fusion.101) | copy-start | bytes 9220
  56.3 1.8 %copy-start.12 = (f32[1,32,4,384]{3,1,2,0:T(8,128)}, f32[1,32,4,384]{3,1,2,0:T(8,128)S(1)}, u32[]{:S(2)}) copy-start(f32[1,32,4,384]{3,1,2,0:T(8,128)S(1)} %convolution_bitcast_fusion.14) | copy-start | bytes 589828
  57.7 1.1 copy-start.10
  57.8 1.0 copy-start.51
  59.8 12.2 %all-to-all-start.2 = ((bf16[32,1,4,384]{3,2,1,0:T(4,128)(2,1)}), bf16[32,1,4,384]{3,2,1,0:T(4,128)(2,1)S(1)}, u32[]{:S(2)}, u32[]{:S(2)}) async-start(bf16[32,1,4,384]{3,2,1,0:T(4,128)(2,1)} %copy.218), calls=%async_computation.2 | async-start | bytes 196608 | tf_op jit(solution)/shard_map/all_to_all | solution.py:82
  72.0 52.0 %all-to-all-start = ((bf16[8,1,16,384]{3,2,1,0:T(8,128)(2,1)}), bf16[8,1,16,384]{3,2,1,0:T(8,128)(2,1)}, u32[]{:S(2)}, u32[]{:S(2)}) async-start(bf16[8,1,16,384]{3,2,1,0:T(8,128)(2,1)} %param.5), calls=%async_computation | async-start | bytes 196608 | tf_op jit(solution)/shard_map/all_to_all | solution.py:99
  77.1 36.9 %copy-start = (f32[4,32,384]{2,1,0:T(8,128)}, f32[4,32,384]{2,1,0:T(8,128)S(1)}, u32[]{:S(2)}) copy-start(f32[4,32,384]{2,1,0:T(8,128)S(1)} %reshape.895) | copy-start | bytes 589828
  94.3 1.4 slice-start
  94.7 13.2 %copy-start.36 = (f32[4,32,6]{1,2,0:T(8,128)}, f32[4,32,6]{1,2,0:T(8,128)S(1)}, u32[]{:S(2)}) copy-start(f32[4,32,6]{1,2,0:T(8,128)S(1)} %fusion.99) | copy-start | bytes 9220
  95.1 12.4 %copy-start.38 = (f32[4,32,6]{1,2,0:T(8,128)}, f32[4,32,6]{1,2,0:T(8,128)S(1)}, u32[]{:S(2)}) copy-start(f32[4,32,6]{1,2,0:T(8,128)S(1)} %fusion.100) | copy-start | bytes 9220
  103.4 10.6 %copy-start.4 = (bf16[1,384,8,48]{1,3,2,0:T(8,128)(2,1)}, bf16[1,384,8,48]{1,3,2,0:T(8,128)(2,1)S(1)}, u32[]{:S(2)}) copy-start(bf16[1,384,8,48]{1,3,2,0:T(8,128)(2,1)S(1)} %copy.225) | copy-start | bytes 884740
  107.5 1.5 copy-start.61
  107.9 1.1 copy-start.16
  109.0 3.4 %copy-start.53 = (bf16[4,32,384,1]{2,1,0,3:T(8,128)(2,1)}, bf16[4,32,384,1]{2,1,0,3:T(8,128)(2,1)S(1)}, u32[]{:S(2)}) copy-start(bf16[4,32,384,1]{2,1,0,3:T(8,128)(2,1)S(1)} %get-tuple-element.11) | copy-start | bytes 294916
  109.9 3.3 %copy-start.47 = (bf16[4,32,384,1]{2,1,0,3:T(8,128)(2,1)S(1)}, bf16[4,32,384,1]{2,1,0,3:T(8,128)(2,1)}, u32[]{:S(2)}) copy-start(bf16[4,32,384,1]{2,1,0,3:T(8,128)(2,1)} %fusion.238) | copy-start | bytes 294916
  112.4 2.0 %copy-start.31 = (f32[32,6,4]{1,2,0:T(4,128)}, f32[32,6,4]{1,2,0:T(4,128)S(1)}, u32[]{:S(2)}) copy-start(f32[32,6,4]{1,2,0:T(4,128)S(1)} %get-tuple-element.27) | copy-start | bytes 9220
  113.2 2.2 %copy-start.44 = (bf16[32,6,4,4]{1,2,3,0:T(4,128)(2,1)}, bf16[32,6,4,4]{1,2,3,0:T(4,128)(2,1)S(1)}, u32[]{:S(2)}) copy-start(bf16[32,6,4,4]{1,2,3,0:T(4,128)(2,1)S(1)} %fusion.226) | copy-start | bytes 18436
  114.9 1.5 copy-start.65
  119.5 2.2 %copy-start.62 = (bf16[6,384]{1,0:T(8,128)(2,1)S(1)}, bf16[6,384]{1,0:T(8,128)(2,1)}, u32[]{:S(2)}) copy-start(bf16[6,384]{1,0:T(8,128)(2,1)} %copy-done.60) | copy-start | bytes 13828
  120.5 2.3 %copy-start.18 = (f32[4,32,384]{2,1,0:T(8,128)}, f32[4,32,384]{2,1,0:T(8,128)S(1)}, u32[]{:S(2)}) copy-start(f32[4,32,384]{2,1,0:T(8,128)S(1)} %fusion.259) | copy-start | bytes 589828
  121.6 1.2 copy-start.20
  121.7 1.1 copy-start.55
  121.7 1.1 copy-start.57
  124.0 2.6 %copy-start.30 = (f32[4,1,6,32,32]{3,4,2,0,1:T(8,128)S(1)}, f32[4,1,6,32,32]{3,4,2,0,1:T(8,128)}, u32[]{:S(2)}) copy-start(f32[4,1,6,32,32]{3,4,2,0,1:T(8,128)} %get-tuple-element.32) | copy-start | bytes 294916
  124.0 2.6 %copy-start.59 = (f32[4,6,32]{2,1,0:T(8,128)S(1)}, f32[4,6,32]{2,1,0:T(8,128)}, u32[]{:S(2)}) copy-start(f32[4,6,32]{2,1,0:T(8,128)} %multiply_divide_fusion.2) | copy-start | bytes 9220
  125.3 2.1 %copy-start.58 = (bf16[4,32,384,1]{2,1,3,0:T(8,128)(2,1)S(1)}, bf16[4,32,384,1]{2,1,3,0:T(8,128)(2,1)}, u32[]{:S(2)}) copy-start(bf16[4,32,384,1]{2,1,3,0:T(8,128)(2,1)} %copy-done.57) | copy-start | bytes 294916
  125.3 2.1 %copy-start.63 = (bf16[6,384]{1,0:T(8,128)(2,1)S(1)}, bf16[6,384]{1,0:T(8,128)(2,1)}, u32[]{:S(2)}) copy-start(bf16[6,384]{1,0:T(8,128)(2,1)} %copy-done.60) | copy-start | bytes 13828
  125.3 2.1 %copy-start.72 = (f32[4,6,32]{2,1,0:T(8,128)S(1)}, f32[4,6,32]{2,1,0:T(8,128)}, u32[]{:S(2)}) copy-start(f32[4,6,32]{2,1,0:T(8,128)} %copy-done.71) | copy-start | bytes 9220
  128.3 1.1 copy-start.21
  128.3 1.4 copy-start.40
  129.0 1.1 copy-start.19
  129.0 1.5 copy-start.3
  130.5 1.6 copy-start.5
  131.0 1.5 copy-start.45
  132.4 2.9 %copy-start.25 = (f32[1,32,6,4,4]{2,3,4,1,0:T(4,128)S(1)}, f32[1,32,6,4,4]{2,3,4,1,0:T(4,128)}, u32[]{:S(2)}) copy-start(f32[1,32,6,4,4]{2,3,4,1,0:T(4,128)} %copy-done.24) | copy-start | bytes 36868
  132.5 2.9 %copy-start.33 = (f32[32,6,4]{1,2,0:T(4,128)S(1)}, f32[32,6,4]{1,2,0:T(4,128)}, u32[]{:S(2)}) copy-start(f32[32,6,4]{1,2,0:T(4,128)} %multiply_divide_fusion) | copy-start | bytes 9220
  133.0 2.6 %copy-start.27 = (bf16[4,32,6,384]{3,1,2,0:T(8,128)(2,1)S(1)}, bf16[4,32,6,384]{3,1,2,0:T(8,128)(2,1)}, u32[]{:S(2)}) copy-start(bf16[4,32,6,384]{3,1,2,0:T(8,128)(2,1)} %copy-done.26) | copy-start | bytes 1769476
  133.0 2.6 %copy-start.32 = (f32[32,6,4]{1,2,0:T(4,128)S(1)}, f32[32,6,4]{1,2,0:T(4,128)}, u32[]{:S(2)}) copy-start(f32[32,6,4]{1,2,0:T(4,128)} %copy-done.31) | copy-start | bytes 9220
  136.5 1.2 copy-start.17
  136.5 1.5 copy-start.37
  137.2 1.1 copy-start.15
  137.2 1.5 copy-start.1
  138.7 6.2 %copy-start.70 = (f32[4,6,32]{2,1,0:T(8,128)S(1)}, f32[4,6,32]{2,1,0:T(8,128)}, u32[]{:S(2)}) copy-start(f32[4,6,32]{2,1,0:T(8,128)} %copy-done.69) | copy-start | bytes 9220
  138.8 13.6 %copy-start.7 = (bf16[1,384,8,48]{1,3,2,0:T(8,128)(2,1)S(1)}, bf16[1,384,8,48]{1,3,2,0:T(8,128)(2,1)}, u32[]{:S(2)}) copy-start(bf16[1,384,8,48]{1,3,2,0:T(8,128)(2,1)} %copy-done.6) | copy-start | bytes 884740
  139.2 13.3 %copy-start.29 = (f32[1,4,6,32,32]{3,4,2,1,0:T(8,128)S(1)}, f32[1,4,6,32,32]{3,4,2,1,0:T(8,128)}, u32[]{:S(2)}) copy-start(f32[1,4,6,32,32]{3,4,2,1,0:T(8,128)} %copy-done.28) | copy-start | bytes 294916
  140.1 12.2 %all-to-all-start.3 = ((bf16[32,1,4,384]{3,2,1,0:T(4,128)(2,1)}), bf16[32,1,4,384]{3,2,1,0:T(4,128)(2,1)S(1)}, u32[]{:S(2)}, u32[]{:S(2)}) async-start(bf16[32,1,4,384]{3,2,1,0:T(4,128)(2,1)} %bitcast.140), calls=%async_computation.3 | async-start | bytes 196608 | tf_op jit(solution)/shard_map/all_to_all | solution.py:93
  152.6 1.1 copy-start.52
  152.6 1.1 copy-start.64
  154.5 1.1 copy-start.13
  154.5 1.4 copy-start.35
  155.2 1.1 copy-start.11
  155.2 1.5 copy-start.9
  155.2 1.5 copy-start.23
  (21 other events, 16.2 us)
Sparse Core Ops, SparseCore 0:
  28.3 24.3 all-gather.4
  54.6 30.9 all-gather.2

commit v12 on v9

--- a/solution.py
+++ b/solution.py
@@ -43,16 +43,17 @@
 
 def full_weights(w_project, w_output, sizes):
     subs, din, dproj = w_project.shape
-    cat = jnp.concatenate([w_project, w_output], axis=2)
-    ny = sizes[1]
-    shifted = [cat] + [
-        lax.ppermute(cat, "gy", [(i, (i + s) % ny) for i in range(ny)]) for s in range(1, ny)
+    nz, ny, nx = sizes
+    shifted = [w_project] + [
+        lax.ppermute(w_project, "gy", [(i, (i + s) % ny) for i in range(ny)]) for s in range(1, ny)
     ]
     source = (lax.axis_index("gy") - jnp.arange(ny)) % ny
     rows = jnp.take(jnp.stack(shifted), source, axis=0)
-    rows = jnp.swapaxes(rows, 0, 1).reshape(subs, ny * din, cat.shape[2])
-    proj = lax.all_gather(rows[:, :, :dproj], ("gz", "gx"), axis=2, tiled=True)
-    outp = lax.all_gather(rows[:, :, dproj:], ("gz", "gx"), axis=2, tiled=True)
+    rows = jnp.swapaxes(rows, 0, 1).reshape(subs, ny * din, dproj)
+    proj = lax.all_gather(rows, ("gz", "gx"), axis=2, tiled=True)
+    outp = lax.all_gather(w_output, ALL, axis=0, tiled=False)
+    outp = outp.reshape((nz, ny, nx) + w_output.shape)
+    outp = jnp.transpose(outp, (3, 1, 4, 0, 2, 5)).reshape(subs, ny * din, -1)
     return [(proj[i], outp[i]) for i in range(subs)]
 
 

time: 141 us -> 182 us (1.29)
  blocking collectives: 28.4 us -> 83.6 us
  waiting for transfers between devices: 27.1 us -> 22.5 us
  local copies, waits for them, and re-layouts: 12 us -> 7.61 us
  starting transfers between devices: 24.1 us -> 20.1 us
    all_gather x1, blocking collectives: 21.7 us -> 77 us  [full_weights(): outp = lax.all_gather(w_output, ALL, axis=0, tiled=False)]
    all_to_all x1, waiting for transfers between devices: 4.23 us -> 0.01 us  [local(): depth_act = lax.all_to_all(volume, 'gz', 2, 0, tiled=True)]
    all_to_all x1, starting transfers between devices: 6.93 us -> 3.37 us  [block_to_plane(): got = lax.all_to_all(block, ('gy', 'gx'), 0, 0, tiled=True)]
    ppermute x3, waiting for transfers between devices: 8.3 us -> 6.15 us  [full_weights(): lax.ppermute(w_project, 'gy', [(i, (i + s) % ny) for i in range(ny)])]
  transfers between devices with their start and end apart: 8 -> 8, of which waited for: 5 -> 5; matrix products, arithmetic and copies ran while one was open for 5% -> 4% of each run, Pallas kernels for 0% -> 0%
where the time goes in v12:
time: 182 us
  blocking collectives  83.6 us (46%)
  matrix products  29.8 us (16%)
  waiting for transfers between devices  22.5 us (12%)
  starting transfers between devices  20.1 us (11%)
  between operations  14.1 us (8%)
  local copies, waits for them, and re-layouts  7.61 us (4%)
  other arithmetic  3.87 us (2%)
    all_gather x1, blocking collectives, full_weights(): outp = lax.all_gather(w_output, ALL, axis=0, tiled=False)  77 us
    all_to_all x1, waiting for transfers between devices, from_planes(): return lax.all_to_all(parts, ALL, 0, 0, tiled=True)  7.34 us
    dot_general x6, matrix products, sublayer(): packed = jnp.dot(normed, w_inner, preferred_element_type=jnp.float32)  7.21 us
    all_to_all x1, waiting for transfers between devices, to_planes(): got = lax.all_to_all(depth_lines, ALL, 0, 0, tiled=True)  7.18 us
    ppermute x3, starting transfers between devices, full_weights(): lax.ppermute(w_project, 'gy', [(i, (i + s) % ny) for i in range(ny)])  6.99 us
    dot_general x9, matrix products, sublayer(): jnp.einsum('plqd,pkqhd->pqhlk', queries, key_heads, preferred_element_typ...  6.87 us
    all_to_all x1, blocking collectives, local(): return lax.all_to_all(grad_zero, 'gz', 0, 2, tiled=True)  6.67 us
    ppermute x3, waiting for transfers between devices, full_weights(): lax.ppermute(w_project, 'gy', [(i, (i + s) % ny) for i in range(ny)])  6.15 us
  transfers between devices with their start and end apart: 8, of which 5 were waited for; matrix products, arithmetic and copies ran while one was open for 4% of the time, Pallas kernels for 0%

profile of v12, /device:TPU:0, one launch (start us, length us, event | category | flops | bytes accessed | tf_op | source)
XLA Modules:
  0.0 181.6 jit_solution(7495874746533246598)
XLA Ops:
  6.5 3.1 %collective-permute-start = (bf16[3,96,144]{1,2,0:T(8,128)(2,1)}, bf16[3,96,144]{1,2,0:T(8,128)(2,1)S(1)}, u32[]{:S(2)}, u32[]{:S(2)}) collective-permute-start(bf16[3,96,144]{1,2,0:T(8,128)(2,1)} %param.6), channel_id=1, source_target_pairs={{0,2},{2,4},{4,6},{6,0},{1,3},{3,5},{5,7},{7,1},{8,10},{10,12},{12... | collective-permute-start | bytes 248840 | tf_op jit(solution)/shard_map/ppermute | solution.py:48
  9.6 2.6 %collective-permute-start.1 = (bf16[3,96,144]{1,2,0:T(8,128)(2,1)}, bf16[3,96,144]{1,2,0:T(8,128)(2,1)S(1)}, u32[]{:S(2)}, u32[]{:S(2)}) collective-permute-start(bf16[3,96,144]{1,2,0:T(8,128)(2,1)} %param.6), channel_id=1, source_target_pairs={{0,4},{2,6},{4,0},{6,2},{1,5},{3,7},{5,1},{7,3},{8,12},{10,14},{12... | collective-permute-start | bytes 248840 | tf_op jit(solution)/shard_map/ppermute | solution.py:48
  12.2 1.3 collective-permute-start.2
  13.6 2.3 %collective-permute-done = bf16[3,96,144]{1,2,0:T(8,128)(2,1)S(1)} collective-permute-done((bf16[3,96,144]{1,2,0:T(8,128)(2,1)}, bf16[3,96,144]{1,2,0:T(8,128)(2,1)S(1)}, u32[]{:S(2)}, u32[]{:S(2)}) %collective-permute-start) | collective-permute-done | bytes 82976 | tf_op jit(solution)/shard_map/ppermute | solution.py:48
  15.8 3.9 %collective-permute-done.1 = bf16[3,96,144]{1,2,0:T(8,128)(2,1)S(1)} collective-permute-done((bf16[3,96,144]{1,2,0:T(8,128)(2,1)}, bf16[3,96,144]{1,2,0:T(8,128)(2,1)S(1)}, u32[]{:S(2)}, u32[]{:S(2)}) %collective-permute-start.1) | collective-permute-done | bytes 82976 | tf_op jit(solution)/shard_map/ppermute | solution.py:48
  19.7 1.0 pad_maximum_fusion
  20.8 0.6 gather_fusion
  21.7 1.0 reshape.842
  22.8 0.7 copy.164
  23.4 3.3 %all-to-all-start.1 = ((bf16[8,1,16,384]{3,0,1,2:T(8,128)(2,1)}), bf16[8,1,16,384]{3,0,1,2:T(8,128)(2,1)S(1)}, u32[]{:S(2)}, u32[]{:S(2)}) async-start(bf16[8,1,16,384]{3,0,1,2:T(8,128)(2,1)} %copy.164), calls=%async_computation.1 | async-start | bytes 196608 | tf_op jit(solution)/shard_map/all_to_all | solution.py:99
  26.8 77.0 %all-gather = bf16[96,96,48]{1,2,0:T(8,128)(2,1)S(1)} all-gather(bf16[3,96,48]{1,2,0:T(8,128)(2,1)S(1)} %copy-done.10), channel_id=2, replica_groups=mesh['gz'=4,'gy'=4,'gx'=2] {'gz','gy','gx'}, dimensions={0}, use_global_device_ids=true | all-gather | bytes 912384 | tf_op jit(solution)/shard_map/all_gather | solution.py:54
  103.7 0.6 copy.305
  104.3 0.5 fusion.344
  105.7 3.4 %all-to-all-start = ((bf16[8,1,16,384]{3,2,1,0:T(8,128)(2,1)}), bf16[8,1,16,384]{3,2,1,0:T(8,128)(2,1)S(1)}, u32[]{:S(2)}, u32[]{:S(2)}) async-start(bf16[8,1,16,384]{3,2,1,0:T(8,128)(2,1)} %param.5), calls=%async_computation | async-start | bytes 196608 | tf_op jit(solution)/shard_map/all_to_all | solution.py:91
  109.3 1.6 convolution_bitcast_fusion.2
  110.9 0.4 fusion.101
  111.3 0.4 fusion.100
  111.6 0.3 fusion.265
  112.0 0.3 convolution_bitcast_fusion.14
  113.0 0.4 fusion.9
  113.7 0.7 copy.172
  114.4 1.8 all-to-all-done
  116.1 3.6 %all-to-all-start.2 = ((bf16[32,1,4,384]{3,2,1,0:T(4,128)(2,1)}), bf16[32,1,4,384]{3,2,1,0:T(4,128)(2,1)S(1)}, u32[]{:S(2)}, u32[]{:S(2)}) async-start(bf16[32,1,4,384]{3,2,1,0:T(4,128)(2,1)} %copy.172), calls=%async_computation.2 | async-start | bytes 196608 | tf_op jit(solution)/shard_map/all_to_all | solution.py:74
  120.0 7.2 %all-to-all-done.2 = bf16[32,1,4,384]{3,2,1,0:T(4,128)(2,1)S(1)} async-done(((bf16[32,1,4,384]{3,2,1,0:T(4,128)(2,1)}), bf16[32,1,4,384]{3,2,1,0:T(4,128)(2,1)S(1)}, u32[]{:S(2)}, u32[]{:S(2)}) %all-to-all-start.2) | async-done | bytes 98336 | tf_op jit(solution)/shard_map/all_to_all | solution.py:74
  127.5 1.6 convolution_bitcast_fusion.1
  129.1 0.4 fusion.99
  129.4 0.4 fusion.98
  129.9 0.3 fusion.262
  130.2 0.3 convolution_bitcast_fusion.13
  130.6 0.7 fusion.230
  131.2 0.9 broadcast_multiply_fusion
  132.2 3.7 %fusion.348 = (f32[32,6,4]{1,2,0:T(4,128)S(1)}, f32[1,32,6,4,4]{2,3,4,1,0:T(4,128)S(1)}) fusion(bf16[4,32,384,1]{2,1,0,3:T(8,128)(2,1)} %get-tuple-element.10, bf16[4,32,6,384]{3,1,2,0:T(8,128)(2,1)} %broadcast_multiply_fusion), kind=kOutput, calls=%fused_computation.420 | convolution fusion | flops 2364672 | bytes 703488 | tf_op jit(solution)/shard_map/jvp(plqd,pkqhd->pqhlk)/dot_general | solution.py:35
  135.9 0.8 fusion
  137.1 0.4 convolution_bitcast_fusion
  137.5 0.4 fusion.97
  137.9 0.4 fusion.96
  138.3 0.3 fusion.259
  138.6 0.3 fusion.257
  139.6 0.7 fusion.145
  141.0 0.4 fusion.95
  141.3 0.3 add_add_fusion.8
  141.7 0.4 fusion.94
  142.1 0.3 add_add_fusion.7
  142.4 0.4 multiply_reduce_fusion.1
  143.3 0.4 fusion.53
  143.7 2.4 %fusion.1 = bf16[32,6,4,4]{1,3,2,0:T(4,128)(2,1)S(1)} fusion(f32[4,32,384]{2,0,1:T(4,128)S(1)} %copy.184, f32[6,384]{1,0:T(8,128)S(1)} %get-tuple-element.22, bf16[4,32,384,1]{2,1,0,3:T(8,128)(2,1)S(1)} %fusion.238), kind=kOutput, calls=%fused_computation.6 | convolution fusion | flops 2654208 | bytes 310272 | tf_op jit(solution)/shard_map/transpose(jvp(pqhlk,pkqd->plqhd))/dot_general | solution.py:38
  146.3 0.8 fusion.13
  147.4 0.6 convolution_bitcast_fusion.8
  148.1 0.4 fusion.93
  148.4 0.3 add_add_fusion.5
  148.8 0.4 fusion.92
  149.2 0.3 add_add_fusion.4
  149.6 1.6 multiply_reduce_fusion
  151.4 0.7 copy.193
  152.1 2.8 %all-to-all-start.3 = ((bf16[32,1,4,384]{3,2,1,0:T(4,128)(2,1)}), bf16[32,1,4,384]{3,2,1,0:T(4,128)(2,1)S(1)}, u32[]{:S(2)}, u32[]{:S(2)}) async-start(bf16[32,1,4,384]{3,2,1,0:T(4,128)(2,1)} %bitcast.132), calls=%async_computation.3 | async-start | bytes 196608 | tf_op jit(solution)/shard_map/all_to_all | solution.py:85
  154.9 7.3 %all-to-all-done.3 = bf16[32,1,4,384]{3,2,1,0:T(4,128)(2,1)S(1)} async-done(((bf16[32,1,4,384]{3,2,1,0:T(4,128)(2,1)}), bf16[32,1,4,384]{3,2,1,0:T(4,128)(2,1)S(1)}, u32[]{:S(2)}, u32[]{:S(2)}) %all-to-all-start.3) | async-done | bytes 98336 | tf_op jit(solution)/shard_map/all_to_all | solution.py:85
  162.8 0.7 fusion.141
  164.1 0.4 fusion.91
  164.5 0.3 add_add_fusion.2
  164.9 0.4 fusion.90
  165.2 0.3 add_add_fusion.1
  165.6 1.6 fusion.206
  167.4 6.7 %all_to_all.42 = bf16[32,1,4,384]{3,2,1,0:T(4,128)(2,1)S(1)} all-to-all(bf16[32,1,4,384]{3,2,1,0:T(4,128)(2,1)S(1)} %copy.198), channel_id=1, replica_groups=mesh['gz'=4,'gy'=4,'gx'=2] {'gz'}, dimensions={0} | all-to-all | bytes 196608 | tf_op jit(solution)/shard_map/all_to_all | solution.py:108
  174.1 0.7 all_to_all.36
  (88 shorter events, 7.0 us)
Async XLA Ops:
  6.5 102.8 %all-gather.3.cloned.1.call-start = ((), (), s32[]{:S(2)}) async-start(), calls=%async_computation.5 | async-start | bytes 2985984 | tf_op jit(solution)/shard_map/all_gather | solution.py:53
  6.5 9.3 %collective-permute-start = (bf16[3,96,144]{1,2,0:T(8,128)(2,1)}, bf16[3,96,144]{1,2,0:T(8,128)(2,1)S(1)}, u32[]{:S(2)}, u32[]{:S(2)}) collective-permute-start(bf16[3,96,144]{1,2,0:T(8,128)(2,1)} %param.6), channel_id=1, source_target_pairs={{0,2},{2,4},{4,6},{6,0},{1,3},{3,5},{5,7},{7,1},{8,10},{10,12},{12... | collective-permute-start | bytes 248840 | tf_op jit(solution)/shard_map/ppermute | solution.py:48
  9.6 10.1 %collective-permute-start.1 = (bf16[3,96,144]{1,2,0:T(8,128)(2,1)}, bf16[3,96,144]{1,2,0:T(8,128)(2,1)S(1)}, u32[]{:S(2)}, u32[]{:S(2)}) collective-permute-start(bf16[3,96,144]{1,2,0:T(8,128)(2,1)} %param.6), channel_id=1, source_target_pairs={{0,4},{2,6},{4,0},{6,2},{1,5},{3,7},{5,1},{7,3},{8,12},{10,14},{12... | collective-permute-start | bytes 248840 | tf_op jit(solution)/shard_map/ppermute | solution.py:48
  12.2 7.5 %collective-permute-start.2 = (bf16[3,96,144]{1,2,0:T(8,128)(2,1)}, bf16[3,96,144]{1,2,0:T(8,128)(2,1)S(1)}, u32[]{:S(2)}, u32[]{:S(2)}) collective-permute-start(bf16[3,96,144]{1,2,0:T(8,128)(2,1)} %param.6), channel_id=1, source_target_pairs={{0,6},{2,0},{4,2},{6,4},{1,7},{3,1},{5,3},{7,5},{8,14},{10,8},{12,... | collective-permute-start | bytes 248840 | tf_op jit(solution)/shard_map/ppermute | solution.py:48
  21.4 1.4 copy-start.4
  21.4 5.3 %copy-start.10 = (bf16[3,96,48]{1,2,0:T(8,128)(2,1)S(1)}, bf16[3,96,48]{1,2,0:T(8,128)(2,1)}, u32[]{:S(2)}) copy-start(bf16[3,96,48]{1,2,0:T(8,128)(2,1)} %param.7) | copy-start | bytes 82948
  23.4 82.2 %all-to-all-start.1 = ((bf16[8,1,16,384]{3,0,1,2:T(8,128)(2,1)}), bf16[8,1,16,384]{3,0,1,2:T(8,128)(2,1)S(1)}, u32[]{:S(2)}, u32[]{:S(2)}) async-start(bf16[8,1,16,384]{3,0,1,2:T(8,128)(2,1)} %copy.164), calls=%async_computation.1 | async-start | bytes 196608 | tf_op jit(solution)/shard_map/all_to_all | solution.py:99
  105.7 10.4 %all-to-all-start = ((bf16[8,1,16,384]{3,2,1,0:T(8,128)(2,1)}), bf16[8,1,16,384]{3,2,1,0:T(8,128)(2,1)S(1)}, u32[]{:S(2)}, u32[]{:S(2)}) async-start(bf16[8,1,16,384]{3,2,1,0:T(8,128)(2,1)} %param.5), calls=%async_computation | async-start | bytes 196608 | tf_op jit(solution)/shard_map/all_to_all | solution.py:91
  112.4 0.6 copy-start.5
  112.4 1.0 copy-start.7
  112.7 0.9 copy-start.2
  112.7 7.2 %copy-start.11 = (f32[4,6,32]{2,1,0:T(8,128)}, f32[4,6,32]{2,1,0:T(8,128)S(1)}, u32[]{:S(2)}) copy-start(f32[4,6,32]{2,1,0:T(8,128)S(1)} %get-tuple-element.24) | copy-start | bytes 9220
  116.1 11.0 %all-to-all-start.2 = ((bf16[32,1,4,384]{3,2,1,0:T(4,128)(2,1)}), bf16[32,1,4,384]{3,2,1,0:T(4,128)(2,1)S(1)}, u32[]{:S(2)}, u32[]{:S(2)}) async-start(bf16[32,1,4,384]{3,2,1,0:T(4,128)(2,1)} %copy.172), calls=%async_computation.2 | async-start | bytes 196608 | tf_op jit(solution)/shard_map/all_to_all | solution.py:74
  132.2 4.9 %copy-start = (bf16[3,384,1152]{1,2,0:T(8,128)(2,1)S(1)}, bf16[3,384,1152]{1,2,0:T(8,128)(2,1)}, u32[]{:S(2)}) copy-start(bf16[3,384,1152]{1,2,0:T(8,128)(2,1)} %all-gather.3.cloned.1.call-done) | copy-start | bytes 7962628
  143.3 3.0 %copy-start.9 = (bf16[4,32,384,1]{2,1,0,3:T(8,128)(2,1)S(1)}, bf16[4,32,384,1]{2,1,0,3:T(8,128)(2,1)}, u32[]{:S(2)}) copy-start(bf16[4,32,384,1]{2,1,0,3:T(8,128)(2,1)} %get-tuple-element.10) | copy-start | bytes 294916
  146.3 1.1 copy-start.1
  149.6 5.3 %copy-start.12 = (f32[4,6,32]{2,1,0:T(8,128)S(1)}, f32[4,6,32]{2,1,0:T(8,128)}, u32[]{:S(2)}) copy-start(f32[4,6,32]{2,1,0:T(8,128)} %copy-done.11) | copy-start | bytes 9220
  149.6 12.9 %copy-start.3 = (f32[1,4,6,32,32]{3,4,2,1,0:T(8,128)S(1)}, f32[1,4,6,32,32]{3,4,2,1,0:T(8,128)}, u32[]{:S(2)}) copy-start(f32[1,4,6,32,32]{3,4,2,1,0:T(8,128)} %copy-done.2) | copy-start | bytes 294916
  152.1 10.2 %all-to-all-start.3 = ((bf16[32,1,4,384]{3,2,1,0:T(4,128)(2,1)}), bf16[32,1,4,384]{3,2,1,0:T(4,128)(2,1)S(1)}, u32[]{:S(2)}, u32[]{:S(2)}) async-start(bf16[32,1,4,384]{3,2,1,0:T(4,128)(2,1)} %bitcast.132), calls=%async_computation.3 | async-start | bytes 196608 | tf_op jit(solution)/shard_map/all_to_all | solution.py:85
  162.5 1.0 copy-start.8
  162.7 1.1 copy-start.6
Sparse Core Ops, SparseCore 0:
  22.9 37.6 all-gather.2

commit v13 on v9

--- a/solution.py
+++ b/solution.py
@@ -31,12 +31,24 @@
     queries = head_norm(packed[..., :feat_len], ones)
     key_part = head_norm(packed[..., feat_len : 2 * feat_len], ones)
     value_part = packed[..., 2 * feat_len :].astype(jnp.bfloat16)
-    key_heads = key_part[..., None, :] * mask
-    scores = jnp.einsum("plqd,pkqhd->pqhlk", queries, key_heads, preferred_element_type=jnp.float32) * head_size ** (-0.5)
-    powers = jnp.exp(scores)
-    attn_weights = (powers / jnp.sum(powers, axis=-1, keepdims=True)).astype(jnp.bfloat16)
-    mixed_heads = jnp.einsum("pqhlk,pkqd->plqhd", attn_weights, value_part, preferred_element_type=jnp.float32)
-    mixed_out = jnp.sum(mixed_heads * mask.astype(jnp.float32), axis=-2).astype(jnp.bfloat16)
+    if line_rows.shape[1] <= 8:
+        pairs = queries[:, :, None].astype(jnp.float32) * key_part[:, None].astype(jnp.float32)
+        scores = jnp.dot(pairs, ones, precision=HIGHEST) * head_size ** (-0.5)
+        powers = jnp.exp(scores)
+        attn_weights = (powers / jnp.sum(powers, axis=2, keepdims=True)).astype(jnp.bfloat16)
+        spread = jnp.dot(attn_weights, mask, preferred_element_type=jnp.float32)
+        mixed_out = jnp.sum(spread * value_part[:, None].astype(jnp.float32), axis=2).astype(jnp.bfloat16)
+    else:
+        key_heads = key_part[..., None, :] * mask
+        scores = jnp.einsum(
+            "plqd,pkqhd->pqhlk", queries, key_heads, preferred_element_type=jnp.float32
+        ) * head_size ** (-0.5)
+        powers = jnp.exp(scores)
+        attn_weights = (powers / jnp.sum(powers, axis=-1, keepdims=True)).astype(jnp.bfloat16)
+        mixed_heads = jnp.einsum(
+            "pqhlk,pkqd->plqhd", attn_weights, value_part, preferred_element_type=jnp.float32
+        )
+        mixed_out = jnp.sum(mixed_heads * mask.astype(jnp.float32), axis=-2).astype(jnp.bfloat16)
     update = jnp.dot(mixed_out, w_outer, preferred_element_type=jnp.float32)
     return (stream + update).astype(jnp.bfloat16)
 

time: 141 us -> 135 us (0.957)
  matrix products: 29.8 us -> 25.7 us
    dot_general x9 -> x6, matrix products: 6.87 us -> 1.8 us  [sublayer(): jnp.einsum('plqd,pkqhd->pqhlk', queries, key_heads, preferred_element_typ...]
    dot_general x8 -> x5, matrix products: 5.93 us -> 2.4 us  [sublayer(): jnp.einsum('pqhlk,pkqd->plqhd', attn_weights, value_part, preferred_eleme...]
    dot_general x0 -> x4, matrix products: none -> 2.57 us  [the longest x2 1.81 us: sublayer(): scores = jnp.dot(pairs, ones, precision=HIGHEST) * head_size ** (-0.5)]
    unnamed x46 -> x44, local copies, waits for them, and re-layouts: 2.84 us -> 3.41 us
where the time goes in v13:
time: 135 us; the launch traced here: 134 us
  blocking collectives  28.4 us (21%)
  waiting for transfers between devices  27.3 us (20%)
  matrix products  25.7 us (19%)
  starting transfers between devices  23.9 us (18%)
  between operations  14.1 us (10%)
  local copies, waits for them, and re-layouts  11.7 us (9%)
  other arithmetic  3.27 us (2%)
    all_gather x1, blocking collectives, full_weights(): outp = lax.all_gather(rows[:, :, dproj:], ('gz', 'gx'), axis=2, tiled=True)  21.7 us
    ppermute x3, waiting for transfers between devices, full_weights(): lax.ppermute(cat, 'gy', [(i, (i + s) % ny) for i in range(ny)])  8.3 us
    all_to_all x1, waiting for transfers between devices, from_planes(): return lax.all_to_all(parts, ALL, 0, 0, tiled=True)  7.56 us
    dot_general x6, matrix products, sublayer(): packed = jnp.dot(normed, w_inner, preferred_element_type=jnp.float32)  7.23 us
    all_to_all x1, waiting for transfers between devices, to_planes(): got = lax.all_to_all(depth_lines, ALL, 0, 0, tiled=True)  7.19 us
    ppermute x3, starting transfers between devices, full_weights(): lax.ppermute(cat, 'gy', [(i, (i + s) % ny) for i in range(ny)])  6.99 us
    all_to_all x1, starting transfers between devices, block_to_plane(): got = lax.all_to_all(block, ('gy', 'gx'), 0, 0, tiled=True)  6.93 us
    all_to_all x1, blocking collectives, local(): return lax.all_to_all(grad_zero, 'gz', 0, 2, tiled=True)  6.67 us
  transfers between devices with their start and end apart: 8, of which 5 were waited for; matrix products, arithmetic and copies ran while one was open for 5% of the time, Pallas kernels for 0%

profile of v13, /device:TPU:0, one launch (start us, length us, event | category | flops | bytes accessed | tf_op | source)
XLA Modules:
  0.0 134.4 jit_solution(13024833817430814006)
XLA Ops:
  6.5 0.9 constant_dynamic-update-slice_fusion.1
  7.4 0.8 constant_dynamic-update-slice_fusion
  8.2 3.1 %collective-permute-start = (bf16[3,96,192]{1,2,0:T(8,128)(2,1)S(1)}, bf16[3,96,192]{1,2,0:T(8,128)(2,1)S(1)}, u32[]{:S(2)}, u32[]{:S(2)}) collective-permute-start(bf16[3,96,192]{1,2,0:T(8,128)(2,1)S(1)} %constant_dynamic-update-slice_fusion), channel_id=1, source_target_pairs={{0,2},{2,4},{4,6},{6,0},{1,3},{3,5},{5,7},{7,1},{8,10},{10,12},{12... | collective-permute-start | bytes 331784 | tf_op jit(solution)/shard_map/ppermute | solution.py:61
  11.3 2.6 %collective-permute-start.1 = (bf16[3,96,192]{1,2,0:T(8,128)(2,1)S(1)}, bf16[3,96,192]{1,2,0:T(8,128)(2,1)S(1)}, u32[]{:S(2)}, u32[]{:S(2)}) collective-permute-start(bf16[3,96,192]{1,2,0:T(8,128)(2,1)S(1)} %constant_dynamic-update-slice_fusion), channel_id=1, source_target_pairs={{0,4},{2,6},{4,0},{6,2},{1,5},{3,7},{5,1},{7,3},{8,12},{10,14},{12... | collective-permute-start | bytes 331784 | tf_op jit(solution)/shard_map/ppermute | solution.py:61
  13.9 1.3 %collective-permute-start.2 = (bf16[3,96,192]{1,2,0:T(8,128)(2,1)S(1)}, bf16[3,96,192]{1,2,0:T(8,128)(2,1)S(1)}, u32[]{:S(2)}, u32[]{:S(2)}) collective-permute-start(bf16[3,96,192]{1,2,0:T(8,128)(2,1)S(1)} %constant_dynamic-update-slice_fusion), channel_id=1, source_target_pairs={{0,6},{2,0},{4,2},{6,4},{1,7},{3,1},{5,3},{7,5},{8,14},{10,8},{12,... | collective-permute-start | bytes 331784 | tf_op jit(solution)/shard_map/ppermute | solution.py:61
  15.3 2.8 %collective-permute-done = bf16[3,96,192]{1,2,0:T(8,128)(2,1)S(1)} collective-permute-done((bf16[3,96,192]{1,2,0:T(8,128)(2,1)S(1)}, bf16[3,96,192]{1,2,0:T(8,128)(2,1)S(1)}, u32[]{:S(2)}, u32[]{:S(2)}) %collective-permute-start) | collective-permute-done | bytes 110624 | tf_op jit(solution)/shard_map/ppermute | solution.py:61
  18.1 5.5 %collective-permute-done.1 = bf16[3,96,192]{1,2,0:T(8,128)(2,1)S(1)} collective-permute-done((bf16[3,96,192]{1,2,0:T(8,128)(2,1)S(1)}, bf16[3,96,192]{1,2,0:T(8,128)(2,1)S(1)}, u32[]{:S(2)}, u32[]{:S(2)}) %collective-permute-start.1) | collective-permute-done | bytes 110624 | tf_op jit(solution)/shard_map/ppermute | solution.py:61
  23.7 0.7 gather_fusion
  24.5 0.5 copy.72
  25.0 0.4 reshape.887
  25.4 0.8 slice.75
  26.2 0.7 copy.74
  26.9 3.3 %all-to-all-start.1 = ((bf16[8,1,16,384]{3,0,1,2:T(8,128)(2,1)}), bf16[8,1,16,384]{3,0,1,2:T(8,128)(2,1)S(1)}, u32[]{:S(2)}, u32[]{:S(2)}) async-start(bf16[8,1,16,384]{3,0,1,2:T(8,128)(2,1)} %copy.74), calls=%async_computation.1 | async-start | bytes 196608 | tf_op jit(solution)/shard_map/all_to_all | solution.py:110
  30.2 4.2 %all-to-all-done.1 = bf16[8,1,16,384]{3,0,1,2:T(8,128)(2,1)S(1)} async-done(((bf16[8,1,16,384]{3,0,1,2:T(8,128)(2,1)}), bf16[8,1,16,384]{3,0,1,2:T(8,128)(2,1)S(1)}, u32[]{:S(2)}, u32[]{:S(2)}) %all-to-all-start.1) | async-done | bytes 98336 | tf_op jit(solution)/shard_map/all_to_all | solution.py:110
  34.4 6.9 %all-to-all-start = ((bf16[8,1,16,384]{3,2,1,0:T(8,128)(2,1)}), bf16[8,1,16,384]{3,2,1,0:T(8,128)(2,1)S(1)}, u32[]{:S(2)}, u32[]{:S(2)}) async-start(bf16[8,1,16,384]{3,2,1,0:T(8,128)(2,1)} %param.5), calls=%async_computation | async-start | bytes 196608 | tf_op jit(solution)/shard_map/all_to_all | solution.py:102
  41.5 0.7 add.157
  42.2 21.7 %all_gather.6 = bf16[3,384,384]{1,2,0:T(8,128)(2,1)S(1)} all-gather(bf16[3,384,48]{1,2,0:T(8,128)(2,1)S(1)} %slice.73), channel_id=1, replica_groups=mesh['gz'=4,'gy'=4,'gx'=2] {'gz','gx'}, dimensions={2}, use_global_device_ids=true | all-gather | bytes 995328 | tf_op jit(solution)/shard_map/all_gather | solution.py:67
  63.9 1.6 %convolution_bitcast_fusion.2 = f32[1,32,4,1152]{3,1,2,0:T(8,128)S(1)} fusion(bf16[3,384,1152]{1,2,0:T(8,128)(2,1)} %all-gather.2.cloned.1.call-done, bf16[8,1,4,4,384]{4,0,3,2,1:T(8,128)(2,1)S(1)} %bitcast.580, f32[4,8,4]{1,2,0:T(4,128)S(1)} %get-tuple-element.16), kind=kOutput, calls=%fused_computation.3 | convolution fusion | flops 113393664 | bytes 1573376 | tf_op jit(solution)/shard_map/jvp()/dot_general | solution.py:30
  65.5 0.4 fusion.89
  65.9 0.4 fusion.88
  68.1 0.4 fusion.1
  68.8 0.7 copy.81
  69.5 4.1 %all-to-all-start.2 = ((bf16[32,1,4,384]{3,2,1,0:T(4,128)(2,1)}), bf16[32,1,4,384]{3,2,1,0:T(4,128)(2,1)S(1)}, u32[]{:S(2)}, u32[]{:S(2)}) async-start(bf16[32,1,4,384]{3,2,1,0:T(4,128)(2,1)} %copy.81), calls=%async_computation.2 | async-start | bytes 196608 | tf_op jit(solution)/shard_map/all_to_all | solution.py:85
  73.8 7.2 %all-to-all-done.2 = bf16[32,1,4,384]{3,2,1,0:T(4,128)(2,1)S(1)} async-done(((bf16[32,1,4,384]{3,2,1,0:T(4,128)(2,1)}), bf16[32,1,4,384]{3,2,1,0:T(4,128)(2,1)S(1)}, u32[]{:S(2)}, u32[]{:S(2)}) %all-to-all-start.2) | async-done | bytes 98336 | tf_op jit(solution)/shard_map/all_to_all | solution.py:85
  81.1 0.6 multiply_add_fusion
  81.9 1.6 %convolution_bitcast_fusion.1 = f32[1,4,32,1152]{3,2,1,0:T(8,128)S(1)} fusion(bf16[4,32,384]{2,1,0:T(8,128)(2,1)S(1)} %convert_element_type.547, bf16[3,384,1152]{1,2,0:T(8,128)(2,1)} %all-gather.2.cloned.1.call-done), kind=kOutput, calls=%fused_computation.2 | convolution fusion | flops 113246208 | bytes 1572864 | tf_op jit(solution)/shard_map/jvp()/dot_general | solution.py:30
  83.5 0.4 fusion.86
  83.8 0.4 fusion.87
  84.2 0.7 copy_bitcast_fusion
  85.3 1.0 reshape.919
  86.3 1.0 fusion.204
  87.3 1.1 fusion.335
  89.1 0.4 convolution_bitcast_fusion
  89.6 0.4 fusion.85
  90.0 0.4 fusion.84
  90.3 0.3 fusion.238
  91.7 0.7 fusion.129
  93.1 0.4 fusion.83
  93.5 0.3 add_add_fusion.8
  93.8 0.4 fusion.82
  94.2 0.3 add_add_fusion.7
  94.5 0.4 multiply_reduce_fusion.5
  95.3 0.7 multiply_reduce_fusion.2
  96.0 0.4 multiply_reduce_fusion.9
  96.5 0.7 multiply_reduce_fusion.1
  97.2 0.4 fusion.81
  97.5 0.4 add_add_fusion.5
  97.9 1.0 fusion.80
  98.9 1.4 %add.156 = f32[4,32]{1,0:T(4,128)} reshape(f32[4,2,4,4]{3,2,1,0:T(4,128)} %get-tuple-element.13) | data formatting | bytes 1024 | tf_op jit(solution)/shard_map/jvp()/add | solution.py:29
  100.3 1.0 add_add_fusion.4
  101.4 1.6 %multiply_reduce_fusion.4 = (f32[4,32]{1,0:T(4,128)S(1)}, f32[4,32,384]{2,1,0:T(8,128)S(1)}) fusion(f32[4,32,384]{2,1,0:T(8,128)S(1)} %reshape.919, bf16[3,384,1152]{1,2,0:T(8,128)(2,1)} %all-gather.2.cloned.1.call-done, f32[1,4,32,384]{3,2,1,0:T(8,128)S(1)} %add_add_fusion.4, f32[1,4,32,384]{3,2,1,0:T(8,128)S(1)} %add_add_fusion.5, ...), kind=kOutput, calls=%fused_computation.247 | convolution fusion | flops 113885056 | bytes 1769984 | tf_op jit(solution)/shard_map/transpose(jvp())/dot_general | solution.py:30
  103.2 0.7 copy.87
  103.9 2.6 %all-to-all-start.3 = ((bf16[32,1,4,384]{3,2,1,0:T(4,128)(2,1)}), bf16[32,1,4,384]{3,2,1,0:T(4,128)(2,1)S(1)}, u32[]{:S(2)}, u32[]{:S(2)}) async-start(bf16[32,1,4,384]{3,2,1,0:T(4,128)(2,1)} %bitcast.113), calls=%async_computation.3 | async-start | bytes 196608 | tf_op jit(solution)/shard_map/all_to_all | solution.py:96
  106.5 7.6 %all-to-all-done.3 = bf16[32,1,4,384]{3,2,1,0:T(4,128)(2,1)S(1)} async-done(((bf16[32,1,4,384]{3,2,1,0:T(4,128)(2,1)}), bf16[32,1,4,384]{3,2,1,0:T(4,128)(2,1)S(1)}, u32[]{:S(2)}, u32[]{:S(2)}) %all-to-all-start.3) | async-done | bytes 98336 | tf_op jit(solution)/shard_map/all_to_all | solution.py:96
  114.5 0.7 fusion.125
  115.6 0.5 copy-done.12
  116.5 0.4 copy-done.7
  116.9 0.4 fusion.79
  117.3 0.4 add_add_fusion.2
  117.6 0.4 fusion.78
  118.0 0.3 add_add_fusion.1
  118.4 1.6 %fusion.181 = (f32[32,4]{0,1:T(4,128)S(1)}, f32[32,4,384]{2,0,1:T(8,128)S(1)}) fusion(bf16[3,384,1152]{1,2,0:T(8,128)(2,1)} %all-gather.2.cloned.1.call-done, f32[1,32,4,384]{3,1,2,0:T(8,128)S(1)} %add_add_fusion.1, f32[1,32,4,384]{3,1,2,0:T(8,128)S(1)} %add_add_fusion.2, bf16[1,32,4,384]{3,1,2,0:T(8,128)(2,1)S(1)} %fusion.72, ...), kind=kOutput, calls=%fused_computation.244 | convolution fusion | flops 113934208 | bytes 1671680 | tf_op jit(solution)/shard_map/transpose(jvp())/dot_general | solution.py:30
  120.2 6.7 %all_to_all.42 = bf16[32,1,4,384]{3,2,1,0:T(4,128)(2,1)S(1)} all-to-all(bf16[32,1,4,384]{3,2,1,0:T(4,128)(2,1)S(1)} %copy.91), channel_id=1, replica_groups=mesh['gz'=4,'gy'=4,'gx'=2] {'gz'}, dimensions={0} | all-to-all | bytes 196608 | tf_op jit(solution)/shard_map/all_to_all | solution.py:119
  126.9 0.7 all_to_all.36
  (96 shorter events, 7.5 us)
Async XLA Ops:
  6.5 57.4 %all-gather.2.cloned.1.call-start = ((), (), s32[]{:S(2)}) async-start(), calls=%async_computation.5 | async-start | bytes 2985984 | tf_op jit(solution)/shard_map/all_gather | solution.py:66
  8.2 9.9 %collective-permute-start = (bf16[3,96,192]{1,2,0:T(8,128)(2,1)S(1)}, bf16[3,96,192]{1,2,0:T(8,128)(2,1)S(1)}, u32[]{:S(2)}, u32[]{:S(2)}) collective-permute-start(bf16[3,96,192]{1,2,0:T(8,128)(2,1)S(1)} %constant_dynamic-update-slice_fusion), channel_id=1, source_target_pairs={{0,2},{2,4},{4,6},{6,0},{1,3},{3,5},{5,7},{7,1},{8,10},{10,12},{12... | collective-permute-start | bytes 331784 | tf_op jit(solution)/shard_map/ppermute | solution.py:61
  11.3 12.3 %collective-permute-start.1 = (bf16[3,96,192]{1,2,0:T(8,128)(2,1)S(1)}, bf16[3,96,192]{1,2,0:T(8,128)(2,1)S(1)}, u32[]{:S(2)}, u32[]{:S(2)}) collective-permute-start(bf16[3,96,192]{1,2,0:T(8,128)(2,1)S(1)} %constant_dynamic-update-slice_fusion), channel_id=1, source_target_pairs={{0,4},{2,6},{4,0},{6,2},{1,5},{3,7},{5,1},{7,3},{8,12},{10,14},{12... | collective-permute-start | bytes 331784 | tf_op jit(solution)/shard_map/ppermute | solution.py:61
  13.9 9.7 %collective-permute-start.2 = (bf16[3,96,192]{1,2,0:T(8,128)(2,1)S(1)}, bf16[3,96,192]{1,2,0:T(8,128)(2,1)S(1)}, u32[]{:S(2)}, u32[]{:S(2)}) collective-permute-start(bf16[3,96,192]{1,2,0:T(8,128)(2,1)S(1)} %constant_dynamic-update-slice_fusion), channel_id=1, source_target_pairs={{0,6},{2,0},{4,2},{6,4},{1,7},{3,1},{5,3},{7,5},{8,14},{10,8},{12,... | collective-permute-start | bytes 331784 | tf_op jit(solution)/shard_map/ppermute | solution.py:61
  25.0 1.2 copy-start.10
  26.9 7.6 %all-to-all-start.1 = ((bf16[8,1,16,384]{3,0,1,2:T(8,128)(2,1)}), bf16[8,1,16,384]{3,0,1,2:T(8,128)(2,1)S(1)}, u32[]{:S(2)}, u32[]{:S(2)}) async-start(bf16[8,1,16,384]{3,0,1,2:T(8,128)(2,1)} %copy.74), calls=%async_computation.1 | async-start | bytes 196608 | tf_op jit(solution)/shard_map/all_to_all | solution.py:110
  30.2 62.6 %copy-start.19 = (bf16[6,384]{1,0:T(8,128)(2,1)}, bf16[6,384]{1,0:T(8,128)(2,1)S(1)}, u32[]{:S(2)}) copy-start(bf16[6,384]{1,0:T(8,128)(2,1)S(1)} %get-tuple-element.22) | copy-start | bytes 13828
  34.4 35.0 %all-to-all-start = ((bf16[8,1,16,384]{3,2,1,0:T(8,128)(2,1)}), bf16[8,1,16,384]{3,2,1,0:T(8,128)(2,1)S(1)}, u32[]{:S(2)}, u32[]{:S(2)}) async-start(bf16[8,1,16,384]{3,2,1,0:T(8,128)(2,1)} %param.5), calls=%async_computation | async-start | bytes 196608 | tf_op jit(solution)/shard_map/all_to_all | solution.py:102
  65.9 0.6 copy-start.6
  66.5 0.6 copy-start.8
  67.5 0.6 copy-start.11
  67.5 1.0 copy-start.13
  67.8 0.9 copy-start.2
  67.8 0.9 copy-start.15
  69.5 11.5 %all-to-all-start.2 = ((bf16[32,1,4,384]{3,2,1,0:T(4,128)(2,1)}), bf16[32,1,4,384]{3,2,1,0:T(4,128)(2,1)S(1)}, u32[]{:S(2)}, u32[]{:S(2)}) async-start(bf16[32,1,4,384]{3,2,1,0:T(4,128)(2,1)} %copy.81), calls=%async_computation.2 | async-start | bytes 196608 | tf_op jit(solution)/shard_map/all_to_all | solution.py:85
  84.2 4.2 %copy-start.4 = (f32[4,32,6]{1,2,0:T(8,128)}, f32[4,32,6]{1,2,0:T(8,128)S(1)}, u32[]{:S(2)}) copy-start(f32[4,32,6]{1,2,0:T(8,128)S(1)} %fusion.87) | copy-start | bytes 9220
  86.3 2.9 %copy-start = (bf16[3,384,1152]{1,2,0:T(8,128)(2,1)S(1)}, bf16[3,384,1152]{1,2,0:T(8,128)(2,1)}, u32[]{:S(2)}) copy-start(bf16[3,384,1152]{1,2,0:T(8,128)(2,1)} %all-gather.2.cloned.1.call-done) | copy-start | bytes 7962628
  96.5 1.4 %copy-start.5 = (f32[4,32,6]{1,2,0:T(8,128)S(1)}, f32[4,32,6]{1,2,0:T(8,128)}, u32[]{:S(2)}) copy-start(f32[4,32,6]{1,2,0:T(8,128)} %copy-done.4) | copy-start | bytes 9220
  96.5 3.8 %copy-start.1 = (f32[4,32,384]{2,1,0:T(8,128)S(1)}, f32[4,32,384]{2,1,0:T(8,128)}, u32[]{:S(2)}) copy-start(f32[4,32,384]{2,1,0:T(8,128)} %get-tuple-element.25) | copy-start | bytes 589828
  101.3 1.7 %copy-start.18 = (f32[4,32]{1,0:T(4,128)S(1)}, f32[4,32]{1,0:T(4,128)}, u32[]{:S(2)}) copy-start(f32[4,32]{1,0:T(4,128)} %add.156) | copy-start | bytes 1540
  101.4 5.1 %copy-start.16 = (f32[4,6,32]{2,1,0:T(8,128)S(1)}, f32[4,6,32]{2,1,0:T(8,128)}, u32[]{:S(2)}) copy-start(f32[4,6,32]{2,1,0:T(8,128)} %copy-done.15) | copy-start | bytes 9220
  103.0 11.2 %copy-start.3 = (f32[1,4,6,32,32]{3,4,2,1,0:T(8,128)S(1)}, f32[1,4,6,32,32]{3,4,2,1,0:T(8,128)}, u32[]{:S(2)}) copy-start(f32[1,4,6,32,32]{3,4,2,1,0:T(8,128)} %copy-done.2) | copy-start | bytes 294916
  103.9 10.2 %all-to-all-start.3 = ((bf16[32,1,4,384]{3,2,1,0:T(4,128)(2,1)}), bf16[32,1,4,384]{3,2,1,0:T(4,128)(2,1)S(1)}, u32[]{:S(2)}, u32[]{:S(2)}) async-start(bf16[32,1,4,384]{3,2,1,0:T(4,128)(2,1)} %bitcast.113), calls=%async_computation.3 | async-start | bytes 196608 | tf_op jit(solution)/shard_map/all_to_all | solution.py:96
  114.2 1.1 copy-start.14
  114.3 1.1 copy-start.20
  115.3 0.9 copy-start.12
  116.2 0.7 copy-start.7
  116.2 1.4 %copy-start.9 = (f32[32,4,6]{0,2,1:T(8,128)S(1)}, f32[32,4,6]{0,2,1:T(8,128)}, u32[]{:S(2)}) copy-start(f32[32,4,6]{0,2,1:T(8,128)} %copy-done.8) | copy-start | bytes 9220
  118.4 1.6 %copy-start.17 = (f32[32,4]{0,1:T(4,128)S(1)}, f32[32,4]{0,1:T(4,128)}, u32[]{:S(2)}) copy-start(f32[32,4]{0,1:T(4,128)} %add.157) | copy-start | bytes 1540
Sparse Core Ops, SparseCore 0:
  26.3 35.3 all-gather.1

commit v14 on v13

--- a/solution.py
+++ b/solution.py
@@ -55,16 +55,18 @@
 
 def full_weights(w_project, w_output, sizes):
     subs, din, dproj = w_project.shape
-    cat = jnp.concatenate([w_project, w_output], axis=2)
     ny = sizes[1]
-    shifted = [cat] + [
-        lax.ppermute(cat, "gy", [(i, (i + s) % ny) for i in range(ny)]) for s in range(1, ny)
-    ]
     source = (lax.axis_index("gy") - jnp.arange(ny)) % ny
-    rows = jnp.take(jnp.stack(shifted), source, axis=0)
-    rows = jnp.swapaxes(rows, 0, 1).reshape(subs, ny * din, cat.shape[2])
-    proj = lax.all_gather(rows[:, :, :dproj], ("gz", "gx"), axis=2, tiled=True)
-    outp = lax.all_gather(rows[:, :, dproj:], ("gz", "gx"), axis=2, tiled=True)
+
+    def over_gy(block):
+        shifted = [block] + [
+            lax.ppermute(block, "gy", [(i, (i + s) % ny) for i in range(ny)]) for s in range(1, ny)
+        ]
+        rows = jnp.take(jnp.stack(shifted), source, axis=0)
+        return jnp.swapaxes(rows, 0, 1).reshape(subs, ny * din, block.shape[2])
+
+    proj = lax.all_gather(over_gy(w_project), ("gz", "gx"), axis=2, tiled=True)
+    outp = lax.all_gather(over_gy(w_output), ("gz", "gx"), axis=2, tiled=True)
     return [(proj[i], outp[i]) for i in range(subs)]
 
 

time: 135 us -> 135 us (level)
  waiting for transfers between devices: 27.3 us -> 22.1 us
  starting transfers between devices: 23.9 us -> 28.2 us
  local copies, waits for them, and re-layouts: 11.7 us -> 10.3 us
    ppermute x3 -> x6, starting transfers between devices: 6.99 us -> 12.3 us  [over_gy(): lax.ppermute(block, 'gy', [(i, (i + s) % ny) for i in range(ny)])]
    all_to_all x1, waiting for transfers between devices: 4.23 us -> 0.01 us  [local(): depth_act = lax.all_to_all(volume, 'gz', 2, 0, tiled=True)]
    ppermute x3 -> x6, waiting for transfers between devices: 8.3 us -> 6.16 us  [over_gy(): lax.ppermute(block, 'gy', [(i, (i + s) % ny) for i in range(ny)])]
    all_to_all x1, starting transfers between devices: 6.93 us -> 4.9 us  [block_to_plane(): got = lax.all_to_all(block, ('gy', 'gx'), 0, 0, tiled=True)]
    unnamed x44 -> x45, local copies, waits for them, and re-layouts: 3.41 us -> 2.49 us
  transfers between devices with their start and end apart: 8 -> 11, of which waited for: 5 -> 5; matrix products, arithmetic and copies ran while one was open for 5% -> 5% of each run, Pallas kernels for 0% -> 0%
where the time goes in v14:
time: 135 us; the launch traced here: 134 us
  blocking collectives  29.4 us (22%)
  starting transfers between devices  28.2 us (21%)
  matrix products  25.7 us (19%)
  waiting for transfers between devices  22.1 us (16%)
  between operations  14.2 us (11%)
  local copies, waits for them, and re-layouts  10.3 us (8%)
  other arithmetic  4.24 us (3%)
    all_gather x1, blocking collectives, full_weights(): outp = lax.all_gather(over_gy(w_output), ('gz', 'gx'), axis=2, tiled=True)  22.7 us
    ppermute x6, starting transfers between devices, over_gy(): lax.ppermute(block, 'gy', [(i, (i + s) % ny) for i in range(ny)])  12.3 us
    all_to_all x1, waiting for transfers between devices, from_planes(): return lax.all_to_all(parts, ALL, 0, 0, tiled=True)  7.56 us
    dot_general x6, matrix products, sublayer(): packed = jnp.dot(normed, w_inner, preferred_element_type=jnp.float32)  7.22 us
    all_to_all x1, waiting for transfers between devices, to_planes(): got = lax.all_to_all(depth_lines, ALL, 0, 0, tiled=True)  7.19 us
    all_to_all x1, blocking collectives, local(): return lax.all_to_all(grad_zero, 'gz', 0, 2, tiled=True)  6.67 us
    ppermute x6, waiting for transfers between devices, over_gy(): lax.ppermute(block, 'gy', [(i, (i + s) % ny) for i in range(ny)])  6.16 us
    dot_general x12, matrix products, head_norm(): jnp.dot(scale, ones.T, precision=HIGHEST)  5.51 us
  transfers between devices with their start and end apart: 11, of which 5 were waited for; matrix products, arithmetic and copies ran while one was open for 5% of the time, Pallas kernels for 0%

profile of v14, /device:TPU:0, one launch (start us, length us, event | category | flops | bytes accessed | tf_op | source)
XLA Modules:
  0.0 134.2 jit_solution(14153905588605156996)
XLA Ops:
  6.5 3.1 %collective-permute-start.3 = (bf16[3,96,144]{1,2,0:T(8,128)(2,1)}, bf16[3,96,144]{1,2,0:T(8,128)(2,1)S(1)}, u32[]{:S(2)}, u32[]{:S(2)}) collective-permute-start(bf16[3,96,144]{1,2,0:T(8,128)(2,1)} %param.6), channel_id=1, source_target_pairs={{0,2},{2,4},{4,6},{6,0},{1,3},{3,5},{5,7},{7,1},{8,10},{10,12},{12... | collective-permute-start | bytes 248840 | tf_op jit(solution)/shard_map/ppermute | solution.py:63
  9.6 2.6 %collective-permute-start.4 = (bf16[3,96,144]{1,2,0:T(8,128)(2,1)}, bf16[3,96,144]{1,2,0:T(8,128)(2,1)S(1)}, u32[]{:S(2)}, u32[]{:S(2)}) collective-permute-start(bf16[3,96,144]{1,2,0:T(8,128)(2,1)} %param.6), channel_id=1, source_target_pairs={{0,4},{2,6},{4,0},{6,2},{1,5},{3,7},{5,1},{7,3},{8,12},{10,14},{12... | collective-permute-start | bytes 248840 | tf_op jit(solution)/shard_map/ppermute | solution.py:63
  12.2 1.3 %collective-permute-start.5 = (bf16[3,96,144]{1,2,0:T(8,128)(2,1)}, bf16[3,96,144]{1,2,0:T(8,128)(2,1)S(1)}, u32[]{:S(2)}, u32[]{:S(2)}) collective-permute-start(bf16[3,96,144]{1,2,0:T(8,128)(2,1)} %param.6), channel_id=1, source_target_pairs={{0,6},{2,0},{4,2},{6,4},{1,7},{3,1},{5,3},{7,5},{8,14},{10,8},{12,... | collective-permute-start | bytes 248840 | tf_op jit(solution)/shard_map/ppermute | solution.py:63
  13.6 2.3 %collective-permute-done.3 = bf16[3,96,144]{1,2,0:T(8,128)(2,1)S(1)} collective-permute-done((bf16[3,96,144]{1,2,0:T(8,128)(2,1)}, bf16[3,96,144]{1,2,0:T(8,128)(2,1)S(1)}, u32[]{:S(2)}, u32[]{:S(2)}) %collective-permute-start.3) | collective-permute-done | bytes 82976 | tf_op jit(solution)/shard_map/ppermute | solution.py:63
  15.8 3.9 %collective-permute-done.4 = bf16[3,96,144]{1,2,0:T(8,128)(2,1)S(1)} collective-permute-done((bf16[3,96,144]{1,2,0:T(8,128)(2,1)}, bf16[3,96,144]{1,2,0:T(8,128)(2,1)S(1)}, u32[]{:S(2)}, u32[]{:S(2)}) %collective-permute-start.4) | collective-permute-done | bytes 82976 | tf_op jit(solution)/shard_map/ppermute | solution.py:63
  19.7 1.0 pad_maximum_fusion
  20.8 0.6 gather_fusion.1
  21.7 1.0 reshape.892
  22.8 2.9 %collective-permute-start = (bf16[3,96,48]{1,2,0:T(8,128)(2,1)S(1)}, bf16[3,96,48]{1,2,0:T(8,128)(2,1)S(1)}, u32[]{:S(2)}, u32[]{:S(2)}) collective-permute-start(bf16[3,96,48]{1,2,0:T(8,128)(2,1)S(1)} %copy-done.15), channel_id=1, source_target_pairs={{0,2},{2,4},{4,6},{6,0},{1,3},{3,5},{5,7},{7,1},{8,10},{10,12},{12... | collective-permute-start | bytes 82952 | tf_op jit(solution)/shard_map/ppermute | solution.py:63
  25.7 1.6 %collective-permute-start.1 = (bf16[3,96,48]{1,2,0:T(8,128)(2,1)S(1)}, bf16[3,96,48]{1,2,0:T(8,128)(2,1)S(1)}, u32[]{:S(2)}, u32[]{:S(2)}) collective-permute-start(bf16[3,96,48]{1,2,0:T(8,128)(2,1)S(1)} %copy-done.15), channel_id=1, source_target_pairs={{0,4},{2,6},{4,0},{6,2},{1,5},{3,7},{5,1},{7,3},{8,12},{10,14},{12... | collective-permute-start | bytes 82952 | tf_op jit(solution)/shard_map/ppermute | solution.py:63
  27.3 0.8 collective-permute-start.2
  28.1 0.7 copy.78
  28.8 3.3 %all-to-all-start.1 = ((bf16[8,1,16,384]{3,0,1,2:T(8,128)(2,1)}), bf16[8,1,16,384]{3,0,1,2:T(8,128)(2,1)S(1)}, u32[]{:S(2)}, u32[]{:S(2)}) async-start(bf16[8,1,16,384]{3,0,1,2:T(8,128)(2,1)} %copy.78), calls=%async_computation.1 | async-start | bytes 196608 | tf_op jit(solution)/shard_map/all_to_all | solution.py:112
  32.2 0.6 gather_fusion
  33.1 22.7 %all_gather.6 = bf16[3,384,384]{1,2,0:T(8,128)(2,1)S(1)} all-gather(bf16[3,384,48]{1,2,0:T(8,128)(2,1)S(1)} %reshape.890), channel_id=1, replica_groups=mesh['gz'=4,'gy'=4,'gx'=2] {'gz','gx'}, dimensions={2}, use_global_device_ids=true | all-gather | bytes 995328 | tf_op jit(solution)/shard_map/all_gather | solution.py:69
  55.8 4.9 %all-to-all-start = ((bf16[8,1,16,384]{3,2,1,0:T(8,128)(2,1)}), bf16[8,1,16,384]{3,2,1,0:T(8,128)(2,1)S(1)}, u32[]{:S(2)}, u32[]{:S(2)}) async-start(bf16[8,1,16,384]{3,2,1,0:T(8,128)(2,1)} %param.5), calls=%async_computation | async-start | bytes 196608 | tf_op jit(solution)/shard_map/all_to_all | solution.py:104
  60.9 0.7 add.159
  61.5 1.6 %convolution_bitcast_fusion.2 = f32[1,32,4,1152]{3,1,2,0:T(8,128)S(1)} fusion(bf16[3,384,1152]{1,2,0:T(8,128)(2,1)} %all-gather.2.cloned.1.call-done, bf16[8,1,4,4,384]{4,0,3,2,1:T(8,128)(2,1)S(1)} %bitcast.588, f32[4,8,4]{1,2,0:T(4,128)S(1)} %get-tuple-element.16), kind=kOutput, calls=%fused_computation.4 | convolution fusion | flops 113393664 | bytes 1573376 | tf_op jit(solution)/shard_map/jvp()/dot_general | solution.py:30
  63.1 0.4 fusion.89
  63.5 0.4 fusion.88
  65.8 0.4 fusion.1
  66.4 0.7 copy.86
  67.1 1.2 all-to-all-done
  68.3 5.1 %all-to-all-start.2 = ((bf16[32,1,4,384]{3,2,1,0:T(4,128)(2,1)}), bf16[32,1,4,384]{3,2,1,0:T(4,128)(2,1)S(1)}, u32[]{:S(2)}, u32[]{:S(2)}) async-start(bf16[32,1,4,384]{3,2,1,0:T(4,128)(2,1)} %copy.86), calls=%async_computation.2 | async-start | bytes 196608 | tf_op jit(solution)/shard_map/all_to_all | solution.py:87
  73.6 7.2 %all-to-all-done.2 = bf16[32,1,4,384]{3,2,1,0:T(4,128)(2,1)S(1)} async-done(((bf16[32,1,4,384]{3,2,1,0:T(4,128)(2,1)}), bf16[32,1,4,384]{3,2,1,0:T(4,128)(2,1)S(1)}, u32[]{:S(2)}, u32[]{:S(2)}) %all-to-all-start.2) | async-done | bytes 98336 | tf_op jit(solution)/shard_map/all_to_all | solution.py:87
  80.9 0.6 multiply_add_fusion
  81.7 1.6 %convolution_bitcast_fusion.1 = f32[1,4,32,1152]{3,2,1,0:T(8,128)S(1)} fusion(bf16[4,32,384]{2,1,0:T(8,128)(2,1)S(1)} %convert_element_type.547, bf16[3,384,1152]{1,2,0:T(8,128)(2,1)} %all-gather.2.cloned.1.call-done), kind=kOutput, calls=%fused_computation.3 | convolution fusion | flops 113246208 | bytes 1572864 | tf_op jit(solution)/shard_map/jvp()/dot_general | solution.py:30
  83.3 0.4 fusion.86
  83.6 0.4 fusion.87
  84.0 0.7 copy_bitcast_fusion
  85.1 1.0 reshape.923
  86.1 1.0 fusion.204
  87.1 1.1 fusion.335
  88.9 0.4 convolution_bitcast_fusion
  89.4 0.4 fusion.85
  89.7 0.4 fusion.84
  90.1 0.3 fusion.238
  91.5 0.7 fusion.129
  92.9 0.4 fusion.83
  93.2 0.4 add_add_fusion.8
  93.6 0.4 fusion.82
  94.0 0.3 add_add_fusion.7
  94.3 0.4 multiply_reduce_fusion.5
  95.1 0.7 multiply_reduce_fusion.2
  95.8 0.4 multiply_reduce_fusion.9
  96.3 0.7 multiply_reduce_fusion.1
  97.0 0.4 fusion.81
  97.3 0.4 add_add_fusion.5
  97.7 1.0 fusion.80
  98.7 1.4 %add.158 = f32[4,32]{1,0:T(4,128)} reshape(f32[4,2,4,4]{3,2,1,0:T(4,128)} %get-tuple-element.13) | data formatting | bytes 1024 | tf_op jit(solution)/shard_map/jvp()/add | solution.py:29
  100.1 1.0 add_add_fusion.4
  101.1 1.6 %multiply_reduce_fusion.4 = (f32[4,32]{1,0:T(4,128)S(1)}, f32[4,32,384]{2,1,0:T(8,128)S(1)}) fusion(f32[4,32,384]{2,1,0:T(8,128)S(1)} %reshape.923, bf16[3,384,1152]{1,2,0:T(8,128)(2,1)} %all-gather.2.cloned.1.call-done, f32[1,4,32,384]{3,2,1,0:T(8,128)S(1)} %add_add_fusion.4, f32[1,4,32,384]{3,2,1,0:T(8,128)S(1)} %add_add_fusion.5, ...), kind=kOutput, calls=%fused_computation.248 | convolution fusion | flops 113885056 | bytes 1769984 | tf_op jit(solution)/shard_map/transpose(jvp())/dot_general | solution.py:30
  103.0 0.7 copy.92
  103.7 2.6 %all-to-all-start.3 = ((bf16[32,1,4,384]{3,2,1,0:T(4,128)(2,1)}), bf16[32,1,4,384]{3,2,1,0:T(4,128)(2,1)S(1)}, u32[]{:S(2)}, u32[]{:S(2)}) async-start(bf16[32,1,4,384]{3,2,1,0:T(4,128)(2,1)} %bitcast.118), calls=%async_computation.3 | async-start | bytes 196608 | tf_op jit(solution)/shard_map/all_to_all | solution.py:98
  106.3 7.6 %all-to-all-done.3 = bf16[32,1,4,384]{3,2,1,0:T(4,128)(2,1)S(1)} async-done(((bf16[32,1,4,384]{3,2,1,0:T(4,128)(2,1)}), bf16[32,1,4,384]{3,2,1,0:T(4,128)(2,1)S(1)}, u32[]{:S(2)}, u32[]{:S(2)}) %all-to-all-start.3) | async-done | bytes 98336 | tf_op jit(solution)/shard_map/all_to_all | solution.py:98
  114.3 0.7 fusion.125
  115.4 0.5 copy-done.12
  116.3 0.4 copy-done.7
  116.7 0.4 fusion.79
  117.1 0.4 add_add_fusion.2
  117.4 0.4 fusion.78
  118.2 1.6 %fusion.181 = (f32[32,4]{0,1:T(4,128)S(1)}, f32[32,4,384]{2,0,1:T(8,128)S(1)}) fusion(bf16[3,384,1152]{1,2,0:T(8,128)(2,1)} %all-gather.2.cloned.1.call-done, f32[1,32,4,384]{3,1,2,0:T(8,128)S(1)} %add_add_fusion.1, f32[1,32,4,384]{3,1,2,0:T(8,128)S(1)} %add_add_fusion.2, bf16[1,32,4,384]{3,1,2,0:T(8,128)(2,1)S(1)} %fusion.72, ...), kind=kOutput, calls=%fused_computation.245 | convolution fusion | flops 113934208 | bytes 1671680 | tf_op jit(solution)/shard_map/transpose(jvp())/dot_general | solution.py:30
  120.0 6.7 %all_to_all.42 = bf16[32,1,4,384]{3,2,1,0:T(4,128)(2,1)S(1)} all-to-all(bf16[32,1,4,384]{3,2,1,0:T(4,128)(2,1)S(1)} %copy.96), channel_id=1, replica_groups=mesh['gz'=4,'gy'=4,'gx'=2] {'gz'}, dimensions={0} | all-to-all | bytes 196608 | tf_op jit(solution)/shard_map/all_to_all | solution.py:121
  126.7 0.7 all_to_all.36
  (105 shorter events, 8.1 us)
Async XLA Ops:
  6.5 55.0 %all-gather.2.cloned.1.call-start = ((), (), s32[]{:S(2)}) async-start(), calls=%async_computation.5 | async-start | bytes 2985984 | tf_op jit(solution)/shard_map/all_gather | solution.py:68
  6.5 9.3 %collective-permute-start.3 = (bf16[3,96,144]{1,2,0:T(8,128)(2,1)}, bf16[3,96,144]{1,2,0:T(8,128)(2,1)S(1)}, u32[]{:S(2)}, u32[]{:S(2)}) collective-permute-start(bf16[3,96,144]{1,2,0:T(8,128)(2,1)} %param.6), channel_id=1, source_target_pairs={{0,2},{2,4},{4,6},{6,0},{1,3},{3,5},{5,7},{7,1},{8,10},{10,12},{12... | collective-permute-start | bytes 248840 | tf_op jit(solution)/shard_map/ppermute | solution.py:63
  9.6 10.1 %collective-permute-start.4 = (bf16[3,96,144]{1,2,0:T(8,128)(2,1)}, bf16[3,96,144]{1,2,0:T(8,128)(2,1)S(1)}, u32[]{:S(2)}, u32[]{:S(2)}) collective-permute-start(bf16[3,96,144]{1,2,0:T(8,128)(2,1)} %param.6), channel_id=1, source_target_pairs={{0,4},{2,6},{4,0},{6,2},{1,5},{3,7},{5,1},{7,3},{8,12},{10,14},{12... | collective-permute-start | bytes 248840 | tf_op jit(solution)/shard_map/ppermute | solution.py:63
  12.2 7.5 %collective-permute-start.5 = (bf16[3,96,144]{1,2,0:T(8,128)(2,1)}, bf16[3,96,144]{1,2,0:T(8,128)(2,1)S(1)}, u32[]{:S(2)}, u32[]{:S(2)}) collective-permute-start(bf16[3,96,144]{1,2,0:T(8,128)(2,1)} %param.6), channel_id=1, source_target_pairs={{0,6},{2,0},{4,2},{6,4},{1,7},{3,1},{5,3},{7,5},{8,14},{10,8},{12,... | collective-permute-start | bytes 248840 | tf_op jit(solution)/shard_map/ppermute | solution.py:63
  21.5 1.3 copy-start.15
  21.5 6.6 %copy-start.10 = (bf16[8,1,16,384]{3,2,1,0:T(8,128)(2,1)S(1)}, bf16[8,1,16,384]{3,2,1,0:T(8,128)(2,1)}, u32[]{:S(2)}) copy-start(bf16[8,1,16,384]{3,2,1,0:T(8,128)(2,1)} %param.4) | copy-start | bytes 294916
  22.8 9.3 %collective-permute-start = (bf16[3,96,48]{1,2,0:T(8,128)(2,1)S(1)}, bf16[3,96,48]{1,2,0:T(8,128)(2,1)S(1)}, u32[]{:S(2)}, u32[]{:S(2)}) collective-permute-start(bf16[3,96,48]{1,2,0:T(8,128)(2,1)S(1)} %copy-done.15), channel_id=1, source_target_pairs={{0,2},{2,4},{4,6},{6,0},{1,3},{3,5},{5,7},{7,1},{8,10},{10,12},{12... | collective-permute-start | bytes 82952 | tf_op jit(solution)/shard_map/ppermute | solution.py:63
  25.7 6.5 %collective-permute-start.1 = (bf16[3,96,48]{1,2,0:T(8,128)(2,1)S(1)}, bf16[3,96,48]{1,2,0:T(8,128)(2,1)S(1)}, u32[]{:S(2)}, u32[]{:S(2)}) collective-permute-start(bf16[3,96,48]{1,2,0:T(8,128)(2,1)S(1)} %copy-done.15), channel_id=1, source_target_pairs={{0,4},{2,6},{4,0},{6,2},{1,5},{3,7},{5,1},{7,3},{8,12},{10,14},{12... | collective-permute-start | bytes 82952 | tf_op jit(solution)/shard_map/ppermute | solution.py:63
  27.3 4.9 %collective-permute-start.2 = (bf16[3,96,48]{1,2,0:T(8,128)(2,1)S(1)}, bf16[3,96,48]{1,2,0:T(8,128)(2,1)S(1)}, u32[]{:S(2)}, u32[]{:S(2)}) collective-permute-start(bf16[3,96,48]{1,2,0:T(8,128)(2,1)S(1)} %copy-done.15), channel_id=1, source_target_pairs={{0,6},{2,0},{4,2},{6,4},{1,7},{3,1},{5,3},{7,5},{8,14},{10,8},{12,... | collective-permute-start | bytes 82952 | tf_op jit(solution)/shard_map/ppermute | solution.py:63
  28.8 27.1 %all-to-all-start.1 = ((bf16[8,1,16,384]{3,0,1,2:T(8,128)(2,1)}), bf16[8,1,16,384]{3,0,1,2:T(8,128)(2,1)S(1)}, u32[]{:S(2)}, u32[]{:S(2)}) async-start(bf16[8,1,16,384]{3,0,1,2:T(8,128)(2,1)} %copy.78), calls=%async_computation.1 | async-start | bytes 196608 | tf_op jit(solution)/shard_map/all_to_all | solution.py:112
  32.1 60.4 %copy-start.20 = (bf16[6,384]{1,0:T(8,128)(2,1)}, bf16[6,384]{1,0:T(8,128)(2,1)S(1)}, u32[]{:S(2)}) copy-start(bf16[6,384]{1,0:T(8,128)(2,1)S(1)} %get-tuple-element.22) | copy-start | bytes 13828
  55.8 12.4 %all-to-all-start = ((bf16[8,1,16,384]{3,2,1,0:T(8,128)(2,1)}), bf16[8,1,16,384]{3,2,1,0:T(8,128)(2,1)S(1)}, u32[]{:S(2)}, u32[]{:S(2)}) async-start(bf16[8,1,16,384]{3,2,1,0:T(8,128)(2,1)} %param.5), calls=%async_computation | async-start | bytes 196608 | tf_op jit(solution)/shard_map/all_to_all | solution.py:104
  63.5 0.6 copy-start.6
  64.1 0.6 copy-start.8
  65.1 0.6 copy-start.11
  65.1 1.0 copy-start.13
  65.5 0.9 copy-start.2
  65.5 0.9 copy-start.16
  68.3 12.5 %all-to-all-start.2 = ((bf16[32,1,4,384]{3,2,1,0:T(4,128)(2,1)}), bf16[32,1,4,384]{3,2,1,0:T(4,128)(2,1)S(1)}, u32[]{:S(2)}, u32[]{:S(2)}) async-start(bf16[32,1,4,384]{3,2,1,0:T(4,128)(2,1)} %copy.86), calls=%async_computation.2 | async-start | bytes 196608 | tf_op jit(solution)/shard_map/all_to_all | solution.py:87
  84.0 4.3 %copy-start.4 = (f32[4,32,6]{1,2,0:T(8,128)}, f32[4,32,6]{1,2,0:T(8,128)S(1)}, u32[]{:S(2)}) copy-start(f32[4,32,6]{1,2,0:T(8,128)S(1)} %fusion.87) | copy-start | bytes 9220
  86.1 2.9 %copy-start = (bf16[3,384,1152]{1,2,0:T(8,128)(2,1)S(1)}, bf16[3,384,1152]{1,2,0:T(8,128)(2,1)}, u32[]{:S(2)}) copy-start(bf16[3,384,1152]{1,2,0:T(8,128)(2,1)} %all-gather.2.cloned.1.call-done) | copy-start | bytes 7962628
  96.2 1.5 %copy-start.5 = (f32[4,32,6]{1,2,0:T(8,128)S(1)}, f32[4,32,6]{1,2,0:T(8,128)}, u32[]{:S(2)}) copy-start(f32[4,32,6]{1,2,0:T(8,128)} %copy-done.4) | copy-start | bytes 9220
  96.3 3.8 %copy-start.1 = (f32[4,32,384]{2,1,0:T(8,128)S(1)}, f32[4,32,384]{2,1,0:T(8,128)}, u32[]{:S(2)}) copy-start(f32[4,32,384]{2,1,0:T(8,128)} %get-tuple-element.25) | copy-start | bytes 589828
  101.1 1.7 %copy-start.19 = (f32[4,32]{1,0:T(4,128)S(1)}, f32[4,32]{1,0:T(4,128)}, u32[]{:S(2)}) copy-start(f32[4,32]{1,0:T(4,128)} %add.158) | copy-start | bytes 1540
  101.1 5.1 %copy-start.17 = (f32[4,6,32]{2,1,0:T(8,128)S(1)}, f32[4,6,32]{2,1,0:T(8,128)}, u32[]{:S(2)}) copy-start(f32[4,6,32]{2,1,0:T(8,128)} %copy-done.16) | copy-start | bytes 9220
  102.8 11.2 %copy-start.3 = (f32[1,4,6,32,32]{3,4,2,1,0:T(8,128)S(1)}, f32[1,4,6,32,32]{3,4,2,1,0:T(8,128)}, u32[]{:S(2)}) copy-start(f32[1,4,6,32,32]{3,4,2,1,0:T(8,128)} %copy-done.2) | copy-start | bytes 294916
  103.7 10.2 %all-to-all-start.3 = ((bf16[32,1,4,384]{3,2,1,0:T(4,128)(2,1)}), bf16[32,1,4,384]{3,2,1,0:T(4,128)(2,1)S(1)}, u32[]{:S(2)}, u32[]{:S(2)}) async-start(bf16[32,1,4,384]{3,2,1,0:T(4,128)(2,1)} %bitcast.118), calls=%async_computation.3 | async-start | bytes 196608 | tf_op jit(solution)/shard_map/all_to_all | solution.py:98
  114.0 1.1 copy-start.14
  114.1 1.1 copy-start.21
  115.1 0.9 copy-start.12
  116.0 0.7 copy-start.7
  116.0 1.4 %copy-start.9 = (f32[32,4,6]{0,2,1:T(8,128)S(1)}, f32[32,4,6]{0,2,1:T(8,128)}, u32[]{:S(2)}) copy-start(f32[32,4,6]{0,2,1:T(8,128)} %copy-done.8) | copy-start | bytes 9220
  118.2 1.6 %copy-start.18 = (f32[32,4]{0,1:T(4,128)S(1)}, f32[32,4]{0,1:T(4,128)}, u32[]{:S(2)}) copy-start(f32[32,4]{0,1:T(4,128)} %add.159) | copy-start | bytes 1540
Sparse Core Ops, SparseCore 0:
  22.9 36.2 all-gather.1

commit v15 on v14

--- a/solution.py
+++ b/solution.py
@@ -33,7 +33,7 @@
     value_part = packed[..., 2 * feat_len :].astype(jnp.bfloat16)
     if line_rows.shape[1] <= 8:
         pairs = queries[:, :, None].astype(jnp.float32) * key_part[:, None].astype(jnp.float32)
-        scores = jnp.dot(pairs, ones, precision=HIGHEST) * head_size ** (-0.5)
+        scores = jnp.dot(pairs, ones, precision=lax.Precision.HIGH) * head_size ** (-0.5)
         powers = jnp.exp(scores)
         attn_weights = (powers / jnp.sum(powers, axis=2, keepdims=True)).astype(jnp.bfloat16)
         spread = jnp.dot(attn_weights, mask, preferred_element_type=jnp.float32)

time: 135 us -> 135 us (level)
  no operation moved by 1% of the time
where the time goes in v15:
time: 135 us; the launch traced here: 134 us
  blocking collectives  29.4 us (22%)
  starting transfers between devices  28.2 us (21%)
  matrix products  25.2 us (19%)
  waiting for transfers between devices  22.1 us (16%)
  between operations  14.2 us (11%)
  local copies, waits for them, and re-layouts  10.3 us (8%)
  other arithmetic  4.24 us (3%)
    all_gather x1, blocking collectives, full_weights(): outp = lax.all_gather(over_gy(w_output), ('gz', 'gx'), axis=2, tiled=True)  22.7 us
    ppermute x6, starting transfers between devices, over_gy(): lax.ppermute(block, 'gy', [(i, (i + s) % ny) for i in range(ny)])  12.3 us
    all_to_all x1, waiting for transfers between devices, from_planes(): return lax.all_to_all(parts, ALL, 0, 0, tiled=True)  7.56 us
    dot_general x6, matrix products, sublayer(): packed = jnp.dot(normed, w_inner, preferred_element_type=jnp.float32)  7.23 us
    all_to_all x1, waiting for transfers between devices, to_planes(): got = lax.all_to_all(depth_lines, ALL, 0, 0, tiled=True)  7.19 us
    all_to_all x1, blocking collectives, local(): return lax.all_to_all(grad_zero, 'gz', 0, 2, tiled=True)  6.67 us
    ppermute x6, waiting for transfers between devices, over_gy(): lax.ppermute(block, 'gy', [(i, (i + s) % ny) for i in range(ny)])  6.16 us
    dot_general x12, matrix products, head_norm(): jnp.dot(scale, ones.T, precision=HIGHEST)  5.51 us
  transfers between devices with their start and end apart: 11, of which 5 were waited for; matrix products, arithmetic and copies ran while one was open for 5% of the time, Pallas kernels for 0%

profile of v15, /device:TPU:0, one launch (start us, length us, event | category | flops | bytes accessed | tf_op | source)
XLA Modules:
  0.0 133.7 jit_solution(1457638008226784151)
XLA Ops:
  6.5 3.1 %collective-permute-start.3 = (bf16[3,96,144]{1,2,0:T(8,128)(2,1)}, bf16[3,96,144]{1,2,0:T(8,128)(2,1)S(1)}, u32[]{:S(2)}, u32[]{:S(2)}) collective-permute-start(bf16[3,96,144]{1,2,0:T(8,128)(2,1)} %param.6), channel_id=1, source_target_pairs={{0,2},{2,4},{4,6},{6,0},{1,3},{3,5},{5,7},{7,1},{8,10},{10,12},{12... | collective-permute-start | bytes 248840 | tf_op jit(solution)/shard_map/ppermute | solution.py:63
  9.6 2.6 %collective-permute-start.4 = (bf16[3,96,144]{1,2,0:T(8,128)(2,1)}, bf16[3,96,144]{1,2,0:T(8,128)(2,1)S(1)}, u32[]{:S(2)}, u32[]{:S(2)}) collective-permute-start(bf16[3,96,144]{1,2,0:T(8,128)(2,1)} %param.6), channel_id=1, source_target_pairs={{0,4},{2,6},{4,0},{6,2},{1,5},{3,7},{5,1},{7,3},{8,12},{10,14},{12... | collective-permute-start | bytes 248840 | tf_op jit(solution)/shard_map/ppermute | solution.py:63
  12.2 1.3 %collective-permute-start.5 = (bf16[3,96,144]{1,2,0:T(8,128)(2,1)}, bf16[3,96,144]{1,2,0:T(8,128)(2,1)S(1)}, u32[]{:S(2)}, u32[]{:S(2)}) collective-permute-start(bf16[3,96,144]{1,2,0:T(8,128)(2,1)} %param.6), channel_id=1, source_target_pairs={{0,6},{2,0},{4,2},{6,4},{1,7},{3,1},{5,3},{7,5},{8,14},{10,8},{12,... | collective-permute-start | bytes 248840 | tf_op jit(solution)/shard_map/ppermute | solution.py:63
  13.6 2.3 %collective-permute-done.3 = bf16[3,96,144]{1,2,0:T(8,128)(2,1)S(1)} collective-permute-done((bf16[3,96,144]{1,2,0:T(8,128)(2,1)}, bf16[3,96,144]{1,2,0:T(8,128)(2,1)S(1)}, u32[]{:S(2)}, u32[]{:S(2)}) %collective-permute-start.3) | collective-permute-done | bytes 82976 | tf_op jit(solution)/shard_map/ppermute | solution.py:63
  15.8 3.9 %collective-permute-done.4 = bf16[3,96,144]{1,2,0:T(8,128)(2,1)S(1)} collective-permute-done((bf16[3,96,144]{1,2,0:T(8,128)(2,1)}, bf16[3,96,144]{1,2,0:T(8,128)(2,1)S(1)}, u32[]{:S(2)}, u32[]{:S(2)}) %collective-permute-start.4) | collective-permute-done | bytes 82976 | tf_op jit(solution)/shard_map/ppermute | solution.py:63
  19.7 1.0 pad_maximum_fusion
  20.8 0.6 gather_fusion.1
  21.7 1.0 reshape.892
  22.8 2.9 %collective-permute-start = (bf16[3,96,48]{1,2,0:T(8,128)(2,1)S(1)}, bf16[3,96,48]{1,2,0:T(8,128)(2,1)S(1)}, u32[]{:S(2)}, u32[]{:S(2)}) collective-permute-start(bf16[3,96,48]{1,2,0:T(8,128)(2,1)S(1)} %copy-done.15), channel_id=1, source_target_pairs={{0,2},{2,4},{4,6},{6,0},{1,3},{3,5},{5,7},{7,1},{8,10},{10,12},{12... | collective-permute-start | bytes 82952 | tf_op jit(solution)/shard_map/ppermute | solution.py:63
  25.7 1.6 %collective-permute-start.1 = (bf16[3,96,48]{1,2,0:T(8,128)(2,1)S(1)}, bf16[3,96,48]{1,2,0:T(8,128)(2,1)S(1)}, u32[]{:S(2)}, u32[]{:S(2)}) collective-permute-start(bf16[3,96,48]{1,2,0:T(8,128)(2,1)S(1)} %copy-done.15), channel_id=1, source_target_pairs={{0,4},{2,6},{4,0},{6,2},{1,5},{3,7},{5,1},{7,3},{8,12},{10,14},{12... | collective-permute-start | bytes 82952 | tf_op jit(solution)/shard_map/ppermute | solution.py:63
  27.3 0.8 collective-permute-start.2
  28.1 0.7 copy.78
  28.8 3.3 %all-to-all-start.1 = ((bf16[8,1,16,384]{3,0,1,2:T(8,128)(2,1)}), bf16[8,1,16,384]{3,0,1,2:T(8,128)(2,1)S(1)}, u32[]{:S(2)}, u32[]{:S(2)}) async-start(bf16[8,1,16,384]{3,0,1,2:T(8,128)(2,1)} %copy.78), calls=%async_computation.1 | async-start | bytes 196608 | tf_op jit(solution)/shard_map/all_to_all | solution.py:112
  32.2 0.6 gather_fusion
  33.1 22.7 %all_gather.6 = bf16[3,384,384]{1,2,0:T(8,128)(2,1)S(1)} all-gather(bf16[3,384,48]{1,2,0:T(8,128)(2,1)S(1)} %reshape.890), channel_id=1, replica_groups=mesh['gz'=4,'gy'=4,'gx'=2] {'gz','gx'}, dimensions={2}, use_global_device_ids=true | all-gather | bytes 995328 | tf_op jit(solution)/shard_map/all_gather | solution.py:69
  55.8 4.9 %all-to-all-start = ((bf16[8,1,16,384]{3,2,1,0:T(8,128)(2,1)}), bf16[8,1,16,384]{3,2,1,0:T(8,128)(2,1)S(1)}, u32[]{:S(2)}, u32[]{:S(2)}) async-start(bf16[8,1,16,384]{3,2,1,0:T(8,128)(2,1)} %param.5), calls=%async_computation | async-start | bytes 196608 | tf_op jit(solution)/shard_map/all_to_all | solution.py:104
  60.9 0.7 add.159
  61.5 1.6 %convolution_bitcast_fusion.2 = f32[1,32,4,1152]{3,1,2,0:T(8,128)S(1)} fusion(bf16[3,384,1152]{1,2,0:T(8,128)(2,1)} %all-gather.2.cloned.1.call-done, bf16[8,1,4,4,384]{4,0,3,2,1:T(8,128)(2,1)S(1)} %bitcast.588, f32[4,8,4]{1,2,0:T(4,128)S(1)} %get-tuple-element.16), kind=kOutput, calls=%fused_computation.4 | convolution fusion | flops 113393664 | bytes 1573376 | tf_op jit(solution)/shard_map/jvp()/dot_general | solution.py:30
  63.1 0.4 fusion.89
  63.5 0.4 fusion.88
  65.8 0.4 fusion.1
  66.4 0.7 copy.86
  67.1 1.2 all-to-all-done
  68.3 5.1 %all-to-all-start.2 = ((bf16[32,1,4,384]{3,2,1,0:T(4,128)(2,1)}), bf16[32,1,4,384]{3,2,1,0:T(4,128)(2,1)S(1)}, u32[]{:S(2)}, u32[]{:S(2)}) async-start(bf16[32,1,4,384]{3,2,1,0:T(4,128)(2,1)} %copy.86), calls=%async_computation.2 | async-start | bytes 196608 | tf_op jit(solution)/shard_map/all_to_all | solution.py:87
  73.6 7.2 %all-to-all-done.2 = bf16[32,1,4,384]{3,2,1,0:T(4,128)(2,1)S(1)} async-done(((bf16[32,1,4,384]{3,2,1,0:T(4,128)(2,1)}), bf16[32,1,4,384]{3,2,1,0:T(4,128)(2,1)S(1)}, u32[]{:S(2)}, u32[]{:S(2)}) %all-to-all-start.2) | async-done | bytes 98336 | tf_op jit(solution)/shard_map/all_to_all | solution.py:87
  80.9 0.6 multiply_add_fusion
  81.7 1.6 %convolution_bitcast_fusion.1 = f32[1,4,32,1152]{3,2,1,0:T(8,128)S(1)} fusion(bf16[4,32,384]{2,1,0:T(8,128)(2,1)S(1)} %convert_element_type.547, bf16[3,384,1152]{1,2,0:T(8,128)(2,1)} %all-gather.2.cloned.1.call-done), kind=kOutput, calls=%fused_computation.3 | convolution fusion | flops 113246208 | bytes 1572864 | tf_op jit(solution)/shard_map/jvp()/dot_general | solution.py:30
  83.3 0.4 fusion.86
  83.6 0.4 fusion.87
  84.0 0.7 copy_bitcast_fusion
  85.1 1.0 reshape.923
  86.1 1.0 fusion.204
  87.1 0.8 fusion.335
  88.6 0.4 convolution_bitcast_fusion
  89.0 0.4 fusion.85
  89.4 0.4 fusion.84
  89.8 0.3 fusion.238
  91.1 0.7 fusion.129
  92.5 0.4 fusion.83
  92.9 0.4 add_add_fusion.8
  93.3 0.4 fusion.82
  93.6 0.3 add_add_fusion.7
  94.0 0.4 multiply_reduce_fusion.5
  94.7 0.7 multiply_reduce_fusion.2
  95.5 0.4 multiply_reduce_fusion.9
  95.9 0.5 multiply_reduce_fusion.1
  96.5 0.4 fusion.81
  96.9 0.4 add_add_fusion.5
  97.2 1.0 fusion.80
  98.2 1.4 %add.158 = f32[4,32]{1,0:T(4,128)} reshape(f32[4,2,4,4]{3,2,1,0:T(4,128)} %get-tuple-element.13) | data formatting | bytes 1024 | tf_op jit(solution)/shard_map/jvp()/add | solution.py:29
  99.6 1.0 add_add_fusion.4
  100.7 1.6 %multiply_reduce_fusion.4 = (f32[4,32]{1,0:T(4,128)S(1)}, f32[4,32,384]{2,1,0:T(8,128)S(1)}) fusion(f32[4,32,384]{2,1,0:T(8,128)S(1)} %reshape.923, bf16[3,384,1152]{1,2,0:T(8,128)(2,1)} %all-gather.2.cloned.1.call-done, f32[1,4,32,384]{3,2,1,0:T(8,128)S(1)} %add_add_fusion.4, f32[1,4,32,384]{3,2,1,0:T(8,128)S(1)} %add_add_fusion.5, ...), kind=kOutput, calls=%fused_computation.248 | convolution fusion | flops 113885056 | bytes 1769984 | tf_op jit(solution)/shard_map/transpose(jvp())/dot_general | solution.py:30
  102.5 0.7 copy.92
  103.2 2.6 %all-to-all-start.3 = ((bf16[32,1,4,384]{3,2,1,0:T(4,128)(2,1)}), bf16[32,1,4,384]{3,2,1,0:T(4,128)(2,1)S(1)}, u32[]{:S(2)}, u32[]{:S(2)}) async-start(bf16[32,1,4,384]{3,2,1,0:T(4,128)(2,1)} %bitcast.118), calls=%async_computation.3 | async-start | bytes 196608 | tf_op jit(solution)/shard_map/all_to_all | solution.py:98
  105.8 7.6 %all-to-all-done.3 = bf16[32,1,4,384]{3,2,1,0:T(4,128)(2,1)S(1)} async-done(((bf16[32,1,4,384]{3,2,1,0:T(4,128)(2,1)}), bf16[32,1,4,384]{3,2,1,0:T(4,128)(2,1)S(1)}, u32[]{:S(2)}, u32[]{:S(2)}) %all-to-all-start.3) | async-done | bytes 98336 | tf_op jit(solution)/shard_map/all_to_all | solution.py:98
  113.9 0.7 fusion.125
  114.9 0.5 copy-done.12
  115.8 0.4 copy-done.7
  116.2 0.4 fusion.79
  116.6 0.4 add_add_fusion.2
  116.9 0.4 fusion.78
  117.7 1.6 %fusion.181 = (f32[32,4]{0,1:T(4,128)S(1)}, f32[32,4,384]{2,0,1:T(8,128)S(1)}) fusion(bf16[3,384,1152]{1,2,0:T(8,128)(2,1)} %all-gather.2.cloned.1.call-done, f32[1,32,4,384]{3,1,2,0:T(8,128)S(1)} %add_add_fusion.1, f32[1,32,4,384]{3,1,2,0:T(8,128)S(1)} %add_add_fusion.2, bf16[1,32,4,384]{3,1,2,0:T(8,128)(2,1)S(1)} %fusion.72, ...), kind=kOutput, calls=%fused_computation.245 | convolution fusion | flops 113934208 | bytes 1671680 | tf_op jit(solution)/shard_map/transpose(jvp())/dot_general | solution.py:30
  119.5 6.7 %all_to_all.42 = bf16[32,1,4,384]{3,2,1,0:T(4,128)(2,1)S(1)} all-to-all(bf16[32,1,4,384]{3,2,1,0:T(4,128)(2,1)S(1)} %copy.96), channel_id=1, replica_groups=mesh['gz'=4,'gy'=4,'gx'=2] {'gz'}, dimensions={0} | all-to-all | bytes 196608 | tf_op jit(solution)/shard_map/all_to_all | solution.py:121
  126.2 0.7 all_to_all.36
  (105 shorter events, 8.1 us)
Async XLA Ops:
  6.5 55.0 %all-gather.2.cloned.1.call-start = ((), (), s32[]{:S(2)}) async-start(), calls=%async_computation.5 | async-start | bytes 2985984 | tf_op jit(solution)/shard_map/all_gather | solution.py:68
  6.5 9.3 %collective-permute-start.3 = (bf16[3,96,144]{1,2,0:T(8,128)(2,1)}, bf16[3,96,144]{1,2,0:T(8,128)(2,1)S(1)}, u32[]{:S(2)}, u32[]{:S(2)}) collective-permute-start(bf16[3,96,144]{1,2,0:T(8,128)(2,1)} %param.6), channel_id=1, source_target_pairs={{0,2},{2,4},{4,6},{6,0},{1,3},{3,5},{5,7},{7,1},{8,10},{10,12},{12... | collective-permute-start | bytes 248840 | tf_op jit(solution)/shard_map/ppermute | solution.py:63
  9.6 10.1 %collective-permute-start.4 = (bf16[3,96,144]{1,2,0:T(8,128)(2,1)}, bf16[3,96,144]{1,2,0:T(8,128)(2,1)S(1)}, u32[]{:S(2)}, u32[]{:S(2)}) collective-permute-start(bf16[3,96,144]{1,2,0:T(8,128)(2,1)} %param.6), channel_id=1, source_target_pairs={{0,4},{2,6},{4,0},{6,2},{1,5},{3,7},{5,1},{7,3},{8,12},{10,14},{12... | collective-permute-start | bytes 248840 | tf_op jit(solution)/shard_map/ppermute | solution.py:63
  12.2 7.5 %collective-permute-start.5 = (bf16[3,96,144]{1,2,0:T(8,128)(2,1)}, bf16[3,96,144]{1,2,0:T(8,128)(2,1)S(1)}, u32[]{:S(2)}, u32[]{:S(2)}) collective-permute-start(bf16[3,96,144]{1,2,0:T(8,128)(2,1)} %param.6), channel_id=1, source_target_pairs={{0,6},{2,0},{4,2},{6,4},{1,7},{3,1},{5,3},{7,5},{8,14},{10,8},{12,... | collective-permute-start | bytes 248840 | tf_op jit(solution)/shard_map/ppermute | solution.py:63
  21.5 1.3 copy-start.15
  21.5 6.6 %copy-start.10 = (bf16[8,1,16,384]{3,2,1,0:T(8,128)(2,1)S(1)}, bf16[8,1,16,384]{3,2,1,0:T(8,128)(2,1)}, u32[]{:S(2)}) copy-start(bf16[8,1,16,384]{3,2,1,0:T(8,128)(2,1)} %param.4) | copy-start | bytes 294916
  22.8 9.3 %collective-permute-start = (bf16[3,96,48]{1,2,0:T(8,128)(2,1)S(1)}, bf16[3,96,48]{1,2,0:T(8,128)(2,1)S(1)}, u32[]{:S(2)}, u32[]{:S(2)}) collective-permute-start(bf16[3,96,48]{1,2,0:T(8,128)(2,1)S(1)} %copy-done.15), channel_id=1, source_target_pairs={{0,2},{2,4},{4,6},{6,0},{1,3},{3,5},{5,7},{7,1},{8,10},{10,12},{12... | collective-permute-start | bytes 82952 | tf_op jit(solution)/shard_map/ppermute | solution.py:63
  25.7 6.5 %collective-permute-start.1 = (bf16[3,96,48]{1,2,0:T(8,128)(2,1)S(1)}, bf16[3,96,48]{1,2,0:T(8,128)(2,1)S(1)}, u32[]{:S(2)}, u32[]{:S(2)}) collective-permute-start(bf16[3,96,48]{1,2,0:T(8,128)(2,1)S(1)} %copy-done.15), channel_id=1, source_target_pairs={{0,4},{2,6},{4,0},{6,2},{1,5},{3,7},{5,1},{7,3},{8,12},{10,14},{12... | collective-permute-start | bytes 82952 | tf_op jit(solution)/shard_map/ppermute | solution.py:63
  27.3 4.9 %collective-permute-start.2 = (bf16[3,96,48]{1,2,0:T(8,128)(2,1)S(1)}, bf16[3,96,48]{1,2,0:T(8,128)(2,1)S(1)}, u32[]{:S(2)}, u32[]{:S(2)}) collective-permute-start(bf16[3,96,48]{1,2,0:T(8,128)(2,1)S(1)} %copy-done.15), channel_id=1, source_target_pairs={{0,6},{2,0},{4,2},{6,4},{1,7},{3,1},{5,3},{7,5},{8,14},{10,8},{12,... | collective-permute-start | bytes 82952 | tf_op jit(solution)/shard_map/ppermute | solution.py:63
  28.8 27.1 %all-to-all-start.1 = ((bf16[8,1,16,384]{3,0,1,2:T(8,128)(2,1)}), bf16[8,1,16,384]{3,0,1,2:T(8,128)(2,1)S(1)}, u32[]{:S(2)}, u32[]{:S(2)}) async-start(bf16[8,1,16,384]{3,0,1,2:T(8,128)(2,1)} %copy.78), calls=%async_computation.1 | async-start | bytes 196608 | tf_op jit(solution)/shard_map/all_to_all | solution.py:112
  32.1 60.1 %copy-start.20 = (bf16[6,384]{1,0:T(8,128)(2,1)}, bf16[6,384]{1,0:T(8,128)(2,1)S(1)}, u32[]{:S(2)}) copy-start(bf16[6,384]{1,0:T(8,128)(2,1)S(1)} %get-tuple-element.22) | copy-start | bytes 13828
  55.8 12.4 %all-to-all-start = ((bf16[8,1,16,384]{3,2,1,0:T(8,128)(2,1)}), bf16[8,1,16,384]{3,2,1,0:T(8,128)(2,1)S(1)}, u32[]{:S(2)}, u32[]{:S(2)}) async-start(bf16[8,1,16,384]{3,2,1,0:T(8,128)(2,1)} %param.5), calls=%async_computation | async-start | bytes 196608 | tf_op jit(solution)/shard_map/all_to_all | solution.py:104
  63.5 0.6 copy-start.6
  64.1 0.6 copy-start.8
  65.1 0.6 copy-start.11
  65.1 1.0 copy-start.13
  65.5 0.9 copy-start.2
  65.5 0.9 copy-start.16
  68.3 12.5 %all-to-all-start.2 = ((bf16[32,1,4,384]{3,2,1,0:T(4,128)(2,1)}), bf16[32,1,4,384]{3,2,1,0:T(4,128)(2,1)S(1)}, u32[]{:S(2)}, u32[]{:S(2)}) async-start(bf16[32,1,4,384]{3,2,1,0:T(4,128)(2,1)} %copy.86), calls=%async_computation.2 | async-start | bytes 196608 | tf_op jit(solution)/shard_map/all_to_all | solution.py:87
  84.0 3.9 %copy-start.4 = (f32[4,32,6]{1,2,0:T(8,128)}, f32[4,32,6]{1,2,0:T(8,128)S(1)}, u32[]{:S(2)}) copy-start(f32[4,32,6]{1,2,0:T(8,128)S(1)} %fusion.87) | copy-start | bytes 9220
  86.1 2.5 %copy-start = (bf16[3,384,1152]{1,2,0:T(8,128)(2,1)S(1)}, bf16[3,384,1152]{1,2,0:T(8,128)(2,1)}, u32[]{:S(2)}) copy-start(bf16[3,384,1152]{1,2,0:T(8,128)(2,1)} %all-gather.2.cloned.1.call-done) | copy-start | bytes 7962628
  95.9 1.3 copy-start.5
  95.9 3.7 %copy-start.1 = (f32[4,32,384]{2,1,0:T(8,128)S(1)}, f32[4,32,384]{2,1,0:T(8,128)}, u32[]{:S(2)}) copy-start(f32[4,32,384]{2,1,0:T(8,128)} %get-tuple-element.25) | copy-start | bytes 589828
  100.6 1.7 %copy-start.19 = (f32[4,32]{1,0:T(4,128)S(1)}, f32[4,32]{1,0:T(4,128)}, u32[]{:S(2)}) copy-start(f32[4,32]{1,0:T(4,128)} %add.158) | copy-start | bytes 1540
  100.6 5.1 %copy-start.17 = (f32[4,6,32]{2,1,0:T(8,128)S(1)}, f32[4,6,32]{2,1,0:T(8,128)}, u32[]{:S(2)}) copy-start(f32[4,6,32]{2,1,0:T(8,128)} %copy-done.16) | copy-start | bytes 9220
  102.3 11.2 %copy-start.3 = (f32[1,4,6,32,32]{3,4,2,1,0:T(8,128)S(1)}, f32[1,4,6,32,32]{3,4,2,1,0:T(8,128)}, u32[]{:S(2)}) copy-start(f32[1,4,6,32,32]{3,4,2,1,0:T(8,128)} %copy-done.2) | copy-start | bytes 294916
  103.2 10.2 %all-to-all-start.3 = ((bf16[32,1,4,384]{3,2,1,0:T(4,128)(2,1)}), bf16[32,1,4,384]{3,2,1,0:T(4,128)(2,1)S(1)}, u32[]{:S(2)}, u32[]{:S(2)}) async-start(bf16[32,1,4,384]{3,2,1,0:T(4,128)(2,1)} %bitcast.118), calls=%async_computation.3 | async-start | bytes 196608 | tf_op jit(solution)/shard_map/all_to_all | solution.py:98
  113.6 1.1 copy-start.14
  113.6 1.1 copy-start.21
  114.6 0.9 copy-start.12
  115.5 0.7 copy-start.7
  115.5 1.4 %copy-start.9 = (f32[32,4,6]{0,2,1:T(8,128)S(1)}, f32[32,4,6]{0,2,1:T(8,128)}, u32[]{:S(2)}) copy-start(f32[32,4,6]{0,2,1:T(8,128)} %copy-done.8) | copy-start | bytes 9220
  117.7 1.6 %copy-start.18 = (f32[32,4]{0,1:T(4,128)S(1)}, f32[32,4]{0,1:T(4,128)}, u32[]{:S(2)}) copy-start(f32[32,4]{0,1:T(4,128)} %add.159) | copy-start | bytes 1540
Sparse Core Ops, SparseCore 0:
  22.9 36.2 all-gather.1

commit v16 on v15

--- a/solution.py
+++ b/solution.py
@@ -17,7 +17,7 @@
     head_size = vector.shape[-1] // HEADS
     sums = jnp.dot(vector * vector, ones, precision=HIGHEST)
     scale = lax.rsqrt(sums / head_size + 1e-06)
-    return (vector * jnp.dot(scale, ones.T, precision=HIGHEST)).astype(jnp.bfloat16)
+    return (vector * jnp.dot(scale, ones.T, precision=lax.Precision.HIGH)).astype(jnp.bfloat16)
 
 
 def sublayer(line_rows, w_inner, w_outer):

time: 135 us -> 134 us (level)
  no operation moved by 1% of the time
where the time goes in v16:
time: 134 us; the launch traced here: 133 us
  blocking collectives  29.4 us (22%)
  starting transfers between devices  28.1 us (21%)
  matrix products  24.3 us (18%)
  waiting for transfers between devices  22.2 us (17%)
  between operations  14.2 us (11%)
  local copies, waits for them, and re-layouts  10.4 us (8%)
  other arithmetic  4.24 us (3%)
    all_gather x1, blocking collectives, full_weights(): outp = lax.all_gather(over_gy(w_output), ('gz', 'gx'), axis=2, tiled=True)  22.7 us
    ppermute x6, starting transfers between devices, over_gy(): lax.ppermute(block, 'gy', [(i, (i + s) % ny) for i in range(ny)])  12.3 us
    all_to_all x1, waiting for transfers between devices, from_planes(): return lax.all_to_all(parts, ALL, 0, 0, tiled=True)  7.56 us
    dot_general x6, matrix products, sublayer(): packed = jnp.dot(normed, w_inner, preferred_element_type=jnp.float32)  7.22 us
    all_to_all x1, waiting for transfers between devices, to_planes(): got = lax.all_to_all(depth_lines, ALL, 0, 0, tiled=True)  7.19 us
    all_to_all x1, blocking collectives, local(): return lax.all_to_all(grad_zero, 'gz', 0, 2, tiled=True)  6.67 us
    ppermute x6, waiting for transfers between devices, over_gy(): lax.ppermute(block, 'gy', [(i, (i + s) % ny) for i in range(ny)])  6.16 us
    all_to_all x1, starting transfers between devices, to_planes(): got = lax.all_to_all(depth_lines, ALL, 0, 0, tiled=True)  5.05 us
  transfers between devices with their start and end apart: 11, of which 5 were waited for; matrix products, arithmetic and copies ran while one was open for 5% of the time, Pallas kernels for 0%

profile of v16, /device:TPU:0, one launch (start us, length us, event | category | flops | bytes accessed | tf_op | source)
XLA Modules:
  0.0 132.9 jit_solution(11607030641777172922)
XLA Ops:
  6.5 3.1 %collective-permute-start.3 = (bf16[3,96,144]{1,2,0:T(8,128)(2,1)}, bf16[3,96,144]{1,2,0:T(8,128)(2,1)S(1)}, u32[]{:S(2)}, u32[]{:S(2)}) collective-permute-start(bf16[3,96,144]{1,2,0:T(8,128)(2,1)} %param.6), channel_id=1, source_target_pairs={{0,2},{2,4},{4,6},{6,0},{1,3},{3,5},{5,7},{7,1},{8,10},{10,12},{12... | collective-permute-start | bytes 248840 | tf_op jit(solution)/shard_map/ppermute | solution.py:63
  9.6 2.6 %collective-permute-start.4 = (bf16[3,96,144]{1,2,0:T(8,128)(2,1)}, bf16[3,96,144]{1,2,0:T(8,128)(2,1)S(1)}, u32[]{:S(2)}, u32[]{:S(2)}) collective-permute-start(bf16[3,96,144]{1,2,0:T(8,128)(2,1)} %param.6), channel_id=1, source_target_pairs={{0,4},{2,6},{4,0},{6,2},{1,5},{3,7},{5,1},{7,3},{8,12},{10,14},{12... | collective-permute-start | bytes 248840 | tf_op jit(solution)/shard_map/ppermute | solution.py:63
  12.2 1.3 %collective-permute-start.5 = (bf16[3,96,144]{1,2,0:T(8,128)(2,1)}, bf16[3,96,144]{1,2,0:T(8,128)(2,1)S(1)}, u32[]{:S(2)}, u32[]{:S(2)}) collective-permute-start(bf16[3,96,144]{1,2,0:T(8,128)(2,1)} %param.6), channel_id=1, source_target_pairs={{0,6},{2,0},{4,2},{6,4},{1,7},{3,1},{5,3},{7,5},{8,14},{10,8},{12,... | collective-permute-start | bytes 248840 | tf_op jit(solution)/shard_map/ppermute | solution.py:63
  13.6 2.3 %collective-permute-done.3 = bf16[3,96,144]{1,2,0:T(8,128)(2,1)S(1)} collective-permute-done((bf16[3,96,144]{1,2,0:T(8,128)(2,1)}, bf16[3,96,144]{1,2,0:T(8,128)(2,1)S(1)}, u32[]{:S(2)}, u32[]{:S(2)}) %collective-permute-start.3) | collective-permute-done | bytes 82976 | tf_op jit(solution)/shard_map/ppermute | solution.py:63
  15.8 3.9 %collective-permute-done.4 = bf16[3,96,144]{1,2,0:T(8,128)(2,1)S(1)} collective-permute-done((bf16[3,96,144]{1,2,0:T(8,128)(2,1)}, bf16[3,96,144]{1,2,0:T(8,128)(2,1)S(1)}, u32[]{:S(2)}, u32[]{:S(2)}) %collective-permute-start.4) | collective-permute-done | bytes 82976 | tf_op jit(solution)/shard_map/ppermute | solution.py:63
  19.7 1.0 pad_maximum_fusion
  20.8 0.6 gather_fusion.1
  21.7 1.0 reshape.892
  22.8 2.9 %collective-permute-start = (bf16[3,96,48]{1,2,0:T(8,128)(2,1)S(1)}, bf16[3,96,48]{1,2,0:T(8,128)(2,1)S(1)}, u32[]{:S(2)}, u32[]{:S(2)}) collective-permute-start(bf16[3,96,48]{1,2,0:T(8,128)(2,1)S(1)} %copy-done.15), channel_id=1, source_target_pairs={{0,2},{2,4},{4,6},{6,0},{1,3},{3,5},{5,7},{7,1},{8,10},{10,12},{12... | collective-permute-start | bytes 82952 | tf_op jit(solution)/shard_map/ppermute | solution.py:63
  25.7 1.6 %collective-permute-start.1 = (bf16[3,96,48]{1,2,0:T(8,128)(2,1)S(1)}, bf16[3,96,48]{1,2,0:T(8,128)(2,1)S(1)}, u32[]{:S(2)}, u32[]{:S(2)}) collective-permute-start(bf16[3,96,48]{1,2,0:T(8,128)(2,1)S(1)} %copy-done.15), channel_id=1, source_target_pairs={{0,4},{2,6},{4,0},{6,2},{1,5},{3,7},{5,1},{7,3},{8,12},{10,14},{12... | collective-permute-start | bytes 82952 | tf_op jit(solution)/shard_map/ppermute | solution.py:63
  27.3 0.8 collective-permute-start.2
  28.1 0.7 copy.78
  28.8 3.3 %all-to-all-start.1 = ((bf16[8,1,16,384]{3,0,1,2:T(8,128)(2,1)}), bf16[8,1,16,384]{3,0,1,2:T(8,128)(2,1)S(1)}, u32[]{:S(2)}, u32[]{:S(2)}) async-start(bf16[8,1,16,384]{3,0,1,2:T(8,128)(2,1)} %copy.78), calls=%async_computation.1 | async-start | bytes 196608 | tf_op jit(solution)/shard_map/all_to_all | solution.py:112
  32.2 0.6 gather_fusion
  33.1 22.7 %all_gather.6 = bf16[3,384,384]{1,2,0:T(8,128)(2,1)S(1)} all-gather(bf16[3,384,48]{1,2,0:T(8,128)(2,1)S(1)} %reshape.890), channel_id=1, replica_groups=mesh['gz'=4,'gy'=4,'gx'=2] {'gz','gx'}, dimensions={2}, use_global_device_ids=true | all-gather | bytes 995328 | tf_op jit(solution)/shard_map/all_gather | solution.py:69
  55.8 4.9 %all-to-all-start = ((bf16[8,1,16,384]{3,2,1,0:T(8,128)(2,1)}), bf16[8,1,16,384]{3,2,1,0:T(8,128)(2,1)S(1)}, u32[]{:S(2)}, u32[]{:S(2)}) async-start(bf16[8,1,16,384]{3,2,1,0:T(8,128)(2,1)} %param.5), calls=%async_computation | async-start | bytes 196608 | tf_op jit(solution)/shard_map/all_to_all | solution.py:104
  60.9 0.7 add.159
  61.5 1.6 %convolution_bitcast_fusion.2 = f32[1,32,4,1152]{3,1,2,0:T(8,128)S(1)} fusion(bf16[3,384,1152]{1,2,0:T(8,128)(2,1)} %all-gather.2.cloned.1.call-done, bf16[8,1,4,4,384]{4,0,3,2,1:T(8,128)(2,1)S(1)} %bitcast.588, f32[4,8,4]{1,2,0:T(4,128)S(1)} %get-tuple-element.16), kind=kOutput, calls=%fused_computation.4 | convolution fusion | flops 113393664 | bytes 1573376 | tf_op jit(solution)/shard_map/jvp()/dot_general | solution.py:30
  63.1 0.4 fusion.89
  63.5 0.4 fusion.88
  64.4 0.3 copy-done.8
  65.7 0.4 fusion.1
  66.3 0.7 copy.86
  67.0 1.2 all-to-all-done
  68.3 5.0 %all-to-all-start.2 = ((bf16[32,1,4,384]{3,2,1,0:T(4,128)(2,1)}), bf16[32,1,4,384]{3,2,1,0:T(4,128)(2,1)S(1)}, u32[]{:S(2)}, u32[]{:S(2)}) async-start(bf16[32,1,4,384]{3,2,1,0:T(4,128)(2,1)} %copy.86), calls=%async_computation.2 | async-start | bytes 196608 | tf_op jit(solution)/shard_map/all_to_all | solution.py:87
  73.5 7.2 %all-to-all-done.2 = bf16[32,1,4,384]{3,2,1,0:T(4,128)(2,1)S(1)} async-done(((bf16[32,1,4,384]{3,2,1,0:T(4,128)(2,1)}), bf16[32,1,4,384]{3,2,1,0:T(4,128)(2,1)S(1)}, u32[]{:S(2)}, u32[]{:S(2)}) %all-to-all-start.2) | async-done | bytes 98336 | tf_op jit(solution)/shard_map/all_to_all | solution.py:87
  80.9 0.6 multiply_add_fusion
  81.6 1.6 %convolution_bitcast_fusion.1 = f32[1,4,32,1152]{3,2,1,0:T(8,128)S(1)} fusion(bf16[4,32,384]{2,1,0:T(8,128)(2,1)S(1)} %convert_element_type.547, bf16[3,384,1152]{1,2,0:T(8,128)(2,1)} %all-gather.2.cloned.1.call-done), kind=kOutput, calls=%fused_computation.3 | convolution fusion | flops 113246208 | bytes 1572864 | tf_op jit(solution)/shard_map/jvp()/dot_general | solution.py:30
  83.2 0.4 fusion.86
  83.6 0.4 fusion.87
  84.0 0.7 copy_bitcast_fusion
  85.0 1.0 reshape.923
  86.0 1.0 fusion.204
  86.9 0.8 fusion.335
  87.8 0.3 multiply_reduce_fusion.3
  88.1 0.3 multiply_reduce_fusion.6
  88.4 0.4 convolution_bitcast_fusion
  88.9 0.4 fusion.85
  89.2 0.4 fusion.84
  90.2 0.3 fusion.336
  90.9 0.7 fusion.129
  91.6 0.3 fusion.10
  92.5 0.4 add_add_fusion.8
  93.2 0.3 add_add_fusion.7
  93.5 0.4 multiply_reduce_fusion.5
  94.3 0.7 multiply_reduce_fusion.2
  95.0 0.4 multiply_reduce_fusion.9
  95.5 0.5 multiply_reduce_fusion.1
  96.3 0.4 add_add_fusion.5
  96.7 0.9 fusion.80
  97.6 1.4 %add.158 = f32[4,32]{1,0:T(4,128)} reshape(f32[4,2,4,4]{3,2,1,0:T(4,128)} %get-tuple-element.13) | data formatting | bytes 1024 | tf_op jit(solution)/shard_map/jvp()/add | solution.py:29
  98.9 1.0 add_add_fusion.4
  100.0 1.6 %multiply_reduce_fusion.4 = (f32[4,32]{1,0:T(4,128)S(1)}, f32[4,32,384]{2,1,0:T(8,128)S(1)}) fusion(f32[4,32,384]{2,1,0:T(8,128)S(1)} %reshape.923, bf16[3,384,1152]{1,2,0:T(8,128)(2,1)} %all-gather.2.cloned.1.call-done, f32[1,4,32,384]{3,2,1,0:T(8,128)S(1)} %add_add_fusion.4, f32[1,4,32,384]{3,2,1,0:T(8,128)S(1)} %add_add_fusion.5, ...), kind=kOutput, calls=%fused_computation.248 | convolution fusion | flops 113885056 | bytes 1769984 | tf_op jit(solution)/shard_map/transpose(jvp())/dot_general | solution.py:30
  101.9 0.7 copy.92
  102.5 2.6 %all-to-all-start.3 = ((bf16[32,1,4,384]{3,2,1,0:T(4,128)(2,1)}), bf16[32,1,4,384]{3,2,1,0:T(4,128)(2,1)S(1)}, u32[]{:S(2)}, u32[]{:S(2)}) async-start(bf16[32,1,4,384]{3,2,1,0:T(4,128)(2,1)} %bitcast.118), calls=%async_computation.3 | async-start | bytes 196608 | tf_op jit(solution)/shard_map/all_to_all | solution.py:98
  105.1 7.6 %all-to-all-done.3 = bf16[32,1,4,384]{3,2,1,0:T(4,128)(2,1)S(1)} async-done(((bf16[32,1,4,384]{3,2,1,0:T(4,128)(2,1)}), bf16[32,1,4,384]{3,2,1,0:T(4,128)(2,1)S(1)}, u32[]{:S(2)}, u32[]{:S(2)}) %all-to-all-start.3) | async-done | bytes 98336 | tf_op jit(solution)/shard_map/all_to_all | solution.py:98
  113.2 0.7 fusion.125
  114.3 0.5 copy-done.12
  115.1 0.4 copy-done.7
  115.8 0.4 add_add_fusion.2
  116.5 0.3 add_add_fusion.1
  116.9 1.6 %fusion.181 = (f32[32,4]{0,1:T(4,128)S(1)}, f32[32,4,384]{2,0,1:T(8,128)S(1)}) fusion(bf16[3,384,1152]{1,2,0:T(8,128)(2,1)} %all-gather.2.cloned.1.call-done, f32[1,32,4,384]{3,1,2,0:T(8,128)S(1)} %add_add_fusion.1, f32[1,32,4,384]{3,1,2,0:T(8,128)S(1)} %add_add_fusion.2, bf16[1,32,4,384]{3,1,2,0:T(8,128)(2,1)S(1)} %fusion.72, ...), kind=kOutput, calls=%fused_computation.245 | convolution fusion | flops 113934208 | bytes 1671680 | tf_op jit(solution)/shard_map/transpose(jvp())/dot_general | solution.py:30
  118.7 6.7 %all_to_all.42 = bf16[32,1,4,384]{3,2,1,0:T(4,128)(2,1)S(1)} all-to-all(bf16[32,1,4,384]{3,2,1,0:T(4,128)(2,1)S(1)} %copy.96), channel_id=1, replica_groups=mesh['gz'=4,'gy'=4,'gx'=2] {'gz'}, dimensions={0} | all-to-all | bytes 196608 | tf_op jit(solution)/shard_map/all_to_all | solution.py:121
  125.4 0.7 all_to_all.36
  (105 shorter events, 7.7 us)
Async XLA Ops:
  6.5 55.0 %all-gather.2.cloned.1.call-start = ((), (), s32[]{:S(2)}) async-start(), calls=%async_computation.5 | async-start | bytes 2985984 | tf_op jit(solution)/shard_map/all_gather | solution.py:68
  6.5 9.3 %collective-permute-start.3 = (bf16[3,96,144]{1,2,0:T(8,128)(2,1)}, bf16[3,96,144]{1,2,0:T(8,128)(2,1)S(1)}, u32[]{:S(2)}, u32[]{:S(2)}) collective-permute-start(bf16[3,96,144]{1,2,0:T(8,128)(2,1)} %param.6), channel_id=1, source_target_pairs={{0,2},{2,4},{4,6},{6,0},{1,3},{3,5},{5,7},{7,1},{8,10},{10,12},{12... | collective-permute-start | bytes 248840 | tf_op jit(solution)/shard_map/ppermute | solution.py:63
  9.6 10.1 %collective-permute-start.4 = (bf16[3,96,144]{1,2,0:T(8,128)(2,1)}, bf16[3,96,144]{1,2,0:T(8,128)(2,1)S(1)}, u32[]{:S(2)}, u32[]{:S(2)}) collective-permute-start(bf16[3,96,144]{1,2,0:T(8,128)(2,1)} %param.6), channel_id=1, source_target_pairs={{0,4},{2,6},{4,0},{6,2},{1,5},{3,7},{5,1},{7,3},{8,12},{10,14},{12... | collective-permute-start | bytes 248840 | tf_op jit(solution)/shard_map/ppermute | solution.py:63
  12.2 7.5 %collective-permute-start.5 = (bf16[3,96,144]{1,2,0:T(8,128)(2,1)}, bf16[3,96,144]{1,2,0:T(8,128)(2,1)S(1)}, u32[]{:S(2)}, u32[]{:S(2)}) collective-permute-start(bf16[3,96,144]{1,2,0:T(8,128)(2,1)} %param.6), channel_id=1, source_target_pairs={{0,6},{2,0},{4,2},{6,4},{1,7},{3,1},{5,3},{7,5},{8,14},{10,8},{12,... | collective-permute-start | bytes 248840 | tf_op jit(solution)/shard_map/ppermute | solution.py:63
  21.5 1.3 copy-start.15
  21.5 6.6 %copy-start.10 = (bf16[8,1,16,384]{3,2,1,0:T(8,128)(2,1)S(1)}, bf16[8,1,16,384]{3,2,1,0:T(8,128)(2,1)}, u32[]{:S(2)}) copy-start(bf16[8,1,16,384]{3,2,1,0:T(8,128)(2,1)} %param.4) | copy-start | bytes 294916
  22.8 9.3 %collective-permute-start = (bf16[3,96,48]{1,2,0:T(8,128)(2,1)S(1)}, bf16[3,96,48]{1,2,0:T(8,128)(2,1)S(1)}, u32[]{:S(2)}, u32[]{:S(2)}) collective-permute-start(bf16[3,96,48]{1,2,0:T(8,128)(2,1)S(1)} %copy-done.15), channel_id=1, source_target_pairs={{0,2},{2,4},{4,6},{6,0},{1,3},{3,5},{5,7},{7,1},{8,10},{10,12},{12... | collective-permute-start | bytes 82952 | tf_op jit(solution)/shard_map/ppermute | solution.py:63
  25.7 6.5 %collective-permute-start.1 = (bf16[3,96,48]{1,2,0:T(8,128)(2,1)S(1)}, bf16[3,96,48]{1,2,0:T(8,128)(2,1)S(1)}, u32[]{:S(2)}, u32[]{:S(2)}) collective-permute-start(bf16[3,96,48]{1,2,0:T(8,128)(2,1)S(1)} %copy-done.15), channel_id=1, source_target_pairs={{0,4},{2,6},{4,0},{6,2},{1,5},{3,7},{5,1},{7,3},{8,12},{10,14},{12... | collective-permute-start | bytes 82952 | tf_op jit(solution)/shard_map/ppermute | solution.py:63
  27.3 4.9 %collective-permute-start.2 = (bf16[3,96,48]{1,2,0:T(8,128)(2,1)S(1)}, bf16[3,96,48]{1,2,0:T(8,128)(2,1)S(1)}, u32[]{:S(2)}, u32[]{:S(2)}) collective-permute-start(bf16[3,96,48]{1,2,0:T(8,128)(2,1)S(1)} %copy-done.15), channel_id=1, source_target_pairs={{0,6},{2,0},{4,2},{6,4},{1,7},{3,1},{5,3},{7,5},{8,14},{10,8},{12,... | collective-permute-start | bytes 82952 | tf_op jit(solution)/shard_map/ppermute | solution.py:63
  28.8 27.1 %all-to-all-start.1 = ((bf16[8,1,16,384]{3,0,1,2:T(8,128)(2,1)}), bf16[8,1,16,384]{3,0,1,2:T(8,128)(2,1)S(1)}, u32[]{:S(2)}, u32[]{:S(2)}) async-start(bf16[8,1,16,384]{3,0,1,2:T(8,128)(2,1)} %copy.78), calls=%async_computation.1 | async-start | bytes 196608 | tf_op jit(solution)/shard_map/all_to_all | solution.py:112
  32.1 59.8 %copy-start.20 = (bf16[6,384]{1,0:T(8,128)(2,1)}, bf16[6,384]{1,0:T(8,128)(2,1)S(1)}, u32[]{:S(2)}) copy-start(bf16[6,384]{1,0:T(8,128)(2,1)S(1)} %get-tuple-element.22) | copy-start | bytes 13828
  55.8 12.4 %all-to-all-start = ((bf16[8,1,16,384]{3,2,1,0:T(8,128)(2,1)}), bf16[8,1,16,384]{3,2,1,0:T(8,128)(2,1)S(1)}, u32[]{:S(2)}, u32[]{:S(2)}) async-start(bf16[8,1,16,384]{3,2,1,0:T(8,128)(2,1)} %param.5), calls=%async_computation | async-start | bytes 196608 | tf_op jit(solution)/shard_map/all_to_all | solution.py:104
  63.5 0.6 copy-start.6
  64.1 0.6 copy-start.8
  65.1 0.6 copy-start.11
  65.1 1.0 copy-start.13
  65.4 0.9 copy-start.2
  65.4 0.9 copy-start.16
  68.3 12.5 %all-to-all-start.2 = ((bf16[32,1,4,384]{3,2,1,0:T(4,128)(2,1)}), bf16[32,1,4,384]{3,2,1,0:T(4,128)(2,1)S(1)}, u32[]{:S(2)}, u32[]{:S(2)}) async-start(bf16[32,1,4,384]{3,2,1,0:T(4,128)(2,1)} %copy.86), calls=%async_computation.2 | async-start | bytes 196608 | tf_op jit(solution)/shard_map/all_to_all | solution.py:87
  84.0 3.8 %copy-start.4 = (f32[4,32,6]{1,2,0:T(8,128)}, f32[4,32,6]{1,2,0:T(8,128)S(1)}, u32[]{:S(2)}) copy-start(f32[4,32,6]{1,2,0:T(8,128)S(1)} %fusion.87) | copy-start | bytes 9220
  86.0 2.5 %copy-start = (bf16[3,384,1152]{1,2,0:T(8,128)(2,1)S(1)}, bf16[3,384,1152]{1,2,0:T(8,128)(2,1)}, u32[]{:S(2)}) copy-start(bf16[3,384,1152]{1,2,0:T(8,128)(2,1)} %all-gather.2.cloned.1.call-done) | copy-start | bytes 7962628
  95.4 1.2 copy-start.5
  95.5 3.5 %copy-start.1 = (f32[4,32,384]{2,1,0:T(8,128)S(1)}, f32[4,32,384]{2,1,0:T(8,128)}, u32[]{:S(2)}) copy-start(f32[4,32,384]{2,1,0:T(8,128)} %get-tuple-element.25) | copy-start | bytes 589828
  100.0 1.7 %copy-start.19 = (f32[4,32]{1,0:T(4,128)S(1)}, f32[4,32]{1,0:T(4,128)}, u32[]{:S(2)}) copy-start(f32[4,32]{1,0:T(4,128)} %add.158) | copy-start | bytes 1540
  100.0 5.1 %copy-start.17 = (f32[4,6,32]{2,1,0:T(8,128)S(1)}, f32[4,6,32]{2,1,0:T(8,128)}, u32[]{:S(2)}) copy-start(f32[4,6,32]{2,1,0:T(8,128)} %copy-done.16) | copy-start | bytes 9220
  101.7 11.2 %copy-start.3 = (f32[1,4,6,32,32]{3,4,2,1,0:T(8,128)S(1)}, f32[1,4,6,32,32]{3,4,2,1,0:T(8,128)}, u32[]{:S(2)}) copy-start(f32[1,4,6,32,32]{3,4,2,1,0:T(8,128)} %copy-done.2) | copy-start | bytes 294916
  102.5 10.2 %all-to-all-start.3 = ((bf16[32,1,4,384]{3,2,1,0:T(4,128)(2,1)}), bf16[32,1,4,384]{3,2,1,0:T(4,128)(2,1)S(1)}, u32[]{:S(2)}, u32[]{:S(2)}) async-start(bf16[32,1,4,384]{3,2,1,0:T(4,128)(2,1)} %bitcast.118), calls=%async_computation.3 | async-start | bytes 196608 | tf_op jit(solution)/shard_map/all_to_all | solution.py:98
  112.9 1.1 copy-start.14
  112.9 1.1 copy-start.21
  113.9 0.9 copy-start.12
  114.8 0.7 copy-start.7
  114.8 1.4 %copy-start.9 = (f32[32,4,6]{0,2,1:T(8,128)S(1)}, f32[32,4,6]{0,2,1:T(8,128)}, u32[]{:S(2)}) copy-start(f32[32,4,6]{0,2,1:T(8,128)} %copy-done.8) | copy-start | bytes 9220
  116.8 1.6 %copy-start.18 = (f32[32,4]{0,1:T(4,128)S(1)}, f32[32,4]{0,1:T(4,128)}, u32[]{:S(2)}) copy-start(f32[32,4]{0,1:T(4,128)} %add.159) | copy-start | bytes 1540
Sparse Core Ops, SparseCore 0:
  22.9 36.2 all-gather.1

commit v17 on v16

--- a/solution.py
+++ b/solution.py
@@ -15,7 +15,7 @@
 
 def head_norm(vector, ones):
     head_size = vector.shape[-1] // HEADS
-    sums = jnp.dot(vector * vector, ones, precision=HIGHEST)
+    sums = jnp.dot(vector * vector, ones, precision=lax.Precision.HIGH)
     scale = lax.rsqrt(sums / head_size + 1e-06)
     return (vector * jnp.dot(scale, ones.T, precision=lax.Precision.HIGH)).astype(jnp.bfloat16)
 

time: 134 us -> 133 us (level)
  no operation moved by 1% of the time
where the time goes in v17:
time: 133 us; the launch traced here: 132 us
  blocking collectives  29.4 us (22%)
  starting transfers between devices  28 us (21%)
  matrix products  23.5 us (18%)
  waiting for transfers between devices  22.3 us (17%)
  between operations  14.2 us (11%)
  local copies, waits for them, and re-layouts  10.5 us (8%)
  other arithmetic  4.24 us (3%)
    all_gather x1, blocking collectives, full_weights(): outp = lax.all_gather(over_gy(w_output), ('gz', 'gx'), axis=2, tiled=True)  22.7 us
    ppermute x6, starting transfers between devices, over_gy(): lax.ppermute(block, 'gy', [(i, (i + s) % ny) for i in range(ny)])  12.3 us
    all_to_all x1, waiting for transfers between devices, from_planes(): return lax.all_to_all(parts, ALL, 0, 0, tiled=True)  7.38 us
    all_to_all x1, waiting for transfers between devices, to_planes(): got = lax.all_to_all(depth_lines, ALL, 0, 0, tiled=True)  7.37 us
    dot_general x6, matrix products, sublayer(): packed = jnp.dot(normed, w_inner, preferred_element_type=jnp.float32)  7.22 us
    all_to_all x1, blocking collectives, local(): return lax.all_to_all(grad_zero, 'gz', 0, 2, tiled=True)  6.67 us
    ppermute x6, waiting for transfers between devices, over_gy(): lax.ppermute(block, 'gy', [(i, (i + s) % ny) for i in range(ny)])  6.16 us
    all_to_all x1, starting transfers between devices, block_to_plane(): got = lax.all_to_all(block, ('gy', 'gx'), 0, 0, tiled=True)  4.9 us
  transfers between devices with their start and end apart: 11, of which 5 were waited for; matrix products, arithmetic and copies ran while one was open for 5% of the time, Pallas kernels for 0%

profile of v17, /device:TPU:0, one launch (start us, length us, event | category | flops | bytes accessed | tf_op | source)
XLA Modules:
  0.0 132.1 jit_solution(2418500151631006704)
XLA Ops:
  6.5 3.1 %collective-permute-start.3 = (bf16[3,96,144]{1,2,0:T(8,128)(2,1)}, bf16[3,96,144]{1,2,0:T(8,128)(2,1)S(1)}, u32[]{:S(2)}, u32[]{:S(2)}) collective-permute-start(bf16[3,96,144]{1,2,0:T(8,128)(2,1)} %param.6), channel_id=1, source_target_pairs={{0,2},{2,4},{4,6},{6,0},{1,3},{3,5},{5,7},{7,1},{8,10},{10,12},{12... | collective-permute-start | bytes 248840 | tf_op jit(solution)/shard_map/ppermute | solution.py:63
  9.6 2.6 %collective-permute-start.4 = (bf16[3,96,144]{1,2,0:T(8,128)(2,1)}, bf16[3,96,144]{1,2,0:T(8,128)(2,1)S(1)}, u32[]{:S(2)}, u32[]{:S(2)}) collective-permute-start(bf16[3,96,144]{1,2,0:T(8,128)(2,1)} %param.6), channel_id=1, source_target_pairs={{0,4},{2,6},{4,0},{6,2},{1,5},{3,7},{5,1},{7,3},{8,12},{10,14},{12... | collective-permute-start | bytes 248840 | tf_op jit(solution)/shard_map/ppermute | solution.py:63
  12.2 1.3 %collective-permute-start.5 = (bf16[3,96,144]{1,2,0:T(8,128)(2,1)}, bf16[3,96,144]{1,2,0:T(8,128)(2,1)S(1)}, u32[]{:S(2)}, u32[]{:S(2)}) collective-permute-start(bf16[3,96,144]{1,2,0:T(8,128)(2,1)} %param.6), channel_id=1, source_target_pairs={{0,6},{2,0},{4,2},{6,4},{1,7},{3,1},{5,3},{7,5},{8,14},{10,8},{12,... | collective-permute-start | bytes 248840 | tf_op jit(solution)/shard_map/ppermute | solution.py:63
  13.6 2.3 %collective-permute-done.3 = bf16[3,96,144]{1,2,0:T(8,128)(2,1)S(1)} collective-permute-done((bf16[3,96,144]{1,2,0:T(8,128)(2,1)}, bf16[3,96,144]{1,2,0:T(8,128)(2,1)S(1)}, u32[]{:S(2)}, u32[]{:S(2)}) %collective-permute-start.3) | collective-permute-done | bytes 82976 | tf_op jit(solution)/shard_map/ppermute | solution.py:63
  15.8 3.9 %collective-permute-done.4 = bf16[3,96,144]{1,2,0:T(8,128)(2,1)S(1)} collective-permute-done((bf16[3,96,144]{1,2,0:T(8,128)(2,1)}, bf16[3,96,144]{1,2,0:T(8,128)(2,1)S(1)}, u32[]{:S(2)}, u32[]{:S(2)}) %collective-permute-start.4) | collective-permute-done | bytes 82976 | tf_op jit(solution)/shard_map/ppermute | solution.py:63
  19.7 1.0 pad_maximum_fusion
  20.8 0.6 gather_fusion.1
  21.7 1.0 reshape.892
  22.8 2.9 %collective-permute-start = (bf16[3,96,48]{1,2,0:T(8,128)(2,1)S(1)}, bf16[3,96,48]{1,2,0:T(8,128)(2,1)S(1)}, u32[]{:S(2)}, u32[]{:S(2)}) collective-permute-start(bf16[3,96,48]{1,2,0:T(8,128)(2,1)S(1)} %copy-done.15), channel_id=1, source_target_pairs={{0,2},{2,4},{4,6},{6,0},{1,3},{3,5},{5,7},{7,1},{8,10},{10,12},{12... | collective-permute-start | bytes 82952 | tf_op jit(solution)/shard_map/ppermute | solution.py:63
  25.7 1.6 %collective-permute-start.1 = (bf16[3,96,48]{1,2,0:T(8,128)(2,1)S(1)}, bf16[3,96,48]{1,2,0:T(8,128)(2,1)S(1)}, u32[]{:S(2)}, u32[]{:S(2)}) collective-permute-start(bf16[3,96,48]{1,2,0:T(8,128)(2,1)S(1)} %copy-done.15), channel_id=1, source_target_pairs={{0,4},{2,6},{4,0},{6,2},{1,5},{3,7},{5,1},{7,3},{8,12},{10,14},{12... | collective-permute-start | bytes 82952 | tf_op jit(solution)/shard_map/ppermute | solution.py:63
  27.3 0.8 collective-permute-start.2
  28.1 0.7 copy.78
  28.8 3.3 %all-to-all-start.1 = ((bf16[8,1,16,384]{3,0,1,2:T(8,128)(2,1)}), bf16[8,1,16,384]{3,0,1,2:T(8,128)(2,1)S(1)}, u32[]{:S(2)}, u32[]{:S(2)}) async-start(bf16[8,1,16,384]{3,0,1,2:T(8,128)(2,1)} %copy.78), calls=%async_computation.1 | async-start | bytes 196608 | tf_op jit(solution)/shard_map/all_to_all | solution.py:112
  32.2 0.6 gather_fusion
  33.1 22.7 %all_gather.6 = bf16[3,384,384]{1,2,0:T(8,128)(2,1)S(1)} all-gather(bf16[3,384,48]{1,2,0:T(8,128)(2,1)S(1)} %reshape.890), channel_id=1, replica_groups=mesh['gz'=4,'gy'=4,'gx'=2] {'gz','gx'}, dimensions={2}, use_global_device_ids=true | all-gather | bytes 995328 | tf_op jit(solution)/shard_map/all_gather | solution.py:69
  55.8 4.9 %all-to-all-start = ((bf16[8,1,16,384]{3,2,1,0:T(8,128)(2,1)}), bf16[8,1,16,384]{3,2,1,0:T(8,128)(2,1)S(1)}, u32[]{:S(2)}, u32[]{:S(2)}) async-start(bf16[8,1,16,384]{3,2,1,0:T(8,128)(2,1)} %param.5), calls=%async_computation | async-start | bytes 196608 | tf_op jit(solution)/shard_map/all_to_all | solution.py:104
  60.9 0.7 add.159
  61.5 1.6 %convolution_bitcast_fusion.2 = f32[1,32,4,1152]{3,1,2,0:T(8,128)S(1)} fusion(bf16[3,384,1152]{1,2,0:T(8,128)(2,1)} %all-gather.2.cloned.1.call-done, bf16[8,1,4,4,384]{4,0,3,2,1:T(8,128)(2,1)S(1)} %bitcast.588, f32[4,8,4]{1,2,0:T(4,128)S(1)} %get-tuple-element.16), kind=kOutput, calls=%fused_computation.4 | convolution fusion | flops 113393664 | bytes 1573376 | tf_op jit(solution)/shard_map/jvp()/dot_general | solution.py:30
  63.4 0.3 fusion.88
  63.7 0.3 copy-done.6
  64.3 0.3 copy-done.8
  65.0 0.3 fusion.334
  65.6 0.4 fusion.1
  66.3 0.7 copy.86
  67.0 1.3 all-to-all-done
  68.3 4.8 %all-to-all-start.2 = ((bf16[32,1,4,384]{3,2,1,0:T(4,128)(2,1)}), bf16[32,1,4,384]{3,2,1,0:T(4,128)(2,1)S(1)}, u32[]{:S(2)}, u32[]{:S(2)}) async-start(bf16[32,1,4,384]{3,2,1,0:T(4,128)(2,1)} %copy.86), calls=%async_computation.2 | async-start | bytes 196608 | tf_op jit(solution)/shard_map/all_to_all | solution.py:87
  73.3 7.4 %all-to-all-done.2 = bf16[32,1,4,384]{3,2,1,0:T(4,128)(2,1)S(1)} async-done(((bf16[32,1,4,384]{3,2,1,0:T(4,128)(2,1)}), bf16[32,1,4,384]{3,2,1,0:T(4,128)(2,1)S(1)}, u32[]{:S(2)}, u32[]{:S(2)}) %all-to-all-start.2) | async-done | bytes 98336 | tf_op jit(solution)/shard_map/all_to_all | solution.py:87
  80.8 0.6 multiply_add_fusion
  81.5 1.6 %convolution_bitcast_fusion.1 = f32[1,4,32,1152]{3,2,1,0:T(8,128)S(1)} fusion(bf16[4,32,384]{2,1,0:T(8,128)(2,1)S(1)} %convert_element_type.547, bf16[3,384,1152]{1,2,0:T(8,128)(2,1)} %all-gather.2.cloned.1.call-done), kind=kOutput, calls=%fused_computation.3 | convolution fusion | flops 113246208 | bytes 1572864 | tf_op jit(solution)/shard_map/jvp()/dot_general | solution.py:30
  83.4 0.3 fusion.87
  83.7 0.7 copy_bitcast_fusion
  84.7 1.0 reshape.923
  85.7 1.0 fusion.204
  86.7 0.8 fusion.335
  87.5 0.3 multiply_reduce_fusion.3
  87.8 0.3 multiply_reduce_fusion.6
  88.2 0.4 convolution_bitcast_fusion
  88.9 0.3 fusion.84
  89.8 0.3 fusion.336
  90.4 0.7 fusion.129
  91.2 0.3 fusion.10
  92.1 0.3 add_add_fusion.8
  92.6 0.3 add_add_fusion.7
  92.9 0.4 multiply_reduce_fusion.5
  93.7 0.7 multiply_reduce_fusion.2
  94.4 0.4 multiply_reduce_fusion.9
  94.9 0.5 multiply_reduce_fusion.1
  95.7 0.3 add_add_fusion.5
  96.0 0.9 fusion.80
  96.9 1.4 %add.158 = f32[4,32]{1,0:T(4,128)} reshape(f32[4,2,4,4]{3,2,1,0:T(4,128)} %get-tuple-element.13) | data formatting | bytes 1024 | tf_op jit(solution)/shard_map/jvp()/add | solution.py:29
  98.3 1.0 add_add_fusion.4
  99.3 1.6 %multiply_reduce_fusion.4 = (f32[4,32]{1,0:T(4,128)S(1)}, f32[4,32,384]{2,1,0:T(8,128)S(1)}) fusion(f32[4,32,384]{2,1,0:T(8,128)S(1)} %reshape.923, bf16[3,384,1152]{1,2,0:T(8,128)(2,1)} %all-gather.2.cloned.1.call-done, f32[1,4,32,384]{3,2,1,0:T(8,128)S(1)} %add_add_fusion.4, f32[1,4,32,384]{3,2,1,0:T(8,128)S(1)} %add_add_fusion.5, ...), kind=kOutput, calls=%fused_computation.248 | convolution fusion | flops 113885056 | bytes 1769984 | tf_op jit(solution)/shard_map/transpose(jvp())/dot_general | solution.py:30
  101.2 0.7 copy.92
  101.8 2.7 %all-to-all-start.3 = ((bf16[32,1,4,384]{3,2,1,0:T(4,128)(2,1)}), bf16[32,1,4,384]{3,2,1,0:T(4,128)(2,1)S(1)}, u32[]{:S(2)}, u32[]{:S(2)}) async-start(bf16[32,1,4,384]{3,2,1,0:T(4,128)(2,1)} %bitcast.118), calls=%async_computation.3 | async-start | bytes 196608 | tf_op jit(solution)/shard_map/all_to_all | solution.py:98
  104.6 7.4 %all-to-all-done.3 = bf16[32,1,4,384]{3,2,1,0:T(4,128)(2,1)S(1)} async-done(((bf16[32,1,4,384]{3,2,1,0:T(4,128)(2,1)}), bf16[32,1,4,384]{3,2,1,0:T(4,128)(2,1)S(1)}, u32[]{:S(2)}, u32[]{:S(2)}) %all-to-all-start.3) | async-done | bytes 98336 | tf_op jit(solution)/shard_map/all_to_all | solution.py:98
  112.5 0.7 fusion.125
  113.3 0.3 fusion.9
  113.6 0.5 copy-done.12
  114.4 0.4 copy-done.7
  115.2 0.3 add_add_fusion.2
  115.7 0.3 add_add_fusion.1
  116.1 1.6 %fusion.181 = (f32[32,4]{0,1:T(4,128)S(1)}, f32[32,4,384]{2,0,1:T(8,128)S(1)}) fusion(bf16[3,384,1152]{1,2,0:T(8,128)(2,1)} %all-gather.2.cloned.1.call-done, f32[1,32,4,384]{3,1,2,0:T(8,128)S(1)} %add_add_fusion.1, f32[1,32,4,384]{3,1,2,0:T(8,128)S(1)} %add_add_fusion.2, bf16[1,32,4,384]{3,1,2,0:T(8,128)(2,1)S(1)} %fusion.72, ...), kind=kOutput, calls=%fused_computation.245 | convolution fusion | flops 113934208 | bytes 1671680 | tf_op jit(solution)/shard_map/transpose(jvp())/dot_general | solution.py:30
  117.9 6.7 %all_to_all.42 = bf16[32,1,4,384]{3,2,1,0:T(4,128)(2,1)S(1)} all-to-all(bf16[32,1,4,384]{3,2,1,0:T(4,128)(2,1)S(1)} %copy.96), channel_id=1, replica_groups=mesh['gz'=4,'gy'=4,'gx'=2] {'gz'}, dimensions={0} | all-to-all | bytes 196608 | tf_op jit(solution)/shard_map/all_to_all | solution.py:121
  124.6 0.7 all_to_all.36
  (105 shorter events, 7.7 us)
Async XLA Ops:
  6.5 55.0 %all-gather.2.cloned.1.call-start = ((), (), s32[]{:S(2)}) async-start(), calls=%async_computation.5 | async-start | bytes 2985984 | tf_op jit(solution)/shard_map/all_gather | solution.py:68
  6.5 9.3 %collective-permute-start.3 = (bf16[3,96,144]{1,2,0:T(8,128)(2,1)}, bf16[3,96,144]{1,2,0:T(8,128)(2,1)S(1)}, u32[]{:S(2)}, u32[]{:S(2)}) collective-permute-start(bf16[3,96,144]{1,2,0:T(8,128)(2,1)} %param.6), channel_id=1, source_target_pairs={{0,2},{2,4},{4,6},{6,0},{1,3},{3,5},{5,7},{7,1},{8,10},{10,12},{12... | collective-permute-start | bytes 248840 | tf_op jit(solution)/shard_map/ppermute | solution.py:63
  9.6 10.1 %collective-permute-start.4 = (bf16[3,96,144]{1,2,0:T(8,128)(2,1)}, bf16[3,96,144]{1,2,0:T(8,128)(2,1)S(1)}, u32[]{:S(2)}, u32[]{:S(2)}) collective-permute-start(bf16[3,96,144]{1,2,0:T(8,128)(2,1)} %param.6), channel_id=1, source_target_pairs={{0,4},{2,6},{4,0},{6,2},{1,5},{3,7},{5,1},{7,3},{8,12},{10,14},{12... | collective-permute-start | bytes 248840 | tf_op jit(solution)/shard_map/ppermute | solution.py:63
  12.2 7.5 %collective-permute-start.5 = (bf16[3,96,144]{1,2,0:T(8,128)(2,1)}, bf16[3,96,144]{1,2,0:T(8,128)(2,1)S(1)}, u32[]{:S(2)}, u32[]{:S(2)}) collective-permute-start(bf16[3,96,144]{1,2,0:T(8,128)(2,1)} %param.6), channel_id=1, source_target_pairs={{0,6},{2,0},{4,2},{6,4},{1,7},{3,1},{5,3},{7,5},{8,14},{10,8},{12,... | collective-permute-start | bytes 248840 | tf_op jit(solution)/shard_map/ppermute | solution.py:63
  21.5 1.3 copy-start.15
  21.5 6.6 %copy-start.10 = (bf16[8,1,16,384]{3,2,1,0:T(8,128)(2,1)S(1)}, bf16[8,1,16,384]{3,2,1,0:T(8,128)(2,1)}, u32[]{:S(2)}) copy-start(bf16[8,1,16,384]{3,2,1,0:T(8,128)(2,1)} %param.4) | copy-start | bytes 294916
  22.8 9.3 %collective-permute-start = (bf16[3,96,48]{1,2,0:T(8,128)(2,1)S(1)}, bf16[3,96,48]{1,2,0:T(8,128)(2,1)S(1)}, u32[]{:S(2)}, u32[]{:S(2)}) collective-permute-start(bf16[3,96,48]{1,2,0:T(8,128)(2,1)S(1)} %copy-done.15), channel_id=1, source_target_pairs={{0,2},{2,4},{4,6},{6,0},{1,3},{3,5},{5,7},{7,1},{8,10},{10,12},{12... | collective-permute-start | bytes 82952 | tf_op jit(solution)/shard_map/ppermute | solution.py:63
  25.7 6.5 %collective-permute-start.1 = (bf16[3,96,48]{1,2,0:T(8,128)(2,1)S(1)}, bf16[3,96,48]{1,2,0:T(8,128)(2,1)S(1)}, u32[]{:S(2)}, u32[]{:S(2)}) collective-permute-start(bf16[3,96,48]{1,2,0:T(8,128)(2,1)S(1)} %copy-done.15), channel_id=1, source_target_pairs={{0,4},{2,6},{4,0},{6,2},{1,5},{3,7},{5,1},{7,3},{8,12},{10,14},{12... | collective-permute-start | bytes 82952 | tf_op jit(solution)/shard_map/ppermute | solution.py:63
  27.3 4.9 %collective-permute-start.2 = (bf16[3,96,48]{1,2,0:T(8,128)(2,1)S(1)}, bf16[3,96,48]{1,2,0:T(8,128)(2,1)S(1)}, u32[]{:S(2)}, u32[]{:S(2)}) collective-permute-start(bf16[3,96,48]{1,2,0:T(8,128)(2,1)S(1)} %copy-done.15), channel_id=1, source_target_pairs={{0,6},{2,0},{4,2},{6,4},{1,7},{3,1},{5,3},{7,5},{8,14},{10,8},{12,... | collective-permute-start | bytes 82952 | tf_op jit(solution)/shard_map/ppermute | solution.py:63
  28.8 27.1 %all-to-all-start.1 = ((bf16[8,1,16,384]{3,0,1,2:T(8,128)(2,1)}), bf16[8,1,16,384]{3,0,1,2:T(8,128)(2,1)S(1)}, u32[]{:S(2)}, u32[]{:S(2)}) async-start(bf16[8,1,16,384]{3,0,1,2:T(8,128)(2,1)} %copy.78), calls=%async_computation.1 | async-start | bytes 196608 | tf_op jit(solution)/shard_map/all_to_all | solution.py:112
  32.1 59.4 %copy-start.20 = (bf16[6,384]{1,0:T(8,128)(2,1)}, bf16[6,384]{1,0:T(8,128)(2,1)S(1)}, u32[]{:S(2)}) copy-start(bf16[6,384]{1,0:T(8,128)(2,1)S(1)} %get-tuple-element.22) | copy-start | bytes 13828
  55.8 12.4 %all-to-all-start = ((bf16[8,1,16,384]{3,2,1,0:T(8,128)(2,1)}), bf16[8,1,16,384]{3,2,1,0:T(8,128)(2,1)S(1)}, u32[]{:S(2)}, u32[]{:S(2)}) async-start(bf16[8,1,16,384]{3,2,1,0:T(8,128)(2,1)} %param.5), calls=%async_computation | async-start | bytes 196608 | tf_op jit(solution)/shard_map/all_to_all | solution.py:104
  63.4 0.6 copy-start.6
  64.0 0.6 copy-start.8
  65.0 0.6 copy-start.11
  65.0 1.0 copy-start.13
  65.3 0.9 copy-start.2
  65.3 0.9 copy-start.16
  68.3 12.4 %all-to-all-start.2 = ((bf16[32,1,4,384]{3,2,1,0:T(4,128)(2,1)}), bf16[32,1,4,384]{3,2,1,0:T(4,128)(2,1)S(1)}, u32[]{:S(2)}, u32[]{:S(2)}) async-start(bf16[32,1,4,384]{3,2,1,0:T(4,128)(2,1)} %copy.86), calls=%async_computation.2 | async-start | bytes 196608 | tf_op jit(solution)/shard_map/all_to_all | solution.py:87
  83.7 3.8 %copy-start.4 = (f32[4,32,6]{1,2,0:T(8,128)}, f32[4,32,6]{1,2,0:T(8,128)S(1)}, u32[]{:S(2)}) copy-start(f32[4,32,6]{1,2,0:T(8,128)S(1)} %fusion.87) | copy-start | bytes 9220
  85.7 2.5 %copy-start = (bf16[3,384,1152]{1,2,0:T(8,128)(2,1)S(1)}, bf16[3,384,1152]{1,2,0:T(8,128)(2,1)}, u32[]{:S(2)}) copy-start(bf16[3,384,1152]{1,2,0:T(8,128)(2,1)} %all-gather.2.cloned.1.call-done) | copy-start | bytes 7962628
  94.9 1.2 copy-start.5
  94.9 3.4 %copy-start.1 = (f32[4,32,384]{2,1,0:T(8,128)S(1)}, f32[4,32,384]{2,1,0:T(8,128)}, u32[]{:S(2)}) copy-start(f32[4,32,384]{2,1,0:T(8,128)} %get-tuple-element.25) | copy-start | bytes 589828
  99.3 1.7 %copy-start.19 = (f32[4,32]{1,0:T(4,128)S(1)}, f32[4,32]{1,0:T(4,128)}, u32[]{:S(2)}) copy-start(f32[4,32]{1,0:T(4,128)} %add.158) | copy-start | bytes 1540
  99.3 5.3 %copy-start.17 = (f32[4,6,32]{2,1,0:T(8,128)S(1)}, f32[4,6,32]{2,1,0:T(8,128)}, u32[]{:S(2)}) copy-start(f32[4,6,32]{2,1,0:T(8,128)} %copy-done.16) | copy-start | bytes 9220
  101.0 11.2 %copy-start.3 = (f32[1,4,6,32,32]{3,4,2,1,0:T(8,128)S(1)}, f32[1,4,6,32,32]{3,4,2,1,0:T(8,128)}, u32[]{:S(2)}) copy-start(f32[1,4,6,32,32]{3,4,2,1,0:T(8,128)} %copy-done.2) | copy-start | bytes 294916
  101.8 10.2 %all-to-all-start.3 = ((bf16[32,1,4,384]{3,2,1,0:T(4,128)(2,1)}), bf16[32,1,4,384]{3,2,1,0:T(4,128)(2,1)S(1)}, u32[]{:S(2)}, u32[]{:S(2)}) async-start(bf16[32,1,4,384]{3,2,1,0:T(4,128)(2,1)} %bitcast.118), calls=%async_computation.3 | async-start | bytes 196608 | tf_op jit(solution)/shard_map/all_to_all | solution.py:98
  112.2 1.1 copy-start.14
  112.2 1.1 copy-start.21
  113.3 0.9 copy-start.12
  114.2 0.7 copy-start.7
  114.2 1.3 copy-start.9
  116.0 1.6 %copy-start.18 = (f32[32,4]{0,1:T(4,128)S(1)}, f32[32,4]{0,1:T(4,128)}, u32[]{:S(2)}) copy-start(f32[32,4]{0,1:T(4,128)} %add.159) | copy-start | bytes 1540
Sparse Core Ops, SparseCore 0:
  22.9 36.2 all-gather.1
